TPU v7x, 32 devices: a whole 2x2x4 slice. The times are simulated.
32 devices in a mesh: scene: 2 (over x), view: 16 (over z, y, core).
Axes of the slice: x: 2, y: 2, z: 4, core: 2. Of those that a mesh axis runs over, the one named last changes fastest.
Arguments:
- src_feat: bfloat16 [32, 32, 8192], P(('scene', 'view')), parts along dimension 0, may hold values from -6 to 6
- ref_feat: bfloat16 [32, 32, 512], P(('scene', 'view')), parts along dimension 0, may hold values from -6 to 6
- weight_table: bfloat16 [4, 128, 512], replicated, may hold values from -0.5 to 0.5
- src_block: int32 [32, 64, 4], P(('scene', 'view')), parts along dimension 0, may hold values from 0 to 63
- table_index: int32 [32, 64, 4], P(('scene', 'view')), parts along dimension 0, may hold values from 0 to 3, each once within a row
- block_count: int32 [32, 64], P(('scene', 'view')), parts along dimension 0, may hold values from 0 to 4, as said below
- depth_plane: int32 [32, 64], P(('scene', 'view')), parts along dimension 0, may hold values from 0 to 63
- kern_one: bfloat16 [3, 3, 3, 8, 8], replicated, may hold values from -0.4375 to 0.4375
- kern_two: bfloat16 [3, 3, 3, 8], replicated, may hold values from -0.4375 to 0.4375
Outputs:
- depth_score: float32 [128, 64, 128], P(('scene', 'view')), parts along dimension 0
There are 2 independent parts, one for each index of `scene`. A program takes and returns all parts, laid end to end along the dimension named above; an argument that names none is the same for every part. Nothing has to cross between parts.
Inputs may be any that keep to these rules, and one draw needn't show every extreme that they name: `block_count`: each entry is the number of live block slots of a unit, 0 for an empty unit; the share of live units differs between source views. `table_index`: the 4 table indices of a unit are distinct.
All inputs are finite; a program needn't handle non-finite values.
Results may differ from a plain program's by a relative error of at most 0.019.
Values may be sent and summed in bfloat16 or wider, within the bound.
No kernel may reach another device: no remote copies, remote signals or barrier semaphores. Data moves between devices by JAX's collectives and lax.ppermute only.
A program may use at most 128 MiB of HBM per device.

v0:
```python
import jax
import jax.numpy as jnp
from jax import lax
from jax.sharding import PartitionSpec as P

GROUPS = 8
DEPTH = 64
TROWS = 4


def with_halo(block, sides, width):
    for axis, dim in sides:
        count = lax.axis_size(axis)
        forward = [(i, i + 1) for i in range(count - 1)]
        backward = [(target, source) for source, target in forward]
        low = lax.ppermute(
            lax.slice_in_dim(block, block.shape[dim] - width, None, axis=dim), axis, forward
        )
        high = lax.ppermute(lax.slice_in_dim(block, 0, width, axis=dim), axis, backward)
        block = jnp.concatenate([low, block, high], axis=dim)
    return block


def convolve_full(padded, kernel):
    rows_out = padded.shape[0] - 2
    depth_len = padded.shape[2]
    columns = padded.shape[3]
    framed = jnp.pad(padded, ((0, 0), (0, 0), (1, 1), (1, 1)))
    carried = jnp.zeros((rows_out, kernel.shape[-1], depth_len, columns), jnp.float32)
    for depth_off in range(3):
        for row_off in range(3):
            for col_off in range(3):
                window = framed[
                    row_off : row_off + rows_out,
                    :,
                    depth_off : depth_off + depth_len,
                    col_off : col_off + columns,
                ]
                carried = carried + jnp.einsum(
                    "rcdw,ce->redw",
                    window,
                    kernel[depth_off, row_off, col_off],
                    preferred_element_type=jnp.float32,
                )
    return carried


def convolve_final(padded, kernel):
    rows_out = padded.shape[0] - 2
    depth_len = padded.shape[2]
    columns = padded.shape[3]
    framed = jnp.pad(padded, ((0, 0), (0, 0), (1, 1), (1, 1)))
    carried = jnp.zeros((rows_out, depth_len, columns), jnp.float32)
    for depth_off in range(3):
        for row_off in range(3):
            for col_off in range(3):
                window = framed[
                    row_off : row_off + rows_out,
                    :,
                    depth_off : depth_off + depth_len,
                    col_off : col_off + columns,
                ]
                carried = carried + jnp.einsum(
                    "rcdw,c->rdw",
                    window,
                    kernel[depth_off, row_off, col_off],
                    preferred_element_type=jnp.float32,
                )
    return carried


def pad_rows(volume):
    return with_halo(volume, (("view", 0),), 1)


def body(
    src_feat,
    ref_feat,
    weight_table,
    src_block,
    table_index,
    block_count,
    depth_plane,
    kern_one,
    kern_two,
):
    owners = lax.axis_size("view")
    features = src_feat[0]
    channels, spix = features.shape
    slots, block_width, tpix = weight_table.shape
    blocks = features.reshape(channels, spix // block_width, block_width).transpose(1, 0, 2)
    units = src_block.shape[1]
    cap = units // owners
    counts = block_count[0]
    live_slot = jnp.arange(slots)[None, :] < counts[:, None]
    chosen = (
        (table_index[0][:, :, None] == jnp.arange(slots)[None, None, :]) & live_slot[:, :, None]
    ).astype(jnp.bfloat16)
    depth_code = jnp.where(counts > 0, depth_plane[0], -1).astype(jnp.bfloat16)
    unit_rounds = 8
    per_round = units // unit_rounds
    index_groups = src_block[0].reshape(unit_rounds, per_round, slots)
    chosen_groups = chosen.reshape(unit_rounds, per_round, slots, slots)
    group_size = channels // GROUPS

    def resample(index_rows, chosen_rows):
        gathered = blocks[index_rows]
        arranged = jnp.einsum(
            "ujw,ujck->uwck", chosen_rows, gathered, preferred_element_type=jnp.float32
        ).astype(jnp.bfloat16)
        return jnp.einsum(
            "uwck,wkp->ucp", arranged, weight_table, preferred_element_type=jnp.float32
        ).astype(jnp.bfloat16)

    warped_all = lax.map(
        lambda packed: resample(packed[0], packed[1]), (index_groups, chosen_groups)
    )
    arriving, depth_tags = (
        lax.all_to_all(
            warped_all.reshape(owners, cap, channels, tpix),
            "view",
            split_axis=0,
            concat_axis=0,
            tiled=True,
        ),
        lax.all_to_all(
            depth_code.reshape(owners, cap), "view", split_axis=0, concat_axis=0, tiled=True
        ),
    )
    products = ref_feat[0].astype(jnp.float32)[None, None] * arriving.astype(jnp.float32)
    received = (
        (products.reshape(owners * cap, GROUPS, group_size, tpix).sum(axis=2) * (GROUPS / channels))
        .astype(jnp.bfloat16)
        .reshape(owners * cap, GROUPS * tpix)
    )
    onehot = (
        depth_tags.reshape(-1)[None, :] == jnp.arange(DEPTH).astype(jnp.bfloat16)[:, None]
    ).astype(jnp.bfloat16)
    summed = jnp.dot(onehot, received, preferred_element_type=jnp.float32)
    tallies = jnp.sum(onehot.astype(jnp.float32), axis=1)
    cost_volume = (summed / jnp.maximum(tallies, 1.0)[:, None]).astype(jnp.bfloat16)
    columns = tpix // TROWS
    volume = cost_volume.reshape(DEPTH, GROUPS, TROWS, columns).transpose(2, 1, 0, 3)
    hidden = jax.nn.relu(convolve_full(pad_rows(volume), kern_one)).astype(jnp.bfloat16)
    scores = convolve_final(pad_rows(hidden), kern_two)
    return scores


def solution(mesh):
    in_specs = (
        P(("scene", "view"), None, None),
        P(("scene", "view"), None, None),
        P(),
        P(("scene", "view"), None, None),
        P(("scene", "view"), None, None),
        P(("scene", "view"), None),
        P(("scene", "view"), None),
        P(),
        P(),
    )
    out_specs = P(("scene", "view"), None, None)
    return jax.shard_map(body, mesh=mesh, in_specs=in_specs, out_specs=out_specs, check_vma=False)
```

profile of v0, /device:TPU:13, one launch (start us, length us, event | category | flops | bytes accessed | tf_op | source)
XLA Modules:
  0.0 139.8 jit_solution(11020404430611025248)
XLA Ops:
  1.5 6.6 %all-to-all-start = ((bf16[16,1,4]{2,1,0:T(2,128)(2,1)}), bf16[16,1,4]{2,1,0:T(2,128)(2,1)S(1)}, u32[]{:S(2)}, u32[]{:S(2)}) async-start(bf16[16,1,4]{2,1,0:T(2,128)(2,1)} %convert_element_type.80), calls=%async_computation | async-start | bytes 16384 | tf_op jit(solution)/shard_map/all_to_all | solution.py:126
  8.5 1.2 reduce.8
  10.6 1.2 copy.257
  12.2 17.9 %while.10 = (s32[]{:T(128)}, bf16[8,8,32,512]{3,2,1,0:T(8,128)(2,1)}, bf16[8,8,4,4]{1,3,2,0:T(4,128)(2,1)S(1)}, s32[8,8,4]{1,0,2:T(8,128)S(1)}, bf16[64,32,128]{...) while((s32[]{:T(128)}, bf16[8,8,32,512]{3,2,1,0:T(8,128)(2,1)}, ...), condition=%wide.region_1.2_spmd, body=%wide.region_0.1_spmd.sunk | while | flops 135529568 | bytes 2104405 | solution.py:115
  13.5 1.0 fusion.280
  15.7 1.0 fusion.280
  20.2 1.0 fusion.280
  22.4 1.0 fusion.280
  24.7 1.0 fusion.280
  26.9 1.0 fusion.280
  29.1 1.0 fusion.280
  30.2 6.1 %all-to-all-start.1 = ((bf16[16,4,32,512]{3,2,1,0:T(8,128)(2,1)}), bf16[16,4,32,512]{3,2,1,0:T(8,128)(2,1)S(1)}, u32[]{:S(2)}, u32[]{:S(2)}) async-start(bf16[16,4,32,512]{3,2,1,0:T(8,128)(2,1)} %bitcast.494), calls=%async_computation.1 | async-start | bytes 4194304 | tf_op jit(solution)/shard_map/all_to_all | solution.py:119
  36.7 47.1 %all-to-all-done.1 = bf16[16,4,32,512]{3,2,1,0:T(8,128)(2,1)S(1)} async-done(((bf16[16,4,32,512]{3,2,1,0:T(8,128)(2,1)}), bf16[16,4,32,512]{3,2,1,0:T(8,128)(2,1)S(1)}, u32[]{:S(2)}, u32[]{:S(2)}) %all-to-all-start.1) | async-done | bytes 2097184 | tf_op jit(solution)/shard_map/all_to_all | solution.py:119
  83.7 2.6 %convert_multiply_fusion = f32[16,4,32,512]{3,2,1,0:T(8,128)} fusion(bf16[16,4,32,512]{3,2,1,0:T(8,128)(2,1)S(1)} %all-to-all-done.1, f32[32,512]{1,0:T(8,128)S(1)} %bitcast_convert_fusion), kind=kLoop, calls=%fused_computation.19 | loop fusion | flops 2097152 | bytes 6356992 | tf_op jit(solution)/shard_map/mul | solution.py:130
  86.3 5.2 %reshape.122 = f32[64,8,4,512]{3,2,1,0:T(4,128)} reshape(f32[16,4,32,512]{3,2,1,0:T(8,128)} %convert_multiply_fusion) | data formatting | bytes 8388608 | tf_op jit(solution)/shard_map/reshape | solution.py:132
  91.4 4.8 %reduce_sum.18 = f32[64,8,512]{2,1,0:T(8,128)S(1)} reduce(f32[64,8,4,512]{3,2,1,0:T(4,128)} %reshape.122, f32[]{:T(128)} %constant.12.clone.1), dimensions={2}, to_apply=%region_2.3 | reduce | flops 786432 | bytes 5242884 | tf_op jit(solution)/shard_map/reduce_sum | solution.py:132
  97.4 3.6 %collective-permute-start = (bf16[1,8,64,128]{3,1,2,0:T(8,128)(2,1)S(1)}, bf16[1,8,64,128]{3,1,2,0:T(8,128)(2,1)S(1)}, u32[]{:S(2)}, u32[]{:S(2)}) collective-permute-start(bf16[1,8,64,128]{3,1,2,0:T(8,128)(2,1)S(1)} %get-tuple-element.70), channel_id=1, source_target_pairs={{0,1},{1,2},{2,3},{3,4},{4,5},{5,6},{6,7},{7,8},{8,9},{9,10},{10,1... | collective-permute-start | bytes 393224 | tf_op jit(solution)/shard_map/ppermute | solution.py:16
  101.0 2.1 %collective-permute-start.1 = (bf16[1,8,64,128]{3,1,2,0:T(8,128)(2,1)S(1)}, bf16[1,8,64,128]{3,1,2,0:T(8,128)(2,1)S(1)}, u32[]{:S(2)}, u32[]{:S(2)}) collective-permute-start(bf16[1,8,64,128]{3,1,2,0:T(8,128)(2,1)S(1)} %get-tuple-element.71), channel_id=1, source_target_pairs={{1,0},{2,1},{3,2},{4,3},{5,4},{6,5},{7,6},{8,7},{9,8},{10,9},{11,1... | collective-permute-start | bytes 393224 | tf_op jit(solution)/shard_map/ppermute | solution.py:19
  103.5 4.7 %collective-permute-done.1 = bf16[1,8,64,128]{3,1,2,0:T(8,128)(2,1)S(1)} collective-permute-done((bf16[1,8,64,128]{3,1,2,0:T(8,128)(2,1)S(1)}, bf16[1,8,64,128]{3,1,2,0:T(8,128)(2,1)S(1)}, u32[]{:S(2)}, u32[]{:S(2)}) %collective-permute-start.1) | collective-permute-done | bytes 131104 | tf_op jit(solution)/shard_map/ppermute | solution.py:19
  108.2 1.5 %fusion.17 = bf16[6,8,66,130]{3,1,2,0:T(8,128)(2,1)S(1)} fusion(bf16[1,8,64,128]{3,1,2,0:T(8,128)(2,1)S(1)} %collective-permute-done.1, bf16[4,8,64,128]{3,1,2,0:T(8,128)(2,1)S(1)} %bitcast.489, bf16[1,8,64,128]{3,1,2,0:T(8,128)(2,1)S(1)} %collective-permute-done), kind=kLoop, calls=%fused_computation.32 | loop fusion | flops 7824960 | bytes 1610112 | tf_op jit(solution)/shard_map/concatenate | solution.py:20
  119.9 1.9 %collective-permute-start.2 = (bf16[1,8,64,128]{3,1,2,0:T(8,128)(2,1)S(1)}, bf16[1,8,64,128]{3,1,2,0:T(8,128)(2,1)S(1)}, u32[]{:S(2)}, u32[]{:S(2)}) collective-permute-start(bf16[1,8,64,128]{3,1,2,0:T(8,128)(2,1)S(1)} %get-tuple-element.68), channel_id=1, source_target_pairs={{0,1},{1,2},{2,3},{3,4},{4,5},{5,6},{6,7},{7,8},{8,9},{9,10},{10,1... | collective-permute-start | bytes 393224 | tf_op jit(solution)/shard_map/ppermute | solution.py:16
  121.8 2.6 %collective-permute-start.3 = (bf16[1,8,64,128]{3,1,2,0:T(8,128)(2,1)S(1)}, bf16[1,8,64,128]{3,1,2,0:T(8,128)(2,1)S(1)}, u32[]{:S(2)}, u32[]{:S(2)}) collective-permute-start(bf16[1,8,64,128]{3,1,2,0:T(8,128)(2,1)S(1)} %get-tuple-element.69), channel_id=1, source_target_pairs={{1,0},{2,1},{3,2},{4,3},{5,4},{6,5},{7,6},{8,7},{9,8},{10,9},{11,1... | collective-permute-start | bytes 393224 | tf_op jit(solution)/shard_map/ppermute | solution.py:19
  124.7 4.2 %collective-permute-done.3 = bf16[1,8,64,128]{3,1,2,0:T(8,128)(2,1)S(1)} collective-permute-done((bf16[1,8,64,128]{3,1,2,0:T(8,128)(2,1)S(1)}, bf16[1,8,64,128]{3,1,2,0:T(8,128)(2,1)S(1)}, u32[]{:S(2)}, u32[]{:S(2)}) %collective-permute-start.3) | collective-permute-done | bytes 131104 | tf_op jit(solution)/shard_map/ppermute | solution.py:19
  129.0 1.5 %select_maximum_fusion = bf16[6,8,66,130]{3,1,2,0:T(8,128)(2,1)S(1)} fusion(bf16[1,8,64,128]{3,1,2,0:T(8,128)(2,1)S(1)} %collective-permute-done.3, bf16[4,8,64,128]{3,1,2,0:T(8,128)(2,1)S(1)} %fusion.44, bf16[1,8,64,128]{3,1,2,0:T(8,128)(2,1)S(1)} %collective-permute-done.2), kind=kLoop, calls=%fused_computation.23 | loop fusion | flops 7824960 | bytes 1610112 | tf_op jit(solution)/shard_map/concatenate | solution.py:20
  (165 shorter events, 35.3 us)
Async XLA Ops:
  0.0 12.1 %copy-start.3 = (s32[1,64,4]{1,2,0:T(4,128)S(1)}, s32[1,64,4]{1,2,0:T(4,128)}, u32[]{:S(2)}) copy-start(s32[1,64,4]{1,2,0:T(4,128)} %param.14) | copy-start | bytes 3076
  0.0 12.2 %copy-start.4 = (bf16[4,128,512]{2,1,0:T(8,128)(2,1)S(1)}, bf16[4,128,512]{2,1,0:T(8,128)(2,1)}, u32[]{:S(2)}) copy-start(bf16[4,128,512]{2,1,0:T(8,128)(2,1)} %param.13) | copy-start | bytes 1572868
  1.5 28.7 %all-to-all-start = ((bf16[16,1,4]{2,1,0:T(2,128)(2,1)}), bf16[16,1,4]{2,1,0:T(2,128)(2,1)S(1)}, u32[]{:S(2)}, u32[]{:S(2)}) async-start(bf16[16,1,4]{2,1,0:T(2,128)(2,1)} %convert_element_type.80), calls=%async_computation | async-start | bytes 16384 | tf_op jit(solution)/shard_map/all_to_all | solution.py:126
  30.2 6.2 %copy-start.2 = (bf16[1,32,512]{2,1,0:T(8,128)(2,1)S(1)}, bf16[1,32,512]{2,1,0:T(8,128)(2,1)}, u32[]{:S(2)}) copy-start(bf16[1,32,512]{2,1,0:T(8,128)(2,1)} %param.12) | copy-start | bytes 98308
  30.2 53.6 %all-to-all-start.1 = ((bf16[16,4,32,512]{3,2,1,0:T(8,128)(2,1)}), bf16[16,4,32,512]{3,2,1,0:T(8,128)(2,1)S(1)}, u32[]{:S(2)}, u32[]{:S(2)}) async-start(bf16[16,4,32,512]{3,2,1,0:T(8,128)(2,1)} %bitcast.494), calls=%async_computation.1 | async-start | bytes 4194304 | tf_op jit(solution)/shard_map/all_to_all | solution.py:119
  97.0 6.2 %copy-start.1 = (bf16[3,3,3,8,8]{4,3,2,1,0:T(8,128)(2,1)S(1)}, bf16[3,3,3,8,8]{4,3,2,1,0:T(8,128)(2,1)}, u32[]{:S(2)}) copy-start(bf16[3,3,3,8,8]{4,3,2,1,0:T(8,128)(2,1)} %param.18) | copy-start | bytes 10372
  97.4 6.0 %collective-permute-start = (bf16[1,8,64,128]{3,1,2,0:T(8,128)(2,1)S(1)}, bf16[1,8,64,128]{3,1,2,0:T(8,128)(2,1)S(1)}, u32[]{:S(2)}, u32[]{:S(2)}) collective-permute-start(bf16[1,8,64,128]{3,1,2,0:T(8,128)(2,1)S(1)} %get-tuple-element.70), channel_id=1, source_target_pairs={{0,1},{1,2},{2,3},{3,4},{4,5},{5,6},{6,7},{7,8},{8,9},{9,10},{10,1... | collective-permute-start | bytes 393224 | tf_op jit(solution)/shard_map/ppermute | solution.py:16
  101.0 7.2 %collective-permute-start.1 = (bf16[1,8,64,128]{3,1,2,0:T(8,128)(2,1)S(1)}, bf16[1,8,64,128]{3,1,2,0:T(8,128)(2,1)S(1)}, u32[]{:S(2)}, u32[]{:S(2)}) collective-permute-start(bf16[1,8,64,128]{3,1,2,0:T(8,128)(2,1)S(1)} %get-tuple-element.71), channel_id=1, source_target_pairs={{1,0},{2,1},{3,2},{4,3},{5,4},{6,5},{7,6},{8,7},{9,8},{10,9},{11,1... | collective-permute-start | bytes 393224 | tf_op jit(solution)/shard_map/ppermute | solution.py:19
  119.0 5.4 %copy-start = (bf16[3,3,3,8]{3,2,1,0:T(4,128)(2,1)S(1)}, bf16[3,3,3,8]{3,2,1,0:T(4,128)(2,1)}, u32[]{:S(2)}) copy-start(bf16[3,3,3,8]{3,2,1,0:T(4,128)(2,1)} %param.19) | copy-start | bytes 1300
  119.9 4.9 %collective-permute-start.2 = (bf16[1,8,64,128]{3,1,2,0:T(8,128)(2,1)S(1)}, bf16[1,8,64,128]{3,1,2,0:T(8,128)(2,1)S(1)}, u32[]{:S(2)}, u32[]{:S(2)}) collective-permute-start(bf16[1,8,64,128]{3,1,2,0:T(8,128)(2,1)S(1)} %get-tuple-element.68), channel_id=1, source_target_pairs={{0,1},{1,2},{2,3},{3,4},{4,5},{5,6},{6,7},{7,8},{8,9},{9,10},{10,1... | collective-permute-start | bytes 393224 | tf_op jit(solution)/shard_map/ppermute | solution.py:16
  121.8 7.2 %collective-permute-start.3 = (bf16[1,8,64,128]{3,1,2,0:T(8,128)(2,1)S(1)}, bf16[1,8,64,128]{3,1,2,0:T(8,128)(2,1)S(1)}, u32[]{:S(2)}, u32[]{:S(2)}) collective-permute-start(bf16[1,8,64,128]{3,1,2,0:T(8,128)(2,1)S(1)} %get-tuple-element.69), channel_id=1, source_target_pairs={{1,0},{2,1},{3,2},{4,3},{5,4},{6,5},{7,6},{8,7},{9,8},{10,9},{11,1... | collective-permute-start | bytes 393224 | tf_op jit(solution)/shard_map/ppermute | solution.py:19
where the time goes:
time: 140 us
  waiting for transfers between devices  56 us (40%)
  matrix products  29.7 us (21%)
  starting transfers between devices  22.9 us (16%)
  local copies, waits for them, and re-layouts  16.8 us (12%)
  other arithmetic  13.7 us (10%)
    all_to_all x1, waiting for transfers between devices, body(): lax.all_to_all(warped_all.reshape(owners, cap, channels, tpix), 'view', s...  47.1 us
    dot_general x27, matrix products, convolve_full(): jnp.einsum('rcdw,ce->redw', window, kernel[depth_off, row_off, col_off],...  10.4 us
    ppermute x2, waiting for transfers between devices, with_halo(): lax.ppermute(lax.slice_in_dim(block, 0, width, axis=dim), axis, backward)  8.95 us
    dot_general x27, matrix products, convolve_final(): jnp.einsum('rcdw,c->rdw', window, kernel[depth_off, row_off, col_off], pr...  8.64 us
    dot_general x8, matrix products, resample(): jnp.einsum('uwck,wkp->ucp', arranged, weight_table, preferred_element_typ...  8.06 us
    all_to_all x1, starting transfers between devices, body(): lax.all_to_all(depth_code.reshape(owners, cap), 'view', split_axis=0, con...  6.55 us
    all_to_all x1, starting transfers between devices, body(): lax.all_to_all(warped_all.reshape(owners, cap, channels, tpix), 'view', s...  6.14 us
    ppermute x2, starting transfers between devices, with_halo(): lax.ppermute(lax.slice_in_dim(block, block.shape[dim] - width, None, axis...  5.49 us
  transfers between devices with their start and end apart: 6, of which 3 were waited for; matrix products, arithmetic and copies ran while one was open for 16% of the time, Pallas kernels for 0%

commit v1 on v0

--- a/solution.py
+++ b/solution.py
@@ -103,38 +103,41 @@
     chosen_groups = chosen.reshape(unit_rounds, per_round, slots, slots)
     group_size = channels // GROUPS
 
-    def resample(index_rows, chosen_rows):
+    ref_all = lax.all_gather(ref_feat[0], "view")
+    ref_units = jnp.repeat(ref_all, cap, axis=0).reshape(unit_rounds, per_round, channels, tpix)
+
+    def resample(index_rows, chosen_rows, ref_rows):
         gathered = blocks[index_rows]
         arranged = jnp.einsum(
             "ujw,ujck->uwck", chosen_rows, gathered, preferred_element_type=jnp.float32
         ).astype(jnp.bfloat16)
-        return jnp.einsum(
+        warped = jnp.einsum(
             "uwck,wkp->ucp", arranged, weight_table, preferred_element_type=jnp.float32
         ).astype(jnp.bfloat16)
+        products = ref_rows.astype(jnp.float32) * warped.astype(jnp.float32)
+        return (
+            (products.reshape(per_round, GROUPS, group_size, tpix).sum(axis=2) * (GROUPS / channels))
+            .astype(jnp.bfloat16)
+            .reshape(per_round, GROUPS * tpix)
+        )
 
-    warped_all = lax.map(
-        lambda packed: resample(packed[0], packed[1]), (index_groups, chosen_groups)
-    )
-    arriving, depth_tags = (
-        lax.all_to_all(
-            warped_all.reshape(owners, cap, channels, tpix),
-            "view",
-            split_axis=0,
-            concat_axis=0,
-            tiled=True,
-        ),
-        lax.all_to_all(
-            depth_code.reshape(owners, cap), "view", split_axis=0, concat_axis=0, tiled=True
-        ),
-    )
-    products = ref_feat[0].astype(jnp.float32)[None, None] * arriving.astype(jnp.float32)
-    received = (
-        (products.reshape(owners * cap, GROUPS, group_size, tpix).sum(axis=2) * (GROUPS / channels))
-        .astype(jnp.bfloat16)
-        .reshape(owners * cap, GROUPS * tpix)
-    )
+    corr_all = lax.map(
+        lambda packed: resample(packed[0], packed[1], packed[2]),
+        (index_groups, chosen_groups, ref_units),
+    ).reshape(units, GROUPS * tpix)
+    tag_lanes = jnp.broadcast_to(depth_code[:, None], (units, 128))
+    payload = jnp.concatenate([corr_all, tag_lanes], axis=1)
+    arriving = lax.all_to_all(
+        payload.reshape(owners, cap, GROUPS * tpix + 128),
+        "view",
+        split_axis=0,
+        concat_axis=0,
+        tiled=True,
+    ).reshape(owners * cap, GROUPS * tpix + 128)
+    received = arriving[:, : GROUPS * tpix]
+    depth_tags = arriving[:, GROUPS * tpix]
     onehot = (
-        depth_tags.reshape(-1)[None, :] == jnp.arange(DEPTH).astype(jnp.bfloat16)[:, None]
+        depth_tags[None, :] == jnp.arange(DEPTH).astype(jnp.bfloat16)[:, None]
     ).astype(jnp.bfloat16)
     summed = jnp.dot(onehot, received, preferred_element_type=jnp.float32)
     tallies = jnp.sum(onehot.astype(jnp.float32), axis=1)

time: 140 us -> 118 us (0.84)
  waiting for transfers between devices: 56 us -> 22.9 us
  blocking collectives: 0 us -> 17.3 us
  other arithmetic: 13.7 us -> 9.02 us
  starting transfers between devices: 22.9 us -> 20.4 us
  local copies, waits for them, and re-layouts: 16.8 us -> 14.5 us
  matrix products: 29.7 us -> 31.6 us
    all_to_all x2 -> x1, waiting for transfers between devices: 47.1 us -> 14 us  [body(): lax.all_to_all(payload.reshape(owners, cap, GROUPS * tpix + 128), 'view',...]
    all_gather x0 -> x1, blocking collectives: none -> 17.3 us  [body(): ref_all = lax.all_gather(ref_feat[0], 'view')]
    reshape x1 -> x9, local copies, waits for them, and re-layouts: 5.17 us -> 1.31 us  [the longest x8 1.19 us: resample(): products.reshape(per_round, GROUPS, group_size, tpix).sum(axis=2)]
    mul x1 -> x0, other arithmetic: 2.56 us -> none  [body(): ref_feat[0].astype(jnp.float32)[None, None] * arriving.astype(jnp.float32)]
    all_to_all x2 -> x1, starting transfers between devices: 12.7 us -> 10.2 us  [body(): lax.all_to_all(payload.reshape(owners, cap, GROUPS * tpix + 128), 'view',...]
    reduce_sum x1 -> x8, other arithmetic: 4.83 us -> 2.47 us  [resample(): products.reshape(per_round, GROUPS, group_size, tpix).sum(axis=2)]
    dot_general x8, matrix products: 8.06 us -> 10 us  [resample(): jnp.einsum('uwck,wkp->ucp', arranged, weight_table, preferred_element_typ...]
    broadcast_in_dim x0 -> x2, local copies, waits for them, and re-layouts: none -> 1.7 us  [the longest x1 1.61 us: body(): jnp.repeat(ref_all, cap, axis=0)]
  transfers between devices with their start and end apart: 6 -> 5, of which waited for: 3 -> 3; matrix products, arithmetic and copies ran while one was open for 16% -> 1% of each run, Pallas kernels for 0% -> 0%
where the time goes in v1:
time: 118 us; the launch traced here: 117 us
  matrix products  31.6 us (27%)
  waiting for transfers between devices  22.9 us (19%)
  starting transfers between devices  20.4 us (17%)
  blocking collectives  17.3 us (15%)
  local copies, waits for them, and re-layouts  14.5 us (12%)
  other arithmetic  9.02 us (8%)
    all_gather x1, blocking collectives, body(): ref_all = lax.all_gather(ref_feat[0], 'view')  17.3 us
    all_to_all x1, waiting for transfers between devices, body(): lax.all_to_all(payload.reshape(owners, cap, GROUPS * tpix + 128), 'view',...  14 us
    dot_general x27, matrix products, convolve_full(): jnp.einsum('rcdw,ce->redw', window, kernel[depth_off, row_off, col_off],...  10.4 us
    all_to_all x1, starting transfers between devices, body(): lax.all_to_all(payload.reshape(owners, cap, GROUPS * tpix + 128), 'view',...  10.2 us
    dot_general x8, matrix products, resample(): jnp.einsum('uwck,wkp->ucp', arranged, weight_table, preferred_element_typ...  10 us
    ppermute x2, waiting for transfers between devices, with_halo(): lax.ppermute(lax.slice_in_dim(block, 0, width, axis=dim), axis, backward)  8.95 us
    dot_general x27, matrix products, convolve_final(): jnp.einsum('rcdw,c->rdw', window, kernel[depth_off, row_off, col_off], pr...  8.64 us
    ppermute x2, starting transfers between devices, with_halo(): lax.ppermute(lax.slice_in_dim(block, block.shape[dim] - width, None, axis...  5.51 us
  transfers between devices with their start and end apart: 5, of which 3 were waited for; matrix products, arithmetic and copies ran while one was open for 1% of the time, Pallas kernels for 0%

profile of v1, /device:TPU:13, one launch (start us, length us, event | category | flops | bytes accessed | tf_op | source)
XLA Modules:
  0.0 117.0 jit_solution(15932925088539117504)
XLA Ops:
  0.5 1.2 %reduce.9 = s32[64]{0:T(128)S(1)} reduce(s32[1,64]{1,0:T(1,128)} %param.16, s32[]{:T(128)} %broadcast.207), dimensions={0}, to_apply=%param.16.reduce_sub_computation.3 | reduce | bytes 516 | tf_op args[5]
  2.6 17.3 %all_gather.3 = bf16[16,32,512]{2,1,0:T(8,128)(2,1)S(1)} all-gather(bf16[1,32,512]{2,1,0:T(8,128)(2,1)} %param.12), channel_id=1, replica_groups=mesh['scene'=2,'view'=16] {'view'}, dimensions={0}, use_global_device_ids=true | all-gather | bytes 557056 | tf_op jit(solution)/shard_map/all_gather | solution.py:106
  19.9 1.2 copy.291
  21.6 1.6 %broadcast_in_dim.14 = bf16[16,4,32,512]{3,2,1,0:T(8,128)(2,1)} broadcast(bf16[16,32,512]{2,1,0:T(8,128)(2,1)S(1)} %all_gather.3), dimensions={0,2,3} | broadcast | bytes 2621440 | tf_op jit(solution)/shard_map/broadcast_in_dim | solution.py:107
  23.2 24.6 %while.10 = (s32[]{:T(128)}, bf16[8,8,4096]{2,1,0:T(8,128)(2,1)S(1)}, bf16[8,8,32,512]{3,2,1,0:T(8,128)(2,1)}, bf16[8,8,4,4]{1,3,2,0:T(4,128)(2,1)S(1)}, s32[8,8...) while((s32[]{:T(128)}, ...), condition=%wide.region_2.3_spmd, body=%wide.region_0.2_spmd.sunk | while | flops 136086624 | bytes 4790897 | solution.py:124
  24.4 1.3 %fusion.280 = f32[8,32,512]{2,1,0:T(8,128)S(1)} fusion(bf16[4,128,512]{2,1,0:T(8,128)(2,1)S(1)} %get-tuple-element.156, bf16[8,4,32,128]{3,1,2,0:T(4,128)(2,1)S(1)} %convolution_convert_fusion.2, bf16[8,8,32,512]{3,2,1,0:T(8,128)(2,1)} %get-tuple-element.152, s32[]{:T(128)} %get-tuple-element.141), kind=kOutput, calls=%fused_computation.4.clone.1 | convolution fusion | flops 134742016 | bytes 1572868 | tf_op jit(solution)/shard_map/while/body/eval_jaxpr/uwck,wkp->ucp/dot_general | solution.py:114
  27.5 1.3 %fusion.280 = f32[8,32,512]{2,1,0:T(8,128)S(1)} fusion(bf16[4,128,512]{2,1,0:T(8,128)(2,1)S(1)} %get-tuple-element.156, bf16[8,4,32,128]{3,1,2,0:T(4,128)(2,1)S(1)} %convolution_convert_fusion.2, bf16[8,8,32,512]{3,2,1,0:T(8,128)(2,1)} %get-tuple-element.152, s32[]{:T(128)} %get-tuple-element.141), kind=kOutput, calls=%fused_computation.4.clone.1 | convolution fusion | flops 134742016 | bytes 1572868 | tf_op jit(solution)/shard_map/while/body/eval_jaxpr/uwck,wkp->ucp/dot_general | solution.py:114
  30.6 1.3 %fusion.280 = f32[8,32,512]{2,1,0:T(8,128)S(1)} fusion(bf16[4,128,512]{2,1,0:T(8,128)(2,1)S(1)} %get-tuple-element.156, bf16[8,4,32,128]{3,1,2,0:T(4,128)(2,1)S(1)} %convolution_convert_fusion.2, bf16[8,8,32,512]{3,2,1,0:T(8,128)(2,1)} %get-tuple-element.152, s32[]{:T(128)} %get-tuple-element.141), kind=kOutput, calls=%fused_computation.4.clone.1 | convolution fusion | flops 134742016 | bytes 1572868 | tf_op jit(solution)/shard_map/while/body/eval_jaxpr/uwck,wkp->ucp/dot_general | solution.py:114
  33.6 1.3 %fusion.280 = f32[8,32,512]{2,1,0:T(8,128)S(1)} fusion(bf16[4,128,512]{2,1,0:T(8,128)(2,1)S(1)} %get-tuple-element.156, bf16[8,4,32,128]{3,1,2,0:T(4,128)(2,1)S(1)} %convolution_convert_fusion.2, bf16[8,8,32,512]{3,2,1,0:T(8,128)(2,1)} %get-tuple-element.152, s32[]{:T(128)} %get-tuple-element.141), kind=kOutput, calls=%fused_computation.4.clone.1 | convolution fusion | flops 134742016 | bytes 1572868 | tf_op jit(solution)/shard_map/while/body/eval_jaxpr/uwck,wkp->ucp/dot_general | solution.py:114
  36.7 1.3 %fusion.280 = f32[8,32,512]{2,1,0:T(8,128)S(1)} fusion(bf16[4,128,512]{2,1,0:T(8,128)(2,1)S(1)} %get-tuple-element.156, bf16[8,4,32,128]{3,1,2,0:T(4,128)(2,1)S(1)} %convolution_convert_fusion.2, bf16[8,8,32,512]{3,2,1,0:T(8,128)(2,1)} %get-tuple-element.152, s32[]{:T(128)} %get-tuple-element.141), kind=kOutput, calls=%fused_computation.4.clone.1 | convolution fusion | flops 134742016 | bytes 1572868 | tf_op jit(solution)/shard_map/while/body/eval_jaxpr/uwck,wkp->ucp/dot_general | solution.py:114
  39.8 1.3 %fusion.280 = f32[8,32,512]{2,1,0:T(8,128)S(1)} fusion(bf16[4,128,512]{2,1,0:T(8,128)(2,1)S(1)} %get-tuple-element.156, bf16[8,4,32,128]{3,1,2,0:T(4,128)(2,1)S(1)} %convolution_convert_fusion.2, bf16[8,8,32,512]{3,2,1,0:T(8,128)(2,1)} %get-tuple-element.152, s32[]{:T(128)} %get-tuple-element.141), kind=kOutput, calls=%fused_computation.4.clone.1 | convolution fusion | flops 134742016 | bytes 1572868 | tf_op jit(solution)/shard_map/while/body/eval_jaxpr/uwck,wkp->ucp/dot_general | solution.py:114
  42.8 1.3 %fusion.280 = f32[8,32,512]{2,1,0:T(8,128)S(1)} fusion(bf16[4,128,512]{2,1,0:T(8,128)(2,1)S(1)} %get-tuple-element.156, bf16[8,4,32,128]{3,1,2,0:T(4,128)(2,1)S(1)} %convolution_convert_fusion.2, bf16[8,8,32,512]{3,2,1,0:T(8,128)(2,1)} %get-tuple-element.152, s32[]{:T(128)} %get-tuple-element.141), kind=kOutput, calls=%fused_computation.4.clone.1 | convolution fusion | flops 134742016 | bytes 1572868 | tf_op jit(solution)/shard_map/while/body/eval_jaxpr/uwck,wkp->ucp/dot_general | solution.py:114
  45.9 1.3 %fusion.280 = f32[8,32,512]{2,1,0:T(8,128)S(1)} fusion(bf16[4,128,512]{2,1,0:T(8,128)(2,1)S(1)} %get-tuple-element.156, bf16[8,4,32,128]{3,1,2,0:T(4,128)(2,1)S(1)} %convolution_convert_fusion.2, bf16[8,8,32,512]{3,2,1,0:T(8,128)(2,1)} %get-tuple-element.152, s32[]{:T(128)} %get-tuple-element.141), kind=kOutput, calls=%fused_computation.4.clone.1 | convolution fusion | flops 134742016 | bytes 1572868 | tf_op jit(solution)/shard_map/while/body/eval_jaxpr/uwck,wkp->ucp/dot_general | solution.py:114
  48.2 1.0 pad_maximum_fusion
  49.2 10.2 %all-to-all-start = ((bf16[16,4,4224]{2,1,0:T(4,128)(2,1)}), bf16[16,4,4224]{2,1,0:T(4,128)(2,1)S(1)}, u32[]{:S(2)}, u32[]{:S(2)}) async-start(bf16[16,4,4224]{2,1,0:T(4,128)(2,1)} %pad_maximum_fusion), calls=%async_computation | async-start | bytes 1081344 | tf_op jit(solution)/shard_map/all_to_all | solution.py:130
  59.4 14.0 %all-to-all-done = bf16[16,4,4224]{2,1,0:T(4,128)(2,1)S(1)} async-done(((bf16[16,4,4224]{2,1,0:T(4,128)(2,1)}), bf16[16,4,4224]{2,1,0:T(4,128)(2,1)S(1)}, u32[]{:S(2)}, u32[]{:S(2)}) %all-to-all-start) | async-done | bytes 540704 | tf_op jit(solution)/shard_map/all_to_all | solution.py:130
  74.6 3.6 %collective-permute-start = (bf16[1,8,64,128]{3,1,2,0:T(8,128)(2,1)S(1)}, bf16[1,8,64,128]{3,1,2,0:T(8,128)(2,1)S(1)}, u32[]{:S(2)}, u32[]{:S(2)}) collective-permute-start(bf16[1,8,64,128]{3,1,2,0:T(8,128)(2,1)S(1)} %get-tuple-element.87), channel_id=1, source_target_pairs={{0,1},{1,2},{2,3},{3,4},{4,5},{5,6},{6,7},{7,8},{8,9},{9,10},{10,1... | collective-permute-start | bytes 393224 | tf_op jit(solution)/shard_map/ppermute | solution.py:16
  78.2 2.1 %collective-permute-start.1 = (bf16[1,8,64,128]{3,1,2,0:T(8,128)(2,1)S(1)}, bf16[1,8,64,128]{3,1,2,0:T(8,128)(2,1)S(1)}, u32[]{:S(2)}, u32[]{:S(2)}) collective-permute-start(bf16[1,8,64,128]{3,1,2,0:T(8,128)(2,1)S(1)} %get-tuple-element.88), channel_id=1, source_target_pairs={{1,0},{2,1},{3,2},{4,3},{5,4},{6,5},{7,6},{8,7},{9,8},{10,9},{11,1... | collective-permute-start | bytes 393224 | tf_op jit(solution)/shard_map/ppermute | solution.py:19
  80.7 4.7 %collective-permute-done.1 = bf16[1,8,64,128]{3,1,2,0:T(8,128)(2,1)S(1)} collective-permute-done((bf16[1,8,64,128]{3,1,2,0:T(8,128)(2,1)S(1)}, bf16[1,8,64,128]{3,1,2,0:T(8,128)(2,1)S(1)}, u32[]{:S(2)}, u32[]{:S(2)}) %collective-permute-start.1) | collective-permute-done | bytes 131104 | tf_op jit(solution)/shard_map/ppermute | solution.py:19
  85.4 1.5 %fusion.17 = bf16[6,8,66,130]{3,1,2,0:T(8,128)(2,1)S(1)} fusion(bf16[1,8,64,128]{3,1,2,0:T(8,128)(2,1)S(1)} %collective-permute-done.1, bf16[4,8,64,128]{3,1,2,0:T(8,128)(2,1)S(1)} %bitcast.480, bf16[1,8,64,128]{3,1,2,0:T(8,128)(2,1)S(1)} %collective-permute-done), kind=kLoop, calls=%fused_computation.33 | loop fusion | flops 7824960 | bytes 1610112 | tf_op jit(solution)/shard_map/concatenate | solution.py:20
  97.1 1.9 %collective-permute-start.2 = (bf16[1,8,64,128]{3,1,2,0:T(8,128)(2,1)S(1)}, bf16[1,8,64,128]{3,1,2,0:T(8,128)(2,1)S(1)}, u32[]{:S(2)}, u32[]{:S(2)}) collective-permute-start(bf16[1,8,64,128]{3,1,2,0:T(8,128)(2,1)S(1)} %get-tuple-element.85), channel_id=1, source_target_pairs={{0,1},{1,2},{2,3},{3,4},{4,5},{5,6},{6,7},{7,8},{8,9},{9,10},{10,1... | collective-permute-start | bytes 393224 | tf_op jit(solution)/shard_map/ppermute | solution.py:16
  99.0 2.6 %collective-permute-start.3 = (bf16[1,8,64,128]{3,1,2,0:T(8,128)(2,1)S(1)}, bf16[1,8,64,128]{3,1,2,0:T(8,128)(2,1)S(1)}, u32[]{:S(2)}, u32[]{:S(2)}) collective-permute-start(bf16[1,8,64,128]{3,1,2,0:T(8,128)(2,1)S(1)} %get-tuple-element.86), channel_id=1, source_target_pairs={{1,0},{2,1},{3,2},{4,3},{5,4},{6,5},{7,6},{8,7},{9,8},{10,9},{11,1... | collective-permute-start | bytes 393224 | tf_op jit(solution)/shard_map/ppermute | solution.py:19
  102.0 4.2 %collective-permute-done.3 = bf16[1,8,64,128]{3,1,2,0:T(8,128)(2,1)S(1)} collective-permute-done((bf16[1,8,64,128]{3,1,2,0:T(8,128)(2,1)S(1)}, bf16[1,8,64,128]{3,1,2,0:T(8,128)(2,1)S(1)}, u32[]{:S(2)}, u32[]{:S(2)}) %collective-permute-start.3) | collective-permute-done | bytes 131104 | tf_op jit(solution)/shard_map/ppermute | solution.py:19
  106.2 1.5 %select_maximum_fusion = bf16[6,8,66,130]{3,1,2,0:T(8,128)(2,1)S(1)} fusion(bf16[1,8,64,128]{3,1,2,0:T(8,128)(2,1)S(1)} %collective-permute-done.3, bf16[4,8,64,128]{3,1,2,0:T(8,128)(2,1)S(1)} %fusion.44, bf16[1,8,64,128]{3,1,2,0:T(8,128)(2,1)S(1)} %collective-permute-done.2), kind=kLoop, calls=%fused_computation.24 | loop fusion | flops 7824960 | bytes 1610112 | tf_op jit(solution)/shard_map/concatenate | solution.py:20
  (204 shorter events, 37.2 us)
Async XLA Ops:
  0.0 21.4 %copy-start.3 = (s32[1,64,4]{1,2,0:T(4,128)S(1)}, s32[1,64,4]{1,2,0:T(4,128)}, u32[]{:S(2)}) copy-start(s32[1,64,4]{1,2,0:T(4,128)} %param.14) | copy-start | bytes 3076
  21.1 2.1 %copy-start = (bf16[4,128,512]{2,1,0:T(8,128)(2,1)S(1)}, bf16[4,128,512]{2,1,0:T(8,128)(2,1)}, u32[]{:S(2)}) copy-start(bf16[4,128,512]{2,1,0:T(8,128)(2,1)} %param.13) | copy-start | bytes 1572868
  23.2 24.8 %copy-start.4 = (s32[1,64]{1,0:T(1,128)S(1)}, s32[1,64]{1,0:T(1,128)}, u32[]{:S(2)}) copy-start(s32[1,64]{1,0:T(1,128)} %param.17) | copy-start | bytes 772
  23.2 24.8 %copy-start.5 = (s32[1,64]{1,0:T(1,128)S(1)}, s32[1,64]{1,0:T(1,128)}, u32[]{:S(2)}) copy-start(s32[1,64]{1,0:T(1,128)} %param.16) | copy-start | bytes 772
  49.2 24.1 %all-to-all-start = ((bf16[16,4,4224]{2,1,0:T(4,128)(2,1)}), bf16[16,4,4224]{2,1,0:T(4,128)(2,1)S(1)}, u32[]{:S(2)}, u32[]{:S(2)}) async-start(bf16[16,4,4224]{2,1,0:T(4,128)(2,1)} %pad_maximum_fusion), calls=%async_computation | async-start | bytes 1081344 | tf_op jit(solution)/shard_map/all_to_all | solution.py:130
  74.1 6.2 %copy-start.2 = (bf16[3,3,3,8,8]{4,3,2,1,0:T(8,128)(2,1)S(1)}, bf16[3,3,3,8,8]{4,3,2,1,0:T(8,128)(2,1)}, u32[]{:S(2)}) copy-start(bf16[3,3,3,8,8]{4,3,2,1,0:T(8,128)(2,1)} %param.18) | copy-start | bytes 10372
  74.6 6.1 %collective-permute-start = (bf16[1,8,64,128]{3,1,2,0:T(8,128)(2,1)S(1)}, bf16[1,8,64,128]{3,1,2,0:T(8,128)(2,1)S(1)}, u32[]{:S(2)}, u32[]{:S(2)}) collective-permute-start(bf16[1,8,64,128]{3,1,2,0:T(8,128)(2,1)S(1)} %get-tuple-element.87), channel_id=1, source_target_pairs={{0,1},{1,2},{2,3},{3,4},{4,5},{5,6},{6,7},{7,8},{8,9},{9,10},{10,1... | collective-permute-start | bytes 393224 | tf_op jit(solution)/shard_map/ppermute | solution.py:16
  78.2 7.2 %collective-permute-start.1 = (bf16[1,8,64,128]{3,1,2,0:T(8,128)(2,1)S(1)}, bf16[1,8,64,128]{3,1,2,0:T(8,128)(2,1)S(1)}, u32[]{:S(2)}, u32[]{:S(2)}) collective-permute-start(bf16[1,8,64,128]{3,1,2,0:T(8,128)(2,1)S(1)} %get-tuple-element.88), channel_id=1, source_target_pairs={{1,0},{2,1},{3,2},{4,3},{5,4},{6,5},{7,6},{8,7},{9,8},{10,9},{11,1... | collective-permute-start | bytes 393224 | tf_op jit(solution)/shard_map/ppermute | solution.py:19
  96.2 5.4 %copy-start.1 = (bf16[3,3,3,8]{3,2,1,0:T(4,128)(2,1)S(1)}, bf16[3,3,3,8]{3,2,1,0:T(4,128)(2,1)}, u32[]{:S(2)}) copy-start(bf16[3,3,3,8]{3,2,1,0:T(4,128)(2,1)} %param.19) | copy-start | bytes 1300
  97.1 4.9 %collective-permute-start.2 = (bf16[1,8,64,128]{3,1,2,0:T(8,128)(2,1)S(1)}, bf16[1,8,64,128]{3,1,2,0:T(8,128)(2,1)S(1)}, u32[]{:S(2)}, u32[]{:S(2)}) collective-permute-start(bf16[1,8,64,128]{3,1,2,0:T(8,128)(2,1)S(1)} %get-tuple-element.85), channel_id=1, source_target_pairs={{0,1},{1,2},{2,3},{3,4},{4,5},{5,6},{6,7},{7,8},{8,9},{9,10},{10,1... | collective-permute-start | bytes 393224 | tf_op jit(solution)/shard_map/ppermute | solution.py:16
  99.0 7.2 %collective-permute-start.3 = (bf16[1,8,64,128]{3,1,2,0:T(8,128)(2,1)S(1)}, bf16[1,8,64,128]{3,1,2,0:T(8,128)(2,1)S(1)}, u32[]{:S(2)}, u32[]{:S(2)}) collective-permute-start(bf16[1,8,64,128]{3,1,2,0:T(8,128)(2,1)S(1)} %get-tuple-element.86), channel_id=1, source_target_pairs={{1,0},{2,1},{3,2},{4,3},{5,4},{6,5},{7,6},{8,7},{9,8},{10,9},{11,1... | collective-permute-start | bytes 393224 | tf_op jit(solution)/shard_map/ppermute | solution.py:19

commit v2 on v1

--- a/solution.py
+++ b/solution.py
@@ -103,28 +103,32 @@
     chosen_groups = chosen.reshape(unit_rounds, per_round, slots, slots)
     group_size = channels // GROUPS
 
-    ref_all = lax.all_gather(ref_feat[0], "view")
-    ref_units = jnp.repeat(ref_all, cap, axis=0).reshape(unit_rounds, per_round, channels, tpix)
+    ref_all = lax.all_to_all(
+        jnp.broadcast_to(ref_feat, (owners,) + ref_feat.shape[1:]),
+        "view",
+        split_axis=0,
+        concat_axis=0,
+        tiled=True,
+    )
 
-    def resample(index_rows, chosen_rows, ref_rows):
+    def resample(index_rows, chosen_rows):
         gathered = blocks[index_rows]
         arranged = jnp.einsum(
             "ujw,ujck->uwck", chosen_rows, gathered, preferred_element_type=jnp.float32
         ).astype(jnp.bfloat16)
-        warped = jnp.einsum(
+        return jnp.einsum(
             "uwck,wkp->ucp", arranged, weight_table, preferred_element_type=jnp.float32
         ).astype(jnp.bfloat16)
-        products = ref_rows.astype(jnp.float32) * warped.astype(jnp.float32)
-        return (
-            (products.reshape(per_round, GROUPS, group_size, tpix).sum(axis=2) * (GROUPS / channels))
-            .astype(jnp.bfloat16)
-            .reshape(per_round, GROUPS * tpix)
-        )
 
-    corr_all = lax.map(
-        lambda packed: resample(packed[0], packed[1], packed[2]),
-        (index_groups, chosen_groups, ref_units),
-    ).reshape(units, GROUPS * tpix)
+    warped_all = lax.map(
+        lambda packed: resample(packed[0], packed[1]), (index_groups, chosen_groups)
+    ).reshape(owners, cap, channels, tpix)
+    products = ref_all.astype(jnp.float32)[:, None] * warped_all.astype(jnp.float32)
+    corr_all = (
+        (products.reshape(units, GROUPS, group_size, tpix).sum(axis=2) * (GROUPS / channels))
+        .astype(jnp.bfloat16)
+        .reshape(units, GROUPS * tpix)
+    )
     tag_lanes = jnp.broadcast_to(depth_code[:, None], (units, 128))
     payload = jnp.concatenate([corr_all, tag_lanes], axis=1)
     arriving = lax.all_to_all(

time: 118 us -> 116 us (0.983)
  blocking collectives: 17.3 us -> 0 us
  local copies, waits for them, and re-layouts: 14.5 us -> 22.2 us
  other arithmetic: 9.02 us -> 14 us
  starting transfers between devices: 20.4 us -> 23 us
    all_gather x1 -> x0, blocking collectives: 17.3 us -> none  [body(): ref_all = lax.all_gather(ref_feat[0], 'view')]
    mul x0 -> x2, local copies, waits for them, and re-layouts: none -> 7.69 us  [body(): ref_all.astype(jnp.float32)[:, None] * warped_all.astype(jnp.float32)]
    all_to_all x0 -> x1, starting transfers between devices: none -> 6.69 us  [body(): lax.all_to_all(jnp.broadcast_to(ref_feat, (owners,) + ref_feat.shape[1:])...]
    reduce_sum x8 -> x1, other arithmetic: 2.47 us -> 7.41 us  [body(): products.reshape(units, GROUPS, group_size, tpix).sum(axis=2)]
    all_to_all x1, starting transfers between devices: 10.2 us -> 6.02 us  [body(): lax.all_to_all(payload.reshape(owners, cap, GROUPS * tpix + 128), 'view',...]
    convert_element_type x8 -> x2, local copies, waits for them, and re-layouts: 0.29 us -> 3.4 us  [the longest x1 3.02 us: body(): warped_all.astype(jnp.float32)]
    reshape x8 -> x0, local copies, waits for them, and re-layouts: 1.19 us -> none  [resample(): products.reshape(per_round, GROUPS, group_size, tpix).sum(axis=2)]
  transfers between devices with their start and end apart: 5 -> 6, of which waited for: 3 -> 3; matrix products, arithmetic and copies ran while one was open for 1% -> 23% of each run, Pallas kernels for 0% -> 0%
where the time goes in v2:
time: 116 us; the launch traced here: 115 us
  matrix products  32.3 us (28%)
  starting transfers between devices  23 us (20%)
  waiting for transfers between devices  22.9 us (20%)
  local copies, waits for them, and re-layouts  22.2 us (19%)
  other arithmetic  14 us (12%)
    all_to_all x1, waiting for transfers between devices, body(): lax.all_to_all(payload.reshape(owners, cap, GROUPS * tpix + 128), 'view',...  14 us
    dot_general x8, matrix products, resample(): jnp.einsum('uwck,wkp->ucp', arranged, weight_table, preferred_element_typ...  10.7 us
    dot_general x27, matrix products, convolve_full(): jnp.einsum('rcdw,ce->redw', window, kernel[depth_off, row_off, col_off],...  10.4 us
    ppermute x2, waiting for transfers between devices, with_halo(): lax.ppermute(lax.slice_in_dim(block, 0, width, axis=dim), axis, backward)  8.95 us
    dot_general x27, matrix products, convolve_final(): jnp.einsum('rcdw,c->rdw', window, kernel[depth_off, row_off, col_off], pr...  8.64 us
    mul x2, local copies, waits for them, and re-layouts, body(): ref_all.astype(jnp.float32)[:, None] * warped_all.astype(jnp.float32)  7.69 us
    reduce_sum x1, other arithmetic, body(): products.reshape(units, GROUPS, group_size, tpix).sum(axis=2)  7.41 us
    all_to_all x1, starting transfers between devices, body(): lax.all_to_all(jnp.broadcast_to(ref_feat, (owners,) + ref_feat.shape[1:])...  6.69 us
  transfers between devices with their start and end apart: 6, of which 3 were waited for; matrix products, arithmetic and copies ran while one was open for 23% of the time, Pallas kernels for 0%

profile of v2, /device:TPU:13, one launch (start us, length us, event | category | flops | bytes accessed | tf_op | source)
XLA Modules:
  0.0 115.5 jit_solution(5268535318414478130)
XLA Ops:
  0.0 1.7 %broadcast_in_dim.18 = bf16[16,32,512]{2,1,0:T(8,128)(2,1)} broadcast(bf16[32,512]{1,0:T(8,128)(2,1)} %bitcast.519), dimensions={1,2} | broadcast | bytes 557056 | tf_op jit(solution)/shard_map/broadcast_in_dim | solution.py:107
  1.7 6.7 %all-to-all-start = ((bf16[16,32,512]{2,1,0:T(8,128)(2,1)}), bf16[16,32,512]{2,1,0:T(8,128)(2,1)S(1)}, u32[]{:S(2)}, u32[]{:S(2)}) async-start(bf16[16,32,512]{2,1,0:T(8,128)(2,1)} %broadcast_in_dim.18), calls=%async_computation | async-start | bytes 1048576 | tf_op jit(solution)/shard_map/all_to_all | solution.py:106
  11.0 20.8 %while.10 = (s32[]{:T(128)}, bf16[8,8,32,512]{3,2,1,0:T(8,128)(2,1)S(1)}, bf16[8,8,4,4]{1,3,2,0:T(4,128)(2,1)S(1)}, s32[8,8,4]{1,0,2:T(8,128)S(1)}, bf16[64,32,1...) while((s32[]{:T(128)}, bf16[8,8,32,512]{3,2,1,0:T(8,128)(2,1)S(1)}, ...), condition=%wide.region_1.2_spmd, body=%wide.region_0.1_spmd.sunk | while | flops 135529568 | bytes 2103897 | solution.py:123
  12.2 1.3 %fusion.280 = bf16[8,8,32,512]{3,2,1,0:T(8,128)(2,1)S(1)} fusion(bf16[8,8,32,512]{3,2,1,0:T(8,128)(2,1)S(1)} %get-tuple-element.117, s32[]{:T(128)} %get-tuple-element.116, bf16[4,128,512]{2,1,0:T(8,128)(2,1)} %get-tuple-element.128, bf16[8,4,32,128]{3,1,2,0:T(4,128)(2,1)S(1)} %convolution_convert_fusion.2), kind=kOutput, calls=%fused_computation.5.clone.1 | convolution fusion | flops 134348800 | bytes 1048580 | tf_op jit(solution)/shard_map/while/body/eval_jaxpr/uwck,wkp->ucp/dot_general | solution.py:119
  14.8 1.3 %fusion.280 = bf16[8,8,32,512]{3,2,1,0:T(8,128)(2,1)S(1)} fusion(bf16[8,8,32,512]{3,2,1,0:T(8,128)(2,1)S(1)} %get-tuple-element.117, s32[]{:T(128)} %get-tuple-element.116, bf16[4,128,512]{2,1,0:T(8,128)(2,1)} %get-tuple-element.128, bf16[8,4,32,128]{3,1,2,0:T(4,128)(2,1)S(1)} %convolution_convert_fusion.2), kind=kOutput, calls=%fused_computation.5.clone.1 | convolution fusion | flops 134348800 | bytes 1048580 | tf_op jit(solution)/shard_map/while/body/eval_jaxpr/uwck,wkp->ucp/dot_general | solution.py:119
  17.4 1.3 %fusion.280 = bf16[8,8,32,512]{3,2,1,0:T(8,128)(2,1)S(1)} fusion(bf16[8,8,32,512]{3,2,1,0:T(8,128)(2,1)S(1)} %get-tuple-element.117, s32[]{:T(128)} %get-tuple-element.116, bf16[4,128,512]{2,1,0:T(8,128)(2,1)} %get-tuple-element.128, bf16[8,4,32,128]{3,1,2,0:T(4,128)(2,1)S(1)} %convolution_convert_fusion.2), kind=kOutput, calls=%fused_computation.5.clone.1 | convolution fusion | flops 134348800 | bytes 1048580 | tf_op jit(solution)/shard_map/while/body/eval_jaxpr/uwck,wkp->ucp/dot_general | solution.py:119
  20.0 1.3 %fusion.280 = bf16[8,8,32,512]{3,2,1,0:T(8,128)(2,1)S(1)} fusion(bf16[8,8,32,512]{3,2,1,0:T(8,128)(2,1)S(1)} %get-tuple-element.117, s32[]{:T(128)} %get-tuple-element.116, bf16[4,128,512]{2,1,0:T(8,128)(2,1)} %get-tuple-element.128, bf16[8,4,32,128]{3,1,2,0:T(4,128)(2,1)S(1)} %convolution_convert_fusion.2), kind=kOutput, calls=%fused_computation.5.clone.1 | convolution fusion | flops 134348800 | bytes 1048580 | tf_op jit(solution)/shard_map/while/body/eval_jaxpr/uwck,wkp->ucp/dot_general | solution.py:119
  22.6 1.3 %fusion.280 = bf16[8,8,32,512]{3,2,1,0:T(8,128)(2,1)S(1)} fusion(bf16[8,8,32,512]{3,2,1,0:T(8,128)(2,1)S(1)} %get-tuple-element.117, s32[]{:T(128)} %get-tuple-element.116, bf16[4,128,512]{2,1,0:T(8,128)(2,1)} %get-tuple-element.128, bf16[8,4,32,128]{3,1,2,0:T(4,128)(2,1)S(1)} %convolution_convert_fusion.2), kind=kOutput, calls=%fused_computation.5.clone.1 | convolution fusion | flops 134348800 | bytes 1048580 | tf_op jit(solution)/shard_map/while/body/eval_jaxpr/uwck,wkp->ucp/dot_general | solution.py:119
  27.9 1.3 %fusion.280 = bf16[8,8,32,512]{3,2,1,0:T(8,128)(2,1)S(1)} fusion(bf16[8,8,32,512]{3,2,1,0:T(8,128)(2,1)S(1)} %get-tuple-element.117, s32[]{:T(128)} %get-tuple-element.116, bf16[4,128,512]{2,1,0:T(8,128)(2,1)} %get-tuple-element.128, bf16[8,4,32,128]{3,1,2,0:T(4,128)(2,1)S(1)} %convolution_convert_fusion.2), kind=kOutput, calls=%fused_computation.5.clone.1 | convolution fusion | flops 134348800 | bytes 1048580 | tf_op jit(solution)/shard_map/while/body/eval_jaxpr/uwck,wkp->ucp/dot_general | solution.py:119
  30.5 1.3 %fusion.280 = bf16[8,8,32,512]{3,2,1,0:T(8,128)(2,1)S(1)} fusion(bf16[8,8,32,512]{3,2,1,0:T(8,128)(2,1)S(1)} %get-tuple-element.117, s32[]{:T(128)} %get-tuple-element.116, bf16[4,128,512]{2,1,0:T(8,128)(2,1)} %get-tuple-element.128, bf16[8,4,32,128]{3,1,2,0:T(4,128)(2,1)S(1)} %convolution_convert_fusion.2), kind=kOutput, calls=%fused_computation.5.clone.1 | convolution fusion | flops 134348800 | bytes 1048580 | tf_op jit(solution)/shard_map/while/body/eval_jaxpr/uwck,wkp->ucp/dot_general | solution.py:119
  31.8 3.0 %reshape.111 = f32[64,8,4,512]{3,2,1,0:T(4,128)} reshape(bf16[8,8,32,512]{3,2,1,0:T(8,128)(2,1)S(1)} %get-tuple-element.37) | data formatting | bytes 6291456 | tf_op jit(solution)/shard_map/convert_element_type | solution.py:126
  35.0 2.5 %mul.20 = f32[16,4,32,512]{3,2,1,0:T(8,128)} broadcast(bf16[16,32,512]{2,1,0:T(8,128)(2,1)S(1)} %all-to-all-done), dimensions={0,2,3} | broadcast | bytes 4718592 | tf_op jit(solution)/shard_map/mul | solution.py:126
  37.5 5.2 %mul.21 = f32[64,8,4,512]{3,2,1,0:T(4,128)} reshape(f32[16,4,32,512]{3,2,1,0:T(8,128)} %mul.20) | data formatting | bytes 8388608 | tf_op jit(solution)/shard_map/mul | solution.py:126
  42.7 7.4 %multiply_reduce_fusion = f32[64,8,512]{2,1,0:T(8,128)S(1)} fusion(f32[64,8,4,512]{3,2,1,0:T(4,128)} %mul.21, f32[64,8,4,512]{3,2,1,0:T(4,128)} %reshape.111), kind=kLoop, calls=%fused_computation.19 | loop fusion | flops 1835008 | bytes 9437184 | tf_op jit(solution)/shard_map/reduce_sum | solution.py:128
  51.7 6.0 %all-to-all-start.1 = ((bf16[16,4,4224]{2,1,0:T(4,128)(2,1)}), bf16[16,4,4224]{2,1,0:T(4,128)(2,1)S(1)}, u32[]{:S(2)}, u32[]{:S(2)}) async-start(bf16[16,4,4224]{2,1,0:T(4,128)(2,1)} %pad_maximum_fusion), calls=%async_computation.1 | async-start | bytes 1081344 | tf_op jit(solution)/shard_map/all_to_all | solution.py:134
  57.8 14.0 %all-to-all-done.1 = bf16[16,4,4224]{2,1,0:T(4,128)(2,1)S(1)} async-done(((bf16[16,4,4224]{2,1,0:T(4,128)(2,1)}), bf16[16,4,4224]{2,1,0:T(4,128)(2,1)S(1)}, u32[]{:S(2)}, u32[]{:S(2)}) %all-to-all-start.1) | async-done | bytes 540704 | tf_op jit(solution)/shard_map/all_to_all | solution.py:134
  73.0 3.6 %collective-permute-start = (bf16[1,8,64,128]{3,1,2,0:T(8,128)(2,1)S(1)}, bf16[1,8,64,128]{3,1,2,0:T(8,128)(2,1)S(1)}, u32[]{:S(2)}, u32[]{:S(2)}) collective-permute-start(bf16[1,8,64,128]{3,1,2,0:T(8,128)(2,1)S(1)} %get-tuple-element.70), channel_id=1, source_target_pairs={{0,1},{1,2},{2,3},{3,4},{4,5},{5,6},{6,7},{7,8},{8,9},{9,10},{10,1... | collective-permute-start | bytes 393224 | tf_op jit(solution)/shard_map/ppermute | solution.py:16
  76.6 2.1 %collective-permute-start.1 = (bf16[1,8,64,128]{3,1,2,0:T(8,128)(2,1)S(1)}, bf16[1,8,64,128]{3,1,2,0:T(8,128)(2,1)S(1)}, u32[]{:S(2)}, u32[]{:S(2)}) collective-permute-start(bf16[1,8,64,128]{3,1,2,0:T(8,128)(2,1)S(1)} %get-tuple-element.71), channel_id=1, source_target_pairs={{1,0},{2,1},{3,2},{4,3},{5,4},{6,5},{7,6},{8,7},{9,8},{10,9},{11,1... | collective-permute-start | bytes 393224 | tf_op jit(solution)/shard_map/ppermute | solution.py:19
  79.1 4.7 %collective-permute-done.1 = bf16[1,8,64,128]{3,1,2,0:T(8,128)(2,1)S(1)} collective-permute-done((bf16[1,8,64,128]{3,1,2,0:T(8,128)(2,1)S(1)}, bf16[1,8,64,128]{3,1,2,0:T(8,128)(2,1)S(1)}, u32[]{:S(2)}, u32[]{:S(2)}) %collective-permute-start.1) | collective-permute-done | bytes 131104 | tf_op jit(solution)/shard_map/ppermute | solution.py:19
  83.8 1.5 %fusion.17 = bf16[6,8,66,130]{3,1,2,0:T(8,128)(2,1)S(1)} fusion(bf16[1,8,64,128]{3,1,2,0:T(8,128)(2,1)S(1)} %collective-permute-done.1, bf16[4,8,64,128]{3,1,2,0:T(8,128)(2,1)S(1)} %bitcast.485, bf16[1,8,64,128]{3,1,2,0:T(8,128)(2,1)S(1)} %collective-permute-done), kind=kLoop, calls=%fused_computation.32 | loop fusion | flops 7824960 | bytes 1610112 | tf_op jit(solution)/shard_map/concatenate | solution.py:20
  95.5 1.9 %collective-permute-start.2 = (bf16[1,8,64,128]{3,1,2,0:T(8,128)(2,1)S(1)}, bf16[1,8,64,128]{3,1,2,0:T(8,128)(2,1)S(1)}, u32[]{:S(2)}, u32[]{:S(2)}) collective-permute-start(bf16[1,8,64,128]{3,1,2,0:T(8,128)(2,1)S(1)} %get-tuple-element.68), channel_id=1, source_target_pairs={{0,1},{1,2},{2,3},{3,4},{4,5},{5,6},{6,7},{7,8},{8,9},{9,10},{10,1... | collective-permute-start | bytes 393224 | tf_op jit(solution)/shard_map/ppermute | solution.py:16
  97.4 2.6 %collective-permute-start.3 = (bf16[1,8,64,128]{3,1,2,0:T(8,128)(2,1)S(1)}, bf16[1,8,64,128]{3,1,2,0:T(8,128)(2,1)S(1)}, u32[]{:S(2)}, u32[]{:S(2)}) collective-permute-start(bf16[1,8,64,128]{3,1,2,0:T(8,128)(2,1)S(1)} %get-tuple-element.69), channel_id=1, source_target_pairs={{1,0},{2,1},{3,2},{4,3},{5,4},{6,5},{7,6},{8,7},{9,8},{10,9},{11,1... | collective-permute-start | bytes 393224 | tf_op jit(solution)/shard_map/ppermute | solution.py:19
  100.4 4.2 %collective-permute-done.3 = bf16[1,8,64,128]{3,1,2,0:T(8,128)(2,1)S(1)} collective-permute-done((bf16[1,8,64,128]{3,1,2,0:T(8,128)(2,1)S(1)}, bf16[1,8,64,128]{3,1,2,0:T(8,128)(2,1)S(1)}, u32[]{:S(2)}, u32[]{:S(2)}) %collective-permute-start.3) | collective-permute-done | bytes 131104 | tf_op jit(solution)/shard_map/ppermute | solution.py:19
  104.6 1.5 %select_maximum_fusion = bf16[6,8,66,130]{3,1,2,0:T(8,128)(2,1)S(1)} fusion(bf16[1,8,64,128]{3,1,2,0:T(8,128)(2,1)S(1)} %collective-permute-done.3, bf16[4,8,64,128]{3,1,2,0:T(8,128)(2,1)S(1)} %fusion.44, bf16[1,8,64,128]{3,1,2,0:T(8,128)(2,1)S(1)} %collective-permute-done.2), kind=kLoop, calls=%fused_computation.23 | loop fusion | flops 7824960 | bytes 1610112 | tf_op jit(solution)/shard_map/concatenate | solution.py:20
  (172 shorter events, 36.5 us)
Async XLA Ops:
  0.0 10.3 %copy-start.3 = (s32[1,64,4]{1,2,0:T(4,128)S(1)}, s32[1,64,4]{1,2,0:T(4,128)}, u32[]{:S(2)}) copy-start(s32[1,64,4]{1,2,0:T(4,128)} %param.15) | copy-start | bytes 3076
  0.0 10.4 %copy-start = (bf16[1,32,8192]{2,1,0:T(8,128)(2,1)S(1)}, bf16[1,32,8192]{2,1,0:T(8,128)(2,1)}, u32[]{:S(2)}) copy-start(bf16[1,32,8192]{2,1,0:T(8,128)(2,1)} %param.11) | copy-start | bytes 1572868
  1.7 9.2 %copy-start.4 = (s32[1,64,4]{1,2,0:T(4,128)S(1)}, s32[1,64,4]{1,2,0:T(4,128)}, u32[]{:S(2)}) copy-start(s32[1,64,4]{1,2,0:T(4,128)} %param.14) | copy-start | bytes 3076
  1.7 33.3 %all-to-all-start = ((bf16[16,32,512]{2,1,0:T(8,128)(2,1)}), bf16[16,32,512]{2,1,0:T(8,128)(2,1)S(1)}, u32[]{:S(2)}, u32[]{:S(2)}) async-start(bf16[16,32,512]{2,1,0:T(8,128)(2,1)} %broadcast_in_dim.18), calls=%async_computation | async-start | bytes 1048576 | tf_op jit(solution)/shard_map/all_to_all | solution.py:106
  31.8 3.0 %copy-start.5 = (s32[1,64]{1,0:T(1,128)S(1)}, s32[1,64]{1,0:T(1,128)}, u32[]{:S(2)}) copy-start(s32[1,64]{1,0:T(1,128)} %param.17) | copy-start | bytes 772
  31.8 3.0 %copy-start.6 = (s32[1,64]{1,0:T(1,128)S(1)}, s32[1,64]{1,0:T(1,128)}, u32[]{:S(2)}) copy-start(s32[1,64]{1,0:T(1,128)} %param.16) | copy-start | bytes 772
  51.7 20.0 %all-to-all-start.1 = ((bf16[16,4,4224]{2,1,0:T(4,128)(2,1)}), bf16[16,4,4224]{2,1,0:T(4,128)(2,1)S(1)}, u32[]{:S(2)}, u32[]{:S(2)}) async-start(bf16[16,4,4224]{2,1,0:T(4,128)(2,1)} %pad_maximum_fusion), calls=%async_computation.1 | async-start | bytes 1081344 | tf_op jit(solution)/shard_map/all_to_all | solution.py:134
  72.5 6.2 %copy-start.2 = (bf16[3,3,3,8,8]{4,3,2,1,0:T(8,128)(2,1)S(1)}, bf16[3,3,3,8,8]{4,3,2,1,0:T(8,128)(2,1)}, u32[]{:S(2)}) copy-start(bf16[3,3,3,8,8]{4,3,2,1,0:T(8,128)(2,1)} %param.18) | copy-start | bytes 10372
  73.0 6.1 %collective-permute-start = (bf16[1,8,64,128]{3,1,2,0:T(8,128)(2,1)S(1)}, bf16[1,8,64,128]{3,1,2,0:T(8,128)(2,1)S(1)}, u32[]{:S(2)}, u32[]{:S(2)}) collective-permute-start(bf16[1,8,64,128]{3,1,2,0:T(8,128)(2,1)S(1)} %get-tuple-element.70), channel_id=1, source_target_pairs={{0,1},{1,2},{2,3},{3,4},{4,5},{5,6},{6,7},{7,8},{8,9},{9,10},{10,1... | collective-permute-start | bytes 393224 | tf_op jit(solution)/shard_map/ppermute | solution.py:16
  76.6 7.2 %collective-permute-start.1 = (bf16[1,8,64,128]{3,1,2,0:T(8,128)(2,1)S(1)}, bf16[1,8,64,128]{3,1,2,0:T(8,128)(2,1)S(1)}, u32[]{:S(2)}, u32[]{:S(2)}) collective-permute-start(bf16[1,8,64,128]{3,1,2,0:T(8,128)(2,1)S(1)} %get-tuple-element.71), channel_id=1, source_target_pairs={{1,0},{2,1},{3,2},{4,3},{5,4},{6,5},{7,6},{8,7},{9,8},{10,9},{11,1... | collective-permute-start | bytes 393224 | tf_op jit(solution)/shard_map/ppermute | solution.py:19
  94.6 5.4 %copy-start.1 = (bf16[3,3,3,8]{3,2,1,0:T(4,128)(2,1)S(1)}, bf16[3,3,3,8]{3,2,1,0:T(4,128)(2,1)}, u32[]{:S(2)}) copy-start(bf16[3,3,3,8]{3,2,1,0:T(4,128)(2,1)} %param.19) | copy-start | bytes 1300
  95.5 4.9 %collective-permute-start.2 = (bf16[1,8,64,128]{3,1,2,0:T(8,128)(2,1)S(1)}, bf16[1,8,64,128]{3,1,2,0:T(8,128)(2,1)S(1)}, u32[]{:S(2)}, u32[]{:S(2)}) collective-permute-start(bf16[1,8,64,128]{3,1,2,0:T(8,128)(2,1)S(1)} %get-tuple-element.68), channel_id=1, source_target_pairs={{0,1},{1,2},{2,3},{3,4},{4,5},{5,6},{6,7},{7,8},{8,9},{9,10},{10,1... | collective-permute-start | bytes 393224 | tf_op jit(solution)/shard_map/ppermute | solution.py:16
  97.4 7.2 %collective-permute-start.3 = (bf16[1,8,64,128]{3,1,2,0:T(8,128)(2,1)S(1)}, bf16[1,8,64,128]{3,1,2,0:T(8,128)(2,1)S(1)}, u32[]{:S(2)}, u32[]{:S(2)}) collective-permute-start(bf16[1,8,64,128]{3,1,2,0:T(8,128)(2,1)S(1)} %get-tuple-element.69), channel_id=1, source_target_pairs={{1,0},{2,1},{3,2},{4,3},{5,4},{6,5},{7,6},{8,7},{9,8},{10,9},{11,1... | collective-permute-start | bytes 393224 | tf_op jit(solution)/shard_map/ppermute | solution.py:19

commit v3 on v2

--- a/solution.py
+++ b/solution.py
@@ -1,6 +1,8 @@
 import jax
 import jax.numpy as jnp
 from jax import lax
+from jax.experimental import pallas as pl
+from jax.experimental.pallas import tpu as pltpu
 from jax.sharding import PartitionSpec as P
 
 GROUPS = 8
@@ -69,6 +71,68 @@
     return carried
 
 
+def correlate_kernel(blk_ref, blocks_ref, table_ref, ref_ref, out_ref, arranged, products):
+    chunk = 8
+    slots = table_ref.shape[0] // blocks_ref.shape[2]
+    width = blocks_ref.shape[2]
+    channels = blocks_ref.shape[1]
+    units = out_ref.shape[0] // GROUPS
+    cap = units // ref_ref.shape[0]
+    group_size = channels // GROUPS
+    rows = chunk * channels
+
+    def step(c, carry):
+        for u in range(chunk):
+            unit = c * chunk + u
+            for w in range(slots):
+                arranged[u * channels : (u + 1) * channels, w * width : (w + 1) * width] = blocks_ref[
+                    blk_ref[unit * slots + w]
+                ]
+        warped = jnp.dot(arranged[...], table_ref[...], preferred_element_type=jnp.float32)
+        warped = warped.astype(jnp.bfloat16).astype(jnp.float32)
+        lanes = products.shape[0]
+        for u in range(chunk):
+            unit = c * chunk + u
+            tile = ref_ref[unit // cap].astype(jnp.float32)
+            for j in range(lanes):
+                products[j, u * channels : (u + 1) * channels, :] = (
+                    warped[u * channels : (u + 1) * channels, j * 128 : (j + 1) * 128]
+                    * tile[:, j * 128 : (j + 1) * 128]
+                )
+        start = pl.multiple_of(c * (chunk * GROUPS), chunk * GROUPS)
+        for j in range(lanes):
+            total = products[j, pl.ds(0, rows // group_size, stride=group_size), :]
+            for k in range(1, group_size):
+                total = total + products[j, pl.ds(k, rows // group_size, stride=group_size), :]
+            out_ref[pl.ds(start, chunk * GROUPS), j * 128 : (j + 1) * 128] = (
+                total * (GROUPS / channels)
+            ).astype(out_ref.dtype)
+        return carry
+
+    lax.fori_loop(0, units // chunk, step, 0)
+
+
+def correlate(blk, blocks, table, refs, units):
+    channels, width = blocks.shape[1], blocks.shape[2]
+    tpix = table.shape[1]
+    chunk = 8
+    return pl.pallas_call(
+        correlate_kernel,
+        out_shape=jax.ShapeDtypeStruct((units * GROUPS, tpix), jnp.bfloat16),
+        in_specs=[
+            pl.BlockSpec(memory_space=pltpu.SMEM),
+            pl.BlockSpec(memory_space=pltpu.VMEM),
+            pl.BlockSpec(memory_space=pltpu.VMEM),
+            pl.BlockSpec(memory_space=pltpu.VMEM),
+        ],
+        out_specs=pl.BlockSpec(memory_space=pltpu.VMEM),
+        scratch_shapes=[
+            pltpu.VMEM((chunk * channels, table.shape[0]), jnp.bfloat16),
+            pltpu.VMEM((tpix // 128, chunk * channels, 128), jnp.float32),
+        ],
+    )(blk, blocks, table, refs)
+
+
 def pad_rows(volume):
     return with_halo(volume, (("view", 0),), 1)
 
@@ -92,16 +156,14 @@
     units = src_block.shape[1]
     cap = units // owners
     counts = block_count[0]
-    live_slot = jnp.arange(slots)[None, :] < counts[:, None]
-    chosen = (
-        (table_index[0][:, :, None] == jnp.arange(slots)[None, None, :]) & live_slot[:, :, None]
-    ).astype(jnp.bfloat16)
+    nblocks = spix // block_width
+    blocks = jnp.concatenate([blocks, jnp.zeros_like(blocks[:1])], axis=0)
+    matches = table_index[0][:, :, None] == jnp.arange(slots)[None, None, :]
+    live = (jnp.arange(slots)[None, :] < counts[:, None])[:, :, None] & matches
+    picked = jnp.sum(jnp.where(matches, src_block[0][:, :, None], 0), axis=1)
+    alive = jnp.any(live, axis=1)
+    blk = jnp.where(alive, picked, nblocks).reshape(-1).astype(jnp.int32)
     depth_code = jnp.where(counts > 0, depth_plane[0], -1).astype(jnp.bfloat16)
-    unit_rounds = 8
-    per_round = units // unit_rounds
-    index_groups = src_block[0].reshape(unit_rounds, per_round, slots)
-    chosen_groups = chosen.reshape(unit_rounds, per_round, slots, slots)
-    group_size = channels // GROUPS
 
     ref_all = lax.all_to_all(
         jnp.broadcast_to(ref_feat, (owners,) + ref_feat.shape[1:]),
@@ -110,25 +172,9 @@
         concat_axis=0,
         tiled=True,
     )
-
-    def resample(index_rows, chosen_rows):
-        gathered = blocks[index_rows]
-        arranged = jnp.einsum(
-            "ujw,ujck->uwck", chosen_rows, gathered, preferred_element_type=jnp.float32
-        ).astype(jnp.bfloat16)
-        return jnp.einsum(
-            "uwck,wkp->ucp", arranged, weight_table, preferred_element_type=jnp.float32
-        ).astype(jnp.bfloat16)
-
-    warped_all = lax.map(
-        lambda packed: resample(packed[0], packed[1]), (index_groups, chosen_groups)
-    ).reshape(owners, cap, channels, tpix)
-    products = ref_all.astype(jnp.float32)[:, None] * warped_all.astype(jnp.float32)
-    corr_all = (
-        (products.reshape(units, GROUPS, group_size, tpix).sum(axis=2) * (GROUPS / channels))
-        .astype(jnp.bfloat16)
-        .reshape(units, GROUPS * tpix)
-    )
+    corr_all = correlate(
+        blk, blocks, weight_table.reshape(slots * block_width, tpix), ref_all, units
+    ).reshape(units, GROUPS * tpix)
     tag_lanes = jnp.broadcast_to(depth_code[:, None], (units, 128))
     payload = jnp.concatenate([corr_all, tag_lanes], axis=1)
     arriving = lax.all_to_all(

time: 116 us -> 93.6 us (0.81)
  local copies, waits for them, and re-layouts: 22.2 us -> 6.84 us
  matrix products: 32.3 us -> 19.4 us
  waiting for transfers between devices: 22.9 us -> 32.2 us
  other arithmetic: 14 us -> 7.16 us
  Pallas kernels: 0 us -> 5.03 us
    dot_general x16 -> x0, matrix products: 13 us -> none  [the longest x8 10.7 us: resample(): jnp.einsum('uwck,wkp->ucp', arranged, weight_table, preferred_element_typ...]
    all_to_all x1, waiting for transfers between devices: 0.01 us -> 9.3 us  [body(): lax.all_to_all(jnp.broadcast_to(ref_feat, (owners,) + ref_feat.shape[1:])...]
    mul x2 -> x0, local copies, waits for them, and re-layouts: 7.69 us -> none  [body(): ref_all.astype(jnp.float32)[:, None] * warped_all.astype(jnp.float32)]
    reduce_sum x1, other arithmetic: 7.41 us -> 0.71 us  [body(): picked = jnp.sum(jnp.where(matches, src_block[0][:, :, None], 0), axis=1)]
    pallas_call x0 -> x1, Pallas kernels: none -> 5.03 us  [correlate(): pl.pallas_call(correlate_kernel, out_shape=jax.ShapeDtypeStruct((units *...]
    gather x8 -> x0, local copies, waits for them, and re-layouts: 4.83 us -> none  [resample(): gathered = blocks[index_rows]]
    convert_element_type x2 -> x0, local copies, waits for them, and re-layouts: 3.4 us -> none  [the longest x1 3.02 us: body(): warped_all.astype(jnp.float32)]
    concatenate x0 -> x2, local copies, waits for them, and re-layouts: none -> 2.26 us  [the longest x1 1.43 us: body(): payload = jnp.concatenate([corr_all, tag_lanes], axis=1)]
  transfers between devices with their start and end apart: 6 -> 6, of which waited for: 3 -> 4; matrix products, arithmetic and copies ran while one was open for 23% -> 5% of each run, Pallas kernels for 0% -> 0%
where the time goes in v3:
time: 93.6 us; the launch traced here: 93 us
  waiting for transfers between devices  32.2 us (34%)
  starting transfers between devices  21.9 us (23%)
  matrix products  19.4 us (21%)
  other arithmetic  7.16 us (8%)
  local copies, waits for them, and re-layouts  6.84 us (7%)
  Pallas kernels  5.03 us (5%)
    all_to_all x1, waiting for transfers between devices, body(): lax.all_to_all(payload.reshape(owners, cap, GROUPS * tpix + 128), 'view',...  14 us
    dot_general x27, matrix products, convolve_full(): jnp.einsum('rcdw,ce->redw', window, kernel[depth_off, row_off, col_off],...  10.4 us
    all_to_all x1, waiting for transfers between devices, body(): lax.all_to_all(jnp.broadcast_to(ref_feat, (owners,) + ref_feat.shape[1:])...  9.3 us
    ppermute x2, waiting for transfers between devices, with_halo(): lax.ppermute(lax.slice_in_dim(block, 0, width, axis=dim), axis, backward)  8.95 us
    dot_general x27, matrix products, convolve_final(): jnp.einsum('rcdw,c->rdw', window, kernel[depth_off, row_off, col_off], pr...  8.64 us
    all_to_all x1, starting transfers between devices, body(): lax.all_to_all(jnp.broadcast_to(ref_feat, (owners,) + ref_feat.shape[1:])...  6.69 us
    ppermute x2, starting transfers between devices, with_halo(): lax.ppermute(lax.slice_in_dim(block, block.shape[dim] - width, None, axis...  5.54 us
    pallas_call x1, Pallas kernels, correlate(): pl.pallas_call(correlate_kernel, out_shape=jax.ShapeDtypeStruct((units *...  5.03 us
  transfers between devices with their start and end apart: 6, of which 4 were waited for; matrix products, arithmetic and copies ran while one was open for 5% of the time, Pallas kernels for 0%

profile of v3, /device:TPU:13, one launch (start us, length us, event | category | flops | bytes accessed | tf_op | source)
XLA Modules:
  0.0 93.0 jit_solution(12420813158768110542)
XLA Ops:
  0.0 1.7 %broadcast_in_dim.46 = bf16[16,32,512]{2,1,0:T(8,128)(2,1)} broadcast(bf16[32,512]{1,0:T(8,128)(2,1)} %bitcast.475), dimensions={1,2} | broadcast | bytes 557056 | tf_op jit(solution)/shard_map/broadcast_in_dim | solution.py:169
  1.7 6.7 %all-to-all-start = ((bf16[16,32,512]{2,1,0:T(8,128)(2,1)}), bf16[16,32,512]{2,1,0:T(8,128)(2,1)S(1)}, u32[]{:S(2)}, u32[]{:S(2)}) async-start(bf16[16,32,512]{2,1,0:T(8,128)(2,1)} %broadcast_in_dim.46), calls=%async_computation | async-start | bytes 1048576 | tf_op jit(solution)/shard_map/all_to_all | solution.py:168
  9.0 0.7 fusion.144
  9.7 0.7 select_reduce_fusion
  10.5 0.7 select_n.23.blk_ref
  11.8 0.8 concatenate.27.blocks_ref
  12.6 9.3 %all-to-all-done.ref_ref = bf16[16,32,512]{2,1,0:T(8,128)(2,1)S(1)} async-done(((bf16[16,32,512]{2,1,0:T(8,128)(2,1)}), bf16[16,32,512]{2,1,0:T(8,128)(2,1)S(1)}, u32[]{:S(2)}, u32[]{:S(2)}) %all-to-all-start) | async-done | bytes 524320 | tf_op jit(solution)/shard_map/all_to_all | solution.py:168
  21.9 0.8 copy-done
  22.7 5.0 %shard_map.91 = bf16[512,512]{1,0:T(8,128)(2,1)} custom-call(s32[256]{0:T(256)} %select_n.23.blk_ref, bf16[65,32,128]{2,1,0:T(8,128)(2,1)} %concatenate.27.blocks_ref, bf16[512,512]{1,0:T(8,128)(2,1)} %bitcast.472, bf16[16,32,512]{2,1,0:T(8,128)(2,1)} %copy-done), custom_call_target="tpu_custom_call" | custom-call | tf_op jit(solution)/shard_map/pallas_call | solution.py:119
  27.8 1.4 %concatenate.28 = bf16[16,4,4096]{2,1,0:T(4,128)(2,1)S(1)} reshape(bf16[512,512]{1,0:T(8,128)(2,1)} %shard_map.91) | data formatting | bytes 1048576 | tf_op jit(solution)/shard_map/concatenate | solution.py:179
  29.3 1.0 %pad_maximum_fusion = bf16[16,4,4224]{2,1,0:T(4,128)(2,1)} fusion(bf16[16,4,128]{2,1,0:T(4,128)(2,1)S(1)} %broadcast_in_dim.48, bf16[16,4,4096]{2,1,0:T(4,128)(2,1)S(1)} %concatenate.28), kind=kLoop, calls=%fused_computation.74 | loop fusion | flops 1081344 | bytes 1081344 | tf_op jit(solution)/shard_map/concatenate | solution.py:179
  30.3 5.0 %all-to-all-start.1 = ((bf16[16,4,4224]{2,1,0:T(4,128)(2,1)}), bf16[16,4,4224]{2,1,0:T(4,128)(2,1)S(1)}, u32[]{:S(2)}, u32[]{:S(2)}) async-start(bf16[16,4,4224]{2,1,0:T(4,128)(2,1)} %pad_maximum_fusion), calls=%async_computation.1 | async-start | bytes 1081344 | tf_op jit(solution)/shard_map/all_to_all | solution.py:180
  35.3 14.0 %all-to-all-done.1 = bf16[16,4,4224]{2,1,0:T(4,128)(2,1)S(1)} async-done(((bf16[16,4,4224]{2,1,0:T(4,128)(2,1)}), bf16[16,4,4224]{2,1,0:T(4,128)(2,1)S(1)}, u32[]{:S(2)}, u32[]{:S(2)}) %all-to-all-start.1) | async-done | bytes 540704 | tf_op jit(solution)/shard_map/all_to_all | solution.py:180
  50.6 3.6 %collective-permute-start = (bf16[1,8,64,128]{3,1,2,0:T(8,128)(2,1)S(1)}, bf16[1,8,64,128]{3,1,2,0:T(8,128)(2,1)S(1)}, u32[]{:S(2)}, u32[]{:S(2)}) collective-permute-start(bf16[1,8,64,128]{3,1,2,0:T(8,128)(2,1)S(1)} %get-tuple-element.7), channel_id=1, source_target_pairs={{0,1},{1,2},{2,3},{3,4},{4,5},{5,6},{6,7},{7,8},{8,9},{9,10},{10,1... | collective-permute-start | bytes 393224 | tf_op jit(solution)/shard_map/ppermute | solution.py:18
  54.2 2.1 %collective-permute-start.1 = (bf16[1,8,64,128]{3,1,2,0:T(8,128)(2,1)S(1)}, bf16[1,8,64,128]{3,1,2,0:T(8,128)(2,1)S(1)}, u32[]{:S(2)}, u32[]{:S(2)}) collective-permute-start(bf16[1,8,64,128]{3,1,2,0:T(8,128)(2,1)S(1)} %get-tuple-element.8), channel_id=1, source_target_pairs={{1,0},{2,1},{3,2},{4,3},{5,4},{6,5},{7,6},{8,7},{9,8},{10,9},{11,1... | collective-permute-start | bytes 393224 | tf_op jit(solution)/shard_map/ppermute | solution.py:21
  56.7 4.7 %collective-permute-done.1 = bf16[1,8,64,128]{3,1,2,0:T(8,128)(2,1)S(1)} collective-permute-done((bf16[1,8,64,128]{3,1,2,0:T(8,128)(2,1)S(1)}, bf16[1,8,64,128]{3,1,2,0:T(8,128)(2,1)S(1)}, u32[]{:S(2)}, u32[]{:S(2)}) %collective-permute-start.1) | collective-permute-done | bytes 131104 | tf_op jit(solution)/shard_map/ppermute | solution.py:21
  61.4 1.5 %fusion.11 = bf16[6,8,66,130]{3,1,2,0:T(8,128)(2,1)S(1)} fusion(bf16[1,8,64,128]{3,1,2,0:T(8,128)(2,1)S(1)} %collective-permute-done.1, bf16[4,8,64,128]{3,1,2,0:T(8,128)(2,1)S(1)} %bitcast.441, bf16[1,8,64,128]{3,1,2,0:T(8,128)(2,1)S(1)} %collective-permute-done), kind=kLoop, calls=%fused_computation.18 | loop fusion | flops 7824960 | bytes 1610112 | tf_op jit(solution)/shard_map/concatenate | solution.py:22
  71.0 0.8 fusion.36
  72.2 0.8 fusion.38
  73.1 1.9 %collective-permute-start.2 = (bf16[1,8,64,128]{3,1,2,0:T(8,128)(2,1)S(1)}, bf16[1,8,64,128]{3,1,2,0:T(8,128)(2,1)S(1)}, u32[]{:S(2)}, u32[]{:S(2)}) collective-permute-start(bf16[1,8,64,128]{3,1,2,0:T(8,128)(2,1)S(1)} %get-tuple-element.5), channel_id=1, source_target_pairs={{0,1},{1,2},{2,3},{3,4},{4,5},{5,6},{6,7},{7,8},{8,9},{9,10},{10,1... | collective-permute-start | bytes 393224 | tf_op jit(solution)/shard_map/ppermute | solution.py:18
  75.0 2.6 %collective-permute-start.3 = (bf16[1,8,64,128]{3,1,2,0:T(8,128)(2,1)S(1)}, bf16[1,8,64,128]{3,1,2,0:T(8,128)(2,1)S(1)}, u32[]{:S(2)}, u32[]{:S(2)}) collective-permute-start(bf16[1,8,64,128]{3,1,2,0:T(8,128)(2,1)S(1)} %get-tuple-element.6), channel_id=1, source_target_pairs={{1,0},{2,1},{3,2},{4,3},{5,4},{6,5},{7,6},{8,7},{9,8},{10,9},{11,1... | collective-permute-start | bytes 393224 | tf_op jit(solution)/shard_map/ppermute | solution.py:21
  77.9 4.2 %collective-permute-done.3 = bf16[1,8,64,128]{3,1,2,0:T(8,128)(2,1)S(1)} collective-permute-done((bf16[1,8,64,128]{3,1,2,0:T(8,128)(2,1)S(1)}, bf16[1,8,64,128]{3,1,2,0:T(8,128)(2,1)S(1)}, u32[]{:S(2)}, u32[]{:S(2)}) %collective-permute-start.3) | collective-permute-done | bytes 131104 | tf_op jit(solution)/shard_map/ppermute | solution.py:21
  82.2 1.5 %select_maximum_fusion = bf16[6,8,66,130]{3,1,2,0:T(8,128)(2,1)S(1)} fusion(bf16[1,8,64,128]{3,1,2,0:T(8,128)(2,1)S(1)} %collective-permute-done.3, bf16[4,8,64,128]{3,1,2,0:T(8,128)(2,1)S(1)} %fusion.38, bf16[1,8,64,128]{3,1,2,0:T(8,128)(2,1)S(1)} %collective-permute-done.2), kind=kLoop, calls=%fused_computation.9 | loop fusion | flops 7824960 | bytes 1610112 | tf_op jit(solution)/shard_map/concatenate | solution.py:22
  92.1 0.9 add_add_fusion
  (83 shorter events, 20.1 us)
Async XLA Ops:
  0.0 11.2 %copy-start.1 = (bf16[1,32,8192]{2,1,0:T(8,128)(2,1)S(1)}, bf16[1,32,8192]{2,1,0:T(8,128)(2,1)}, u32[]{:S(2)}) copy-start(bf16[1,32,8192]{2,1,0:T(8,128)(2,1)} %param.9) | copy-start | bytes 1572868
  1.7 10.0 %copy-start.4 = (s32[1,64]{1,0:T(1,128)S(1)}, s32[1,64]{1,0:T(1,128)}, u32[]{:S(2)}) copy-start(s32[1,64]{1,0:T(1,128)} %param.15) | copy-start | bytes 772
  1.7 10.0 %copy-start.5 = (s32[1,64]{1,0:T(1,128)S(1)}, s32[1,64]{1,0:T(1,128)}, u32[]{:S(2)}) copy-start(s32[1,64]{1,0:T(1,128)} %param.14) | copy-start | bytes 772
  1.7 20.3 %all-to-all-start = ((bf16[16,32,512]{2,1,0:T(8,128)(2,1)}), bf16[16,32,512]{2,1,0:T(8,128)(2,1)S(1)}, u32[]{:S(2)}, u32[]{:S(2)}) async-start(bf16[16,32,512]{2,1,0:T(8,128)(2,1)} %broadcast_in_dim.46), calls=%async_computation | async-start | bytes 1048576 | tf_op jit(solution)/shard_map/all_to_all | solution.py:168
  21.9 0.8 copy-start
  30.3 19.0 %all-to-all-start.1 = ((bf16[16,4,4224]{2,1,0:T(4,128)(2,1)}), bf16[16,4,4224]{2,1,0:T(4,128)(2,1)S(1)}, u32[]{:S(2)}, u32[]{:S(2)}) async-start(bf16[16,4,4224]{2,1,0:T(4,128)(2,1)} %pad_maximum_fusion), calls=%async_computation.1 | async-start | bytes 1081344 | tf_op jit(solution)/shard_map/all_to_all | solution.py:180
  50.1 6.2 %copy-start.3 = (bf16[3,3,3,8,8]{4,3,2,1,0:T(8,128)(2,1)S(1)}, bf16[3,3,3,8,8]{4,3,2,1,0:T(8,128)(2,1)}, u32[]{:S(2)}) copy-start(bf16[3,3,3,8,8]{4,3,2,1,0:T(8,128)(2,1)} %param.16) | copy-start | bytes 10372
  50.6 6.1 %collective-permute-start = (bf16[1,8,64,128]{3,1,2,0:T(8,128)(2,1)S(1)}, bf16[1,8,64,128]{3,1,2,0:T(8,128)(2,1)S(1)}, u32[]{:S(2)}, u32[]{:S(2)}) collective-permute-start(bf16[1,8,64,128]{3,1,2,0:T(8,128)(2,1)S(1)} %get-tuple-element.7), channel_id=1, source_target_pairs={{0,1},{1,2},{2,3},{3,4},{4,5},{5,6},{6,7},{7,8},{8,9},{9,10},{10,1... | collective-permute-start | bytes 393224 | tf_op jit(solution)/shard_map/ppermute | solution.py:18
  54.2 7.2 %collective-permute-start.1 = (bf16[1,8,64,128]{3,1,2,0:T(8,128)(2,1)S(1)}, bf16[1,8,64,128]{3,1,2,0:T(8,128)(2,1)S(1)}, u32[]{:S(2)}, u32[]{:S(2)}) collective-permute-start(bf16[1,8,64,128]{3,1,2,0:T(8,128)(2,1)S(1)} %get-tuple-element.8), channel_id=1, source_target_pairs={{1,0},{2,1},{3,2},{4,3},{5,4},{6,5},{7,6},{8,7},{9,8},{10,9},{11,1... | collective-permute-start | bytes 393224 | tf_op jit(solution)/shard_map/ppermute | solution.py:21
  72.2 5.4 %copy-start.2 = (bf16[3,3,3,8]{3,2,1,0:T(4,128)(2,1)S(1)}, bf16[3,3,3,8]{3,2,1,0:T(4,128)(2,1)}, u32[]{:S(2)}) copy-start(bf16[3,3,3,8]{3,2,1,0:T(4,128)(2,1)} %param.17) | copy-start | bytes 1300
  73.1 4.9 %collective-permute-start.2 = (bf16[1,8,64,128]{3,1,2,0:T(8,128)(2,1)S(1)}, bf16[1,8,64,128]{3,1,2,0:T(8,128)(2,1)S(1)}, u32[]{:S(2)}, u32[]{:S(2)}) collective-permute-start(bf16[1,8,64,128]{3,1,2,0:T(8,128)(2,1)S(1)} %get-tuple-element.5), channel_id=1, source_target_pairs={{0,1},{1,2},{2,3},{3,4},{4,5},{5,6},{6,7},{7,8},{8,9},{9,10},{10,1... | collective-permute-start | bytes 393224 | tf_op jit(solution)/shard_map/ppermute | solution.py:18
  75.0 7.2 %collective-permute-start.3 = (bf16[1,8,64,128]{3,1,2,0:T(8,128)(2,1)S(1)}, bf16[1,8,64,128]{3,1,2,0:T(8,128)(2,1)S(1)}, u32[]{:S(2)}, u32[]{:S(2)}) collective-permute-start(bf16[1,8,64,128]{3,1,2,0:T(8,128)(2,1)S(1)} %get-tuple-element.6), channel_id=1, source_target_pairs={{1,0},{2,1},{3,2},{4,3},{5,4},{6,5},{7,6},{8,7},{9,8},{10,9},{11,1... | collective-permute-start | bytes 393224 | tf_op jit(solution)/shard_map/ppermute | solution.py:21

commit v4 on v3

--- a/solution.py
+++ b/solution.py
@@ -1,3 +1,5 @@
+import functools
+
 import jax
 import jax.numpy as jnp
 from jax import lax
@@ -131,6 +133,65 @@
             pltpu.VMEM((tpix // 128, chunk * channels, 128), jnp.float32),
         ],
     )(blk, blocks, table, refs)
+
+
+def conv_kernel(x_ref, m_ref, out_ref, *, relu, rows, cols):
+    width = rows * cols
+    lane = lax.broadcasted_iota(jnp.int32, (m_ref.shape[2], width), 1) % cols
+    acc = None
+    for e in range(3):
+        y = None
+        for b in range(3):
+            part = jnp.dot(
+                m_ref[e, b], x_ref[:, b * cols : b * cols + width], preferred_element_type=jnp.float32
+            )
+            y = part if y is None else y + part
+        if e == 0:
+            y = jnp.where(lane >= 1, pltpu.roll(y, 1, 1), 0.0)
+        elif e == 2:
+            y = jnp.where(lane <= cols - 2, pltpu.roll(y, width - 1, 1), 0.0)
+        acc = y if acc is None else acc + y
+    if relu:
+        out_ref[...] = jnp.maximum(acc, 0.0).astype(out_ref.dtype)
+    else:
+        for r in range(rows):
+            out_ref[r] = acc[:, r * cols : (r + 1) * cols]
+
+
+def banded(kernel, depth):
+    shift = (
+        jnp.arange(depth)[None, :, None] + jnp.arange(3)[:, None, None] - 1
+        == jnp.arange(depth)[None, None, :]
+    ).astype(kernel.dtype)
+    if kernel.ndim == 5:
+        mats = jnp.einsum("abeio,adz->ebodiz", kernel, shift, preferred_element_type=jnp.float32)
+    else:
+        mats = jnp.einsum("abei,adz->ebdiz", kernel, shift, preferred_element_type=jnp.float32)
+    outs = mats.shape[2] * mats.shape[3] if kernel.ndim == 5 else mats.shape[2]
+    return mats.astype(kernel.dtype).reshape(3, 3, outs, -1)
+
+
+def conv_rows(framed, mats, relu, rows, cols):
+    outs = mats.shape[2]
+    if relu:
+        out_shape = jax.ShapeDtypeStruct((outs, rows * cols), jnp.bfloat16)
+    else:
+        out_shape = jax.ShapeDtypeStruct((rows, outs, cols), jnp.float32)
+    return pl.pallas_call(
+        functools.partial(conv_kernel, relu=relu, rows=rows, cols=cols),
+        out_shape=out_shape,
+        in_specs=[pl.BlockSpec(memory_space=pltpu.VMEM), pl.BlockSpec(memory_space=pltpu.VMEM)],
+        out_specs=pl.BlockSpec(memory_space=pltpu.VMEM),
+    )(framed, mats)
+
+
+def halo_cols(block, cols):
+    count = lax.axis_size("view")
+    forward = [(i, i + 1) for i in range(count - 1)]
+    backward = [(target, source) for source, target in forward]
+    low = lax.ppermute(block[:, block.shape[1] - cols :], "view", forward)
+    high = lax.ppermute(block[:, :cols], "view", backward)
+    return jnp.concatenate([low, block, high], axis=1)
 
 
 def pad_rows(volume):
@@ -193,9 +254,10 @@
     tallies = jnp.sum(onehot.astype(jnp.float32), axis=1)
     cost_volume = (summed / jnp.maximum(tallies, 1.0)[:, None]).astype(jnp.bfloat16)
     columns = tpix // TROWS
-    volume = cost_volume.reshape(DEPTH, GROUPS, TROWS, columns).transpose(2, 1, 0, 3)
-    hidden = jax.nn.relu(convolve_full(pad_rows(volume), kern_one)).astype(jnp.bfloat16)
-    scores = convolve_final(pad_rows(hidden), kern_two)
+    volume = cost_volume.reshape(DEPTH, GROUPS, TROWS * columns).transpose(1, 0, 2)
+    volume = volume.reshape(GROUPS * DEPTH, TROWS * columns)
+    hidden = conv_rows(halo_cols(volume, columns), banded(kern_one, DEPTH), True, TROWS, columns)
+    scores = conv_rows(halo_cols(hidden, columns), banded(kern_two, DEPTH), False, TROWS, columns)
     return scores
 
 

time: 93.6 us -> 109 us (1.16)
  local copies, waits for them, and re-layouts: 6.84 us -> 32.2 us
  matrix products: 19.4 us -> 6.01 us
  Pallas kernels: 5.03 us -> 14.2 us
  waiting for transfers between devices: 32.2 us -> 28 us
  other arithmetic: 7.16 us -> 3.24 us
  starting transfers between devices: 21.9 us -> 23.7 us
    reshape x2 -> x4, local copies, waits for them, and re-layouts: 0.44 us -> 15.1 us  [the longest x3 15 us: banded(): return mats.astype(kernel.dtype).reshape(3, 3, outs, -1)]
    dot_general x54 -> x2, matrix products: 19 us -> 5.66 us  [the longest x1 5.11 us: banded(): jnp.einsum('abeio,adz->ebodiz', kernel, shift, preferred_element_type=jnp...]
    convert_element_type x0 -> x1, local copies, waits for them, and re-layouts: none -> 9.76 us  [banded(): return mats.astype(kernel.dtype).reshape(3, 3, outs, -1)]
    pallas_call x0 -> x2, Pallas kernels: none -> 9.17 us  [conv_rows(): pl.pallas_call(functools.partial(conv_kernel, relu=relu, rows=rows, cols=...]
    ppermute x4, waiting for transfers between devices: 8.95 us -> 2.8 us  [the longest x2 2.8 us: halo_cols(): high = lax.ppermute(block[:, :cols], 'view', backward)]
    all_to_all x1, waiting for transfers between devices: 9.3 us -> 11.3 us  [body(): lax.all_to_all(jnp.broadcast_to(ref_feat, (owners,) + ref_feat.shape[1:])...]
    ppermute x4, starting transfers between devices: 10.3 us -> 12 us  [the longest x2 8.16 us: halo_cols(): low = lax.ppermute(block[:, block.shape[1] - cols:], 'view', forward)]
  transfers between devices with their start and end apart: 6 -> 6, of which waited for: 4 -> 3; matrix products, arithmetic and copies ran while one was open for 5% -> 30% of each run, Pallas kernels for 0% -> 0%
where the time goes in v4:
time: 109 us; the launch traced here: 108 us
  local copies, waits for them, and re-layouts  32.2 us (30%)
  waiting for transfers between devices  28 us (26%)
  starting transfers between devices  23.7 us (22%)
  Pallas kernels  14.2 us (13%)
  matrix products  6.01 us (6%)
  other arithmetic  3.24 us (3%)
    reshape x3, local copies, waits for them, and re-layouts, banded(): return mats.astype(kernel.dtype).reshape(3, 3, outs, -1)  15 us
    all_to_all x1, waiting for transfers between devices, body(): lax.all_to_all(payload.reshape(owners, cap, GROUPS * tpix + 128), 'view',...  13.9 us
    all_to_all x1, waiting for transfers between devices, body(): lax.all_to_all(jnp.broadcast_to(ref_feat, (owners,) + ref_feat.shape[1:])...  11.3 us
    convert_element_type x1, local copies, waits for them, and re-layouts, banded(): return mats.astype(kernel.dtype).reshape(3, 3, outs, -1)  9.76 us
    pallas_call x2, Pallas kernels, conv_rows(): pl.pallas_call(functools.partial(conv_kernel, relu=relu, rows=rows, cols=...  9.17 us
    ppermute x2, starting transfers between devices, halo_cols(): low = lax.ppermute(block[:, block.shape[1] - cols:], 'view', forward)  8.16 us
    all_to_all x1, starting transfers between devices, body(): lax.all_to_all(jnp.broadcast_to(ref_feat, (owners,) + ref_feat.shape[1:])...  6.69 us
    dot_general x1, matrix products, banded(): jnp.einsum('abeio,adz->ebodiz', kernel, shift, preferred_element_type=jnp...  5.11 us
  transfers between devices with their start and end apart: 6, of which 3 were waited for; matrix products, arithmetic and copies ran while one was open for 30% of the time, Pallas kernels for 0%

profile of v4, /device:TPU:13, one launch (start us, length us, event | category | flops | bytes accessed | tf_op | source)
XLA Modules:
  0.0 107.6 jit_solution(4075555409336179165)
XLA Ops:
  0.0 1.7 %broadcast_in_dim.52 = bf16[16,32,512]{2,1,0:T(8,128)(2,1)} broadcast(bf16[32,512]{1,0:T(8,128)(2,1)} %bitcast.51), dimensions={1,2} | broadcast | bytes 557056 | tf_op jit(solution)/shard_map/broadcast_in_dim | solution.py:230
  1.7 6.7 %all-to-all-start = ((bf16[16,32,512]{2,1,0:T(8,128)(2,1)}), bf16[16,32,512]{2,1,0:T(8,128)(2,1)S(1)}, u32[]{:S(2)}, u32[]{:S(2)}) async-start(bf16[16,32,512]{2,1,0:T(8,128)(2,1)} %broadcast_in_dim.52), calls=%async_computation | async-start | bytes 1048576 | tf_op jit(solution)/shard_map/all_to_all | solution.py:229
  9.8 0.8 concatenate.15.blocks_ref
  10.7 11.3 %all-to-all-done.ref_ref = bf16[16,32,512]{2,1,0:T(8,128)(2,1)S(1)} async-done(((bf16[16,32,512]{2,1,0:T(8,128)(2,1)}), bf16[16,32,512]{2,1,0:T(8,128)(2,1)S(1)}, u32[]{:S(2)}, u32[]{:S(2)}) %all-to-all-start) | async-done | bytes 524320 | tf_op jit(solution)/shard_map/all_to_all | solution.py:229
  22.8 5.0 %shard_map.91 = bf16[512,512]{1,0:T(8,128)(2,1)} custom-call(s32[256]{0:T(256)} %select_n.23.blk_ref, bf16[65,32,128]{2,1,0:T(8,128)(2,1)} %concatenate.15.blocks_ref, bf16[512,512]{1,0:T(8,128)(2,1)} %bitcast.50, bf16[16,32,512]{2,1,0:T(8,128)(2,1)} %copy-done.1), custom_call_target="tpu_custom_call" | custom-call | tf_op jit(solution)/shard_map/pallas_call | solution.py:121
  27.8 1.4 %concatenate.16 = bf16[16,4,4096]{2,1,0:T(4,128)(2,1)S(1)} reshape(bf16[512,512]{1,0:T(8,128)(2,1)} %shard_map.91) | data formatting | bytes 1048576 | tf_op jit(solution)/shard_map/concatenate | solution.py:240
  29.3 1.0 pad_maximum_fusion.2
  30.4 5.0 %all-to-all-start.1 = ((bf16[16,4,4224]{2,1,0:T(4,128)(2,1)}), bf16[16,4,4224]{2,1,0:T(4,128)(2,1)S(1)}, u32[]{:S(2)}, u32[]{:S(2)}) async-start(bf16[16,4,4224]{2,1,0:T(4,128)(2,1)} %pad_maximum_fusion.2), calls=%async_computation.1 | async-start | bytes 1081344 | tf_op jit(solution)/shard_map/all_to_all | solution.py:241
  35.4 13.9 %all-to-all-done.1 = bf16[16,4,4224]{2,1,0:T(4,128)(2,1)S(1)} async-done(((bf16[16,4,4224]{2,1,0:T(4,128)(2,1)}), bf16[16,4,4224]{2,1,0:T(4,128)(2,1)S(1)}, u32[]{:S(2)}, u32[]{:S(2)}) %all-to-all-start.1) | async-done | bytes 540704 | tf_op jit(solution)/shard_map/all_to_all | solution.py:241
  50.2 3.6 %collective-permute-start = (bf16[512,128]{1,0:T(8,128)(2,1)S(1)}, bf16[512,128]{1,0:T(8,128)(2,1)S(1)}, u32[]{:S(2)}, u32[]{:S(2)}) collective-permute-start(bf16[512,128]{1,0:T(8,128)(2,1)S(1)} %get-tuple-element.7), channel_id=1, source_target_pairs={{0,1},{1,2},{2,3},{3,4},{4,5},{5,6},{6,7},{7,8},{8,9},{9,10},{10,1... | collective-permute-start | bytes 393224 | tf_op jit(solution)/shard_map/ppermute | solution.py:192
  53.8 1.9 %collective-permute-start.1 = (bf16[512,128]{1,0:T(8,128)(2,1)S(1)}, bf16[512,128]{1,0:T(8,128)(2,1)S(1)}, u32[]{:S(2)}, u32[]{:S(2)}) collective-permute-start(bf16[512,128]{1,0:T(8,128)(2,1)S(1)} %get-tuple-element.8), channel_id=1, source_target_pairs={{1,0},{2,1},{3,2},{4,3},{5,4},{6,5},{7,6},{8,7},{9,8},{10,9},{11,1... | collective-permute-start | bytes 393224 | tf_op jit(solution)/shard_map/ppermute | solution.py:193
  55.8 5.1 %convert_bitcast_fusion = bf16[3,3,8,64,8,64]{5,2,4,0,1,3:T(8,128)(2,1)} fusion(bf16[3,3,3,8,8]{4,3,2,1,0:T(8,128)(2,1)S(1)} %copy-done.3, s32[3,64]{0,1:T(8,128)S(1)} %add_add_fusion), kind=kOutput, calls=%fused_computation | convolution fusion | flops 16527360 | bytes 4722816 | tf_op jit(solution)/shard_map/abeio,adz->ebodiz/dot_general | solution.py:167
  60.9 9.8 %copy.38 = bf16[3,3,8,64,8,64]{5,4,3,2,1,0:T(8,128)(2,1)} copy(bf16[3,3,8,64,8,64]{5,2,4,0,1,3:T(8,128)(2,1)} %convert_bitcast_fusion) | data formatting | bytes 9437184 | tf_op jit(solution)/shard_map/convert_element_type | solution.py:171
  70.6 13.2 %reshape.104.m_ref = bf16[3,3,512,512]{3,2,1,0:T(8,128)(2,1)} reshape(bf16[3,3,8,64,8,64]{5,4,3,2,1,0:T(8,128)(2,1)} %copy.38) | data formatting | bytes 9437184 | tf_op jit(solution)/shard_map/reshape | solution.py:171
  83.8 1.0 pad_maximum_fusion.x_ref
  84.8 6.2 %shard_map.92 = bf16[512,512]{1,0:T(8,128)(2,1)} custom-call(bf16[512,768]{1,0:T(8,128)(2,1)} %pad_maximum_fusion.x_ref, bf16[3,3,512,512]{3,2,1,0:T(8,128)(2,1)} %reshape.104.m_ref), custom_call_target="tpu_custom_call" | custom-call | tf_op jit(solution)/shard_map/pallas_call | solution.py:180
  91.0 1.0 fusion.20
  91.9 4.5 %collective-permute-start.2 = (bf16[512,128]{1,0:T(8,128)(2,1)S(1)}, bf16[512,128]{1,0:T(8,128)(2,1)S(1)}, u32[]{:S(2)}, u32[]{:S(2)}) collective-permute-start(bf16[512,128]{1,0:T(8,128)(2,1)S(1)} %get-tuple-element.5), channel_id=1, source_target_pairs={{0,1},{1,2},{2,3},{3,4},{4,5},{5,6},{6,7},{7,8},{8,9},{9,10},{10,1... | collective-permute-start | bytes 393224 | tf_op jit(solution)/shard_map/ppermute | solution.py:192
  96.5 1.9 %collective-permute-start.3 = (bf16[512,128]{1,0:T(8,128)(2,1)S(1)}, bf16[512,128]{1,0:T(8,128)(2,1)S(1)}, u32[]{:S(2)}, u32[]{:S(2)}) collective-permute-start(bf16[512,128]{1,0:T(8,128)(2,1)S(1)} %get-tuple-element.6), channel_id=1, source_target_pairs={{1,0},{2,1},{3,2},{4,3},{5,4},{6,5},{7,6},{8,7},{9,8},{10,9},{11,1... | collective-permute-start | bytes 393224 | tf_op jit(solution)/shard_map/ppermute | solution.py:193
  99.0 0.9 reshape.110
  99.9 1.0 copy.43.m_ref
  100.9 2.8 %collective-permute-done.3 = bf16[512,128]{1,0:T(8,128)(2,1)S(1)} collective-permute-done((bf16[512,128]{1,0:T(8,128)(2,1)S(1)}, bf16[512,128]{1,0:T(8,128)(2,1)S(1)}, u32[]{:S(2)}, u32[]{:S(2)}) %collective-permute-start.3) | collective-permute-done | bytes 131104 | tf_op jit(solution)/shard_map/ppermute | solution.py:193
  103.7 1.0 pad_maximum_fusion.1.x_ref
  104.6 3.0 %shard_map.93 = f32[4,64,128]{2,1,0:T(8,128)} custom-call(bf16[512,768]{1,0:T(8,128)(2,1)} %pad_maximum_fusion.1.x_ref, bf16[3,3,64,512]{3,2,1,0:T(8,128)(2,1)} %copy.43.m_ref), custom_call_target="tpu_custom_call" | custom-call | tf_op jit(solution)/shard_map/pallas_call | solution.py:180
  (42 shorter events, 3.7 us)
Async XLA Ops:
  0.0 8.4 %copy-start.8 = (s32[1,64]{1,0:T(1,128)S(1)}, s32[1,64]{1,0:T(1,128)}, u32[]{:S(2)}) copy-start(s32[1,64]{1,0:T(1,128)} %param.14) | copy-start | bytes 772
  0.0 8.4 %copy-start.5 = (s32[1,64,4]{1,2,0:T(4,128)S(1)}, s32[1,64,4]{1,2,0:T(4,128)}, u32[]{:S(2)}) copy-start(s32[1,64,4]{1,2,0:T(4,128)} %param.13) | copy-start | bytes 3076
  0.0 8.4 %copy-start.6 = (s32[1,64,4]{1,2,0:T(4,128)S(1)}, s32[1,64,4]{1,2,0:T(4,128)}, u32[]{:S(2)}) copy-start(s32[1,64,4]{1,2,0:T(4,128)} %param.12) | copy-start | bytes 3076
  0.0 9.2 %copy-start.2 = (bf16[1,32,8192]{2,1,0:T(8,128)(2,1)S(1)}, bf16[1,32,8192]{2,1,0:T(8,128)(2,1)}, u32[]{:S(2)}) copy-start(bf16[1,32,8192]{2,1,0:T(8,128)(2,1)} %param.9) | copy-start | bytes 1572868
  1.7 8.0 %copy-start.7 = (s32[1,64]{1,0:T(1,128)S(1)}, s32[1,64]{1,0:T(1,128)}, u32[]{:S(2)}) copy-start(s32[1,64]{1,0:T(1,128)} %param.15) | copy-start | bytes 772
  1.7 20.3 %all-to-all-start = ((bf16[16,32,512]{2,1,0:T(8,128)(2,1)}), bf16[16,32,512]{2,1,0:T(8,128)(2,1)S(1)}, u32[]{:S(2)}, u32[]{:S(2)}) async-start(bf16[16,32,512]{2,1,0:T(8,128)(2,1)} %broadcast_in_dim.52), calls=%async_computation | async-start | bytes 1048576 | tf_op jit(solution)/shard_map/all_to_all | solution.py:229
  22.0 0.8 copy-start.1
  30.4 19.0 %all-to-all-start.1 = ((bf16[16,4,4224]{2,1,0:T(4,128)(2,1)}), bf16[16,4,4224]{2,1,0:T(4,128)(2,1)S(1)}, u32[]{:S(2)}, u32[]{:S(2)}) async-start(bf16[16,4,4224]{2,1,0:T(4,128)(2,1)} %pad_maximum_fusion.2), calls=%async_computation.1 | async-start | bytes 1081344 | tf_op jit(solution)/shard_map/all_to_all | solution.py:241
  50.1 5.6 %copy-start.3 = (bf16[3,3,3,8,8]{4,3,2,1,0:T(8,128)(2,1)S(1)}, bf16[3,3,3,8,8]{4,3,2,1,0:T(8,128)(2,1)}, u32[]{:S(2)}) copy-start(bf16[3,3,3,8,8]{4,3,2,1,0:T(8,128)(2,1)} %param.16) | copy-start | bytes 10372
  50.2 33.6 %collective-permute-start = (bf16[512,128]{1,0:T(8,128)(2,1)S(1)}, bf16[512,128]{1,0:T(8,128)(2,1)S(1)}, u32[]{:S(2)}, u32[]{:S(2)}) collective-permute-start(bf16[512,128]{1,0:T(8,128)(2,1)S(1)} %get-tuple-element.7), channel_id=1, source_target_pairs={{0,1},{1,2},{2,3},{3,4},{4,5},{5,6},{6,7},{7,8},{8,9},{9,10},{10,1... | collective-permute-start | bytes 393224 | tf_op jit(solution)/shard_map/ppermute | solution.py:192
  53.8 30.0 %collective-permute-start.1 = (bf16[512,128]{1,0:T(8,128)(2,1)S(1)}, bf16[512,128]{1,0:T(8,128)(2,1)S(1)}, u32[]{:S(2)}, u32[]{:S(2)}) collective-permute-start(bf16[512,128]{1,0:T(8,128)(2,1)S(1)} %get-tuple-element.8), channel_id=1, source_target_pairs={{1,0},{2,1},{3,2},{4,3},{5,4},{6,5},{7,6},{8,7},{9,8},{10,9},{11,1... | collective-permute-start | bytes 393224 | tf_op jit(solution)/shard_map/ppermute | solution.py:193
  84.8 13.7 %copy-start.4 = (bf16[3,3,3,8]{3,2,1,0:T(4,128)(2,1)S(1)}, bf16[3,3,3,8]{3,2,1,0:T(4,128)(2,1)}, u32[]{:S(2)}) copy-start(bf16[3,3,3,8]{3,2,1,0:T(4,128)(2,1)} %param.17) | copy-start | bytes 1300
  91.9 8.9 %collective-permute-start.2 = (bf16[512,128]{1,0:T(8,128)(2,1)S(1)}, bf16[512,128]{1,0:T(8,128)(2,1)S(1)}, u32[]{:S(2)}, u32[]{:S(2)}) collective-permute-start(bf16[512,128]{1,0:T(8,128)(2,1)S(1)} %get-tuple-element.5), channel_id=1, source_target_pairs={{0,1},{1,2},{2,3},{3,4},{4,5},{5,6},{6,7},{7,8},{8,9},{9,10},{10,1... | collective-permute-start | bytes 393224 | tf_op jit(solution)/shard_map/ppermute | solution.py:192
  96.5 7.2 %collective-permute-start.3 = (bf16[512,128]{1,0:T(8,128)(2,1)S(1)}, bf16[512,128]{1,0:T(8,128)(2,1)S(1)}, u32[]{:S(2)}, u32[]{:S(2)}) collective-permute-start(bf16[512,128]{1,0:T(8,128)(2,1)S(1)} %get-tuple-element.6), channel_id=1, source_target_pairs={{1,0},{2,1},{3,2},{4,3},{5,4},{6,5},{7,6},{8,7},{9,8},{10,9},{11,1... | collective-permute-start | bytes 393224 | tf_op jit(solution)/shard_map/ppermute | solution.py:193
  99.0 4.7 %copy-start = (bf16[512,512]{1,0:T(8,128)(2,1)S(1)}, bf16[512,512]{1,0:T(8,128)(2,1)}, u32[]{:S(2)}) copy-start(bf16[512,512]{1,0:T(8,128)(2,1)} %shard_map.92) | copy-start | bytes 1572868

commit v5 on v3

--- a/solution.py
+++ b/solution.py
@@ -1,3 +1,5 @@
+import functools
+
 import jax
 import jax.numpy as jnp
 from jax import lax
@@ -133,6 +135,76 @@
     )(blk, blocks, table, refs)
 
 
+def conv_kernel(x_ref, m_ref, out_ref, *, relu, rows, cols, groups, chunk):
+    width = rows * cols
+    outs = m_ref.shape[2]
+    depth = x_ref.shape[0] // groups - 2
+    lane = lax.broadcasted_iota(jnp.int32, (outs, width), 1) % cols
+    for k in range(depth // chunk):
+        acc = None
+        for e in range(3):
+            y = None
+            for b in range(3):
+                window = x_ref[k * chunk * groups : (k * chunk + chunk + 2) * groups, b * cols : b * cols + width]
+                part = jnp.dot(m_ref[e, b], window, preferred_element_type=jnp.float32)
+                y = part if y is None else y + part
+            if e == 0:
+                y = jnp.where(lane >= 1, pltpu.roll(y, 1, 1), 0.0)
+            elif e == 2:
+                y = jnp.where(lane <= cols - 2, pltpu.roll(y, width - 1, 1), 0.0)
+            acc = y if acc is None else acc + y
+        if relu:
+            out_ref[(k * chunk + 1) * outs // chunk : (k * chunk + chunk + 1) * outs // chunk, :] = (
+                jnp.maximum(acc, 0.0).astype(out_ref.dtype)
+            )
+        else:
+            for r in range(rows):
+                out_ref[r, k * chunk : (k + 1) * chunk, :] = acc[:, r * cols : (r + 1) * cols]
+    if relu:
+        pad = jnp.zeros((outs // chunk, width), out_ref.dtype)
+        out_ref[: outs // chunk, :] = pad
+        out_ref[out_ref.shape[0] - outs // chunk :, :] = pad
+
+
+def banded(kernel, chunk):
+    shift = (
+        jnp.arange(chunk)[None, :, None] + jnp.arange(3)[:, None, None]
+        == jnp.arange(chunk + 2)[None, None, :]
+    ).astype(kernel.dtype)
+    if kernel.ndim == 5:
+        mats = jnp.einsum("abeio,adz->ebdozi", kernel, shift, preferred_element_type=jnp.float32)
+        outs = chunk * kernel.shape[4]
+    else:
+        mats = jnp.einsum("abei,adz->ebdzi", kernel, shift, preferred_element_type=jnp.float32)
+        outs = chunk
+    return mats.astype(kernel.dtype).reshape(3, 3, outs, -1)
+
+
+def conv_rows(framed, mats, relu, rows, cols, chunk):
+    outs = mats.shape[2]
+    groups = mats.shape[3] // (chunk + 2)
+    depth = framed.shape[0] // groups - 2
+    if relu:
+        out_shape = jax.ShapeDtypeStruct(((depth + 2) * outs // chunk, rows * cols), jnp.bfloat16)
+    else:
+        out_shape = jax.ShapeDtypeStruct((rows, depth, cols), jnp.float32)
+    return pl.pallas_call(
+        functools.partial(conv_kernel, relu=relu, rows=rows, cols=cols, groups=groups, chunk=chunk),
+        out_shape=out_shape,
+        in_specs=[pl.BlockSpec(memory_space=pltpu.VMEM), pl.BlockSpec(memory_space=pltpu.VMEM)],
+        out_specs=pl.BlockSpec(memory_space=pltpu.VMEM),
+    )(framed, mats)
+
+
+def halo_cols(block, cols):
+    count = lax.axis_size("view")
+    forward = [(i, i + 1) for i in range(count - 1)]
+    backward = [(target, source) for source, target in forward]
+    low = lax.ppermute(block[:, block.shape[1] - cols :], "view", forward)
+    high = lax.ppermute(block[:, :cols], "view", backward)
+    return jnp.concatenate([low, block, high], axis=1)
+
+
 def pad_rows(volume):
     return with_halo(volume, (("view", 0),), 1)
 
@@ -193,9 +265,14 @@
     tallies = jnp.sum(onehot.astype(jnp.float32), axis=1)
     cost_volume = (summed / jnp.maximum(tallies, 1.0)[:, None]).astype(jnp.bfloat16)
     columns = tpix // TROWS
-    volume = cost_volume.reshape(DEPTH, GROUPS, TROWS, columns).transpose(2, 1, 0, 3)
-    hidden = jax.nn.relu(convolve_full(pad_rows(volume), kern_one)).astype(jnp.bfloat16)
-    scores = convolve_final(pad_rows(hidden), kern_two)
+    volume = cost_volume.reshape(DEPTH * GROUPS, TROWS * columns)
+    volume = jnp.pad(volume, ((GROUPS, GROUPS), (0, 0)))
+    hidden = conv_rows(
+        halo_cols(volume, columns), banded(kern_one, DEPTH // 4), True, TROWS, columns, DEPTH // 4
+    )
+    scores = conv_rows(
+        halo_cols(hidden, columns), banded(kern_two, DEPTH), False, TROWS, columns, DEPTH
+    )
     return scores
 
 

time: 93.6 us -> 98.9 us (1.057)
  local copies, waits for them, and re-layouts: 6.84 us -> 30.4 us
  matrix products: 19.4 us -> 1.74 us
  waiting for transfers between devices: 32.2 us -> 25 us
  Pallas kernels: 5.03 us -> 11.9 us
  other arithmetic: 7.16 us -> 5.3 us
  starting transfers between devices: 21.9 us -> 23.7 us
    dot_general x54 -> x2, matrix products: 19 us -> 1.38 us  [the longest x1 0.83 us: banded(): jnp.einsum('abeio,adz->ebdozi', kernel, shift, preferred_element_type=jnp...]
    convert_element_type x0 -> x2, local copies, waits for them, and re-layouts: none -> 12.9 us  [banded(): return mats.astype(kernel.dtype).reshape(3, 3, outs, -1)]
    reshape x2 -> x4, local copies, waits for them, and re-layouts: 0.44 us -> 10 us  [the longest x3 9.8 us: banded(): return mats.astype(kernel.dtype).reshape(3, 3, outs, -1)]
    ppermute x4, waiting for transfers between devices: 8.95 us -> 1.75 us  [the longest x2 1.74 us: halo_cols(): high = lax.ppermute(block[:, :cols], 'view', backward)]
    pallas_call x0 -> x2, Pallas kernels: none -> 6.83 us  [conv_rows(): pl.pallas_call(functools.partial(conv_kernel, relu=relu, rows=rows, cols=...]
    ppermute x4, starting transfers between devices: 10.3 us -> 12 us  [the longest x2 8.16 us: halo_cols(): low = lax.ppermute(block[:, block.shape[1] - cols:], 'view', forward)]
  transfers between devices with their start and end apart: 6 -> 6, of which waited for: 4 -> 3; matrix products, arithmetic and copies ran while one was open for 5% -> 29% of each run, Pallas kernels for 0% -> 0%
where the time goes in v5:
time: 98.9 us; the launch traced here: 98.2 us
  local copies, waits for them, and re-layouts  30.4 us (31%)
  waiting for transfers between devices  25 us (25%)
  starting transfers between devices  23.7 us (24%)
  Pallas kernels  11.9 us (12%)
  other arithmetic  5.3 us (5%)
  matrix products  1.74 us (2%)
    all_to_all x1, waiting for transfers between devices, body(): lax.all_to_all(payload.reshape(owners, cap, GROUPS * tpix + 128), 'view',...  14 us
    convert_element_type x2, local copies, waits for them, and re-layouts, banded(): return mats.astype(kernel.dtype).reshape(3, 3, outs, -1)  12.9 us
    reshape x3, local copies, waits for them, and re-layouts, banded(): return mats.astype(kernel.dtype).reshape(3, 3, outs, -1)  9.8 us
    all_to_all x1, waiting for transfers between devices, body(): lax.all_to_all(jnp.broadcast_to(ref_feat, (owners,) + ref_feat.shape[1:])...  9.29 us
    ppermute x2, starting transfers between devices, halo_cols(): low = lax.ppermute(block[:, block.shape[1] - cols:], 'view', forward)  8.16 us
    pallas_call x2, Pallas kernels, conv_rows(): pl.pallas_call(functools.partial(conv_kernel, relu=relu, rows=rows, cols=...  6.83 us
    all_to_all x1, starting transfers between devices, body(): lax.all_to_all(jnp.broadcast_to(ref_feat, (owners,) + ref_feat.shape[1:])...  6.69 us
    pallas_call x1, Pallas kernels, correlate(): pl.pallas_call(correlate_kernel, out_shape=jax.ShapeDtypeStruct((units *...  5.04 us
  transfers between devices with their start and end apart: 6, of which 3 were waited for; matrix products, arithmetic and copies ran while one was open for 29% of the time, Pallas kernels for 0%

profile of v5, /device:TPU:13, one launch (start us, length us, event | category | flops | bytes accessed | tf_op | source)
XLA Modules:
  0.0 98.2 jit_solution(3896949447879828036)
XLA Ops:
  0.0 1.6 %broadcast_in_dim.52 = bf16[16,32,512]{2,1,0:T(8,128)(2,1)} broadcast(bf16[32,512]{1,0:T(8,128)(2,1)} %bitcast.41), dimensions={1,2} | broadcast | bytes 557056 | tf_op jit(solution)/shard_map/broadcast_in_dim | solution.py:241
  1.7 6.7 %all-to-all-start = ((bf16[16,32,512]{2,1,0:T(8,128)(2,1)}), bf16[16,32,512]{2,1,0:T(8,128)(2,1)S(1)}, u32[]{:S(2)}, u32[]{:S(2)}) async-start(bf16[16,32,512]{2,1,0:T(8,128)(2,1)} %broadcast_in_dim.52), calls=%async_computation | async-start | bytes 1048576 | tf_op jit(solution)/shard_map/all_to_all | solution.py:240
  11.8 0.8 concatenate.15.blocks_ref
  12.6 9.3 %all-to-all-done.ref_ref = bf16[16,32,512]{2,1,0:T(8,128)(2,1)S(1)} async-done(((bf16[16,32,512]{2,1,0:T(8,128)(2,1)}), bf16[16,32,512]{2,1,0:T(8,128)(2,1)S(1)}, u32[]{:S(2)}, u32[]{:S(2)}) %all-to-all-start) | async-done | bytes 524320 | tf_op jit(solution)/shard_map/all_to_all | solution.py:240
  22.7 5.0 %shard_map.91 = bf16[512,512]{1,0:T(8,128)(2,1)} custom-call(s32[256]{0:T(256)} %select_n.23.blk_ref, bf16[65,32,128]{2,1,0:T(8,128)(2,1)} %concatenate.15.blocks_ref, bf16[512,512]{1,0:T(8,128)(2,1)} %bitcast.40, bf16[16,32,512]{2,1,0:T(8,128)(2,1)} %copy-done.1), custom_call_target="tpu_custom_call" | custom-call | tf_op jit(solution)/shard_map/pallas_call | solution.py:121
  27.8 1.4 %concatenate.16 = bf16[16,4,4096]{2,1,0:T(4,128)(2,1)S(1)} reshape(bf16[512,512]{1,0:T(8,128)(2,1)} %shard_map.91) | data formatting | bytes 1048576 | tf_op jit(solution)/shard_map/concatenate | solution.py:251
  29.3 1.0 %pad_maximum_fusion.2 = bf16[16,4,4224]{2,1,0:T(4,128)(2,1)} fusion(bf16[16,4,128]{2,1,0:T(4,128)(2,1)S(1)} %broadcast_in_dim.54, bf16[16,4,4096]{2,1,0:T(4,128)(2,1)S(1)} %concatenate.16), kind=kLoop, calls=%fused_computation.7 | loop fusion | flops 1081344 | bytes 1081344 | tf_op jit(solution)/shard_map/concatenate | solution.py:251
  30.3 5.0 %all-to-all-start.1 = ((bf16[16,4,4224]{2,1,0:T(4,128)(2,1)}), bf16[16,4,4224]{2,1,0:T(4,128)(2,1)S(1)}, u32[]{:S(2)}, u32[]{:S(2)}) async-start(bf16[16,4,4224]{2,1,0:T(4,128)(2,1)} %pad_maximum_fusion.2), calls=%async_computation.1 | async-start | bytes 1081344 | tf_op jit(solution)/shard_map/all_to_all | solution.py:252
  35.3 14.0 %all-to-all-done.1 = bf16[16,4,4224]{2,1,0:T(4,128)(2,1)S(1)} async-done(((bf16[16,4,4224]{2,1,0:T(4,128)(2,1)}), bf16[16,4,4224]{2,1,0:T(4,128)(2,1)S(1)}, u32[]{:S(2)}, u32[]{:S(2)}) %all-to-all-start.1) | async-done | bytes 540704 | tf_op jit(solution)/shard_map/all_to_all | solution.py:252
  50.4 3.6 %collective-permute-start = (bf16[528,128]{1,0:T(8,128)(2,1)S(1)}, bf16[528,128]{1,0:T(8,128)(2,1)S(1)}, u32[]{:S(2)}, u32[]{:S(2)}) collective-permute-start(bf16[528,128]{1,0:T(8,128)(2,1)S(1)} %get-tuple-element.7), channel_id=1, source_target_pairs={{0,1},{1,2},{2,3},{3,4},{4,5},{5,6},{6,7},{7,8},{8,9},{9,10},{10,1... | collective-permute-start | bytes 405512 | tf_op jit(solution)/shard_map/ppermute | solution.py:203
  54.0 1.9 %collective-permute-start.1 = (bf16[528,128]{1,0:T(8,128)(2,1)S(1)}, bf16[528,128]{1,0:T(8,128)(2,1)S(1)}, u32[]{:S(2)}, u32[]{:S(2)}) collective-permute-start(bf16[528,128]{1,0:T(8,128)(2,1)S(1)} %get-tuple-element.8), channel_id=1, source_target_pairs={{1,0},{2,1},{3,2},{4,3},{5,4},{6,5},{7,6},{8,7},{9,8},{10,9},{11,1... | collective-permute-start | bytes 405512 | tf_op jit(solution)/shard_map/ppermute | solution.py:204
  56.8 11.6 %copy.38 = bf16[3,3,16,8,18,8]{3,2,5,4,1,0:T(8,128)(2,1)} copy(bf16[3,3,16,8,18,8]{4,3,5,0,1,2:T(8,128)(2,1)S(1)} %convert_bitcast_fusion) | data formatting | bytes 663552 | tf_op jit(solution)/shard_map/convert_element_type | solution.py:180
  68.3 7.1 %reshape.113 = bf16[3,3,128,144]{2,3,1,0:T(8,128)(2,1)S(1)} reshape(bf16[3,3,16,8,18,8]{3,2,5,4,1,0:T(8,128)(2,1)} %copy.38) | data formatting | bytes 663552 | tf_op jit(solution)/shard_map/reshape | solution.py:180
  75.4 1.1 %copy.39.m_ref = bf16[3,3,128,144]{3,2,1,0:T(8,128)(2,1)} copy(bf16[3,3,128,144]{2,3,1,0:T(8,128)(2,1)S(1)} %reshape.113) | data formatting | bytes 663552 | tf_op jit(solution)/shard_map/reshape | solution.py:180
  76.6 1.0 pad_maximum_fusion.x_ref
  77.6 3.6 %shard_map.92 = bf16[528,512]{1,0:T(8,128)(2,1)} custom-call(bf16[528,768]{1,0:T(8,128)(2,1)} %pad_maximum_fusion.x_ref, bf16[3,3,128,144]{3,2,1,0:T(8,128)(2,1)} %copy.39.m_ref), custom_call_target="tpu_custom_call" | custom-call | tf_op jit(solution)/shard_map/pallas_call | solution.py:191
  81.2 1.0 %fusion.20 = (bf16[528,128]{1,0:T(8,128)(2,1)S(1)}, bf16[528,128]{1,0:T(8,128)(2,1)S(1)}) fusion(bf16[528,512]{1,0:T(8,128)(2,1)} %shard_map.92), kind=kLoop, calls=%fused_computation.41 | loop fusion | bytes 540672 | tf_op jit(solution)/shard_map/slice | solution.py:203
  82.2 4.5 %collective-permute-start.2 = (bf16[528,128]{1,0:T(8,128)(2,1)S(1)}, bf16[528,128]{1,0:T(8,128)(2,1)S(1)}, u32[]{:S(2)}, u32[]{:S(2)}) collective-permute-start(bf16[528,128]{1,0:T(8,128)(2,1)S(1)} %get-tuple-element.5), channel_id=1, source_target_pairs={{0,1},{1,2},{2,3},{3,4},{4,5},{5,6},{6,7},{7,8},{8,9},{9,10},{10,1... | collective-permute-start | bytes 405512 | tf_op jit(solution)/shard_map/ppermute | solution.py:203
  86.7 1.9 %collective-permute-start.3 = (bf16[528,128]{1,0:T(8,128)(2,1)S(1)}, bf16[528,128]{1,0:T(8,128)(2,1)S(1)}, u32[]{:S(2)}, u32[]{:S(2)}) collective-permute-start(bf16[528,128]{1,0:T(8,128)(2,1)S(1)} %get-tuple-element.6), channel_id=1, source_target_pairs={{1,0},{2,1},{3,2},{4,3},{5,4},{6,5},{7,6},{8,7},{9,8},{10,9},{11,1... | collective-permute-start | bytes 405512 | tf_op jit(solution)/shard_map/ppermute | solution.py:204
  89.2 1.3 %copy.41 = bf16[3,3,64,66,8]{2,4,3,1,0:T(8,128)(2,1)S(1)} copy(bf16[3,3,64,66,8]{3,4,0,1,2:T(8,128)(2,1)S(1)} %fusion.1) | data formatting | bytes 1216512 | tf_op jit(solution)/shard_map/convert_element_type | solution.py:180
  90.6 1.6 %copy.42.m_ref = bf16[3,3,64,528]{3,2,1,0:T(8,128)(2,1)} copy(bf16[3,3,64,528]{2,3,1,0:T(8,128)(2,1)S(1)} %bitcast.36) | data formatting | bytes 1216512 | tf_op jit(solution)/shard_map/reshape | solution.py:180
  92.2 1.7 %collective-permute-done.3 = bf16[528,128]{1,0:T(8,128)(2,1)S(1)} collective-permute-done((bf16[528,128]{1,0:T(8,128)(2,1)S(1)}, bf16[528,128]{1,0:T(8,128)(2,1)S(1)}, u32[]{:S(2)}, u32[]{:S(2)}) %collective-permute-start.3) | collective-permute-done | bytes 135200 | tf_op jit(solution)/shard_map/ppermute | solution.py:204
  94.0 1.0 pad_maximum_fusion.1.x_ref
  94.9 3.2 %shard_map.93 = f32[4,64,128]{2,1,0:T(8,128)} custom-call(bf16[528,768]{1,0:T(8,128)(2,1)} %pad_maximum_fusion.1.x_ref, bf16[3,3,64,528]{3,2,1,0:T(8,128)(2,1)} %copy.42.m_ref), custom_call_target="tpu_custom_call" | custom-call | tf_op jit(solution)/shard_map/pallas_call | solution.py:191
  (41 shorter events, 6.8 us)
Async XLA Ops:
  0.0 11.2 %copy-start.2 = (bf16[1,32,8192]{2,1,0:T(8,128)(2,1)S(1)}, bf16[1,32,8192]{2,1,0:T(8,128)(2,1)}, u32[]{:S(2)}) copy-start(bf16[1,32,8192]{2,1,0:T(8,128)(2,1)} %param.9) | copy-start | bytes 1572868
  1.7 10.0 %copy-start.5 = (s32[1,64]{1,0:T(1,128)S(1)}, s32[1,64]{1,0:T(1,128)}, u32[]{:S(2)}) copy-start(s32[1,64]{1,0:T(1,128)} %param.15) | copy-start | bytes 772
  1.7 10.0 %copy-start.6 = (s32[1,64]{1,0:T(1,128)S(1)}, s32[1,64]{1,0:T(1,128)}, u32[]{:S(2)}) copy-start(s32[1,64]{1,0:T(1,128)} %param.14) | copy-start | bytes 772
  1.7 20.3 %all-to-all-start = ((bf16[16,32,512]{2,1,0:T(8,128)(2,1)}), bf16[16,32,512]{2,1,0:T(8,128)(2,1)S(1)}, u32[]{:S(2)}, u32[]{:S(2)}) async-start(bf16[16,32,512]{2,1,0:T(8,128)(2,1)} %broadcast_in_dim.52), calls=%async_computation | async-start | bytes 1048576 | tf_op jit(solution)/shard_map/all_to_all | solution.py:240
  21.9 0.8 copy-start.1
  30.3 19.0 %all-to-all-start.1 = ((bf16[16,4,4224]{2,1,0:T(4,128)(2,1)}), bf16[16,4,4224]{2,1,0:T(4,128)(2,1)S(1)}, u32[]{:S(2)}, u32[]{:S(2)}) async-start(bf16[16,4,4224]{2,1,0:T(4,128)(2,1)} %pad_maximum_fusion.2), calls=%async_computation.1 | async-start | bytes 1081344 | tf_op jit(solution)/shard_map/all_to_all | solution.py:252
  50.1 5.8 %copy-start.3 = (bf16[3,3,3,8,8]{4,3,2,1,0:T(8,128)(2,1)S(1)}, bf16[3,3,3,8,8]{4,3,2,1,0:T(8,128)(2,1)}, u32[]{:S(2)}) copy-start(bf16[3,3,3,8,8]{4,3,2,1,0:T(8,128)(2,1)} %param.16) | copy-start | bytes 10372
  50.4 26.2 %collective-permute-start = (bf16[528,128]{1,0:T(8,128)(2,1)S(1)}, bf16[528,128]{1,0:T(8,128)(2,1)S(1)}, u32[]{:S(2)}, u32[]{:S(2)}) collective-permute-start(bf16[528,128]{1,0:T(8,128)(2,1)S(1)} %get-tuple-element.7), channel_id=1, source_target_pairs={{0,1},{1,2},{2,3},{3,4},{4,5},{5,6},{6,7},{7,8},{8,9},{9,10},{10,1... | collective-permute-start | bytes 405512 | tf_op jit(solution)/shard_map/ppermute | solution.py:203
  54.0 22.6 %collective-permute-start.1 = (bf16[528,128]{1,0:T(8,128)(2,1)S(1)}, bf16[528,128]{1,0:T(8,128)(2,1)S(1)}, u32[]{:S(2)}, u32[]{:S(2)}) collective-permute-start(bf16[528,128]{1,0:T(8,128)(2,1)S(1)} %get-tuple-element.8), channel_id=1, source_target_pairs={{1,0},{2,1},{3,2},{4,3},{5,4},{6,5},{7,6},{8,7},{9,8},{10,9},{11,1... | collective-permute-start | bytes 405512 | tf_op jit(solution)/shard_map/ppermute | solution.py:204
  77.6 11.1 %copy-start.4 = (bf16[3,3,3,8]{3,2,1,0:T(4,128)(2,1)S(1)}, bf16[3,3,3,8]{3,2,1,0:T(4,128)(2,1)}, u32[]{:S(2)}) copy-start(bf16[3,3,3,8]{3,2,1,0:T(4,128)(2,1)} %param.17) | copy-start | bytes 1300
  82.2 10.0 %collective-permute-start.2 = (bf16[528,128]{1,0:T(8,128)(2,1)S(1)}, bf16[528,128]{1,0:T(8,128)(2,1)S(1)}, u32[]{:S(2)}, u32[]{:S(2)}) collective-permute-start(bf16[528,128]{1,0:T(8,128)(2,1)S(1)} %get-tuple-element.5), channel_id=1, source_target_pairs={{0,1},{1,2},{2,3},{3,4},{4,5},{5,6},{6,7},{7,8},{8,9},{9,10},{10,1... | collective-permute-start | bytes 405512 | tf_op jit(solution)/shard_map/ppermute | solution.py:203
  86.7 7.2 %collective-permute-start.3 = (bf16[528,128]{1,0:T(8,128)(2,1)S(1)}, bf16[528,128]{1,0:T(8,128)(2,1)S(1)}, u32[]{:S(2)}, u32[]{:S(2)}) collective-permute-start(bf16[528,128]{1,0:T(8,128)(2,1)S(1)} %get-tuple-element.6), channel_id=1, source_target_pairs={{1,0},{2,1},{3,2},{4,3},{5,4},{6,5},{7,6},{8,7},{9,8},{10,9},{11,1... | collective-permute-start | bytes 405512 | tf_op jit(solution)/shard_map/ppermute | solution.py:204
  89.2 4.7 %copy-start = (bf16[528,512]{1,0:T(8,128)(2,1)S(1)}, bf16[528,512]{1,0:T(8,128)(2,1)}, u32[]{:S(2)}) copy-start(bf16[528,512]{1,0:T(8,128)(2,1)} %shard_map.92) | copy-start | bytes 1622020

commit v6 on v5

--- a/solution.py
+++ b/solution.py
@@ -146,7 +146,7 @@
             y = None
             for b in range(3):
                 window = x_ref[k * chunk * groups : (k * chunk + chunk + 2) * groups, b * cols : b * cols + width]
-                part = jnp.dot(m_ref[e, b], window, preferred_element_type=jnp.float32)
+                part = jnp.dot(m_ref[b, e], window, preferred_element_type=jnp.float32)
                 y = part if y is None else y + part
             if e == 0:
                 y = jnp.where(lane >= 1, pltpu.roll(y, 1, 1), 0.0)
@@ -167,17 +167,29 @@
 
 
 def banded(kernel, chunk):
-    shift = (
-        jnp.arange(chunk)[None, :, None] + jnp.arange(3)[:, None, None]
-        == jnp.arange(chunk + 2)[None, None, :]
-    ).astype(kernel.dtype)
+    groups = kernel.shape[3]
+    cols = (chunk + 2) * groups
+    taps = kernel.reshape((3, 9) + kernel.shape[3:])
+    col = lax.iota(jnp.int32, cols)
+    spread = (col[None, :] % groups == jnp.arange(groups)[:, None]).astype(kernel.dtype)
     if kernel.ndim == 5:
-        mats = jnp.einsum("abeio,adz->ebdozi", kernel, shift, preferred_element_type=jnp.float32)
-        outs = chunk * kernel.shape[4]
+        outs = kernel.shape[4]
+        rows = chunk * outs
+        row = lax.iota(jnp.int32, rows)
+        pick = (row[:, None] % outs == jnp.arange(outs)[None, :]).astype(kernel.dtype)
+        lanes = jnp.einsum("xyio,ic->xyoc", taps, spread, preferred_element_type=jnp.float32)
+        tiles = jnp.einsum(
+            "ro,xyoc->xyrc", pick, lanes.astype(kernel.dtype), preferred_element_type=jnp.float32
+        )
+        depth_of_row = row // outs
     else:
-        mats = jnp.einsum("abei,adz->ebdzi", kernel, shift, preferred_element_type=jnp.float32)
-        outs = chunk
-    return mats.astype(kernel.dtype).reshape(3, 3, outs, -1)
+        rows = chunk
+        lanes = jnp.einsum("xyi,ic->xyc", taps, spread, preferred_element_type=jnp.float32)
+        tiles = lanes[:, :, None, :]
+        depth_of_row = lax.iota(jnp.int32, rows)
+    band = col[None, None, :] // groups == depth_of_row[None, :, None] + jnp.arange(3)[:, None, None]
+    mats = jnp.sum(jnp.where(band[:, None], tiles, 0.0), axis=0)
+    return mats.astype(kernel.dtype).reshape(3, 3, rows, cols)
 
 
 def conv_rows(framed, mats, relu, rows, cols, chunk):

time: 98.9 us -> 80.8 us (0.82)
  local copies, waits for them, and re-layouts: 30.4 us -> 9.01 us
  waiting for transfers between devices: 25 us -> 31.5 us
  starting transfers between devices: 23.7 us -> 21.4 us
    convert_element_type x2 -> x1, local copies, waits for them, and re-layouts: 12.9 us -> 1.06 us  [banded(): return mats.astype(kernel.dtype).reshape(3, 3, rows, cols)]
    reshape x3 -> x0, local copies, waits for them, and re-layouts: 9.8 us -> none  [banded(): return mats.astype(kernel.dtype).reshape(3, 3, outs, -1)]
    ppermute x2, waiting for transfers between devices: 1.74 us -> 8.55 us  [halo_cols(): high = lax.ppermute(block[:, :cols], 'view', backward)]
    ppermute x2, starting transfers between devices: 8.16 us -> 5.54 us  [halo_cols(): low = lax.ppermute(block[:, block.shape[1] - cols:], 'view', forward)]
    all_to_all x1, waiting for transfers between devices: 14 us -> 11.8 us  [body(): lax.all_to_all(payload.reshape(owners, cap, GROUPS * tpix + 128), 'view',...]
    all_to_all x1, waiting for transfers between devices: 9.29 us -> 11.1 us  [body(): lax.all_to_all(jnp.broadcast_to(ref_feat, (owners,) + ref_feat.shape[1:])...]
    reduce_sum x0 -> x1, other arithmetic: none -> 1.36 us  [banded(): mats = jnp.sum(jnp.where(band[:, None], tiles, 0.0), axis=0)]
  transfers between devices with their start and end apart: 6 -> 6, of which waited for: 3 -> 4; matrix products, arithmetic and copies ran while one was open for 29% -> 7% of each run, Pallas kernels for 0% -> 0%
where the time goes in v6:
time: 80.8 us; the launch traced here: 80.2 us
  waiting for transfers between devices  31.5 us (39%)
  starting transfers between devices  21.4 us (26%)
  Pallas kernels  11.9 us (15%)
  local copies, waits for them, and re-layouts  9.01 us (11%)
  other arithmetic  4.91 us (6%)
  matrix products  1.24 us (2%)
    all_to_all x1, waiting for transfers between devices, body(): lax.all_to_all(payload.reshape(owners, cap, GROUPS * tpix + 128), 'view',...  11.8 us
    all_to_all x1, waiting for transfers between devices, body(): lax.all_to_all(jnp.broadcast_to(ref_feat, (owners,) + ref_feat.shape[1:])...  11.1 us
    ppermute x2, waiting for transfers between devices, halo_cols(): high = lax.ppermute(block[:, :cols], 'view', backward)  8.55 us
    pallas_call x2, Pallas kernels, conv_rows(): pl.pallas_call(functools.partial(conv_kernel, relu=relu, rows=rows, cols=...  6.82 us
    all_to_all x1, starting transfers between devices, body(): lax.all_to_all(jnp.broadcast_to(ref_feat, (owners,) + ref_feat.shape[1:])...  6.55 us
    ppermute x2, starting transfers between devices, halo_cols(): low = lax.ppermute(block[:, block.shape[1] - cols:], 'view', forward)  5.54 us
    pallas_call x1, Pallas kernels, correlate(): pl.pallas_call(correlate_kernel, out_shape=jax.ShapeDtypeStruct((units *...  5.05 us
    all_to_all x1, starting transfers between devices, body(): lax.all_to_all(payload.reshape(owners, cap, GROUPS * tpix + 128), 'view',...  4.98 us
  transfers between devices with their start and end apart: 6, of which 4 were waited for; matrix products, arithmetic and copies ran while one was open for 7% of the time, Pallas kernels for 0%

profile of v6, /device:TPU:13, one launch (start us, length us, event | category | flops | bytes accessed | tf_op | source)
XLA Modules:
  0.0 80.2 jit_solution(14404305516551657801)
XLA Ops:
  0.0 1.7 %broadcast_in_dim.93 = bf16[16,32,512]{2,1,0:T(8,128)(2,1)} broadcast(bf16[32,512]{1,0:T(8,128)(2,1)} %bitcast.48), dimensions={1,2} | broadcast | bytes 557056 | tf_op jit(solution)/shard_map/broadcast_in_dim | solution.py:253
  1.7 6.6 %all-to-all-start = ((bf16[16,32,512]{2,1,0:T(8,128)(2,1)}), bf16[16,32,512]{2,1,0:T(8,128)(2,1)S(1)}, u32[]{:S(2)}, u32[]{:S(2)}) async-start(bf16[16,32,512]{2,1,0:T(8,128)(2,1)} %broadcast_in_dim.93), calls=%async_computation | async-start | bytes 1048576 | tf_op jit(solution)/shard_map/all_to_all | solution.py:252
  9.9 0.8 %concatenate.15.blocks_ref = bf16[65,32,128]{2,1,0:T(8,128)(2,1)} pad(bf16[64,32,128]{2,1,0:T(8,128)(2,1)S(1)} %bitcast.43, bf16[]{:T(256)} %constant.77.clone.1), padding=0_1x0_0x0_0 | pad | bytes 1056770 | tf_op jit(solution)/shard_map/concatenate | solution.py:244
  10.8 11.1 %all-to-all-done.ref_ref = bf16[16,32,512]{2,1,0:T(8,128)(2,1)S(1)} async-done(((bf16[16,32,512]{2,1,0:T(8,128)(2,1)}), bf16[16,32,512]{2,1,0:T(8,128)(2,1)S(1)}, u32[]{:S(2)}, u32[]{:S(2)}) %all-to-all-start) | async-done | bytes 524320 | tf_op jit(solution)/shard_map/all_to_all | solution.py:252
  21.9 0.8 %copy-done.2 = bf16[16,32,512]{2,1,0:T(8,128)(2,1)} copy-done((bf16[16,32,512]{2,1,0:T(8,128)(2,1)}, bf16[16,32,512]{2,1,0:T(8,128)(2,1)S(1)}, u32[]{:S(2)}) %copy-start.2) | copy-done | bytes 524312
  22.7 5.1 %shard_map.91 = bf16[512,512]{1,0:T(8,128)(2,1)} custom-call(s32[256]{0:T(256)} %select_n.94.blk_ref, bf16[65,32,128]{2,1,0:T(8,128)(2,1)} %concatenate.15.blocks_ref, bf16[512,512]{1,0:T(8,128)(2,1)} %bitcast.46, bf16[16,32,512]{2,1,0:T(8,128)(2,1)} %copy-done.2), custom_call_target="tpu_custom_call" | custom-call | tf_op jit(solution)/shard_map/pallas_call | solution.py:121
  27.7 1.4 %concatenate.16 = bf16[16,4,4096]{2,1,0:T(4,128)(2,1)S(1)} reshape(bf16[512,512]{1,0:T(8,128)(2,1)} %shard_map.91) | data formatting | bytes 1048576 | tf_op jit(solution)/shard_map/concatenate | solution.py:263
  29.2 1.0 %pad_maximum_fusion.2 = bf16[16,4,4224]{2,1,0:T(4,128)(2,1)} fusion(bf16[16,4,128]{2,1,0:T(4,128)(2,1)S(1)} %broadcast_in_dim.95, bf16[16,4,4096]{2,1,0:T(4,128)(2,1)S(1)} %concatenate.16), kind=kLoop, calls=%fused_computation.10 | loop fusion | flops 1081344 | bytes 1081344 | tf_op jit(solution)/shard_map/concatenate | solution.py:263
  30.3 5.0 %all-to-all-start.1 = ((bf16[16,4,4224]{2,1,0:T(4,128)(2,1)}), bf16[16,4,4224]{2,1,0:T(4,128)(2,1)S(1)}, u32[]{:S(2)}, u32[]{:S(2)}) async-start(bf16[16,4,4224]{2,1,0:T(4,128)(2,1)} %pad_maximum_fusion.2), calls=%async_computation.1 | async-start | bytes 1081344 | tf_op jit(solution)/shard_map/all_to_all | solution.py:264
  35.4 0.7 fusion.1
  36.1 1.1 %copy.35 = bf16[9,128,144]{2,1,0:T(8,128)(2,1)} copy(bf16[9,128,144]{1,2,0:T(8,128)(2,1)S(1)} %fusion.1) | data formatting | bytes 663552 | tf_op jit(solution)/shard_map/convert_element_type | solution.py:192
  37.4 11.8 %all-to-all-done.1 = bf16[16,4,4224]{2,1,0:T(4,128)(2,1)S(1)} async-done(((bf16[16,4,4224]{2,1,0:T(4,128)(2,1)}), bf16[16,4,4224]{2,1,0:T(4,128)(2,1)S(1)}, u32[]{:S(2)}, u32[]{:S(2)}) %all-to-all-start.1) | async-done | bytes 540704 | tf_op jit(solution)/shard_map/all_to_all | solution.py:264
  50.3 3.6 %collective-permute-start = (bf16[528,128]{1,0:T(8,128)(2,1)S(1)}, bf16[528,128]{1,0:T(8,128)(2,1)S(1)}, u32[]{:S(2)}, u32[]{:S(2)}) collective-permute-start(bf16[528,128]{1,0:T(8,128)(2,1)S(1)} %get-tuple-element.7), channel_id=1, source_target_pairs={{0,1},{1,2},{2,3},{3,4},{4,5},{5,6},{6,7},{7,8},{8,9},{9,10},{10,1... | collective-permute-start | bytes 405512 | tf_op jit(solution)/shard_map/ppermute | solution.py:215
  53.9 1.9 %collective-permute-start.1 = (bf16[528,128]{1,0:T(8,128)(2,1)S(1)}, bf16[528,128]{1,0:T(8,128)(2,1)S(1)}, u32[]{:S(2)}, u32[]{:S(2)}) collective-permute-start(bf16[528,128]{1,0:T(8,128)(2,1)S(1)} %get-tuple-element.8), channel_id=1, source_target_pairs={{1,0},{2,1},{3,2},{4,3},{5,4},{6,5},{7,6},{8,7},{9,8},{10,9},{11,1... | collective-permute-start | bytes 405512 | tf_op jit(solution)/shard_map/ppermute | solution.py:216
  56.1 5.1 %collective-permute-done.1 = bf16[528,128]{1,0:T(8,128)(2,1)S(1)} collective-permute-done((bf16[528,128]{1,0:T(8,128)(2,1)S(1)}, bf16[528,128]{1,0:T(8,128)(2,1)S(1)}, u32[]{:S(2)}, u32[]{:S(2)}) %collective-permute-start.1) | collective-permute-done | bytes 135200 | tf_op jit(solution)/shard_map/ppermute | solution.py:216
  61.2 1.0 %pad_maximum_fusion.x_ref = bf16[528,768]{1,0:T(8,128)(2,1)} fusion(bf16[528,128]{1,0:T(8,128)(2,1)S(1)} %collective-permute-done.1, bf16[528,512]{1,0:T(8,128)(2,1)S(1)} %pad.5, bf16[528,128]{1,0:T(8,128)(2,1)S(1)} %collective-permute-done), kind=kLoop, calls=%fused_computation.8 | loop fusion | flops 2433024 | bytes 1622016 | tf_op jit(solution)/shard_map/concatenate | solution.py:217
  62.2 3.6 %shard_map.92 = bf16[528,512]{1,0:T(8,128)(2,1)} custom-call(bf16[528,768]{1,0:T(8,128)(2,1)} %pad_maximum_fusion.x_ref, bf16[3,3,128,144]{3,2,1,0:T(8,128)(2,1)} %bitcast.42), custom_call_target="tpu_custom_call" | custom-call | tf_op jit(solution)/shard_map/pallas_call | solution.py:203
  65.8 1.1 %fusion.32 = (bf16[528,128]{1,0:T(8,128)(2,1)S(1)}, bf16[528,128]{1,0:T(8,128)(2,1)S(1)}) fusion(bf16[528,512]{1,0:T(8,128)(2,1)} %shard_map.92), kind=kLoop, calls=%fused_computation.69 | loop fusion | bytes 540672 | tf_op jit(solution)/shard_map/slice | solution.py:215
  66.8 1.9 %collective-permute-start.2 = (bf16[528,128]{1,0:T(8,128)(2,1)S(1)}, bf16[528,128]{1,0:T(8,128)(2,1)S(1)}, u32[]{:S(2)}, u32[]{:S(2)}) collective-permute-start(bf16[528,128]{1,0:T(8,128)(2,1)S(1)} %get-tuple-element.5), channel_id=1, source_target_pairs={{0,1},{1,2},{2,3},{3,4},{4,5},{5,6},{6,7},{7,8},{8,9},{9,10},{10,1... | collective-permute-start | bytes 405512 | tf_op jit(solution)/shard_map/ppermute | solution.py:215
  68.8 2.4 %collective-permute-start.3 = (bf16[528,128]{1,0:T(8,128)(2,1)S(1)}, bf16[528,128]{1,0:T(8,128)(2,1)S(1)}, u32[]{:S(2)}, u32[]{:S(2)}) collective-permute-start(bf16[528,128]{1,0:T(8,128)(2,1)S(1)} %get-tuple-element.6), channel_id=1, source_target_pairs={{1,0},{2,1},{3,2},{4,3},{5,4},{6,5},{7,6},{8,7},{9,8},{10,9},{11,1... | collective-permute-start | bytes 405512 | tf_op jit(solution)/shard_map/ppermute | solution.py:216
  71.2 1.4 %select_reduce_fusion = bf16[9,64,528]{2,1,0:T(8,128)(2,1)} fusion(f32[3,9,528]{2,1,0:T(8,128)S(1)} %convolution_bitcast_fusion, pred[3,64,528]{2,1,0:T(8,128)(4,1)S(1)} %broadcast_compare_fusion), kind=kLoop, calls=%fused_computation.2 | loop fusion | flops 1520640 | bytes 766656 | tf_op jit(solution)/shard_map/reduce_sum | solution.py:191
  72.5 3.4 %collective-permute-done.3 = bf16[528,128]{1,0:T(8,128)(2,1)S(1)} collective-permute-done((bf16[528,128]{1,0:T(8,128)(2,1)S(1)}, bf16[528,128]{1,0:T(8,128)(2,1)S(1)}, u32[]{:S(2)}, u32[]{:S(2)}) %collective-permute-start.3) | collective-permute-done | bytes 135200 | tf_op jit(solution)/shard_map/ppermute | solution.py:216
  76.0 1.0 %pad_maximum_fusion.1.x_ref = bf16[528,768]{1,0:T(8,128)(2,1)} fusion(bf16[528,128]{1,0:T(8,128)(2,1)S(1)} %collective-permute-done.3, bf16[528,512]{1,0:T(8,128)(2,1)S(1)} %copy-done.1, bf16[528,128]{1,0:T(8,128)(2,1)S(1)} %collective-permute-done.2), kind=kLoop, calls=%fused_computation.9 | loop fusion | flops 2433024 | bytes 1622016 | tf_op jit(solution)/shard_map/concatenate | solution.py:217
  77.0 3.2 %shard_map.93 = f32[4,64,128]{2,1,0:T(8,128)} custom-call(bf16[528,768]{1,0:T(8,128)(2,1)} %pad_maximum_fusion.1.x_ref, bf16[3,3,64,528]{3,2,1,0:T(8,128)(2,1)} %bitcast.41), custom_call_target="tpu_custom_call" | custom-call | tf_op jit(solution)/shard_map/pallas_call | solution.py:203
  (51 shorter events, 3.2 us)
Async XLA Ops:
  0.0 35.4 %copy-start = (bf16[3,3,3,8,8]{4,3,2,1,0:T(8,128)(2,1)S(1)}, bf16[3,3,3,8,8]{4,3,2,1,0:T(8,128)(2,1)}, u32[]{:S(2)}) copy-start(bf16[3,3,3,8,8]{4,3,2,1,0:T(8,128)(2,1)} %param.16) | copy-start | bytes 10372
  0.0 8.3 %copy-start.8 = (s32[1,64]{1,0:T(1,128)S(1)}, s32[1,64]{1,0:T(1,128)}, u32[]{:S(2)}) copy-start(s32[1,64]{1,0:T(1,128)} %param.14) | copy-start | bytes 772
  0.0 8.3 %copy-start.5 = (s32[1,64,4]{1,2,0:T(4,128)S(1)}, s32[1,64,4]{1,2,0:T(4,128)}, u32[]{:S(2)}) copy-start(s32[1,64,4]{1,2,0:T(4,128)} %param.13) | copy-start | bytes 3076
  0.0 8.3 %copy-start.6 = (s32[1,64,4]{1,2,0:T(4,128)S(1)}, s32[1,64,4]{1,2,0:T(4,128)}, u32[]{:S(2)}) copy-start(s32[1,64,4]{1,2,0:T(4,128)} %param.12) | copy-start | bytes 3076
  0.0 9.1 %copy-start.3 = (bf16[1,32,8192]{2,1,0:T(8,128)(2,1)S(1)}, bf16[1,32,8192]{2,1,0:T(8,128)(2,1)}, u32[]{:S(2)}) copy-start(bf16[1,32,8192]{2,1,0:T(8,128)(2,1)} %param.9) | copy-start | bytes 1572868
  1.7 20.1 %all-to-all-start = ((bf16[16,32,512]{2,1,0:T(8,128)(2,1)}), bf16[16,32,512]{2,1,0:T(8,128)(2,1)S(1)}, u32[]{:S(2)}, u32[]{:S(2)}) async-start(bf16[16,32,512]{2,1,0:T(8,128)(2,1)} %broadcast_in_dim.93), calls=%async_computation | async-start | bytes 1048576 | tf_op jit(solution)/shard_map/all_to_all | solution.py:252
  9.1 0.7 copy-start.7
  21.9 0.8 %copy-start.2 = (bf16[16,32,512]{2,1,0:T(8,128)(2,1)}, bf16[16,32,512]{2,1,0:T(8,128)(2,1)S(1)}, u32[]{:S(2)}) copy-start(bf16[16,32,512]{2,1,0:T(8,128)(2,1)S(1)} %all-to-all-done.ref_ref) | copy-start | bytes 1572868
  30.3 19.0 %all-to-all-start.1 = ((bf16[16,4,4224]{2,1,0:T(4,128)(2,1)}), bf16[16,4,4224]{2,1,0:T(4,128)(2,1)S(1)}, u32[]{:S(2)}, u32[]{:S(2)}) async-start(bf16[16,4,4224]{2,1,0:T(4,128)(2,1)} %pad_maximum_fusion.2), calls=%async_computation.1 | async-start | bytes 1081344 | tf_op jit(solution)/shard_map/all_to_all | solution.py:264
  36.1 1.1 %copy-start.4 = (bf16[3,3,3,8]{3,2,1,0:T(4,128)(2,1)S(1)}, bf16[3,3,3,8]{3,2,1,0:T(4,128)(2,1)}, u32[]{:S(2)}) copy-start(bf16[3,3,3,8]{3,2,1,0:T(4,128)(2,1)} %param.17) | copy-start | bytes 1300
  50.3 5.7 %collective-permute-start = (bf16[528,128]{1,0:T(8,128)(2,1)S(1)}, bf16[528,128]{1,0:T(8,128)(2,1)S(1)}, u32[]{:S(2)}, u32[]{:S(2)}) collective-permute-start(bf16[528,128]{1,0:T(8,128)(2,1)S(1)} %get-tuple-element.7), channel_id=1, source_target_pairs={{0,1},{1,2},{2,3},{3,4},{4,5},{5,6},{6,7},{7,8},{8,9},{9,10},{10,1... | collective-permute-start | bytes 405512 | tf_op jit(solution)/shard_map/ppermute | solution.py:215
  53.9 7.2 %collective-permute-start.1 = (bf16[528,128]{1,0:T(8,128)(2,1)S(1)}, bf16[528,128]{1,0:T(8,128)(2,1)S(1)}, u32[]{:S(2)}, u32[]{:S(2)}) collective-permute-start(bf16[528,128]{1,0:T(8,128)(2,1)S(1)} %get-tuple-element.8), channel_id=1, source_target_pairs={{1,0},{2,1},{3,2},{4,3},{5,4},{6,5},{7,6},{8,7},{9,8},{10,9},{11,1... | collective-permute-start | bytes 405512 | tf_op jit(solution)/shard_map/ppermute | solution.py:216
  65.8 10.2 %copy-start.1 = (bf16[528,512]{1,0:T(8,128)(2,1)S(1)}, bf16[528,512]{1,0:T(8,128)(2,1)}, u32[]{:S(2)}) copy-start(bf16[528,512]{1,0:T(8,128)(2,1)} %shard_map.92) | copy-start | bytes 1622020
  66.8 5.7 %collective-permute-start.2 = (bf16[528,128]{1,0:T(8,128)(2,1)S(1)}, bf16[528,128]{1,0:T(8,128)(2,1)S(1)}, u32[]{:S(2)}, u32[]{:S(2)}) collective-permute-start(bf16[528,128]{1,0:T(8,128)(2,1)S(1)} %get-tuple-element.5), channel_id=1, source_target_pairs={{0,1},{1,2},{2,3},{3,4},{4,5},{5,6},{6,7},{7,8},{8,9},{9,10},{10,1... | collective-permute-start | bytes 405512 | tf_op jit(solution)/shard_map/ppermute | solution.py:215
  68.8 7.2 %collective-permute-start.3 = (bf16[528,128]{1,0:T(8,128)(2,1)S(1)}, bf16[528,128]{1,0:T(8,128)(2,1)S(1)}, u32[]{:S(2)}, u32[]{:S(2)}) collective-permute-start(bf16[528,128]{1,0:T(8,128)(2,1)S(1)} %get-tuple-element.6), channel_id=1, source_target_pairs={{1,0},{2,1},{3,2},{4,3},{5,4},{6,5},{7,6},{8,7},{9,8},{10,9},{11,1... | collective-permute-start | bytes 405512 | tf_op jit(solution)/shard_map/ppermute | solution.py:216

commit v7 on v6

--- a/solution.py
+++ b/solution.py
@@ -217,6 +217,27 @@
     return jnp.concatenate([low, block, high], axis=1)
 
 
+def gather_view(block):
+    count = lax.axis_size("view")
+    if count & (count - 1):
+        return lax.all_to_all(
+            jnp.broadcast_to(block, (count,) + block.shape[1:]), "view", 0, 0, tiled=True
+        )
+    index = lax.axis_index("view")
+    gathered = block[0]
+    level = 0
+    stride = count // 2
+    while stride >= 1:
+        other = lax.ppermute(gathered, "view", [(i, i ^ stride) for i in range(count)])
+        low = (index // stride) % 2 == 0
+        gathered = jnp.where(
+            low, jnp.stack([gathered, other], axis=level), jnp.stack([other, gathered], axis=level)
+        )
+        level += 1
+        stride //= 2
+    return gathered.reshape((count,) + block.shape[1:])
+
+
 def pad_rows(volume):
     return with_halo(volume, (("view", 0),), 1)
 
@@ -249,13 +270,7 @@
     blk = jnp.where(alive, picked, nblocks).reshape(-1).astype(jnp.int32)
     depth_code = jnp.where(counts > 0, depth_plane[0], -1).astype(jnp.bfloat16)
 
-    ref_all = lax.all_to_all(
-        jnp.broadcast_to(ref_feat, (owners,) + ref_feat.shape[1:]),
-        "view",
-        split_axis=0,
-        concat_axis=0,
-        tiled=True,
-    )
+    ref_all = gather_view(ref_feat)
     corr_all = correlate(
         blk, blocks, weight_table.reshape(slots * block_width, tpix), ref_all, units
     ).reshape(units, GROUPS * tpix)

time: 80.8 us -> 78.7 us (0.974)
  waiting for transfers between devices: 31.5 us -> 25.2 us
  other arithmetic: 4.91 us -> 10.3 us
  local copies, waits for them, and re-layouts: 9.01 us -> 7.18 us
    all_to_all x1 -> x0, waiting for transfers between devices: 11.1 us -> none  [body(): lax.all_to_all(jnp.broadcast_to(ref_feat, (owners,) + ref_feat.shape[1:])...]
    all_to_all x1 -> x0, starting transfers between devices: 6.55 us -> none  [body(): lax.all_to_all(jnp.broadcast_to(ref_feat, (owners,) + ref_feat.shape[1:])...]
    ppermute x0 -> x4, starting transfers between devices: none -> 6.15 us  [gather_view(): lax.ppermute(gathered, 'view', [(i, i ^ stride) for i in range(count)])]
    ppermute x0 -> x4, waiting for transfers between devices: none -> 4.83 us  [gather_view(): lax.ppermute(gathered, 'view', [(i, i ^ stride) for i in range(count)])]
    select_n x0 -> x7, other arithmetic: none -> 1.85 us  [gather_view(): jnp.where(low, jnp.stack([gathered, other], axis=level), jnp.stack([other...]
    broadcast_in_dim x1 -> x0, local copies, waits for them, and re-layouts: 1.68 us -> none  [body(): jnp.broadcast_to(ref_feat, (owners,) + ref_feat.shape[1:])]
    unnamed x20 -> x10, local copies, waits for them, and re-layouts: 1.14 us -> 0.14 us
    another operation x0 -> x2, other arithmetic: none -> 0.86 us  [gather_view(): jnp.stack([gathered, other], axis=level)]
  transfers between devices with their start and end apart: 6 -> 9, of which waited for: 4 -> 5; matrix products, arithmetic and copies ran while one was open for 7% -> 13% of each run, Pallas kernels for 0% -> 0%
where the time goes in v7:
time: 78.7 us; the launch traced here: 78 us
  waiting for transfers between devices  25.2 us (32%)
  starting transfers between devices  21.8 us (28%)
  Pallas kernels  11.9 us (15%)
  other arithmetic  10.3 us (13%)
  local copies, waits for them, and re-layouts  7.18 us (9%)
  matrix products  1.24 us (2%)
    all_to_all x1, waiting for transfers between devices, body(): lax.all_to_all(payload.reshape(owners, cap, GROUPS * tpix + 128), 'view',...  11.8 us
    ppermute x2, waiting for transfers between devices, halo_cols(): high = lax.ppermute(block[:, :cols], 'view', backward)  8.55 us
    pallas_call x2, Pallas kernels, conv_rows(): pl.pallas_call(functools.partial(conv_kernel, relu=relu, rows=rows, cols=...  6.82 us
    ppermute x4, starting transfers between devices, gather_view(): lax.ppermute(gathered, 'view', [(i, i ^ stride) for i in range(count)])  6.15 us
    all_to_all x1, starting transfers between devices, body(): lax.all_to_all(payload.reshape(owners, cap, GROUPS * tpix + 128), 'view',...  5.76 us
    ppermute x2, starting transfers between devices, halo_cols(): low = lax.ppermute(block[:, block.shape[1] - cols:], 'view', forward)  5.54 us
    pallas_call x1, Pallas kernels, correlate(): pl.pallas_call(correlate_kernel, out_shape=jax.ShapeDtypeStruct((units *...  5.05 us
    ppermute x4, waiting for transfers between devices, gather_view(): lax.ppermute(gathered, 'view', [(i, i ^ stride) for i in range(count)])  4.83 us
  transfers between devices with their start and end apart: 9, of which 5 were waited for; matrix products, arithmetic and copies ran while one was open for 13% of the time, Pallas kernels for 0%

profile of v7, /device:TPU:13, one launch (start us, length us, event | category | flops | bytes accessed | tf_op | source)
XLA Modules:
  0.0 78.0 jit_solution(17387780746972625551)
XLA Ops:
  0.0 2.3 %collective-permute-start = (bf16[32,512]{1,0:T(8,128)(2,1)}, bf16[32,512]{1,0:T(8,128)(2,1)S(1)}, u32[]{:S(2)}, u32[]{:S(2)}) collective-permute-start(bf16[32,512]{1,0:T(8,128)(2,1)} %bitcast.66), channel_id=1, source_target_pairs={{0,8},{1,9},{2,10},{3,11},{4,12},{5,13},{6,14},{7,15},{8,0},{9,1},... | collective-permute-start | bytes 98312 | tf_op jit(solution)/shard_map/ppermute | solution.py:231
  5.2 0.8 %maximum_select_fusion.6 = bf16[2,32,512]{2,1,0:T(8,128)(2,1)S(1)} fusion(bf16[1,32,512]{2,1,0:T(8,128)(2,1)S(1)} %bitcast.69, bf16[1,32,512]{2,1,0:T(8,128)(2,1)} %param.10, pred[]{:T(512)S(6)} %eq.133), kind=kLoop, calls=%fused_computation.21 | loop fusion | flops 98304 | bytes 131073 | tf_op jit(solution)/shard_map/jit(_where)/select_n | solution.py:233
  7.1 2.1 %collective-permute-done.1 = bf16[2,32,512]{2,1,0:T(8,128)(2,1)S(1)} collective-permute-done((bf16[2,32,512]{2,1,0:T(8,128)(2,1)S(1)}, bf16[2,32,512]{2,1,0:T(8,128)(2,1)S(1)}, u32[]{:S(2)}, u32[]{:S(2)}) %collective-permute-start.1) | collective-permute-done | bytes 65568 | tf_op jit(solution)/shard_map/ppermute | solution.py:231
  10.4 2.7 %collective-permute-done.2 = bf16[2,2,32,512]{3,2,0,1:T(8,128)(2,1)S(1)} collective-permute-done((bf16[2,2,32,512]{3,2,0,1:T(8,128)(2,1)S(1)}, bf16[2,2,32,512]{3,2,0,1:T(8,128)(2,1)S(1)}, u32[]{:S(2)}, u32[]{:S(2)}) %collective-permute-start.2) | collective-permute-done | bytes 131104 | tf_op jit(solution)/shard_map/ppermute | solution.py:231
  13.2 3.3 %collective-permute-start.3 = (bf16[2,2,2,32,512]{4,3,0,1,2:T(8,128)(2,1)S(1)}, bf16[2,2,2,32,512]{4,3,0,1,2:T(8,128)(2,1)S(1)}, u32[]{:S(2)}, u32[]{:S(2)}) collective-permute-start(bf16[2,2,2,32,512]{4,3,0,1,2:T(8,128)(2,1)S(1)} %maximum_select_fusion.2), channel_id=1, source_target_pairs={{0,1},{1,0},{2,3},{3,2},{4,5},{5,4},{6,7},{7,6},{8,9},{9,8},{10,11... | collective-permute-start | bytes 786440 | tf_op jit(solution)/shard_map/ppermute | solution.py:231
  18.8 0.9 %copy.38 = bf16[2,2,2,2,32,512]{5,4,3,2,1,0:T(8,128)(2,1)} copy(bf16[2,2,2,2,32,512]{5,4,0,1,2,3:T(8,128)(2,1)S(1)} %maximum_select_fusion) | data formatting | bytes 1048576 | tf_op jit(solution)/shard_map/jit(_where)/select_n | solution.py:233
  19.7 5.1 %shard_map.91 = bf16[512,512]{1,0:T(8,128)(2,1)} custom-call(s32[256]{0:T(256)} %select_n.210.blk_ref, bf16[65,32,128]{2,1,0:T(8,128)(2,1)} %concatenate.93.blocks_ref, bf16[512,512]{1,0:T(8,128)(2,1)} %bitcast.65, bf16[16,32,512]{2,1,0:T(8,128)(2,1)} %bitcast.58), custom_call_target="tpu_custom_call" | custom-call | tf_op jit(solution)/shard_map/pallas_call | solution.py:121
  24.7 1.4 %concatenate.94 = bf16[16,4,4096]{2,1,0:T(4,128)(2,1)S(1)} reshape(bf16[512,512]{1,0:T(8,128)(2,1)} %shard_map.91) | data formatting | bytes 1048576 | tf_op jit(solution)/shard_map/concatenate | solution.py:278
  26.2 1.0 %pad_maximum_fusion.2 = bf16[16,4,4224]{2,1,0:T(4,128)(2,1)} fusion(bf16[16,4,128]{2,1,0:T(4,128)(2,1)S(1)} %broadcast_in_dim.86, bf16[16,4,4096]{2,1,0:T(4,128)(2,1)S(1)} %concatenate.94), kind=kLoop, calls=%fused_computation.10 | loop fusion | flops 1081344 | bytes 1081344 | tf_op jit(solution)/shard_map/concatenate | solution.py:278
  27.3 5.8 %all-to-all-start = ((bf16[16,4,4224]{2,1,0:T(4,128)(2,1)}), bf16[16,4,4224]{2,1,0:T(4,128)(2,1)S(1)}, u32[]{:S(2)}, u32[]{:S(2)}) async-start(bf16[16,4,4224]{2,1,0:T(4,128)(2,1)} %pad_maximum_fusion.2), calls=%async_computation | async-start | bytes 1081344 | tf_op jit(solution)/shard_map/all_to_all | solution.py:279
  33.9 1.1 %copy.40 = bf16[9,128,144]{2,1,0:T(8,128)(2,1)} copy(bf16[9,128,144]{1,2,0:T(8,128)(2,1)S(1)} %fusion.1) | data formatting | bytes 663552 | tf_op jit(solution)/shard_map/convert_element_type | solution.py:192
  35.2 11.8 %all-to-all-done = bf16[16,4,4224]{2,1,0:T(4,128)(2,1)S(1)} async-done(((bf16[16,4,4224]{2,1,0:T(4,128)(2,1)}), bf16[16,4,4224]{2,1,0:T(4,128)(2,1)S(1)}, u32[]{:S(2)}, u32[]{:S(2)}) %all-to-all-start) | async-done | bytes 540704 | tf_op jit(solution)/shard_map/all_to_all | solution.py:279
  48.1 3.6 %collective-permute-start.4 = (bf16[528,128]{1,0:T(8,128)(2,1)S(1)}, bf16[528,128]{1,0:T(8,128)(2,1)S(1)}, u32[]{:S(2)}, u32[]{:S(2)}) collective-permute-start(bf16[528,128]{1,0:T(8,128)(2,1)S(1)} %get-tuple-element.7), channel_id=1, source_target_pairs={{0,1},{1,2},{2,3},{3,4},{4,5},{5,6},{6,7},{7,8},{8,9},{9,10},{10,1... | collective-permute-start | bytes 405512 | tf_op jit(solution)/shard_map/ppermute | solution.py:215
  51.7 1.9 %collective-permute-start.5 = (bf16[528,128]{1,0:T(8,128)(2,1)S(1)}, bf16[528,128]{1,0:T(8,128)(2,1)S(1)}, u32[]{:S(2)}, u32[]{:S(2)}) collective-permute-start(bf16[528,128]{1,0:T(8,128)(2,1)S(1)} %get-tuple-element.8), channel_id=1, source_target_pairs={{1,0},{2,1},{3,2},{4,3},{5,4},{6,5},{7,6},{8,7},{9,8},{10,9},{11,1... | collective-permute-start | bytes 405512 | tf_op jit(solution)/shard_map/ppermute | solution.py:216
  53.9 5.1 %collective-permute-done.5 = bf16[528,128]{1,0:T(8,128)(2,1)S(1)} collective-permute-done((bf16[528,128]{1,0:T(8,128)(2,1)S(1)}, bf16[528,128]{1,0:T(8,128)(2,1)S(1)}, u32[]{:S(2)}, u32[]{:S(2)}) %collective-permute-start.5) | collective-permute-done | bytes 135200 | tf_op jit(solution)/shard_map/ppermute | solution.py:216
  59.0 1.0 %pad_maximum_fusion.x_ref = bf16[528,768]{1,0:T(8,128)(2,1)} fusion(bf16[528,128]{1,0:T(8,128)(2,1)S(1)} %collective-permute-done.5, bf16[528,512]{1,0:T(8,128)(2,1)S(1)} %pad.5, bf16[528,128]{1,0:T(8,128)(2,1)S(1)} %collective-permute-done.4), kind=kLoop, calls=%fused_computation.8 | loop fusion | flops 2433024 | bytes 1622016 | tf_op jit(solution)/shard_map/concatenate | solution.py:217
  60.0 3.6 %shard_map.92 = bf16[528,512]{1,0:T(8,128)(2,1)} custom-call(bf16[528,768]{1,0:T(8,128)(2,1)} %pad_maximum_fusion.x_ref, bf16[3,3,128,144]{3,2,1,0:T(8,128)(2,1)} %bitcast.55), custom_call_target="tpu_custom_call" | custom-call | tf_op jit(solution)/shard_map/pallas_call | solution.py:203
  63.6 1.1 %fusion.32 = (bf16[528,128]{1,0:T(8,128)(2,1)S(1)}, bf16[528,128]{1,0:T(8,128)(2,1)S(1)}) fusion(bf16[528,512]{1,0:T(8,128)(2,1)} %shard_map.92), kind=kLoop, calls=%fused_computation.76 | loop fusion | bytes 540672 | tf_op jit(solution)/shard_map/slice | solution.py:215
  64.6 1.9 %collective-permute-start.6 = (bf16[528,128]{1,0:T(8,128)(2,1)S(1)}, bf16[528,128]{1,0:T(8,128)(2,1)S(1)}, u32[]{:S(2)}, u32[]{:S(2)}) collective-permute-start(bf16[528,128]{1,0:T(8,128)(2,1)S(1)} %get-tuple-element.5), channel_id=1, source_target_pairs={{0,1},{1,2},{2,3},{3,4},{4,5},{5,6},{6,7},{7,8},{8,9},{9,10},{10,1... | collective-permute-start | bytes 405512 | tf_op jit(solution)/shard_map/ppermute | solution.py:215
  66.5 2.4 %collective-permute-start.7 = (bf16[528,128]{1,0:T(8,128)(2,1)S(1)}, bf16[528,128]{1,0:T(8,128)(2,1)S(1)}, u32[]{:S(2)}, u32[]{:S(2)}) collective-permute-start(bf16[528,128]{1,0:T(8,128)(2,1)S(1)} %get-tuple-element.6), channel_id=1, source_target_pairs={{1,0},{2,1},{3,2},{4,3},{5,4},{6,5},{7,6},{8,7},{9,8},{10,9},{11,1... | collective-permute-start | bytes 405512 | tf_op jit(solution)/shard_map/ppermute | solution.py:216
  69.0 1.4 %select_reduce_fusion = bf16[9,64,528]{2,1,0:T(8,128)(2,1)} fusion(f32[3,9,528]{2,1,0:T(8,128)S(1)} %convolution_bitcast_fusion, pred[3,64,528]{2,1,0:T(8,128)(4,1)S(1)} %broadcast_compare_fusion), kind=kLoop, calls=%fused_computation.2 | loop fusion | flops 1520640 | bytes 766656 | tf_op jit(solution)/shard_map/reduce_sum | solution.py:191
  70.3 3.4 %collective-permute-done.7 = bf16[528,128]{1,0:T(8,128)(2,1)S(1)} collective-permute-done((bf16[528,128]{1,0:T(8,128)(2,1)S(1)}, bf16[528,128]{1,0:T(8,128)(2,1)S(1)}, u32[]{:S(2)}, u32[]{:S(2)}) %collective-permute-start.7) | collective-permute-done | bytes 135200 | tf_op jit(solution)/shard_map/ppermute | solution.py:216
  73.8 1.0 %pad_maximum_fusion.1.x_ref = bf16[528,768]{1,0:T(8,128)(2,1)} fusion(bf16[528,128]{1,0:T(8,128)(2,1)S(1)} %collective-permute-done.7, bf16[528,512]{1,0:T(8,128)(2,1)S(1)} %copy-done.1, bf16[528,128]{1,0:T(8,128)(2,1)S(1)} %collective-permute-done.6), kind=kLoop, calls=%fused_computation.9 | loop fusion | flops 2433024 | bytes 1622016 | tf_op jit(solution)/shard_map/concatenate | solution.py:217
  74.8 3.2 %shard_map.93 = f32[4,64,128]{2,1,0:T(8,128)} custom-call(bf16[528,768]{1,0:T(8,128)(2,1)} %pad_maximum_fusion.1.x_ref, bf16[3,3,64,528]{3,2,1,0:T(8,128)(2,1)} %bitcast.54), custom_call_target="tpu_custom_call" | custom-call | tf_op jit(solution)/shard_map/pallas_call | solution.py:203
  (56 shorter events, 9.6 us)
Async XLA Ops:
  0.0 33.2 %copy-start = (bf16[3,3,3,8,8]{4,3,2,1,0:T(8,128)(2,1)S(1)}, bf16[3,3,3,8,8]{4,3,2,1,0:T(8,128)(2,1)}, u32[]{:S(2)}) copy-start(bf16[3,3,3,8,8]{4,3,2,1,0:T(8,128)(2,1)} %param.16) | copy-start | bytes 10372
  0.0 5.2 %collective-permute-start = (bf16[32,512]{1,0:T(8,128)(2,1)}, bf16[32,512]{1,0:T(8,128)(2,1)S(1)}, u32[]{:S(2)}, u32[]{:S(2)}) collective-permute-start(bf16[32,512]{1,0:T(8,128)(2,1)} %bitcast.66), channel_id=1, source_target_pairs={{0,8},{1,9},{2,10},{3,11},{4,12},{5,13},{6,14},{7,15},{8,0},{9,1},... | collective-permute-start | bytes 98312 | tf_op jit(solution)/shard_map/ppermute | solution.py:231
  5.1 12.1 %copy-start.2 = (bf16[1,32,8192]{2,1,0:T(8,128)(2,1)S(1)}, bf16[1,32,8192]{2,1,0:T(8,128)(2,1)}, u32[]{:S(2)}) copy-start(bf16[1,32,8192]{2,1,0:T(8,128)(2,1)} %param.9) | copy-start | bytes 1572868
  6.1 3.2 %collective-permute-start.1 = (bf16[2,32,512]{2,1,0:T(8,128)(2,1)S(1)}, bf16[2,32,512]{2,1,0:T(8,128)(2,1)S(1)}, u32[]{:S(2)}, u32[]{:S(2)}) collective-permute-start(bf16[2,32,512]{2,1,0:T(8,128)(2,1)S(1)} %maximum_select_fusion.6), channel_id=1, source_target_pairs={{0,4},{1,5},{2,6},{3,7},{4,0},{5,1},{6,2},{7,3},{8,12},{9,13},{10,... | collective-permute-start | bytes 196616 | tf_op jit(solution)/shard_map/ppermute | solution.py:231
  9.3 3.9 %collective-permute-start.2 = (bf16[2,2,32,512]{3,2,0,1:T(8,128)(2,1)S(1)}, bf16[2,2,32,512]{3,2,0,1:T(8,128)(2,1)S(1)}, u32[]{:S(2)}, u32[]{:S(2)}) collective-permute-start(bf16[2,2,32,512]{3,2,0,1:T(8,128)(2,1)S(1)} %maximum_select_fusion.4), channel_id=1, source_target_pairs={{0,2},{1,3},{2,0},{3,1},{4,6},{5,7},{6,4},{7,5},{8,10},{9,11},{10,... | collective-permute-start | bytes 393224 | tf_op jit(solution)/shard_map/ppermute | solution.py:231
  13.2 5.5 %collective-permute-start.3 = (bf16[2,2,2,32,512]{4,3,0,1,2:T(8,128)(2,1)S(1)}, bf16[2,2,2,32,512]{4,3,0,1,2:T(8,128)(2,1)S(1)}, u32[]{:S(2)}, u32[]{:S(2)}) collective-permute-start(bf16[2,2,2,32,512]{4,3,0,1,2:T(8,128)(2,1)S(1)} %maximum_select_fusion.2), channel_id=1, source_target_pairs={{0,1},{1,0},{2,3},{3,2},{4,5},{5,4},{6,7},{7,6},{8,9},{9,8},{10,11... | collective-permute-start | bytes 786440 | tf_op jit(solution)/shard_map/ppermute | solution.py:231
  27.3 19.7 %all-to-all-start = ((bf16[16,4,4224]{2,1,0:T(4,128)(2,1)}), bf16[16,4,4224]{2,1,0:T(4,128)(2,1)S(1)}, u32[]{:S(2)}, u32[]{:S(2)}) async-start(bf16[16,4,4224]{2,1,0:T(4,128)(2,1)} %pad_maximum_fusion.2), calls=%async_computation | async-start | bytes 1081344 | tf_op jit(solution)/shard_map/all_to_all | solution.py:279
  33.9 1.1 %copy-start.3 = (bf16[3,3,3,8]{3,2,1,0:T(4,128)(2,1)S(1)}, bf16[3,3,3,8]{3,2,1,0:T(4,128)(2,1)}, u32[]{:S(2)}) copy-start(bf16[3,3,3,8]{3,2,1,0:T(4,128)(2,1)} %param.17) | copy-start | bytes 1300
  48.1 5.7 %collective-permute-start.4 = (bf16[528,128]{1,0:T(8,128)(2,1)S(1)}, bf16[528,128]{1,0:T(8,128)(2,1)S(1)}, u32[]{:S(2)}, u32[]{:S(2)}) collective-permute-start(bf16[528,128]{1,0:T(8,128)(2,1)S(1)} %get-tuple-element.7), channel_id=1, source_target_pairs={{0,1},{1,2},{2,3},{3,4},{4,5},{5,6},{6,7},{7,8},{8,9},{9,10},{10,1... | collective-permute-start | bytes 405512 | tf_op jit(solution)/shard_map/ppermute | solution.py:215
  51.7 7.2 %collective-permute-start.5 = (bf16[528,128]{1,0:T(8,128)(2,1)S(1)}, bf16[528,128]{1,0:T(8,128)(2,1)S(1)}, u32[]{:S(2)}, u32[]{:S(2)}) collective-permute-start(bf16[528,128]{1,0:T(8,128)(2,1)S(1)} %get-tuple-element.8), channel_id=1, source_target_pairs={{1,0},{2,1},{3,2},{4,3},{5,4},{6,5},{7,6},{8,7},{9,8},{10,9},{11,1... | collective-permute-start | bytes 405512 | tf_op jit(solution)/shard_map/ppermute | solution.py:216
  63.6 10.2 %copy-start.1 = (bf16[528,512]{1,0:T(8,128)(2,1)S(1)}, bf16[528,512]{1,0:T(8,128)(2,1)}, u32[]{:S(2)}) copy-start(bf16[528,512]{1,0:T(8,128)(2,1)} %shard_map.92) | copy-start | bytes 1622020
  64.6 5.7 %collective-permute-start.6 = (bf16[528,128]{1,0:T(8,128)(2,1)S(1)}, bf16[528,128]{1,0:T(8,128)(2,1)S(1)}, u32[]{:S(2)}, u32[]{:S(2)}) collective-permute-start(bf16[528,128]{1,0:T(8,128)(2,1)S(1)} %get-tuple-element.5), channel_id=1, source_target_pairs={{0,1},{1,2},{2,3},{3,4},{4,5},{5,6},{6,7},{7,8},{8,9},{9,10},{10,1... | collective-permute-start | bytes 405512 | tf_op jit(solution)/shard_map/ppermute | solution.py:215
  66.5 7.2 %collective-permute-start.7 = (bf16[528,128]{1,0:T(8,128)(2,1)S(1)}, bf16[528,128]{1,0:T(8,128)(2,1)S(1)}, u32[]{:S(2)}, u32[]{:S(2)}) collective-permute-start(bf16[528,128]{1,0:T(8,128)(2,1)S(1)} %get-tuple-element.6), channel_id=1, source_target_pairs={{1,0},{2,1},{3,2},{4,3},{5,4},{6,5},{7,6},{8,7},{9,8},{10,9},{11,1... | collective-permute-start | bytes 405512 | tf_op jit(solution)/shard_map/ppermute | solution.py:216

commit v8 on v7

--- a/solution.py
+++ b/solution.py
@@ -135,7 +135,11 @@
     )(blk, blocks, table, refs)
 
 
-def conv_kernel(x_ref, m_ref, out_ref, *, relu, rows, cols, groups, chunk):
+def conv_kernel(*refs, relu, rows, cols, groups, chunk):
+    if relu:
+        ends_ref, x_ref, m_ref, out_ref = refs
+    else:
+        x_ref, m_ref, out_ref = refs
     width = rows * cols
     outs = m_ref.shape[2]
     depth = x_ref.shape[0] // groups - 2
@@ -154,6 +158,9 @@
                 y = jnp.where(lane <= cols - 2, pltpu.roll(y, width - 1, 1), 0.0)
             acc = y if acc is None else acc + y
         if relu:
+            block = lax.broadcasted_iota(jnp.int32, (outs, width), 1) // cols
+            outside = ((block == 0) & (ends_ref[0] > 0)) | ((block == rows - 1) & (ends_ref[1] > 0))
+            acc = jnp.where(outside, 0.0, acc)
             out_ref[(k * chunk + 1) * outs // chunk : (k * chunk + chunk + 1) * outs // chunk, :] = (
                 jnp.maximum(acc, 0.0).astype(out_ref.dtype)
             )
@@ -192,7 +199,7 @@
     return mats.astype(kernel.dtype).reshape(3, 3, rows, cols)
 
 
-def conv_rows(framed, mats, relu, rows, cols, chunk):
+def conv_rows(framed, mats, relu, rows, cols, chunk, ends=None):
     outs = mats.shape[2]
     groups = mats.shape[3] // (chunk + 2)
     depth = framed.shape[0] // groups - 2
@@ -200,12 +207,16 @@
         out_shape = jax.ShapeDtypeStruct(((depth + 2) * outs // chunk, rows * cols), jnp.bfloat16)
     else:
         out_shape = jax.ShapeDtypeStruct((rows, depth, cols), jnp.float32)
+    operands = (framed, mats) if ends is None else (ends, framed, mats)
+    in_specs = [pl.BlockSpec(memory_space=pltpu.VMEM), pl.BlockSpec(memory_space=pltpu.VMEM)]
+    if ends is not None:
+        in_specs = [pl.BlockSpec(memory_space=pltpu.SMEM)] + in_specs
     return pl.pallas_call(
         functools.partial(conv_kernel, relu=relu, rows=rows, cols=cols, groups=groups, chunk=chunk),
         out_shape=out_shape,
-        in_specs=[pl.BlockSpec(memory_space=pltpu.VMEM), pl.BlockSpec(memory_space=pltpu.VMEM)],
+        in_specs=in_specs,
         out_specs=pl.BlockSpec(memory_space=pltpu.VMEM),
-    )(framed, mats)
+    )(*operands)
 
 
 def halo_cols(block, cols):
@@ -294,12 +305,19 @@
     columns = tpix // TROWS
     volume = cost_volume.reshape(DEPTH * GROUPS, TROWS * columns)
     volume = jnp.pad(volume, ((GROUPS, GROUPS), (0, 0)))
+    count = lax.axis_size("view")
+    place = lax.axis_index("view")
+    ends = jnp.stack([place == 0, place == count - 1]).astype(jnp.int32)
     hidden = conv_rows(
-        halo_cols(volume, columns), banded(kern_one, DEPTH // 4), True, TROWS, columns, DEPTH // 4
+        halo_cols(volume, 2 * columns),
+        banded(kern_one, DEPTH // 4),
+        True,
+        TROWS + 2,
+        columns,
+        DEPTH // 4,
+        ends,
     )
-    scores = conv_rows(
-        halo_cols(hidden, columns), banded(kern_two, DEPTH), False, TROWS, columns, DEPTH
-    )
+    scores = conv_rows(hidden, banded(kern_two, DEPTH), False, TROWS, columns, DEPTH)
     return scores
 
 

time: 78.7 us -> 69.9 us (0.89)
  starting transfers between devices: 21.8 us -> 17.3 us
  waiting for transfers between devices: 25.2 us -> 21.4 us
  local copies, waits for them, and re-layouts: 7.18 us -> 6.15 us
  Pallas kernels: 11.9 us -> 12.7 us
    ppermute x2 -> x1, waiting for transfers between devices: 8.55 us -> 4.77 us  [halo_cols(): high = lax.ppermute(block[:, :cols], 'view', backward)]
    ppermute x2 -> x1, starting transfers between devices: 4.33 us -> 1.92 us  [halo_cols(): high = lax.ppermute(block[:, :cols], 'view', backward)]
    ppermute x2 -> x1, starting transfers between devices: 5.54 us -> 3.61 us  [halo_cols(): low = lax.ppermute(block[:, block.shape[1] - cols:], 'view', forward)]
    slice x2 -> x1, local copies, waits for them, and re-layouts: 1.07 us -> 0.04 us  [halo_cols(): low = lax.ppermute(block[:, block.shape[1] - cols:], 'view', forward)]
    pallas_call x2, Pallas kernels: 6.82 us -> 7.67 us  [conv_rows(): pl.pallas_call(functools.partial(conv_kernel, relu=relu, rows=rows, cols=...]
    concatenate x2 -> x1, other arithmetic: 1.98 us -> 1.14 us  [halo_cols(): return jnp.concatenate([low, block, high], axis=1)]
  transfers between devices with their start and end apart: 9 -> 7, of which waited for: 5 -> 4; matrix products, arithmetic and copies ran while one was open for 13% -> 16% of each run, Pallas kernels for 0% -> 0%
where the time goes in v8:
time: 69.9 us; the launch traced here: 69.2 us
  waiting for transfers between devices  21.4 us (31%)
  starting transfers between devices  17.3 us (25%)
  Pallas kernels  12.7 us (18%)
  other arithmetic  10 us (14%)
  local copies, waits for them, and re-layouts  6.15 us (9%)
  matrix products  1.24 us (2%)
    all_to_all x1, waiting for transfers between devices, body(): lax.all_to_all(payload.reshape(owners, cap, GROUPS * tpix + 128), 'view',...  11.8 us
    pallas_call x2, Pallas kernels, conv_rows(): pl.pallas_call(functools.partial(conv_kernel, relu=relu, rows=rows, cols=...  7.67 us
    ppermute x4, starting transfers between devices, gather_view(): lax.ppermute(gathered, 'view', [(i, i ^ stride) for i in range(count)])  6.15 us
    all_to_all x1, starting transfers between devices, body(): lax.all_to_all(payload.reshape(owners, cap, GROUPS * tpix + 128), 'view',...  5.67 us
    pallas_call x1, Pallas kernels, correlate(): pl.pallas_call(correlate_kernel, out_shape=jax.ShapeDtypeStruct((units *...  5.05 us
    ppermute x4, waiting for transfers between devices, gather_view(): lax.ppermute(gathered, 'view', [(i, i ^ stride) for i in range(count)])  4.83 us
    ppermute x1, waiting for transfers between devices, halo_cols(): high = lax.ppermute(block[:, :cols], 'view', backward)  4.77 us
    ppermute x1, starting transfers between devices, halo_cols(): low = lax.ppermute(block[:, block.shape[1] - cols:], 'view', forward)  3.61 us
  transfers between devices with their start and end apart: 7, of which 4 were waited for; matrix products, arithmetic and copies ran while one was open for 16% of the time, Pallas kernels for 0%

profile of v8, /device:TPU:13, one launch (start us, length us, event | category | flops | bytes accessed | tf_op | source)
XLA Modules:
  0.0 69.2 jit_solution(2615711250208528732)
XLA Ops:
  0.0 2.3 %collective-permute-start = (bf16[32,512]{1,0:T(8,128)(2,1)}, bf16[32,512]{1,0:T(8,128)(2,1)S(1)}, u32[]{:S(2)}, u32[]{:S(2)}) collective-permute-start(bf16[32,512]{1,0:T(8,128)(2,1)} %bitcast.68), channel_id=1, source_target_pairs={{0,8},{1,9},{2,10},{3,11},{4,12},{5,13},{6,14},{7,15},{8,0},{9,1},... | collective-permute-start | bytes 98312 | tf_op jit(solution)/shard_map/ppermute | solution.py:242
  3.0 0.7 %select_reduce_fusion.1 = s32[64,4]{0,1:T(4,128)S(1)} fusion(s32[64,4]{0,1:T(4,128)} %bitcast.78, s32[64,4]{0,1:T(4,128)} %bitcast.76), kind=kLoop, calls=%fused_computation.38 | loop fusion | flops 2816 | bytes 3072 | tf_op jit(solution)/shard_map/reduce_sum | solution.py:279
  5.3 0.8 %maximum_select_fusion.6 = bf16[2,32,512]{2,1,0:T(8,128)(2,1)S(1)} fusion(bf16[1,32,512]{2,1,0:T(8,128)(2,1)S(1)} %bitcast.71, bf16[1,32,512]{2,1,0:T(8,128)(2,1)} %param.10, pred[]{:T(512)S(6)} %eq.141), kind=kLoop, calls=%fused_computation.20 | loop fusion | flops 98304 | bytes 131073 | tf_op jit(solution)/shard_map/jit(_where)/select_n | solution.py:244
  6.4 0.8 %maximum_select_fusion.5 = bf16[2,1,32,512]{3,2,0,1:T(8,128)(2,1)S(1)} fusion(bf16[1,1,32,512]{3,2,0,1:T(8,128)(2,1)S(1)} %bitcast.72, bf16[1,1,32,512]{3,2,0,1:T(8,128)(2,1)} %bitcast.69, pred[]{:T(512)S(6)} %eq.141), kind=kLoop, calls=%fused_computation.19 | loop fusion | flops 98304 | bytes 131073 | tf_op jit(solution)/shard_map/jit(_where)/select_n | solution.py:244
  7.2 2.1 %collective-permute-done.1 = bf16[2,32,512]{2,1,0:T(8,128)(2,1)S(1)} collective-permute-done((bf16[2,32,512]{2,1,0:T(8,128)(2,1)S(1)}, bf16[2,32,512]{2,1,0:T(8,128)(2,1)S(1)}, u32[]{:S(2)}, u32[]{:S(2)}) %collective-permute-start.1) | collective-permute-done | bytes 65568 | tf_op jit(solution)/shard_map/ppermute | solution.py:242
  9.7 0.8 %fusion.34 = bf16[2,1,1,32,512]{4,3,0,1,2:T(8,128)(2,1)S(1)} fusion(bf16[1,1,32,512]{3,2,0,1:T(8,128)(2,1)} %bitcast.70, bf16[1,1,32,512]{3,2,0,1:T(8,128)(2,1)S(1)} %bitcast.73, pred[]{:T(512)S(6)} %eq.141), kind=kLoop, calls=%fused_computation.77 | loop fusion | flops 98304 | bytes 131073 | tf_op jit(solution)/shard_map/stack | solution.py:245
  10.5 2.7 %collective-permute-done.2 = bf16[2,2,32,512]{3,2,0,1:T(8,128)(2,1)S(1)} collective-permute-done((bf16[2,2,32,512]{3,2,0,1:T(8,128)(2,1)S(1)}, bf16[2,2,32,512]{3,2,0,1:T(8,128)(2,1)S(1)}, u32[]{:S(2)}, u32[]{:S(2)}) %collective-permute-start.2) | collective-permute-done | bytes 131104 | tf_op jit(solution)/shard_map/ppermute | solution.py:242
  13.3 3.3 %collective-permute-start.3 = (bf16[2,2,2,32,512]{4,3,0,1,2:T(8,128)(2,1)S(1)}, bf16[2,2,2,32,512]{4,3,0,1,2:T(8,128)(2,1)S(1)}, u32[]{:S(2)}, u32[]{:S(2)}) collective-permute-start(bf16[2,2,2,32,512]{4,3,0,1,2:T(8,128)(2,1)S(1)} %maximum_select_fusion.2), channel_id=1, source_target_pairs={{0,1},{1,0},{2,3},{3,2},{4,5},{5,4},{6,7},{7,6},{8,9},{9,8},{10,11... | collective-permute-start | bytes 786440 | tf_op jit(solution)/shard_map/ppermute | solution.py:242
  17.9 0.8 %concatenate.90.blocks_ref = bf16[65,32,128]{2,1,0:T(8,128)(2,1)} pad(bf16[64,32,128]{2,1,0:T(8,128)(2,1)S(1)} %bitcast.58, bf16[]{:T(256)} %constant.140.clone.1), padding=0_1x0_0x0_0 | pad | bytes 1056770 | tf_op jit(solution)/shard_map/concatenate | solution.py:276
  18.9 0.9 %copy.38 = bf16[2,2,2,2,32,512]{5,4,3,2,1,0:T(8,128)(2,1)} copy(bf16[2,2,2,2,32,512]{5,4,0,1,2,3:T(8,128)(2,1)S(1)} %maximum_select_fusion) | data formatting | bytes 1048576 | tf_op jit(solution)/shard_map/jit(_where)/select_n | solution.py:244
  19.8 5.1 %shard_map.91 = bf16[512,512]{1,0:T(8,128)(2,1)} custom-call(s32[256]{0:T(256)} %select_n.210.blk_ref, bf16[65,32,128]{2,1,0:T(8,128)(2,1)} %concatenate.90.blocks_ref, bf16[512,512]{1,0:T(8,128)(2,1)} %bitcast.67, bf16[16,32,512]{2,1,0:T(8,128)(2,1)} %bitcast.60), custom_call_target="tpu_custom_call" | custom-call | tf_op jit(solution)/shard_map/pallas_call | solution.py:121
  24.8 1.4 %concatenate.91 = bf16[16,4,4096]{2,1,0:T(4,128)(2,1)S(1)} reshape(bf16[512,512]{1,0:T(8,128)(2,1)} %shard_map.91) | data formatting | bytes 1048576 | tf_op jit(solution)/shard_map/concatenate | solution.py:289
  26.3 1.0 %pad_maximum_fusion.1 = bf16[16,4,4224]{2,1,0:T(4,128)(2,1)} fusion(bf16[16,4,128]{2,1,0:T(4,128)(2,1)S(1)} %broadcast_in_dim.86, bf16[16,4,4096]{2,1,0:T(4,128)(2,1)S(1)} %concatenate.91), kind=kLoop, calls=%fused_computation.9 | loop fusion | flops 1081344 | bytes 1081344 | tf_op jit(solution)/shard_map/concatenate | solution.py:289
  27.4 5.7 %all-to-all-start = ((bf16[16,4,4224]{2,1,0:T(4,128)(2,1)}), bf16[16,4,4224]{2,1,0:T(4,128)(2,1)S(1)}, u32[]{:S(2)}, u32[]{:S(2)}) async-start(bf16[16,4,4224]{2,1,0:T(4,128)(2,1)} %pad_maximum_fusion.1), calls=%async_computation | async-start | bytes 1081344 | tf_op jit(solution)/shard_map/all_to_all | solution.py:290
  33.1 0.7 %fusion.1 = bf16[9,128,144]{1,2,0:T(8,128)(2,1)S(1)} fusion(bf16[3,9,8,8]{3,2,1,0:T(8,128)(2,1)S(1)} %bitcast.55, pred[3,128,144]{1,2,0:T(8,128)(4,1)S(1)} %broadcast_compare_fusion.1, s32[144]{0:T(256)S(1)} %and_select_fusion.1, s32[128]{0:T(128)S(1)} %and_select_fusion), kind=kOutput, calls=%fused_computation.4 | convolution fusion | flops 9323008 | bytes 391616 | tf_op jit(solution)/shard_map/ro,xyoc->xyrc/dot_general | solution.py:188
  33.8 1.1 %copy.40 = bf16[9,128,144]{2,1,0:T(8,128)(2,1)} copy(bf16[9,128,144]{1,2,0:T(8,128)(2,1)S(1)} %fusion.1) | data formatting | bytes 663552 | tf_op jit(solution)/shard_map/convert_element_type | solution.py:199
  35.2 11.8 %all-to-all-done = bf16[16,4,4224]{2,1,0:T(4,128)(2,1)S(1)} async-done(((bf16[16,4,4224]{2,1,0:T(4,128)(2,1)}), bf16[16,4,4224]{2,1,0:T(4,128)(2,1)S(1)}, u32[]{:S(2)}, u32[]{:S(2)}) %all-to-all-start) | async-done | bytes 540704 | tf_op jit(solution)/shard_map/all_to_all | solution.py:290
  48.1 3.6 %collective-permute-start.4 = (bf16[528,256]{1,0:T(8,128)(2,1)S(1)}, bf16[528,256]{1,0:T(8,128)(2,1)S(1)}, u32[]{:S(2)}, u32[]{:S(2)}) collective-permute-start(bf16[528,256]{1,0:T(8,128)(2,1)S(1)} %get-tuple-element.5), channel_id=1, source_target_pairs={{0,1},{1,2},{2,3},{3,4},{4,5},{5,6},{6,7},{7,8},{8,9},{9,10},{10,1... | collective-permute-start | bytes 811016 | tf_op jit(solution)/shard_map/ppermute | solution.py:226
  51.7 1.9 %collective-permute-start.5 = (bf16[528,256]{1,0:T(8,128)(2,1)S(1)}, bf16[528,256]{1,0:T(8,128)(2,1)S(1)}, u32[]{:S(2)}, u32[]{:S(2)}) collective-permute-start(bf16[528,256]{1,0:T(8,128)(2,1)S(1)} %get-tuple-element.6), channel_id=1, source_target_pairs={{1,0},{2,1},{3,2},{4,3},{5,4},{6,5},{7,6},{8,7},{9,8},{10,9},{11,1... | collective-permute-start | bytes 811016 | tf_op jit(solution)/shard_map/ppermute | solution.py:227
  54.2 1.3 %select_reduce_fusion = bf16[9,64,528]{2,1,0:T(8,128)(2,1)} fusion(f32[3,9,528]{2,1,0:T(8,128)S(1)} %convolution_bitcast_fusion, pred[3,64,528]{2,1,0:T(8,128)(4,1)S(1)} %broadcast_compare_fusion), kind=kLoop, calls=%fused_computation.2 | loop fusion | flops 1520640 | bytes 766656 | tf_op jit(solution)/shard_map/reduce_sum | solution.py:198
  55.6 4.8 %collective-permute-done.5 = bf16[528,256]{1,0:T(8,128)(2,1)S(1)} collective-permute-done((bf16[528,256]{1,0:T(8,128)(2,1)S(1)}, bf16[528,256]{1,0:T(8,128)(2,1)S(1)}, u32[]{:S(2)}, u32[]{:S(2)}) %collective-permute-start.5) | collective-permute-done | bytes 270368 | tf_op jit(solution)/shard_map/ppermute | solution.py:227
  60.4 1.1 %pad_maximum_fusion.refs_1_ = bf16[528,1024]{1,0:T(8,128)(2,1)} fusion(bf16[528,256]{1,0:T(8,128)(2,1)S(1)} %collective-permute-done.5, bf16[528,512]{1,0:T(8,128)(2,1)S(1)} %pad.5, bf16[528,256]{1,0:T(8,128)(2,1)S(1)} %collective-permute-done.4), kind=kLoop, calls=%fused_computation.8 | loop fusion | flops 3244032 | bytes 2162688 | tf_op jit(solution)/shard_map/concatenate | solution.py:228
  61.5 4.4 %shard_map.92.refs_0_ = bf16[528,768]{1,0:T(8,128)(2,1)} custom-call(s32[2]{0:T(128)} %add_convert_fusion.refs_0_, bf16[528,1024]{1,0:T(8,128)(2,1)} %pad_maximum_fusion.refs_1_, bf16[3,3,128,144]{3,2,1,0:T(8,128)(2,1)} %bitcast.57), custom_call_target="tpu_custom_call" | custom-call | tf_op jit(solution)/shard_map/pallas_call | solution.py:214
  66.0 3.2 %shard_map.93 = f32[4,64,128]{2,1,0:T(8,128)} custom-call(bf16[528,768]{1,0:T(8,128)(2,1)} %shard_map.92.refs_0_, bf16[3,3,64,528]{3,2,1,0:T(8,128)(2,1)} %bitcast.56), custom_call_target="tpu_custom_call" | custom-call | tf_op jit(solution)/shard_map/pallas_call | solution.py:214
  (49 shorter events, 6.3 us)
Async XLA Ops:
  0.0 33.0 %copy-start = (bf16[3,3,3,8,8]{4,3,2,1,0:T(8,128)(2,1)S(1)}, bf16[3,3,3,8,8]{4,3,2,1,0:T(8,128)(2,1)}, u32[]{:S(2)}) copy-start(bf16[3,3,3,8,8]{4,3,2,1,0:T(8,128)(2,1)} %param.16) | copy-start | bytes 10372
  0.0 17.4 %copy-start.1 = (bf16[1,32,8192]{2,1,0:T(8,128)(2,1)S(1)}, bf16[1,32,8192]{2,1,0:T(8,128)(2,1)}, u32[]{:S(2)}) copy-start(bf16[1,32,8192]{2,1,0:T(8,128)(2,1)} %param.9) | copy-start | bytes 1572868
  0.0 5.3 %collective-permute-start = (bf16[32,512]{1,0:T(8,128)(2,1)}, bf16[32,512]{1,0:T(8,128)(2,1)S(1)}, u32[]{:S(2)}, u32[]{:S(2)}) collective-permute-start(bf16[32,512]{1,0:T(8,128)(2,1)} %bitcast.68), channel_id=1, source_target_pairs={{0,8},{1,9},{2,10},{3,11},{4,12},{5,13},{6,14},{7,15},{8,0},{9,1},... | collective-permute-start | bytes 98312 | tf_op jit(solution)/shard_map/ppermute | solution.py:242
  6.2 3.2 %collective-permute-start.1 = (bf16[2,32,512]{2,1,0:T(8,128)(2,1)S(1)}, bf16[2,32,512]{2,1,0:T(8,128)(2,1)S(1)}, u32[]{:S(2)}, u32[]{:S(2)}) collective-permute-start(bf16[2,32,512]{2,1,0:T(8,128)(2,1)S(1)} %maximum_select_fusion.6), channel_id=1, source_target_pairs={{0,4},{1,5},{2,6},{3,7},{4,0},{5,1},{6,2},{7,3},{8,12},{9,13},{10,... | collective-permute-start | bytes 196616 | tf_op jit(solution)/shard_map/ppermute | solution.py:242
  9.4 3.9 %collective-permute-start.2 = (bf16[2,2,32,512]{3,2,0,1:T(8,128)(2,1)S(1)}, bf16[2,2,32,512]{3,2,0,1:T(8,128)(2,1)S(1)}, u32[]{:S(2)}, u32[]{:S(2)}) collective-permute-start(bf16[2,2,32,512]{3,2,0,1:T(8,128)(2,1)S(1)} %maximum_select_fusion.4), channel_id=1, source_target_pairs={{0,2},{1,3},{2,0},{3,1},{4,6},{5,7},{6,4},{7,5},{8,10},{9,11},{10,... | collective-permute-start | bytes 393224 | tf_op jit(solution)/shard_map/ppermute | solution.py:242
  13.3 5.5 %collective-permute-start.3 = (bf16[2,2,2,32,512]{4,3,0,1,2:T(8,128)(2,1)S(1)}, bf16[2,2,2,32,512]{4,3,0,1,2:T(8,128)(2,1)S(1)}, u32[]{:S(2)}, u32[]{:S(2)}) collective-permute-start(bf16[2,2,2,32,512]{4,3,0,1,2:T(8,128)(2,1)S(1)} %maximum_select_fusion.2), channel_id=1, source_target_pairs={{0,1},{1,0},{2,3},{3,2},{4,5},{5,4},{6,7},{7,6},{8,9},{9,8},{10,11... | collective-permute-start | bytes 786440 | tf_op jit(solution)/shard_map/ppermute | solution.py:242
  27.4 19.6 %all-to-all-start = ((bf16[16,4,4224]{2,1,0:T(4,128)(2,1)}), bf16[16,4,4224]{2,1,0:T(4,128)(2,1)S(1)}, u32[]{:S(2)}, u32[]{:S(2)}) async-start(bf16[16,4,4224]{2,1,0:T(4,128)(2,1)} %pad_maximum_fusion.1), calls=%async_computation | async-start | bytes 1081344 | tf_op jit(solution)/shard_map/all_to_all | solution.py:290
  33.1 1.9 %copy-start.2 = (bf16[3,3,3,8]{3,2,1,0:T(4,128)(2,1)S(1)}, bf16[3,3,3,8]{3,2,1,0:T(4,128)(2,1)}, u32[]{:S(2)}) copy-start(bf16[3,3,3,8]{3,2,1,0:T(4,128)(2,1)} %param.17) | copy-start | bytes 1300
  48.1 7.5 %collective-permute-start.4 = (bf16[528,256]{1,0:T(8,128)(2,1)S(1)}, bf16[528,256]{1,0:T(8,128)(2,1)S(1)}, u32[]{:S(2)}, u32[]{:S(2)}) collective-permute-start(bf16[528,256]{1,0:T(8,128)(2,1)S(1)} %get-tuple-element.5), channel_id=1, source_target_pairs={{0,1},{1,2},{2,3},{3,4},{4,5},{5,6},{6,7},{7,8},{8,9},{9,10},{10,1... | collective-permute-start | bytes 811016 | tf_op jit(solution)/shard_map/ppermute | solution.py:226
  51.7 8.7 %collective-permute-start.5 = (bf16[528,256]{1,0:T(8,128)(2,1)S(1)}, bf16[528,256]{1,0:T(8,128)(2,1)S(1)}, u32[]{:S(2)}, u32[]{:S(2)}) collective-permute-start(bf16[528,256]{1,0:T(8,128)(2,1)S(1)} %get-tuple-element.6), channel_id=1, source_target_pairs={{1,0},{2,1},{3,2},{4,3},{5,4},{6,5},{7,6},{8,7},{9,8},{10,9},{11,1... | collective-permute-start | bytes 811016 | tf_op jit(solution)/shard_map/ppermute | solution.py:227

commit v9 on v8

--- a/solution.py
+++ b/solution.py
@@ -73,15 +73,15 @@
     return carried
 
 
-def correlate_kernel(blk_ref, blocks_ref, table_ref, ref_ref, out_ref, arranged, products):
+def correlate_kernel(blk_ref, tag_ref, blocks_ref, table_ref, ref_ref, out_ref, arranged, products):
     chunk = 8
     slots = table_ref.shape[0] // blocks_ref.shape[2]
     width = blocks_ref.shape[2]
     channels = blocks_ref.shape[1]
-    units = out_ref.shape[0] // GROUPS
+    units = out_ref.shape[0]
+    tpix = table_ref.shape[1]
     cap = units // ref_ref.shape[0]
     group_size = channels // GROUPS
-    rows = chunk * channels
 
     def step(c, carry):
         for u in range(chunk):
@@ -101,27 +101,33 @@
                     warped[u * channels : (u + 1) * channels, j * 128 : (j + 1) * 128]
                     * tile[:, j * 128 : (j + 1) * 128]
                 )
-        start = pl.multiple_of(c * (chunk * GROUPS), chunk * GROUPS)
-        for j in range(lanes):
-            total = products[j, pl.ds(0, rows // group_size, stride=group_size), :]
-            for k in range(1, group_size):
-                total = total + products[j, pl.ds(k, rows // group_size, stride=group_size), :]
-            out_ref[pl.ds(start, chunk * GROUPS), j * 128 : (j + 1) * 128] = (
-                total * (GROUPS / channels)
-            ).astype(out_ref.dtype)
+        start = pl.multiple_of(c * chunk, chunk)
+        for g in range(GROUPS):
+            for j in range(lanes):
+                total = products[j, pl.ds(g * group_size, chunk, stride=channels), :]
+                for k in range(1, group_size):
+                    total = total + products[j, pl.ds(g * group_size + k, chunk, stride=channels), :]
+                out_ref[pl.ds(start, chunk), g * tpix + j * 128 : g * tpix + (j + 1) * 128] = (
+                    total * (GROUPS / channels)
+                ).astype(out_ref.dtype)
+        tags = jnp.concatenate(
+            [jnp.full((1, 128), tag_ref[c * chunk + u], jnp.int32) for u in range(chunk)], axis=0
+        )
+        out_ref[pl.ds(start, chunk), GROUPS * tpix :] = tags.astype(jnp.float32).astype(out_ref.dtype)
         return carry
 
     lax.fori_loop(0, units // chunk, step, 0)
 
 
-def correlate(blk, blocks, table, refs, units):
-    channels, width = blocks.shape[1], blocks.shape[2]
+def correlate(blk, tags, blocks, table, refs, units):
+    channels = blocks.shape[1]
     tpix = table.shape[1]
     chunk = 8
     return pl.pallas_call(
         correlate_kernel,
-        out_shape=jax.ShapeDtypeStruct((units * GROUPS, tpix), jnp.bfloat16),
+        out_shape=jax.ShapeDtypeStruct((units, GROUPS * tpix + 128), jnp.bfloat16),
         in_specs=[
+            pl.BlockSpec(memory_space=pltpu.SMEM),
             pl.BlockSpec(memory_space=pltpu.SMEM),
             pl.BlockSpec(memory_space=pltpu.VMEM),
             pl.BlockSpec(memory_space=pltpu.VMEM),
@@ -132,7 +138,7 @@
             pltpu.VMEM((chunk * channels, table.shape[0]), jnp.bfloat16),
             pltpu.VMEM((tpix // 128, chunk * channels, 128), jnp.float32),
         ],
-    )(blk, blocks, table, refs)
+    )(blk, tags, blocks, table, refs)
 
 
 def conv_kernel(*refs, relu, rows, cols, groups, chunk):
@@ -279,14 +285,12 @@
     picked = jnp.sum(jnp.where(matches, src_block[0][:, :, None], 0), axis=1)
     alive = jnp.any(live, axis=1)
     blk = jnp.where(alive, picked, nblocks).reshape(-1).astype(jnp.int32)
-    depth_code = jnp.where(counts > 0, depth_plane[0], -1).astype(jnp.bfloat16)
+    depth_code = jnp.where(counts > 0, depth_plane[0], -1).astype(jnp.int32)
 
     ref_all = gather_view(ref_feat)
-    corr_all = correlate(
-        blk, blocks, weight_table.reshape(slots * block_width, tpix), ref_all, units
-    ).reshape(units, GROUPS * tpix)
-    tag_lanes = jnp.broadcast_to(depth_code[:, None], (units, 128))
-    payload = jnp.concatenate([corr_all, tag_lanes], axis=1)
+    payload = correlate(
+        blk, depth_code, blocks, weight_table.reshape(slots * block_width, tpix), ref_all, units
+    )
     arriving = lax.all_to_all(
         payload.reshape(owners, cap, GROUPS * tpix + 128),
         "view",

time: 69.9 us -> 72.1 us (1.031)
  Pallas kernels: 12.7 us -> 15.6 us
    pallas_call x1, Pallas kernels: 5.05 us -> 7.89 us  [correlate(): pl.pallas_call(correlate_kernel, out_shape=jax.ShapeDtypeStruct((units, G...]
    reshape x0 -> x1, local copies, waits for them, and re-layouts: none -> 1.98 us  [body(): payload.reshape(owners, cap, GROUPS * tpix + 128)]
    concatenate x1 -> x0, local copies, waits for them, and re-layouts: 1.43 us -> none  [body(): payload = jnp.concatenate([corr_all, tag_lanes], axis=1)]
    select_n x0 -> x1, other arithmetic: none -> 1.15 us  [body(): depth_code = jnp.where(counts > 0, depth_plane[0], -1).astype(jnp.int32)]
    concatenate x1 -> x0, other arithmetic: 1.03 us -> none  [body(): payload = jnp.concatenate([corr_all, tag_lanes], axis=1)]
where the time goes in v9:
time: 72.1 us; the launch traced here: 71.4 us
  waiting for transfers between devices  21.4 us (30%)
  starting transfers between devices  16.9 us (23%)
  Pallas kernels  15.6 us (22%)
  other arithmetic  9.47 us (13%)
  local copies, waits for them, and re-layouts  6.55 us (9%)
  matrix products  1.24 us (2%)
    all_to_all x1, waiting for transfers between devices, body(): lax.all_to_all(payload.reshape(owners, cap, GROUPS * tpix + 128), 'view',...  11.8 us
    pallas_call x1, Pallas kernels, correlate(): pl.pallas_call(correlate_kernel, out_shape=jax.ShapeDtypeStruct((units, G...  7.89 us
    pallas_call x2, Pallas kernels, conv_rows(): pl.pallas_call(functools.partial(conv_kernel, relu=relu, rows=rows, cols=...  7.67 us
    ppermute x4, starting transfers between devices, gather_view(): lax.ppermute(gathered, 'view', [(i, i ^ stride) for i in range(count)])  6.15 us
    all_to_all x1, starting transfers between devices, body(): lax.all_to_all(payload.reshape(owners, cap, GROUPS * tpix + 128), 'view',...  5.21 us
    ppermute x4, waiting for transfers between devices, gather_view(): lax.ppermute(gathered, 'view', [(i, i ^ stride) for i in range(count)])  4.83 us
    ppermute x1, waiting for transfers between devices, halo_cols(): high = lax.ppermute(block[:, :cols], 'view', backward)  4.77 us
    ppermute x1, starting transfers between devices, halo_cols(): low = lax.ppermute(block[:, block.shape[1] - cols:], 'view', forward)  3.61 us
  transfers between devices with their start and end apart: 7, of which 4 were waited for; matrix products, arithmetic and copies ran while one was open for 16% of the time, Pallas kernels for 0%

profile of v9, /device:TPU:13, one launch (start us, length us, event | category | flops | bytes accessed | tf_op | source)
XLA Modules:
  0.0 71.4 jit_solution(206689194505773237)
XLA Ops:
  0.0 2.3 %collective-permute-start = (bf16[32,512]{1,0:T(8,128)(2,1)}, bf16[32,512]{1,0:T(8,128)(2,1)S(1)}, u32[]{:S(2)}, u32[]{:S(2)}) collective-permute-start(bf16[32,512]{1,0:T(8,128)(2,1)} %bitcast.71), channel_id=1, source_target_pairs={{0,8},{1,9},{2,10},{3,11},{4,12},{5,13},{6,14},{7,15},{8,0},{9,1},... | collective-permute-start | bytes 98312 | tf_op jit(solution)/shard_map/ppermute | solution.py:248
  3.0 0.7 select_reduce_fusion.1
  4.4 1.2 %compare_select_fusion.tag_ref = s32[64]{0:T(128)} fusion(s32[1,64]{1,0:T(1,128)} %param.15, s32[1,64]{1,0:T(1,128)} %param.14), kind=kLoop, calls=%fused_computation.62 | loop fusion | flops 128 | bytes 768 | tf_op jit(solution)/shard_map/jit(_where)/select_n | solution.py:288
  5.8 0.8 %maximum_select_fusion.6 = bf16[2,32,512]{2,1,0:T(8,128)(2,1)S(1)} fusion(bf16[1,32,512]{2,1,0:T(8,128)(2,1)S(1)} %bitcast.74, bf16[1,32,512]{2,1,0:T(8,128)(2,1)} %param.10, pred[]{:T(512)S(6)} %eq.141), kind=kLoop, calls=%fused_computation.19 | loop fusion | flops 98304 | bytes 131073 | tf_op jit(solution)/shard_map/jit(_where)/select_n | solution.py:250
  6.9 0.8 %maximum_select_fusion.5 = bf16[2,1,32,512]{3,2,0,1:T(8,128)(2,1)S(1)} fusion(bf16[1,1,32,512]{3,2,0,1:T(8,128)(2,1)S(1)} %bitcast.75, bf16[1,1,32,512]{3,2,0,1:T(8,128)(2,1)} %bitcast.72, pred[]{:T(512)S(6)} %eq.141), kind=kLoop, calls=%fused_computation.18 | loop fusion | flops 98304 | bytes 131073 | tf_op jit(solution)/shard_map/jit(_where)/select_n | solution.py:250
  7.7 2.1 %collective-permute-done.1 = bf16[2,32,512]{2,1,0:T(8,128)(2,1)S(1)} collective-permute-done((bf16[2,32,512]{2,1,0:T(8,128)(2,1)S(1)}, bf16[2,32,512]{2,1,0:T(8,128)(2,1)S(1)}, u32[]{:S(2)}, u32[]{:S(2)}) %collective-permute-start.1) | collective-permute-done | bytes 65568 | tf_op jit(solution)/shard_map/ppermute | solution.py:248
  10.1 0.8 %fusion.32 = bf16[2,1,1,32,512]{4,3,0,1,2:T(8,128)(2,1)S(1)} fusion(bf16[1,1,32,512]{3,2,0,1:T(8,128)(2,1)} %bitcast.73, bf16[1,1,32,512]{3,2,0,1:T(8,128)(2,1)S(1)} %bitcast.76, pred[]{:T(512)S(6)} %eq.141), kind=kLoop, calls=%fused_computation.74 | loop fusion | flops 98304 | bytes 131073 | tf_op jit(solution)/shard_map/stack | solution.py:251
  11.0 2.7 %collective-permute-done.2 = bf16[2,2,32,512]{3,2,0,1:T(8,128)(2,1)S(1)} collective-permute-done((bf16[2,2,32,512]{3,2,0,1:T(8,128)(2,1)S(1)}, bf16[2,2,32,512]{3,2,0,1:T(8,128)(2,1)S(1)}, u32[]{:S(2)}, u32[]{:S(2)}) %collective-permute-start.2) | collective-permute-done | bytes 131104 | tf_op jit(solution)/shard_map/ppermute | solution.py:248
  13.7 3.3 %collective-permute-start.3 = (bf16[2,2,2,32,512]{4,3,0,1,2:T(8,128)(2,1)S(1)}, bf16[2,2,2,32,512]{4,3,0,1,2:T(8,128)(2,1)S(1)}, u32[]{:S(2)}, u32[]{:S(2)}) collective-permute-start(bf16[2,2,2,32,512]{4,3,0,1,2:T(8,128)(2,1)S(1)} %maximum_select_fusion.2), channel_id=1, source_target_pairs={{0,1},{1,0},{2,3},{3,2},{4,5},{5,4},{6,7},{7,6},{8,9},{9,8},{10,11... | collective-permute-start | bytes 786440 | tf_op jit(solution)/shard_map/ppermute | solution.py:248
  18.3 0.8 %concatenate.84.blocks_ref = bf16[65,32,128]{2,1,0:T(8,128)(2,1)} pad(bf16[64,32,128]{2,1,0:T(8,128)(2,1)S(1)} %bitcast.61, bf16[]{:T(256)} %constant.141.clone.1), padding=0_1x0_0x0_0 | pad | bytes 1056770 | tf_op jit(solution)/shard_map/concatenate | solution.py:282
  19.3 0.9 %copy.38 = bf16[2,2,2,2,32,512]{5,4,3,2,1,0:T(8,128)(2,1)} copy(bf16[2,2,2,2,32,512]{5,4,0,1,2,3:T(8,128)(2,1)S(1)} %maximum_select_fusion) | data formatting | bytes 1048576 | tf_op jit(solution)/shard_map/jit(_where)/select_n | solution.py:250
  20.2 7.9 %shard_map.91 = bf16[64,4224]{1,0:T(8,128)(2,1)} custom-call(s32[256]{0:T(256)} %select_n.205.blk_ref, s32[64]{0:T(128)} %compare_select_fusion.tag_ref, bf16[65,32,128]{2,1,0:T(8,128)(2,1)} %concatenate.84.blocks_ref, bf16[512,512]{1,0:T(8,128)(2,1)} %bitcast.70, bf16[16,32,512]{2,1,0:T(8,128)(2,1)} %bitcast.63), custom_call_target="tpu_custom_call" | custom-call | tf_op jit(solution)/shard_map/pallas_call | solution.py:126
  28.0 2.0 %reshape.533 = bf16[16,4,4224]{2,1,0:T(4,128)(2,1)} reshape(bf16[64,4224]{1,0:T(8,128)(2,1)} %shard_map.91) | data formatting | bytes 1081344 | tf_op jit(solution)/shard_map/reshape | solution.py:295
  30.0 5.2 %all-to-all-start = ((bf16[16,4,4224]{2,1,0:T(4,128)(2,1)}), bf16[16,4,4224]{2,1,0:T(4,128)(2,1)S(1)}, u32[]{:S(2)}, u32[]{:S(2)}) async-start(bf16[16,4,4224]{2,1,0:T(4,128)(2,1)} %reshape.533), calls=%async_computation | async-start | bytes 1081344 | tf_op jit(solution)/shard_map/all_to_all | solution.py:294
  35.3 0.7 %fusion.1 = bf16[9,128,144]{1,2,0:T(8,128)(2,1)S(1)} fusion(bf16[3,9,8,8]{3,2,1,0:T(8,128)(2,1)S(1)} %bitcast.58, pred[3,128,144]{1,2,0:T(8,128)(4,1)S(1)} %broadcast_compare_fusion.1, s32[144]{0:T(256)S(1)} %and_select_fusion.1, s32[128]{0:T(128)S(1)} %and_select_fusion), kind=kOutput, calls=%fused_computation.4 | convolution fusion | flops 9323008 | bytes 391616 | tf_op jit(solution)/shard_map/ro,xyoc->xyrc/dot_general | solution.py:194
  36.0 1.1 %copy.40 = bf16[9,128,144]{2,1,0:T(8,128)(2,1)} copy(bf16[9,128,144]{1,2,0:T(8,128)(2,1)S(1)} %fusion.1) | data formatting | bytes 663552 | tf_op jit(solution)/shard_map/convert_element_type | solution.py:205
  37.4 11.8 %all-to-all-done = bf16[16,4,4224]{2,1,0:T(4,128)(2,1)S(1)} async-done(((bf16[16,4,4224]{2,1,0:T(4,128)(2,1)}), bf16[16,4,4224]{2,1,0:T(4,128)(2,1)S(1)}, u32[]{:S(2)}, u32[]{:S(2)}) %all-to-all-start) | async-done | bytes 540704 | tf_op jit(solution)/shard_map/all_to_all | solution.py:294
  50.3 3.6 %collective-permute-start.4 = (bf16[528,256]{1,0:T(8,128)(2,1)S(1)}, bf16[528,256]{1,0:T(8,128)(2,1)S(1)}, u32[]{:S(2)}, u32[]{:S(2)}) collective-permute-start(bf16[528,256]{1,0:T(8,128)(2,1)S(1)} %get-tuple-element.5), channel_id=1, source_target_pairs={{0,1},{1,2},{2,3},{3,4},{4,5},{5,6},{6,7},{7,8},{8,9},{9,10},{10,1... | collective-permute-start | bytes 811016 | tf_op jit(solution)/shard_map/ppermute | solution.py:232
  53.9 1.9 %collective-permute-start.5 = (bf16[528,256]{1,0:T(8,128)(2,1)S(1)}, bf16[528,256]{1,0:T(8,128)(2,1)S(1)}, u32[]{:S(2)}, u32[]{:S(2)}) collective-permute-start(bf16[528,256]{1,0:T(8,128)(2,1)S(1)} %get-tuple-element.6), channel_id=1, source_target_pairs={{1,0},{2,1},{3,2},{4,3},{5,4},{6,5},{7,6},{8,7},{9,8},{10,9},{11,1... | collective-permute-start | bytes 811016 | tf_op jit(solution)/shard_map/ppermute | solution.py:233
  56.4 1.3 %select_reduce_fusion = bf16[9,64,528]{2,1,0:T(8,128)(2,1)} fusion(f32[3,9,528]{2,1,0:T(8,128)S(1)} %convolution_bitcast_fusion, pred[3,64,528]{2,1,0:T(8,128)(4,1)S(1)} %broadcast_compare_fusion), kind=kLoop, calls=%fused_computation.2 | loop fusion | flops 1520640 | bytes 766656 | tf_op jit(solution)/shard_map/reduce_sum | solution.py:204
  57.8 4.8 %collective-permute-done.5 = bf16[528,256]{1,0:T(8,128)(2,1)S(1)} collective-permute-done((bf16[528,256]{1,0:T(8,128)(2,1)S(1)}, bf16[528,256]{1,0:T(8,128)(2,1)S(1)}, u32[]{:S(2)}, u32[]{:S(2)}) %collective-permute-start.5) | collective-permute-done | bytes 270368 | tf_op jit(solution)/shard_map/ppermute | solution.py:233
  62.6 1.1 %pad_maximum_fusion.refs_1_ = bf16[528,1024]{1,0:T(8,128)(2,1)} fusion(bf16[528,256]{1,0:T(8,128)(2,1)S(1)} %collective-permute-done.5, bf16[528,512]{1,0:T(8,128)(2,1)S(1)} %pad.5, bf16[528,256]{1,0:T(8,128)(2,1)S(1)} %collective-permute-done.4), kind=kLoop, calls=%fused_computation.8 | loop fusion | flops 3244032 | bytes 2162688 | tf_op jit(solution)/shard_map/concatenate | solution.py:234
  63.7 4.4 %shard_map.92.refs_0_ = bf16[528,768]{1,0:T(8,128)(2,1)} custom-call(s32[2]{0:T(128)} %add_convert_fusion.refs_0_, bf16[528,1024]{1,0:T(8,128)(2,1)} %pad_maximum_fusion.refs_1_, bf16[3,3,128,144]{3,2,1,0:T(8,128)(2,1)} %bitcast.60), custom_call_target="tpu_custom_call" | custom-call | tf_op jit(solution)/shard_map/pallas_call | solution.py:220
  68.2 3.2 %shard_map.93 = f32[4,64,128]{2,1,0:T(8,128)} custom-call(bf16[528,768]{1,0:T(8,128)(2,1)} %shard_map.92.refs_0_, bf16[3,3,64,528]{3,2,1,0:T(8,128)(2,1)} %bitcast.59), custom_call_target="tpu_custom_call" | custom-call | tf_op jit(solution)/shard_map/pallas_call | solution.py:220
  (46 shorter events, 5.4 us)
Async XLA Ops:
  0.0 35.2 %copy-start = (bf16[3,3,3,8,8]{4,3,2,1,0:T(8,128)(2,1)S(1)}, bf16[3,3,3,8,8]{4,3,2,1,0:T(8,128)(2,1)}, u32[]{:S(2)}) copy-start(bf16[3,3,3,8,8]{4,3,2,1,0:T(8,128)(2,1)} %param.16) | copy-start | bytes 10372
  0.0 17.8 %copy-start.1 = (bf16[1,32,8192]{2,1,0:T(8,128)(2,1)S(1)}, bf16[1,32,8192]{2,1,0:T(8,128)(2,1)}, u32[]{:S(2)}) copy-start(bf16[1,32,8192]{2,1,0:T(8,128)(2,1)} %param.9) | copy-start | bytes 1572868
  0.0 5.8 %collective-permute-start = (bf16[32,512]{1,0:T(8,128)(2,1)}, bf16[32,512]{1,0:T(8,128)(2,1)S(1)}, u32[]{:S(2)}, u32[]{:S(2)}) collective-permute-start(bf16[32,512]{1,0:T(8,128)(2,1)} %bitcast.71), channel_id=1, source_target_pairs={{0,8},{1,9},{2,10},{3,11},{4,12},{5,13},{6,14},{7,15},{8,0},{9,1},... | collective-permute-start | bytes 98312 | tf_op jit(solution)/shard_map/ppermute | solution.py:248
  6.6 3.2 %collective-permute-start.1 = (bf16[2,32,512]{2,1,0:T(8,128)(2,1)S(1)}, bf16[2,32,512]{2,1,0:T(8,128)(2,1)S(1)}, u32[]{:S(2)}, u32[]{:S(2)}) collective-permute-start(bf16[2,32,512]{2,1,0:T(8,128)(2,1)S(1)} %maximum_select_fusion.6), channel_id=1, source_target_pairs={{0,4},{1,5},{2,6},{3,7},{4,0},{5,1},{6,2},{7,3},{8,12},{9,13},{10,... | collective-permute-start | bytes 196616 | tf_op jit(solution)/shard_map/ppermute | solution.py:248
  9.8 3.9 %collective-permute-start.2 = (bf16[2,2,32,512]{3,2,0,1:T(8,128)(2,1)S(1)}, bf16[2,2,32,512]{3,2,0,1:T(8,128)(2,1)S(1)}, u32[]{:S(2)}, u32[]{:S(2)}) collective-permute-start(bf16[2,2,32,512]{3,2,0,1:T(8,128)(2,1)S(1)} %maximum_select_fusion.4), channel_id=1, source_target_pairs={{0,2},{1,3},{2,0},{3,1},{4,6},{5,7},{6,4},{7,5},{8,10},{9,11},{10,... | collective-permute-start | bytes 393224 | tf_op jit(solution)/shard_map/ppermute | solution.py:248
  13.7 5.5 %collective-permute-start.3 = (bf16[2,2,2,32,512]{4,3,0,1,2:T(8,128)(2,1)S(1)}, bf16[2,2,2,32,512]{4,3,0,1,2:T(8,128)(2,1)S(1)}, u32[]{:S(2)}, u32[]{:S(2)}) collective-permute-start(bf16[2,2,2,32,512]{4,3,0,1,2:T(8,128)(2,1)S(1)} %maximum_select_fusion.2), channel_id=1, source_target_pairs={{0,1},{1,0},{2,3},{3,2},{4,5},{5,4},{6,7},{7,6},{8,9},{9,8},{10,11... | collective-permute-start | bytes 786440 | tf_op jit(solution)/shard_map/ppermute | solution.py:248
  30.0 19.2 %all-to-all-start = ((bf16[16,4,4224]{2,1,0:T(4,128)(2,1)}), bf16[16,4,4224]{2,1,0:T(4,128)(2,1)S(1)}, u32[]{:S(2)}, u32[]{:S(2)}) async-start(bf16[16,4,4224]{2,1,0:T(4,128)(2,1)} %reshape.533), calls=%async_computation | async-start | bytes 1081344 | tf_op jit(solution)/shard_map/all_to_all | solution.py:294
  35.2 1.9 %copy-start.2 = (bf16[3,3,3,8]{3,2,1,0:T(4,128)(2,1)S(1)}, bf16[3,3,3,8]{3,2,1,0:T(4,128)(2,1)}, u32[]{:S(2)}) copy-start(bf16[3,3,3,8]{3,2,1,0:T(4,128)(2,1)} %param.17) | copy-start | bytes 1300
  50.3 7.5 %collective-permute-start.4 = (bf16[528,256]{1,0:T(8,128)(2,1)S(1)}, bf16[528,256]{1,0:T(8,128)(2,1)S(1)}, u32[]{:S(2)}, u32[]{:S(2)}) collective-permute-start(bf16[528,256]{1,0:T(8,128)(2,1)S(1)} %get-tuple-element.5), channel_id=1, source_target_pairs={{0,1},{1,2},{2,3},{3,4},{4,5},{5,6},{6,7},{7,8},{8,9},{9,10},{10,1... | collective-permute-start | bytes 811016 | tf_op jit(solution)/shard_map/ppermute | solution.py:232
  53.9 8.7 %collective-permute-start.5 = (bf16[528,256]{1,0:T(8,128)(2,1)S(1)}, bf16[528,256]{1,0:T(8,128)(2,1)S(1)}, u32[]{:S(2)}, u32[]{:S(2)}) collective-permute-start(bf16[528,256]{1,0:T(8,128)(2,1)S(1)} %get-tuple-element.6), channel_id=1, source_target_pairs={{1,0},{2,1},{3,2},{4,3},{5,4},{6,5},{7,6},{8,7},{9,8},{10,9},{11,1... | collective-permute-start | bytes 811016 | tf_op jit(solution)/shard_map/ppermute | solution.py:233

commit v10 on v8

--- a/solution.py
+++ b/solution.py
@@ -236,16 +236,12 @@
         )
     index = lax.axis_index("view")
     gathered = block[0]
-    level = 0
-    stride = count // 2
-    while stride >= 1:
+    stride = 1
+    while stride < count:
         other = lax.ppermute(gathered, "view", [(i, i ^ stride) for i in range(count)])
         low = (index // stride) % 2 == 0
-        gathered = jnp.where(
-            low, jnp.stack([gathered, other], axis=level), jnp.stack([other, gathered], axis=level)
-        )
-        level += 1
-        stride //= 2
+        gathered = jnp.where(low, jnp.stack([gathered, other]), jnp.stack([other, gathered]))
+        stride *= 2
     return gathered.reshape((count,) + block.shape[1:])
 
 

time: 69.9 us -> 78.9 us (1.13)
  waiting for transfers between devices: 21.4 us -> 31.6 us
  starting transfers between devices: 17.3 us -> 16.3 us
  local copies, waits for them, and re-layouts: 6.15 us -> 5.29 us
  other arithmetic: 10 us -> 10.8 us
    ppermute x4, waiting for transfers between devices: 4.83 us -> 15 us  [gather_view(): lax.ppermute(gathered, 'view', [(i, i ^ stride) for i in range(count)])]
    ppermute x4, starting transfers between devices: 6.15 us -> 3.59 us  [gather_view(): lax.ppermute(gathered, 'view', [(i, i ^ stride) for i in range(count)])]
    all_to_all x1, starting transfers between devices: 5.67 us -> 7.16 us  [body(): lax.all_to_all(payload.reshape(owners, cap, GROUPS * tpix + 128), 'view',...]
    select_n x1 -> x0, local copies, waits for them, and re-layouts: 0.86 us -> none  [gather_view(): jnp.where(low, jnp.stack([gathered, other], axis=level), jnp.stack([other...]
    select_n x7, other arithmetic: 1.86 us -> 2.66 us  [gather_view(): jnp.where(low, jnp.stack([gathered, other]), jnp.stack([other, gathered]))]
  transfers between devices with their start and end apart: 7 -> 7, of which waited for: 4 -> 5; matrix products, arithmetic and copies ran while one was open for 16% -> 14% of each run, Pallas kernels for 0% -> 0%
where the time goes in v10:
time: 78.9 us; the launch traced here: 78.3 us
  waiting for transfers between devices  31.6 us (40%)
  starting transfers between devices  16.3 us (21%)
  Pallas kernels  12.7 us (16%)
  other arithmetic  10.8 us (14%)
  local copies, waits for them, and re-layouts  5.29 us (7%)
  matrix products  1.24 us (2%)
    ppermute x4, waiting for transfers between devices, gather_view(): lax.ppermute(gathered, 'view', [(i, i ^ stride) for i in range(count)])  15 us
    all_to_all x1, waiting for transfers between devices, body(): lax.all_to_all(payload.reshape(owners, cap, GROUPS * tpix + 128), 'view',...  11.8 us
    pallas_call x2, Pallas kernels, conv_rows(): pl.pallas_call(functools.partial(conv_kernel, relu=relu, rows=rows, cols=...  7.67 us
    all_to_all x1, starting transfers between devices, body(): lax.all_to_all(payload.reshape(owners, cap, GROUPS * tpix + 128), 'view',...  7.16 us
    pallas_call x1, Pallas kernels, correlate(): pl.pallas_call(correlate_kernel, out_shape=jax.ShapeDtypeStruct((units *...  5.05 us
    ppermute x1, waiting for transfers between devices, halo_cols(): high = lax.ppermute(block[:, :cols], 'view', backward)  4.77 us
    ppermute x1, starting transfers between devices, halo_cols(): low = lax.ppermute(block[:, block.shape[1] - cols:], 'view', forward)  3.6 us
    ppermute x4, starting transfers between devices, gather_view(): lax.ppermute(gathered, 'view', [(i, i ^ stride) for i in range(count)])  3.59 us
  transfers between devices with their start and end apart: 7, of which 5 were waited for; matrix products, arithmetic and copies ran while one was open for 14% of the time, Pallas kernels for 0%

profile of v10, /device:TPU:13, one launch (start us, length us, event | category | flops | bytes accessed | tf_op | source)
XLA Modules:
  0.0 78.3 jit_solution(18044772713603666206)
XLA Ops:
  1.3 0.7 select_reduce_fusion.1
  3.7 0.8 %maximum_select_fusion.6 = bf16[2,32,512]{2,1,0:T(8,128)(2,1)S(1)} fusion(bf16[1,32,512]{2,1,0:T(8,128)(2,1)S(1)} %bitcast.71, bf16[1,32,512]{2,1,0:T(8,128)(2,1)} %param.10, pred[]{:T(512)S(6)} %eq.141), kind=kLoop, calls=%fused_computation.20 | loop fusion | flops 98304 | bytes 131073 | tf_op jit(solution)/shard_map/jit(_where)/select_n | solution.py:243
  4.8 0.8 %maximum_select_fusion.5 = bf16[1,2,32,512]{3,2,1,0:T(8,128)(2,1)S(1)} fusion(bf16[1,1,32,512]{3,2,1,0:T(8,128)(2,1)S(1)} %bitcast.72, bf16[1,1,32,512]{3,2,1,0:T(8,128)(2,1)} %bitcast.69, pred[]{:T(512)S(6)} %eq.141), kind=kLoop, calls=%fused_computation.19 | loop fusion | flops 98304 | bytes 131073 | tf_op jit(solution)/shard_map/jit(_where)/select_n | solution.py:243
  5.7 2.6 %collective-permute-done.1 = bf16[2,32,512]{2,1,0:T(8,128)(2,1)S(1)} collective-permute-done((bf16[2,32,512]{2,1,0:T(8,128)(2,1)S(1)}, bf16[2,32,512]{2,1,0:T(8,128)(2,1)S(1)}, u32[]{:S(2)}, u32[]{:S(2)}) %collective-permute-start.1) | collective-permute-done | bytes 65568 | tf_op jit(solution)/shard_map/ppermute | solution.py:241
  8.5 0.8 %fusion.34 = bf16[1,1,2,32,512]{4,3,2,1,0:T(8,128)(2,1)S(1)} fusion(bf16[1,1,32,512]{3,2,1,0:T(8,128)(2,1)} %bitcast.70, bf16[1,1,32,512]{3,2,1,0:T(8,128)(2,1)S(1)} %bitcast.73, pred[]{:T(512)S(6)} %eq.141), kind=kLoop, calls=%fused_computation.77 | loop fusion | flops 98304 | bytes 131073 | tf_op jit(solution)/shard_map/stack | solution.py:243
  9.4 3.1 %collective-permute-done.2 = bf16[2,2,32,512]{3,2,1,0:T(8,128)(2,1)S(1)} collective-permute-done((bf16[2,2,32,512]{3,2,1,0:T(8,128)(2,1)S(1)}, bf16[2,2,32,512]{3,2,1,0:T(8,128)(2,1)S(1)}, u32[]{:S(2)}, u32[]{:S(2)}) %collective-permute-start.2) | collective-permute-done | bytes 131104 | tf_op jit(solution)/shard_map/ppermute | solution.py:241
  12.5 2.4 %collective-permute-start.3 = (bf16[2,2,2,32,512]{4,3,2,1,0:T(8,128)(2,1)S(1)}, bf16[2,2,2,32,512]{4,3,2,1,0:T(8,128)(2,1)S(1)}, u32[]{:S(2)}, u32[]{:S(2)}) collective-permute-start(bf16[2,2,2,32,512]{4,3,2,1,0:T(8,128)(2,1)S(1)} %maximum_select_fusion.2), channel_id=1, source_target_pairs={{0,8},{1,9},{2,10},{3,11},{4,12},{5,13},{6,14},{7,15},{8,0},{9,1},... | collective-permute-start | bytes 786440 | tf_op jit(solution)/shard_map/ppermute | solution.py:241
  16.2 0.8 %concatenate.90.blocks_ref = bf16[65,32,128]{2,1,0:T(8,128)(2,1)} pad(bf16[64,32,128]{2,1,0:T(8,128)(2,1)S(1)} %bitcast.58, bf16[]{:T(256)} %constant.140.clone.1), padding=0_1x0_0x0_0 | pad | bytes 1056770 | tf_op jit(solution)/shard_map/concatenate | solution.py:272
  17.1 9.3 %collective-permute-done.3 = bf16[2,2,2,32,512]{4,3,2,1,0:T(8,128)(2,1)S(1)} collective-permute-done((bf16[2,2,2,32,512]{4,3,2,1,0:T(8,128)(2,1)S(1)}, bf16[2,2,2,32,512]{4,3,2,1,0:T(8,128)(2,1)S(1)}, u32[]{:S(2)}, u32[]{:S(2)}) %collective-permute-start.3) | collective-permute-done | bytes 262176 | tf_op jit(solution)/shard_map/ppermute | solution.py:241
  26.4 0.9 %maximum_select_fusion = bf16[2,2,2,2,32,512]{5,4,3,2,1,0:T(8,128)(2,1)} fusion(bf16[1,2,2,2,32,512]{5,4,3,2,1,0:T(8,128)(2,1)S(1)} %bitcast.74, bf16[1,2,2,2,32,512]{5,4,3,2,1,0:T(8,128)(2,1)S(1)} %maximum_select_fusion.1, pred[]{:T(512)S(6)} %eq.138), kind=kLoop, calls=%fused_computation.11 | loop fusion | flops 786432 | bytes 1048577 | tf_op jit(solution)/shard_map/jit(_where)/select_n | solution.py:243
  27.3 5.1 %shard_map.91 = bf16[512,512]{1,0:T(8,128)(2,1)} custom-call(s32[256]{0:T(256)} %select_n.210.blk_ref, bf16[65,32,128]{2,1,0:T(8,128)(2,1)} %concatenate.90.blocks_ref, bf16[512,512]{1,0:T(8,128)(2,1)} %bitcast.67, bf16[16,32,512]{2,1,0:T(8,128)(2,1)} %bitcast.60), custom_call_target="tpu_custom_call" | custom-call | tf_op jit(solution)/shard_map/pallas_call | solution.py:121
  32.4 1.4 %concatenate.91 = bf16[16,4,4096]{2,1,0:T(4,128)(2,1)S(1)} reshape(bf16[512,512]{1,0:T(8,128)(2,1)} %shard_map.91) | data formatting | bytes 1048576 | tf_op jit(solution)/shard_map/concatenate | solution.py:285
  33.9 1.0 %pad_maximum_fusion.1 = bf16[16,4,4224]{2,1,0:T(4,128)(2,1)} fusion(bf16[16,4,128]{2,1,0:T(4,128)(2,1)S(1)} %broadcast_in_dim.86, bf16[16,4,4096]{2,1,0:T(4,128)(2,1)S(1)} %concatenate.91), kind=kLoop, calls=%fused_computation.9 | loop fusion | flops 1081344 | bytes 1081344 | tf_op jit(solution)/shard_map/concatenate | solution.py:285
  34.9 7.2 %all-to-all-start = ((bf16[16,4,4224]{2,1,0:T(4,128)(2,1)}), bf16[16,4,4224]{2,1,0:T(4,128)(2,1)S(1)}, u32[]{:S(2)}, u32[]{:S(2)}) async-start(bf16[16,4,4224]{2,1,0:T(4,128)(2,1)} %pad_maximum_fusion.1), calls=%async_computation | async-start | bytes 1081344 | tf_op jit(solution)/shard_map/all_to_all | solution.py:286
  42.1 0.7 fusion.1
  42.9 1.1 %copy.35 = bf16[9,128,144]{2,1,0:T(8,128)(2,1)} copy(bf16[9,128,144]{1,2,0:T(8,128)(2,1)S(1)} %fusion.1) | data formatting | bytes 663552 | tf_op jit(solution)/shard_map/convert_element_type | solution.py:199
  44.3 11.8 %all-to-all-done = bf16[16,4,4224]{2,1,0:T(4,128)(2,1)S(1)} async-done(((bf16[16,4,4224]{2,1,0:T(4,128)(2,1)}), bf16[16,4,4224]{2,1,0:T(4,128)(2,1)S(1)}, u32[]{:S(2)}, u32[]{:S(2)}) %all-to-all-start) | async-done | bytes 540704 | tf_op jit(solution)/shard_map/all_to_all | solution.py:286
  57.2 3.6 %collective-permute-start.4 = (bf16[528,256]{1,0:T(8,128)(2,1)S(1)}, bf16[528,256]{1,0:T(8,128)(2,1)S(1)}, u32[]{:S(2)}, u32[]{:S(2)}) collective-permute-start(bf16[528,256]{1,0:T(8,128)(2,1)S(1)} %get-tuple-element.5), channel_id=1, source_target_pairs={{0,1},{1,2},{2,3},{3,4},{4,5},{5,6},{6,7},{7,8},{8,9},{9,10},{10,1... | collective-permute-start | bytes 811016 | tf_op jit(solution)/shard_map/ppermute | solution.py:226
  60.8 1.9 %collective-permute-start.5 = (bf16[528,256]{1,0:T(8,128)(2,1)S(1)}, bf16[528,256]{1,0:T(8,128)(2,1)S(1)}, u32[]{:S(2)}, u32[]{:S(2)}) collective-permute-start(bf16[528,256]{1,0:T(8,128)(2,1)S(1)} %get-tuple-element.6), channel_id=1, source_target_pairs={{1,0},{2,1},{3,2},{4,3},{5,4},{6,5},{7,6},{8,7},{9,8},{10,9},{11,1... | collective-permute-start | bytes 811016 | tf_op jit(solution)/shard_map/ppermute | solution.py:227
  63.3 1.3 %select_reduce_fusion = bf16[9,64,528]{2,1,0:T(8,128)(2,1)} fusion(f32[3,9,528]{2,1,0:T(8,128)S(1)} %convolution_bitcast_fusion, pred[3,64,528]{2,1,0:T(8,128)(4,1)S(1)} %broadcast_compare_fusion), kind=kLoop, calls=%fused_computation.2 | loop fusion | flops 1520640 | bytes 766656 | tf_op jit(solution)/shard_map/reduce_sum | solution.py:198
  64.7 4.8 %collective-permute-done.5 = bf16[528,256]{1,0:T(8,128)(2,1)S(1)} collective-permute-done((bf16[528,256]{1,0:T(8,128)(2,1)S(1)}, bf16[528,256]{1,0:T(8,128)(2,1)S(1)}, u32[]{:S(2)}, u32[]{:S(2)}) %collective-permute-start.5) | collective-permute-done | bytes 270368 | tf_op jit(solution)/shard_map/ppermute | solution.py:227
  69.4 1.1 %pad_maximum_fusion.refs_1_ = bf16[528,1024]{1,0:T(8,128)(2,1)} fusion(bf16[528,256]{1,0:T(8,128)(2,1)S(1)} %collective-permute-done.5, bf16[528,512]{1,0:T(8,128)(2,1)S(1)} %pad.5, bf16[528,256]{1,0:T(8,128)(2,1)S(1)} %collective-permute-done.4), kind=kLoop, calls=%fused_computation.8 | loop fusion | flops 3244032 | bytes 2162688 | tf_op jit(solution)/shard_map/concatenate | solution.py:228
  70.6 4.4 %shard_map.92.refs_0_ = bf16[528,768]{1,0:T(8,128)(2,1)} custom-call(s32[2]{0:T(128)} %add_convert_fusion.refs_0_, bf16[528,1024]{1,0:T(8,128)(2,1)} %pad_maximum_fusion.refs_1_, bf16[3,3,128,144]{3,2,1,0:T(8,128)(2,1)} %bitcast.57), custom_call_target="tpu_custom_call" | custom-call | tf_op jit(solution)/shard_map/pallas_call | solution.py:214
  75.0 3.2 %shard_map.93 = f32[4,64,128]{2,1,0:T(8,128)} custom-call(bf16[528,768]{1,0:T(8,128)(2,1)} %shard_map.92.refs_0_, bf16[3,3,64,528]{3,2,1,0:T(8,128)(2,1)} %bitcast.56), custom_call_target="tpu_custom_call" | custom-call | tf_op jit(solution)/shard_map/pallas_call | solution.py:214
  (48 shorter events, 6.9 us)
Async XLA Ops:
  0.0 42.1 %copy-start = (bf16[3,3,3,8,8]{4,3,2,1,0:T(8,128)(2,1)S(1)}, bf16[3,3,3,8,8]{4,3,2,1,0:T(8,128)(2,1)}, u32[]{:S(2)}) copy-start(bf16[3,3,3,8,8]{4,3,2,1,0:T(8,128)(2,1)} %param.16) | copy-start | bytes 10372
  0.0 15.7 %copy-start.1 = (bf16[1,32,8192]{2,1,0:T(8,128)(2,1)S(1)}, bf16[1,32,8192]{2,1,0:T(8,128)(2,1)}, u32[]{:S(2)}) copy-start(bf16[1,32,8192]{2,1,0:T(8,128)(2,1)} %param.9) | copy-start | bytes 1572868
  0.0 3.6 %collective-permute-start = (bf16[32,512]{1,0:T(8,128)(2,1)}, bf16[32,512]{1,0:T(8,128)(2,1)S(1)}, u32[]{:S(2)}, u32[]{:S(2)}) collective-permute-start(bf16[32,512]{1,0:T(8,128)(2,1)} %bitcast.68), channel_id=1, source_target_pairs={{0,1},{1,0},{2,3},{3,2},{4,5},{5,4},{6,7},{7,6},{8,9},{9,8},{10,11... | collective-permute-start | bytes 98312 | tf_op jit(solution)/shard_map/ppermute | solution.py:241
  4.5 3.7 %collective-permute-start.1 = (bf16[2,32,512]{2,1,0:T(8,128)(2,1)S(1)}, bf16[2,32,512]{2,1,0:T(8,128)(2,1)S(1)}, u32[]{:S(2)}, u32[]{:S(2)}) collective-permute-start(bf16[2,32,512]{2,1,0:T(8,128)(2,1)S(1)} %maximum_select_fusion.6), channel_id=1, source_target_pairs={{0,2},{1,3},{2,0},{3,1},{4,6},{5,7},{6,4},{7,5},{8,10},{9,11},{10,... | collective-permute-start | bytes 196616 | tf_op jit(solution)/shard_map/ppermute | solution.py:241
  8.3 4.2 %collective-permute-start.2 = (bf16[2,2,32,512]{3,2,1,0:T(8,128)(2,1)S(1)}, bf16[2,2,32,512]{3,2,1,0:T(8,128)(2,1)S(1)}, u32[]{:S(2)}, u32[]{:S(2)}) collective-permute-start(bf16[2,2,32,512]{3,2,1,0:T(8,128)(2,1)S(1)} %maximum_select_fusion.4), channel_id=1, source_target_pairs={{0,4},{1,5},{2,6},{3,7},{4,0},{5,1},{6,2},{7,3},{8,12},{9,13},{10,... | collective-permute-start | bytes 393224 | tf_op jit(solution)/shard_map/ppermute | solution.py:241
  12.5 13.9 %collective-permute-start.3 = (bf16[2,2,2,32,512]{4,3,2,1,0:T(8,128)(2,1)S(1)}, bf16[2,2,2,32,512]{4,3,2,1,0:T(8,128)(2,1)S(1)}, u32[]{:S(2)}, u32[]{:S(2)}) collective-permute-start(bf16[2,2,2,32,512]{4,3,2,1,0:T(8,128)(2,1)S(1)} %maximum_select_fusion.2), channel_id=1, source_target_pairs={{0,8},{1,9},{2,10},{3,11},{4,12},{5,13},{6,14},{7,15},{8,0},{9,1},... | collective-permute-start | bytes 786440 | tf_op jit(solution)/shard_map/ppermute | solution.py:241
  34.9 21.1 %all-to-all-start = ((bf16[16,4,4224]{2,1,0:T(4,128)(2,1)}), bf16[16,4,4224]{2,1,0:T(4,128)(2,1)S(1)}, u32[]{:S(2)}, u32[]{:S(2)}) async-start(bf16[16,4,4224]{2,1,0:T(4,128)(2,1)} %pad_maximum_fusion.1), calls=%async_computation | async-start | bytes 1081344 | tf_op jit(solution)/shard_map/all_to_all | solution.py:286
  42.1 1.9 %copy-start.2 = (bf16[3,3,3,8]{3,2,1,0:T(4,128)(2,1)S(1)}, bf16[3,3,3,8]{3,2,1,0:T(4,128)(2,1)}, u32[]{:S(2)}) copy-start(bf16[3,3,3,8]{3,2,1,0:T(4,128)(2,1)} %param.17) | copy-start | bytes 1300
  57.2 7.5 %collective-permute-start.4 = (bf16[528,256]{1,0:T(8,128)(2,1)S(1)}, bf16[528,256]{1,0:T(8,128)(2,1)S(1)}, u32[]{:S(2)}, u32[]{:S(2)}) collective-permute-start(bf16[528,256]{1,0:T(8,128)(2,1)S(1)} %get-tuple-element.5), channel_id=1, source_target_pairs={{0,1},{1,2},{2,3},{3,4},{4,5},{5,6},{6,7},{7,8},{8,9},{9,10},{10,1... | collective-permute-start | bytes 811016 | tf_op jit(solution)/shard_map/ppermute | solution.py:226
  60.8 8.7 %collective-permute-start.5 = (bf16[528,256]{1,0:T(8,128)(2,1)S(1)}, bf16[528,256]{1,0:T(8,128)(2,1)S(1)}, u32[]{:S(2)}, u32[]{:S(2)}) collective-permute-start(bf16[528,256]{1,0:T(8,128)(2,1)S(1)} %get-tuple-element.6), channel_id=1, source_target_pairs={{1,0},{2,1},{3,2},{4,3},{5,4},{6,5},{7,6},{8,7},{9,8},{10,9},{11,1... | collective-permute-start | bytes 811016 | tf_op jit(solution)/shard_map/ppermute | solution.py:227

commit v11 on v8

--- a/solution.py
+++ b/solution.py
@@ -74,7 +74,7 @@
 
 
 def correlate_kernel(blk_ref, blocks_ref, table_ref, ref_ref, out_ref, arranged, products):
-    chunk = 8
+    chunk = 16
     slots = table_ref.shape[0] // blocks_ref.shape[2]
     width = blocks_ref.shape[2]
     channels = blocks_ref.shape[1]
@@ -111,13 +111,13 @@
             ).astype(out_ref.dtype)
         return carry
 
-    lax.fori_loop(0, units // chunk, step, 0)
+    lax.fori_loop(0, units // chunk, step, 0, unroll=2)
 
 
 def correlate(blk, blocks, table, refs, units):
     channels, width = blocks.shape[1], blocks.shape[2]
     tpix = table.shape[1]
-    chunk = 8
+    chunk = 16
     return pl.pallas_call(
         correlate_kernel,
         out_shape=jax.ShapeDtypeStruct((units * GROUPS, tpix), jnp.bfloat16),

time: 69.9 us -> 69 us (0.987)
  Pallas kernels: 12.7 us -> 11.8 us
    pallas_call x1, Pallas kernels: 5.05 us -> 4.15 us  [correlate(): pl.pallas_call(correlate_kernel, out_shape=jax.ShapeDtypeStruct((units *...]
where the time goes in v11:
time: 69 us; the launch traced here: 68.3 us
  waiting for transfers between devices  21.4 us (31%)
  starting transfers between devices  17.3 us (25%)
  Pallas kernels  11.8 us (17%)
  other arithmetic  10 us (14%)
  local copies, waits for them, and re-layouts  6.15 us (9%)
  matrix products  1.23 us (2%)
    all_to_all x1, waiting for transfers between devices, body(): lax.all_to_all(payload.reshape(owners, cap, GROUPS * tpix + 128), 'view',...  11.8 us
    pallas_call x2, Pallas kernels, conv_rows(): pl.pallas_call(functools.partial(conv_kernel, relu=relu, rows=rows, cols=...  7.67 us
    ppermute x4, starting transfers between devices, gather_view(): lax.ppermute(gathered, 'view', [(i, i ^ stride) for i in range(count)])  6.15 us
    all_to_all x1, starting transfers between devices, body(): lax.all_to_all(payload.reshape(owners, cap, GROUPS * tpix + 128), 'view',...  5.66 us
    ppermute x4, waiting for transfers between devices, gather_view(): lax.ppermute(gathered, 'view', [(i, i ^ stride) for i in range(count)])  4.83 us
    ppermute x1, waiting for transfers between devices, halo_cols(): high = lax.ppermute(block[:, :cols], 'view', backward)  4.77 us
    pallas_call x1, Pallas kernels, correlate(): pl.pallas_call(correlate_kernel, out_shape=jax.ShapeDtypeStruct((units *...  4.15 us
    ppermute x1, starting transfers between devices, halo_cols(): low = lax.ppermute(block[:, block.shape[1] - cols:], 'view', forward)  3.62 us
  transfers between devices with their start and end apart: 7, of which 4 were waited for; matrix products, arithmetic and copies ran while one was open for 16% of the time, Pallas kernels for 0%

profile of v11, /device:TPU:13, one launch (start us, length us, event | category | flops | bytes accessed | tf_op | source)
XLA Modules:
  0.0 68.3 jit_solution(9191312899733787821)
XLA Ops:
  0.0 2.3 %collective-permute-start = (bf16[32,512]{1,0:T(8,128)(2,1)}, bf16[32,512]{1,0:T(8,128)(2,1)S(1)}, u32[]{:S(2)}, u32[]{:S(2)}) collective-permute-start(bf16[32,512]{1,0:T(8,128)(2,1)} %bitcast.68), channel_id=1, source_target_pairs={{0,8},{1,9},{2,10},{3,11},{4,12},{5,13},{6,14},{7,15},{8,0},{9,1},... | collective-permute-start | bytes 98312 | tf_op jit(solution)/shard_map/ppermute | solution.py:242
  3.0 0.7 %select_reduce_fusion.1 = s32[64,4]{0,1:T(4,128)S(1)} fusion(s32[64,4]{0,1:T(4,128)} %bitcast.78, s32[64,4]{0,1:T(4,128)} %bitcast.76), kind=kLoop, calls=%fused_computation.38 | loop fusion | flops 2816 | bytes 3072 | tf_op jit(solution)/shard_map/reduce_sum | solution.py:279
  5.3 0.8 %maximum_select_fusion.6 = bf16[2,32,512]{2,1,0:T(8,128)(2,1)S(1)} fusion(bf16[1,32,512]{2,1,0:T(8,128)(2,1)S(1)} %bitcast.71, bf16[1,32,512]{2,1,0:T(8,128)(2,1)} %param.10, pred[]{:T(512)S(6)} %eq.141), kind=kLoop, calls=%fused_computation.20 | loop fusion | flops 98304 | bytes 131073 | tf_op jit(solution)/shard_map/jit(_where)/select_n | solution.py:244
  6.4 0.8 %maximum_select_fusion.5 = bf16[2,1,32,512]{3,2,0,1:T(8,128)(2,1)S(1)} fusion(bf16[1,1,32,512]{3,2,0,1:T(8,128)(2,1)S(1)} %bitcast.72, bf16[1,1,32,512]{3,2,0,1:T(8,128)(2,1)} %bitcast.69, pred[]{:T(512)S(6)} %eq.141), kind=kLoop, calls=%fused_computation.19 | loop fusion | flops 98304 | bytes 131073 | tf_op jit(solution)/shard_map/jit(_where)/select_n | solution.py:244
  7.2 2.1 %collective-permute-done.1 = bf16[2,32,512]{2,1,0:T(8,128)(2,1)S(1)} collective-permute-done((bf16[2,32,512]{2,1,0:T(8,128)(2,1)S(1)}, bf16[2,32,512]{2,1,0:T(8,128)(2,1)S(1)}, u32[]{:S(2)}, u32[]{:S(2)}) %collective-permute-start.1) | collective-permute-done | bytes 65568 | tf_op jit(solution)/shard_map/ppermute | solution.py:242
  9.7 0.8 %fusion.34 = bf16[2,1,1,32,512]{4,3,0,1,2:T(8,128)(2,1)S(1)} fusion(bf16[1,1,32,512]{3,2,0,1:T(8,128)(2,1)} %bitcast.70, bf16[1,1,32,512]{3,2,0,1:T(8,128)(2,1)S(1)} %bitcast.73, pred[]{:T(512)S(6)} %eq.141), kind=kLoop, calls=%fused_computation.77 | loop fusion | flops 98304 | bytes 131073 | tf_op jit(solution)/shard_map/stack | solution.py:245
  10.5 2.7 %collective-permute-done.2 = bf16[2,2,32,512]{3,2,0,1:T(8,128)(2,1)S(1)} collective-permute-done((bf16[2,2,32,512]{3,2,0,1:T(8,128)(2,1)S(1)}, bf16[2,2,32,512]{3,2,0,1:T(8,128)(2,1)S(1)}, u32[]{:S(2)}, u32[]{:S(2)}) %collective-permute-start.2) | collective-permute-done | bytes 131104 | tf_op jit(solution)/shard_map/ppermute | solution.py:242
  13.3 3.3 %collective-permute-start.3 = (bf16[2,2,2,32,512]{4,3,0,1,2:T(8,128)(2,1)S(1)}, bf16[2,2,2,32,512]{4,3,0,1,2:T(8,128)(2,1)S(1)}, u32[]{:S(2)}, u32[]{:S(2)}) collective-permute-start(bf16[2,2,2,32,512]{4,3,0,1,2:T(8,128)(2,1)S(1)} %maximum_select_fusion.2), channel_id=1, source_target_pairs={{0,1},{1,0},{2,3},{3,2},{4,5},{5,4},{6,7},{7,6},{8,9},{9,8},{10,11... | collective-permute-start | bytes 786440 | tf_op jit(solution)/shard_map/ppermute | solution.py:242
  17.9 0.8 %concatenate.90.blocks_ref = bf16[65,32,128]{2,1,0:T(8,128)(2,1)} pad(bf16[64,32,128]{2,1,0:T(8,128)(2,1)S(1)} %bitcast.58, bf16[]{:T(256)} %constant.140.clone.1), padding=0_1x0_0x0_0 | pad | bytes 1056770 | tf_op jit(solution)/shard_map/concatenate | solution.py:276
  18.9 0.9 %copy.38 = bf16[2,2,2,2,32,512]{5,4,3,2,1,0:T(8,128)(2,1)} copy(bf16[2,2,2,2,32,512]{5,4,0,1,2,3:T(8,128)(2,1)S(1)} %maximum_select_fusion) | data formatting | bytes 1048576 | tf_op jit(solution)/shard_map/jit(_where)/select_n | solution.py:244
  19.8 4.1 %shard_map.91 = bf16[512,512]{1,0:T(8,128)(2,1)} custom-call(s32[256]{0:T(256)} %select_n.210.blk_ref, bf16[65,32,128]{2,1,0:T(8,128)(2,1)} %concatenate.90.blocks_ref, bf16[512,512]{1,0:T(8,128)(2,1)} %bitcast.67, bf16[16,32,512]{2,1,0:T(8,128)(2,1)} %bitcast.60), custom_call_target="tpu_custom_call" | custom-call | tf_op jit(solution)/shard_map/pallas_call | solution.py:121
  23.9 1.4 %concatenate.91 = bf16[16,4,4096]{2,1,0:T(4,128)(2,1)S(1)} reshape(bf16[512,512]{1,0:T(8,128)(2,1)} %shard_map.91) | data formatting | bytes 1048576 | tf_op jit(solution)/shard_map/concatenate | solution.py:289
  25.4 1.0 %pad_maximum_fusion.1 = bf16[16,4,4224]{2,1,0:T(4,128)(2,1)} fusion(bf16[16,4,128]{2,1,0:T(4,128)(2,1)S(1)} %broadcast_in_dim.86, bf16[16,4,4096]{2,1,0:T(4,128)(2,1)S(1)} %concatenate.91), kind=kLoop, calls=%fused_computation.9 | loop fusion | flops 1081344 | bytes 1081344 | tf_op jit(solution)/shard_map/concatenate | solution.py:289
  26.5 5.7 %all-to-all-start = ((bf16[16,4,4224]{2,1,0:T(4,128)(2,1)}), bf16[16,4,4224]{2,1,0:T(4,128)(2,1)S(1)}, u32[]{:S(2)}, u32[]{:S(2)}) async-start(bf16[16,4,4224]{2,1,0:T(4,128)(2,1)} %pad_maximum_fusion.1), calls=%async_computation | async-start | bytes 1081344 | tf_op jit(solution)/shard_map/all_to_all | solution.py:290
  32.2 0.7 %fusion.1 = bf16[9,128,144]{1,2,0:T(8,128)(2,1)S(1)} fusion(bf16[3,9,8,8]{3,2,1,0:T(8,128)(2,1)S(1)} %bitcast.55, pred[3,128,144]{1,2,0:T(8,128)(4,1)S(1)} %broadcast_compare_fusion.1, s32[144]{0:T(256)S(1)} %and_select_fusion.1, s32[128]{0:T(128)S(1)} %and_select_fusion), kind=kOutput, calls=%fused_computation.4 | convolution fusion | flops 9323008 | bytes 391616 | tf_op jit(solution)/shard_map/ro,xyoc->xyrc/dot_general | solution.py:188
  32.9 1.1 %copy.40 = bf16[9,128,144]{2,1,0:T(8,128)(2,1)} copy(bf16[9,128,144]{1,2,0:T(8,128)(2,1)S(1)} %fusion.1) | data formatting | bytes 663552 | tf_op jit(solution)/shard_map/convert_element_type | solution.py:199
  34.3 11.8 %all-to-all-done = bf16[16,4,4224]{2,1,0:T(4,128)(2,1)S(1)} async-done(((bf16[16,4,4224]{2,1,0:T(4,128)(2,1)}), bf16[16,4,4224]{2,1,0:T(4,128)(2,1)S(1)}, u32[]{:S(2)}, u32[]{:S(2)}) %all-to-all-start) | async-done | bytes 540704 | tf_op jit(solution)/shard_map/all_to_all | solution.py:290
  47.2 3.6 %collective-permute-start.4 = (bf16[528,256]{1,0:T(8,128)(2,1)S(1)}, bf16[528,256]{1,0:T(8,128)(2,1)S(1)}, u32[]{:S(2)}, u32[]{:S(2)}) collective-permute-start(bf16[528,256]{1,0:T(8,128)(2,1)S(1)} %get-tuple-element.5), channel_id=1, source_target_pairs={{0,1},{1,2},{2,3},{3,4},{4,5},{5,6},{6,7},{7,8},{8,9},{9,10},{10,1... | collective-permute-start | bytes 811016 | tf_op jit(solution)/shard_map/ppermute | solution.py:226
  50.8 1.9 %collective-permute-start.5 = (bf16[528,256]{1,0:T(8,128)(2,1)S(1)}, bf16[528,256]{1,0:T(8,128)(2,1)S(1)}, u32[]{:S(2)}, u32[]{:S(2)}) collective-permute-start(bf16[528,256]{1,0:T(8,128)(2,1)S(1)} %get-tuple-element.6), channel_id=1, source_target_pairs={{1,0},{2,1},{3,2},{4,3},{5,4},{6,5},{7,6},{8,7},{9,8},{10,9},{11,1... | collective-permute-start | bytes 811016 | tf_op jit(solution)/shard_map/ppermute | solution.py:227
  53.3 1.3 %select_reduce_fusion = bf16[9,64,528]{2,1,0:T(8,128)(2,1)} fusion(f32[3,9,528]{2,1,0:T(8,128)S(1)} %convolution_bitcast_fusion, pred[3,64,528]{2,1,0:T(8,128)(4,1)S(1)} %broadcast_compare_fusion), kind=kLoop, calls=%fused_computation.2 | loop fusion | flops 1520640 | bytes 766656 | tf_op jit(solution)/shard_map/reduce_sum | solution.py:198
  54.7 4.8 %collective-permute-done.5 = bf16[528,256]{1,0:T(8,128)(2,1)S(1)} collective-permute-done((bf16[528,256]{1,0:T(8,128)(2,1)S(1)}, bf16[528,256]{1,0:T(8,128)(2,1)S(1)}, u32[]{:S(2)}, u32[]{:S(2)}) %collective-permute-start.5) | collective-permute-done | bytes 270368 | tf_op jit(solution)/shard_map/ppermute | solution.py:227
  59.5 1.1 %pad_maximum_fusion.refs_1_ = bf16[528,1024]{1,0:T(8,128)(2,1)} fusion(bf16[528,256]{1,0:T(8,128)(2,1)S(1)} %collective-permute-done.5, bf16[528,512]{1,0:T(8,128)(2,1)S(1)} %pad.5, bf16[528,256]{1,0:T(8,128)(2,1)S(1)} %collective-permute-done.4), kind=kLoop, calls=%fused_computation.8 | loop fusion | flops 3244032 | bytes 2162688 | tf_op jit(solution)/shard_map/concatenate | solution.py:228
  60.6 4.4 %shard_map.92.refs_0_ = bf16[528,768]{1,0:T(8,128)(2,1)} custom-call(s32[2]{0:T(128)} %add_convert_fusion.refs_0_, bf16[528,1024]{1,0:T(8,128)(2,1)} %pad_maximum_fusion.refs_1_, bf16[3,3,128,144]{3,2,1,0:T(8,128)(2,1)} %bitcast.57), custom_call_target="tpu_custom_call" | custom-call | tf_op jit(solution)/shard_map/pallas_call | solution.py:214
  65.1 3.2 %shard_map.93 = f32[4,64,128]{2,1,0:T(8,128)} custom-call(bf16[528,768]{1,0:T(8,128)(2,1)} %shard_map.92.refs_0_, bf16[3,3,64,528]{3,2,1,0:T(8,128)(2,1)} %bitcast.56), custom_call_target="tpu_custom_call" | custom-call | tf_op jit(solution)/shard_map/pallas_call | solution.py:214
  (49 shorter events, 6.2 us)
Async XLA Ops:
  0.0 32.1 %copy-start = (bf16[3,3,3,8,8]{4,3,2,1,0:T(8,128)(2,1)S(1)}, bf16[3,3,3,8,8]{4,3,2,1,0:T(8,128)(2,1)}, u32[]{:S(2)}) copy-start(bf16[3,3,3,8,8]{4,3,2,1,0:T(8,128)(2,1)} %param.16) | copy-start | bytes 10372
  0.0 17.4 %copy-start.1 = (bf16[1,32,8192]{2,1,0:T(8,128)(2,1)S(1)}, bf16[1,32,8192]{2,1,0:T(8,128)(2,1)}, u32[]{:S(2)}) copy-start(bf16[1,32,8192]{2,1,0:T(8,128)(2,1)} %param.9) | copy-start | bytes 1572868
  0.0 5.3 %collective-permute-start = (bf16[32,512]{1,0:T(8,128)(2,1)}, bf16[32,512]{1,0:T(8,128)(2,1)S(1)}, u32[]{:S(2)}, u32[]{:S(2)}) collective-permute-start(bf16[32,512]{1,0:T(8,128)(2,1)} %bitcast.68), channel_id=1, source_target_pairs={{0,8},{1,9},{2,10},{3,11},{4,12},{5,13},{6,14},{7,15},{8,0},{9,1},... | collective-permute-start | bytes 98312 | tf_op jit(solution)/shard_map/ppermute | solution.py:242
  6.2 3.2 %collective-permute-start.1 = (bf16[2,32,512]{2,1,0:T(8,128)(2,1)S(1)}, bf16[2,32,512]{2,1,0:T(8,128)(2,1)S(1)}, u32[]{:S(2)}, u32[]{:S(2)}) collective-permute-start(bf16[2,32,512]{2,1,0:T(8,128)(2,1)S(1)} %maximum_select_fusion.6), channel_id=1, source_target_pairs={{0,4},{1,5},{2,6},{3,7},{4,0},{5,1},{6,2},{7,3},{8,12},{9,13},{10,... | collective-permute-start | bytes 196616 | tf_op jit(solution)/shard_map/ppermute | solution.py:242
  9.4 3.9 %collective-permute-start.2 = (bf16[2,2,32,512]{3,2,0,1:T(8,128)(2,1)S(1)}, bf16[2,2,32,512]{3,2,0,1:T(8,128)(2,1)S(1)}, u32[]{:S(2)}, u32[]{:S(2)}) collective-permute-start(bf16[2,2,32,512]{3,2,0,1:T(8,128)(2,1)S(1)} %maximum_select_fusion.4), channel_id=1, source_target_pairs={{0,2},{1,3},{2,0},{3,1},{4,6},{5,7},{6,4},{7,5},{8,10},{9,11},{10,... | collective-permute-start | bytes 393224 | tf_op jit(solution)/shard_map/ppermute | solution.py:242
  13.3 5.5 %collective-permute-start.3 = (bf16[2,2,2,32,512]{4,3,0,1,2:T(8,128)(2,1)S(1)}, bf16[2,2,2,32,512]{4,3,0,1,2:T(8,128)(2,1)S(1)}, u32[]{:S(2)}, u32[]{:S(2)}) collective-permute-start(bf16[2,2,2,32,512]{4,3,0,1,2:T(8,128)(2,1)S(1)} %maximum_select_fusion.2), channel_id=1, source_target_pairs={{0,1},{1,0},{2,3},{3,2},{4,5},{5,4},{6,7},{7,6},{8,9},{9,8},{10,11... | collective-permute-start | bytes 786440 | tf_op jit(solution)/shard_map/ppermute | solution.py:242
  26.5 19.6 %all-to-all-start = ((bf16[16,4,4224]{2,1,0:T(4,128)(2,1)}), bf16[16,4,4224]{2,1,0:T(4,128)(2,1)S(1)}, u32[]{:S(2)}, u32[]{:S(2)}) async-start(bf16[16,4,4224]{2,1,0:T(4,128)(2,1)} %pad_maximum_fusion.1), calls=%async_computation | async-start | bytes 1081344 | tf_op jit(solution)/shard_map/all_to_all | solution.py:290
  32.1 1.9 %copy-start.2 = (bf16[3,3,3,8]{3,2,1,0:T(4,128)(2,1)S(1)}, bf16[3,3,3,8]{3,2,1,0:T(4,128)(2,1)}, u32[]{:S(2)}) copy-start(bf16[3,3,3,8]{3,2,1,0:T(4,128)(2,1)} %param.17) | copy-start | bytes 1300
  47.2 7.5 %collective-permute-start.4 = (bf16[528,256]{1,0:T(8,128)(2,1)S(1)}, bf16[528,256]{1,0:T(8,128)(2,1)S(1)}, u32[]{:S(2)}, u32[]{:S(2)}) collective-permute-start(bf16[528,256]{1,0:T(8,128)(2,1)S(1)} %get-tuple-element.5), channel_id=1, source_target_pairs={{0,1},{1,2},{2,3},{3,4},{4,5},{5,6},{6,7},{7,8},{8,9},{9,10},{10,1... | collective-permute-start | bytes 811016 | tf_op jit(solution)/shard_map/ppermute | solution.py:226
  50.8 8.7 %collective-permute-start.5 = (bf16[528,256]{1,0:T(8,128)(2,1)S(1)}, bf16[528,256]{1,0:T(8,128)(2,1)S(1)}, u32[]{:S(2)}, u32[]{:S(2)}) collective-permute-start(bf16[528,256]{1,0:T(8,128)(2,1)S(1)} %get-tuple-element.6), channel_id=1, source_target_pairs={{1,0},{2,1},{3,2},{4,3},{5,4},{6,5},{7,6},{8,7},{9,8},{10,9},{11,1... | collective-permute-start | bytes 811016 | tf_op jit(solution)/shard_map/ppermute | solution.py:227

commit v12 on v11

--- a/solution.py
+++ b/solution.py
@@ -238,6 +238,16 @@
     gathered = block[0]
     level = 0
     stride = count // 2
+    if count >= 4:
+        top = count // 4
+        parts = [gathered] + [
+            lax.ppermute(gathered, "view", [(i, i ^ (m * top)) for i in range(count)])
+            for m in (1, 2, 3)
+        ]
+        order = jnp.arange(4) ^ ((index // top) % 4)
+        gathered = jnp.take(jnp.stack(parts), order, axis=0).reshape((2, 2) + gathered.shape)
+        level = 2
+        stride = top // 2
     while stride >= 1:
         other = lax.ppermute(gathered, "view", [(i, i ^ stride) for i in range(count)])
         low = (index // stride) % 2 == 0

time: 69 us -> 68.9 us (level)
  other arithmetic: 10 us -> 8.57 us
  starting transfers between devices: 17.3 us -> 18.4 us
  local copies, waits for them, and re-layouts: 6.15 us -> 6.89 us
    ppermute x0 -> x3, starting transfers between devices: none -> 3.49 us  [gather_view(): lax.ppermute(gathered, 'view', [(i, i ^ m * top) for i in range(count)])]
    ppermute x4 -> x2, starting transfers between devices: 6.15 us -> 2.74 us  [gather_view(): lax.ppermute(gathered, 'view', [(i, i ^ stride) for i in range(count)])]
    unnamed x8, local copies, waits for them, and re-layouts: 0.13 us -> 1.18 us
    all_to_all x1, starting transfers between devices: 5.66 us -> 6.62 us  [body(): lax.all_to_all(payload.reshape(owners, cap, GROUPS * tpix + 128), 'view',...]
    select_n x7 -> x3, other arithmetic: 1.86 us -> 0.91 us  [gather_view(): jnp.where(low, jnp.stack([gathered, other], axis=level), jnp.stack([other...]
    select_n x1 -> x0, local copies, waits for them, and re-layouts: 0.86 us -> none  [gather_view(): jnp.where(low, jnp.stack([gathered, other], axis=level), jnp.stack([other...]
    another operation x2, other arithmetic: 0.86 us -> 0.12 us  [gather_view(): jnp.stack([gathered, other], axis=level)]
    ppermute x4 -> x2, waiting for transfers between devices: 4.83 us -> 4.59 us  [gather_view(): lax.ppermute(gathered, 'view', [(i, i ^ stride) for i in range(count)])]
  transfers between devices with their start and end apart: 7 -> 8, of which waited for: 4 -> 4; matrix products, arithmetic and copies ran while one was open for 16% -> 15% of each run, Pallas kernels for 0% -> 0%
where the time goes in v12:
time: 68.9 us; the launch traced here: 68.4 us
  waiting for transfers between devices  21.2 us (31%)
  starting transfers between devices  18.4 us (27%)
  Pallas kernels  11.8 us (17%)
  other arithmetic  8.57 us (12%)
  local copies, waits for them, and re-layouts  6.89 us (10%)
  matrix products  1.23 us (2%)
    all_to_all x1, waiting for transfers between devices, body(): lax.all_to_all(payload.reshape(owners, cap, GROUPS * tpix + 128), 'view',...  11.8 us
    pallas_call x2, Pallas kernels, conv_rows(): pl.pallas_call(functools.partial(conv_kernel, relu=relu, rows=rows, cols=...  7.67 us
    all_to_all x1, starting transfers between devices, body(): lax.all_to_all(payload.reshape(owners, cap, GROUPS * tpix + 128), 'view',...  6.62 us
    ppermute x1, waiting for transfers between devices, halo_cols(): high = lax.ppermute(block[:, :cols], 'view', backward)  4.77 us
    ppermute x2, waiting for transfers between devices, gather_view(): lax.ppermute(gathered, 'view', [(i, i ^ stride) for i in range(count)])  4.59 us
    pallas_call x1, Pallas kernels, correlate(): pl.pallas_call(correlate_kernel, out_shape=jax.ShapeDtypeStruct((units *...  4.13 us
    ppermute x1, starting transfers between devices, halo_cols(): low = lax.ppermute(block[:, block.shape[1] - cols:], 'view', forward)  3.62 us
    ppermute x3, starting transfers between devices, gather_view(): lax.ppermute(gathered, 'view', [(i, i ^ m * top) for i in range(count)])  3.49 us
  transfers between devices with their start and end apart: 8, of which 4 were waited for; matrix products, arithmetic and copies ran while one was open for 15% of the time, Pallas kernels for 0%

profile of v12, /device:TPU:13, one launch (start us, length us, event | category | flops | bytes accessed | tf_op | source)
XLA Modules:
  0.0 68.4 jit_solution(8835122778604355519)
XLA Ops:
  0.0 1.3 %collective-permute-start.2 = (bf16[32,512]{1,0:T(8,128)(2,1)}, bf16[32,512]{1,0:T(8,128)(2,1)S(1)}, u32[]{:S(2)}, u32[]{:S(2)}) collective-permute-start(bf16[32,512]{1,0:T(8,128)(2,1)} %bitcast.72), channel_id=1, source_target_pairs={{0,12},{1,13},{2,14},{3,15},{4,8},{5,9},{6,10},{7,11},{8,4},{9,5},... | collective-permute-start | bytes 98312 | tf_op jit(solution)/shard_map/ppermute | solution.py:244
  1.3 2.2 %collective-permute-start = (bf16[32,512]{1,0:T(8,128)(2,1)}, bf16[32,512]{1,0:T(8,128)(2,1)S(1)}, u32[]{:S(2)}, u32[]{:S(2)}) collective-permute-start(bf16[32,512]{1,0:T(8,128)(2,1)} %bitcast.73), channel_id=1, source_target_pairs={{0,4},{1,5},{2,6},{3,7},{4,0},{5,1},{6,2},{7,3},{8,12},{9,13},{10,... | collective-permute-start | bytes 98312 | tf_op jit(solution)/shard_map/ppermute | solution.py:244
  4.2 0.7 %select_reduce_fusion.1 = s32[64,4]{0,1:T(4,128)S(1)} fusion(s32[64,4]{0,1:T(4,128)} %bitcast.80, s32[64,4]{0,1:T(4,128)} %bitcast.78), kind=kLoop, calls=%fused_computation.40 | loop fusion | flops 2816 | bytes 3072 | tf_op jit(solution)/shard_map/reduce_sum | solution.py:289
  4.9 0.7 %fusion.16 = pred[64,4]{0,1:T(4,128)(4,1)S(1)} fusion(s32[64,4]{0,1:T(4,128)} %bitcast.79, pred[64,4]{0,1:T(4,128)(4,1)S(1)} %iota_compare_fusion.4), kind=kLoop, calls=%fused_computation.44 | loop fusion | flops 2816 | bytes 1536 | tf_op jit(solution)/shard_map/reduce_or | solution.py:290
  7.3 1.2 %copy.56 = bf16[4,8,64,128]{3,2,1,0:T(8,128)(2,1)S(1)} copy(bf16[4,8,64,128]{3,1,2,0:T(8,128)(2,1)} %bitcast.66) | data formatting | bytes 1048576
  8.9 0.8 %concatenate.26.blocks_ref = bf16[65,32,128]{2,1,0:T(8,128)(2,1)} pad(bf16[64,32,128]{2,1,0:T(8,128)(2,1)S(1)} %bitcast.60, bf16[]{:T(256)} %constant.145.clone.1), padding=0_1x0_0x0_0 | pad | bytes 1056770 | tf_op jit(solution)/shard_map/concatenate | solution.py:286
  10.9 3.5 %collective-permute-done.3 = bf16[2,2,32,512]{3,2,1,0:T(8,128)(2,1)S(1)} collective-permute-done((bf16[2,2,32,512]{3,2,1,0:T(8,128)(2,1)S(1)}, bf16[2,2,32,512]{3,2,1,0:T(8,128)(2,1)S(1)}, u32[]{:S(2)}, u32[]{:S(2)}) %collective-permute-start.3) | collective-permute-done | bytes 131104 | tf_op jit(solution)/shard_map/ppermute | solution.py:252
  14.4 2.5 %collective-permute-start.4 = (bf16[2,2,2,32,512]{4,3,2,1,0:T(8,128)(2,1)S(1)}, bf16[2,2,2,32,512]{4,3,2,1,0:T(8,128)(2,1)S(1)}, u32[]{:S(2)}, u32[]{:S(2)}) collective-permute-start(bf16[2,2,2,32,512]{4,3,2,1,0:T(8,128)(2,1)S(1)} %maximum_select_fusion.1), channel_id=1, source_target_pairs={{0,1},{1,0},{2,3},{3,2},{4,5},{5,4},{6,7},{7,6},{8,9},{9,8},{10,11... | collective-permute-start | bytes 786440 | tf_op jit(solution)/shard_map/ppermute | solution.py:252
  16.9 1.1 %collective-permute-done.4 = bf16[2,2,2,32,512]{4,3,2,1,0:T(8,128)(2,1)S(1)} collective-permute-done((bf16[2,2,2,32,512]{4,3,2,1,0:T(8,128)(2,1)S(1)}, bf16[2,2,2,32,512]{4,3,2,1,0:T(8,128)(2,1)S(1)}, u32[]{:S(2)}, u32[]{:S(2)}) %collective-permute-start.4) | collective-permute-done | bytes 262176 | tf_op jit(solution)/shard_map/ppermute | solution.py:252
  18.0 0.9 %maximum_select_fusion = bf16[2,2,2,2,32,512]{5,4,3,2,1,0:T(8,128)(2,1)} fusion(bf16[2,2,2,1,32,512]{5,4,3,2,1,0:T(8,128)(2,1)S(1)} %bitcast.70, bf16[2,2,2,1,32,512]{5,4,3,2,1,0:T(8,128)(2,1)S(1)} %copy_select_fusion, pred[]{:T(512)S(6)} %eq.131), kind=kLoop, calls=%fused_computation.12 | loop fusion | flops 786432 | bytes 1048577 | tf_op jit(solution)/shard_map/jit(_where)/select_n | solution.py:254
  18.9 4.1 %shard_map.91 = bf16[512,512]{1,0:T(8,128)(2,1)} custom-call(s32[256]{0:T(256)} %select_n.187.blk_ref, bf16[65,32,128]{2,1,0:T(8,128)(2,1)} %concatenate.26.blocks_ref, bf16[512,512]{1,0:T(8,128)(2,1)} %bitcast.69, bf16[16,32,512]{2,1,0:T(8,128)(2,1)} %bitcast.65), custom_call_target="tpu_custom_call" | custom-call | tf_op jit(solution)/shard_map/pallas_call | solution.py:121
  23.0 1.4 %concatenate.27 = bf16[16,4,4096]{2,1,0:T(4,128)(2,1)S(1)} reshape(bf16[512,512]{1,0:T(8,128)(2,1)} %shard_map.91) | data formatting | bytes 1048576 | tf_op jit(solution)/shard_map/concatenate | solution.py:299
  24.5 1.0 %pad_maximum_fusion.1 = bf16[16,4,4224]{2,1,0:T(4,128)(2,1)} fusion(bf16[16,4,128]{2,1,0:T(4,128)(2,1)S(1)} %broadcast_in_dim.104, bf16[16,4,4096]{2,1,0:T(4,128)(2,1)S(1)} %concatenate.27), kind=kLoop, calls=%fused_computation.10 | loop fusion | flops 1081344 | bytes 1081344 | tf_op jit(solution)/shard_map/concatenate | solution.py:299
  25.6 6.6 %all-to-all-start = ((bf16[16,4,4224]{2,1,0:T(4,128)(2,1)}), bf16[16,4,4224]{2,1,0:T(4,128)(2,1)S(1)}, u32[]{:S(2)}, u32[]{:S(2)}) async-start(bf16[16,4,4224]{2,1,0:T(4,128)(2,1)} %pad_maximum_fusion.1), calls=%async_computation | async-start | bytes 1081344 | tf_op jit(solution)/shard_map/all_to_all | solution.py:300
  32.2 0.7 %fusion.1 = bf16[9,128,144]{1,2,0:T(8,128)(2,1)S(1)} fusion(bf16[3,9,8,8]{3,2,1,0:T(8,128)(2,1)S(1)} %bitcast.57, pred[3,128,144]{1,2,0:T(8,128)(4,1)S(1)} %broadcast_compare_fusion.1, s32[144]{0:T(256)S(1)} %and_select_fusion.1, s32[128]{0:T(128)S(1)} %and_select_fusion), kind=kOutput, calls=%fused_computation.5 | convolution fusion | flops 9323008 | bytes 391616 | tf_op jit(solution)/shard_map/ro,xyoc->xyrc/dot_general | solution.py:188
  33.0 1.1 %copy.50 = bf16[9,128,144]{2,1,0:T(8,128)(2,1)} copy(bf16[9,128,144]{1,2,0:T(8,128)(2,1)S(1)} %fusion.1) | data formatting | bytes 663552 | tf_op jit(solution)/shard_map/convert_element_type | solution.py:199
  34.4 11.8 %all-to-all-done = bf16[16,4,4224]{2,1,0:T(4,128)(2,1)S(1)} async-done(((bf16[16,4,4224]{2,1,0:T(4,128)(2,1)}), bf16[16,4,4224]{2,1,0:T(4,128)(2,1)S(1)}, u32[]{:S(2)}, u32[]{:S(2)}) %all-to-all-start) | async-done | bytes 540704 | tf_op jit(solution)/shard_map/all_to_all | solution.py:300
  47.3 3.6 %collective-permute-start.5 = (bf16[528,256]{1,0:T(8,128)(2,1)S(1)}, bf16[528,256]{1,0:T(8,128)(2,1)S(1)}, u32[]{:S(2)}, u32[]{:S(2)}) collective-permute-start(bf16[528,256]{1,0:T(8,128)(2,1)S(1)} %get-tuple-element.5), channel_id=1, source_target_pairs={{0,1},{1,2},{2,3},{3,4},{4,5},{5,6},{6,7},{7,8},{8,9},{9,10},{10,1... | collective-permute-start | bytes 811016 | tf_op jit(solution)/shard_map/ppermute | solution.py:226
  50.9 1.9 %collective-permute-start.6 = (bf16[528,256]{1,0:T(8,128)(2,1)S(1)}, bf16[528,256]{1,0:T(8,128)(2,1)S(1)}, u32[]{:S(2)}, u32[]{:S(2)}) collective-permute-start(bf16[528,256]{1,0:T(8,128)(2,1)S(1)} %get-tuple-element.6), channel_id=1, source_target_pairs={{1,0},{2,1},{3,2},{4,3},{5,4},{6,5},{7,6},{8,7},{9,8},{10,9},{11,1... | collective-permute-start | bytes 811016 | tf_op jit(solution)/shard_map/ppermute | solution.py:227
  53.4 1.3 %select_reduce_fusion = bf16[9,64,528]{2,1,0:T(8,128)(2,1)} fusion(f32[3,9,528]{2,1,0:T(8,128)S(1)} %convolution_bitcast_fusion, pred[3,64,528]{2,1,0:T(8,128)(4,1)S(1)} %broadcast_compare_fusion), kind=kLoop, calls=%fused_computation.3 | loop fusion | flops 1520640 | bytes 766656 | tf_op jit(solution)/shard_map/reduce_sum | solution.py:198
  54.8 4.8 %collective-permute-done.6 = bf16[528,256]{1,0:T(8,128)(2,1)S(1)} collective-permute-done((bf16[528,256]{1,0:T(8,128)(2,1)S(1)}, bf16[528,256]{1,0:T(8,128)(2,1)S(1)}, u32[]{:S(2)}, u32[]{:S(2)}) %collective-permute-start.6) | collective-permute-done | bytes 270368 | tf_op jit(solution)/shard_map/ppermute | solution.py:227
  59.6 1.1 %pad_maximum_fusion.refs_1_ = bf16[528,1024]{1,0:T(8,128)(2,1)} fusion(bf16[528,256]{1,0:T(8,128)(2,1)S(1)} %collective-permute-done.6, bf16[528,512]{1,0:T(8,128)(2,1)S(1)} %pad.5, bf16[528,256]{1,0:T(8,128)(2,1)S(1)} %collective-permute-done.5), kind=kLoop, calls=%fused_computation.9 | loop fusion | flops 3244032 | bytes 2162688 | tf_op jit(solution)/shard_map/concatenate | solution.py:228
  60.7 4.4 %shard_map.92.refs_0_ = bf16[528,768]{1,0:T(8,128)(2,1)} custom-call(s32[2]{0:T(128)} %add_convert_fusion.refs_0_, bf16[528,1024]{1,0:T(8,128)(2,1)} %pad_maximum_fusion.refs_1_, bf16[3,3,128,144]{3,2,1,0:T(8,128)(2,1)} %bitcast.59), custom_call_target="tpu_custom_call" | custom-call | tf_op jit(solution)/shard_map/pallas_call | solution.py:214
  65.2 3.2 %shard_map.93 = f32[4,64,128]{2,1,0:T(8,128)} custom-call(bf16[528,768]{1,0:T(8,128)(2,1)} %shard_map.92.refs_0_, bf16[3,3,64,528]{3,2,1,0:T(8,128)(2,1)} %bitcast.58), custom_call_target="tpu_custom_call" | custom-call | tf_op jit(solution)/shard_map/pallas_call | solution.py:214
  (53 shorter events, 6.0 us)
Async XLA Ops:
  0.0 32.2 %copy-start = (bf16[3,3,3,8,8]{4,3,2,1,0:T(8,128)(2,1)S(1)}, bf16[3,3,3,8,8]{4,3,2,1,0:T(8,128)(2,1)}, u32[]{:S(2)}) copy-start(bf16[3,3,3,8,8]{4,3,2,1,0:T(8,128)(2,1)} %param.16) | copy-start | bytes 10372
  0.0 9.7 %collective-permute-start.2 = (bf16[32,512]{1,0:T(8,128)(2,1)}, bf16[32,512]{1,0:T(8,128)(2,1)S(1)}, u32[]{:S(2)}, u32[]{:S(2)}) collective-permute-start(bf16[32,512]{1,0:T(8,128)(2,1)} %bitcast.72), channel_id=1, source_target_pairs={{0,12},{1,13},{2,14},{3,15},{4,8},{5,9},{6,10},{7,11},{8,4},{9,5},... | collective-permute-start | bytes 98312 | tf_op jit(solution)/shard_map/ppermute | solution.py:244
  1.3 8.4 %collective-permute-start = (bf16[32,512]{1,0:T(8,128)(2,1)}, bf16[32,512]{1,0:T(8,128)(2,1)S(1)}, u32[]{:S(2)}, u32[]{:S(2)}) collective-permute-start(bf16[32,512]{1,0:T(8,128)(2,1)} %bitcast.73), channel_id=1, source_target_pairs={{0,4},{1,5},{2,6},{3,7},{4,0},{5,1},{6,2},{7,3},{8,12},{9,13},{10,... | collective-permute-start | bytes 98312 | tf_op jit(solution)/shard_map/ppermute | solution.py:244
  3.5 6.2 %collective-permute-start.1 = (bf16[32,512]{1,0:T(8,128)(2,1)}, bf16[32,512]{1,0:T(8,128)(2,1)S(1)}, u32[]{:S(2)}, u32[]{:S(2)}) collective-permute-start(bf16[32,512]{1,0:T(8,128)(2,1)} %bitcast.74), channel_id=1, source_target_pairs={{0,8},{1,9},{2,10},{3,11},{4,12},{5,13},{6,14},{7,15},{8,0},{9,1},... | collective-permute-start | bytes 98312 | tf_op jit(solution)/shard_map/ppermute | solution.py:244
  8.4 1.3 %copy-start.1 = (bf16[1,32,512]{2,1,0:T(8,128)(2,1)S(1)}, bf16[1,32,512]{2,1,0:T(8,128)(2,1)}, u32[]{:S(2)}) copy-start(bf16[1,32,512]{2,1,0:T(8,128)(2,1)} %param.10) | copy-start | bytes 98308
  10.5 3.9 %collective-permute-start.3 = (bf16[2,2,32,512]{3,2,1,0:T(8,128)(2,1)S(1)}, bf16[2,2,32,512]{3,2,1,0:T(8,128)(2,1)S(1)}, u32[]{:S(2)}, u32[]{:S(2)}) collective-permute-start(bf16[2,2,32,512]{3,2,1,0:T(8,128)(2,1)S(1)} %broadcast_select_fusion), channel_id=1, source_target_pairs={{0,2},{1,3},{2,0},{3,1},{4,6},{5,7},{6,4},{7,5},{8,10},{9,11},{10,... | collective-permute-start | bytes 393224 | tf_op jit(solution)/shard_map/ppermute | solution.py:252
  14.4 3.6 %collective-permute-start.4 = (bf16[2,2,2,32,512]{4,3,2,1,0:T(8,128)(2,1)S(1)}, bf16[2,2,2,32,512]{4,3,2,1,0:T(8,128)(2,1)S(1)}, u32[]{:S(2)}, u32[]{:S(2)}) collective-permute-start(bf16[2,2,2,32,512]{4,3,2,1,0:T(8,128)(2,1)S(1)} %maximum_select_fusion.1), channel_id=1, source_target_pairs={{0,1},{1,0},{2,3},{3,2},{4,5},{5,4},{6,7},{7,6},{8,9},{9,8},{10,11... | collective-permute-start | bytes 786440 | tf_op jit(solution)/shard_map/ppermute | solution.py:252
  25.6 20.6 %all-to-all-start = ((bf16[16,4,4224]{2,1,0:T(4,128)(2,1)}), bf16[16,4,4224]{2,1,0:T(4,128)(2,1)S(1)}, u32[]{:S(2)}, u32[]{:S(2)}) async-start(bf16[16,4,4224]{2,1,0:T(4,128)(2,1)} %pad_maximum_fusion.1), calls=%async_computation | async-start | bytes 1081344 | tf_op jit(solution)/shard_map/all_to_all | solution.py:300
  32.2 1.9 %copy-start.2 = (bf16[3,3,3,8]{3,2,1,0:T(4,128)(2,1)S(1)}, bf16[3,3,3,8]{3,2,1,0:T(4,128)(2,1)}, u32[]{:S(2)}) copy-start(bf16[3,3,3,8]{3,2,1,0:T(4,128)(2,1)} %param.17) | copy-start | bytes 1300
  47.3 7.5 %collective-permute-start.5 = (bf16[528,256]{1,0:T(8,128)(2,1)S(1)}, bf16[528,256]{1,0:T(8,128)(2,1)S(1)}, u32[]{:S(2)}, u32[]{:S(2)}) collective-permute-start(bf16[528,256]{1,0:T(8,128)(2,1)S(1)} %get-tuple-element.5), channel_id=1, source_target_pairs={{0,1},{1,2},{2,3},{3,4},{4,5},{5,6},{6,7},{7,8},{8,9},{9,10},{10,1... | collective-permute-start | bytes 811016 | tf_op jit(solution)/shard_map/ppermute | solution.py:226
  50.9 8.7 %collective-permute-start.6 = (bf16[528,256]{1,0:T(8,128)(2,1)S(1)}, bf16[528,256]{1,0:T(8,128)(2,1)S(1)}, u32[]{:S(2)}, u32[]{:S(2)}) collective-permute-start(bf16[528,256]{1,0:T(8,128)(2,1)S(1)} %get-tuple-element.6), channel_id=1, source_target_pairs={{1,0},{2,1},{3,2},{4,3},{5,4},{6,5},{7,6},{8,7},{9,8},{10,9},{11,1... | collective-permute-start | bytes 811016 | tf_op jit(solution)/shard_map/ppermute | solution.py:227

commit v13 on v12

--- a/solution.py
+++ b/solution.py
@@ -291,27 +291,27 @@
     blk = jnp.where(alive, picked, nblocks).reshape(-1).astype(jnp.int32)
     depth_code = jnp.where(counts > 0, depth_plane[0], -1).astype(jnp.bfloat16)
 
-    ref_all = gather_view(ref_feat)
+    tag_block = jnp.pad(depth_code, (0, channels * 128 - units)).reshape(channels, 128)
+    ref_all = gather_view(jnp.concatenate([ref_feat[0], tag_block], axis=1)[None])
     corr_all = correlate(
         blk, blocks, weight_table.reshape(slots * block_width, tpix), ref_all, units
-    ).reshape(units, GROUPS * tpix)
-    tag_lanes = jnp.broadcast_to(depth_code[:, None], (units, 128))
-    payload = jnp.concatenate([corr_all, tag_lanes], axis=1)
+    )
     arriving = lax.all_to_all(
-        payload.reshape(owners, cap, GROUPS * tpix + 128),
+        corr_all.reshape(owners, cap * GROUPS, tpix),
         "view",
         split_axis=0,
         concat_axis=0,
         tiled=True,
-    ).reshape(owners * cap, GROUPS * tpix + 128)
-    received = arriving[:, : GROUPS * tpix]
-    depth_tags = arriving[:, GROUPS * tpix]
+    ).reshape(owners * cap, GROUPS, tpix)
+    depth_tags = lax.dynamic_slice_in_dim(
+        ref_all[:, :, tpix:].reshape(owners, channels * 128), lax.axis_index("view") * cap, cap, axis=1
+    ).reshape(owners * cap)
     onehot = (
         depth_tags[None, :] == jnp.arange(DEPTH).astype(jnp.bfloat16)[:, None]
     ).astype(jnp.bfloat16)
-    summed = jnp.dot(onehot, received, preferred_element_type=jnp.float32)
+    summed = jnp.einsum("dn,ngp->dgp", onehot, arriving, preferred_element_type=jnp.float32)
     tallies = jnp.sum(onehot.astype(jnp.float32), axis=1)
-    cost_volume = (summed / jnp.maximum(tallies, 1.0)[:, None]).astype(jnp.bfloat16)
+    cost_volume = (summed / jnp.maximum(tallies, 1.0)[:, None, None]).astype(jnp.bfloat16)
     columns = tpix // TROWS
     volume = cost_volume.reshape(DEPTH * GROUPS, TROWS * columns)
     volume = jnp.pad(volume, ((GROUPS, GROUPS), (0, 0)))

time: 68.9 us -> 67.7 us (0.983)
  local copies, waits for them, and re-layouts: 6.89 us -> 5.26 us
    concatenate x1 -> x0, local copies, waits for them, and re-layouts: 1.43 us -> none  [body(): payload = jnp.concatenate([corr_all, tag_lanes], axis=1)]
    concatenate x1 -> x0, other arithmetic: 1.03 us -> none  [body(): payload = jnp.concatenate([corr_all, tag_lanes], axis=1)]
    unnamed x8 -> x9, local copies, waits for them, and re-layouts: 1.18 us -> 0.19 us
    ppermute x3, starting transfers between devices: 3.49 us -> 2.65 us  [gather_view(): lax.ppermute(gathered, 'view', [(i, i ^ m * top) for i in range(count)])]
    slice x1, local copies, waits for them, and re-layouts: 0.1 us -> 0.91 us  [body(): ref_all[:, :, tpix:].reshape(owners, channels * 128)]
    broadcast_in_dim x0 -> x1, other arithmetic: none -> 0.76 us  [body(): jnp.concatenate([ref_feat[0], tag_block], axis=1)[None]]
where the time goes in v13:
time: 67.7 us; the launch traced here: 67.2 us
  waiting for transfers between devices  21.7 us (32%)
  starting transfers between devices  18.4 us (27%)
  Pallas kernels  11.8 us (17%)
  other arithmetic  8.49 us (13%)
  local copies, waits for them, and re-layouts  5.26 us (8%)
  matrix products  1.24 us (2%)
    all_to_all x1, waiting for transfers between devices, body(): lax.all_to_all(corr_all.reshape(owners, cap * GROUPS, tpix), 'view', spli...  11.9 us
    pallas_call x2, Pallas kernels, conv_rows(): pl.pallas_call(functools.partial(conv_kernel, relu=relu, rows=rows, cols=...  7.67 us
    all_to_all x1, starting transfers between devices, body(): lax.all_to_all(corr_all.reshape(owners, cap * GROUPS, tpix), 'view', spli...  7.15 us
    ppermute x2, waiting for transfers between devices, gather_view(): lax.ppermute(gathered, 'view', [(i, i ^ stride) for i in range(count)])  4.99 us
    ppermute x1, waiting for transfers between devices, halo_cols(): high = lax.ppermute(block[:, :cols], 'view', backward)  4.79 us
    pallas_call x1, Pallas kernels, correlate(): pl.pallas_call(correlate_kernel, out_shape=jax.ShapeDtypeStruct((units *...  4.15 us
    ppermute x1, starting transfers between devices, halo_cols(): low = lax.ppermute(block[:, block.shape[1] - cols:], 'view', forward)  3.64 us
    ppermute x2, starting transfers between devices, gather_view(): lax.ppermute(gathered, 'view', [(i, i ^ stride) for i in range(count)])  3.02 us
  transfers between devices with their start and end apart: 8, of which 4 were waited for; matrix products, arithmetic and copies ran while one was open for 15% of the time, Pallas kernels for 0%

profile of v13, /device:TPU:13, one launch (start us, length us, event | category | flops | bytes accessed | tf_op | source)
XLA Modules:
  0.0 67.2 jit_solution(4775211643118566162)
XLA Ops:
  0.0 0.7 %fusion.29 = bf16[64]{0:T(256)(128)(2,1)S(1)} fusion(s32[1,64]{1,0:T(1,128)} %param.15, s32[1,64]{1,0:T(1,128)} %param.14), kind=kLoop, calls=%fused_computation.78 | loop fusion | flops 192 | bytes 640 | tf_op jit(solution)/shard_map/convert_element_type | solution.py:292
  0.7 0.8 %fusion.31 = (bf16[1,32,640]{2,1,0:T(8,128)(2,1)S(1)}, bf16[32,640]{1,0:T(8,128)(2,1)S(1)}) fusion(bf16[32,128]{1,0:T(8,128)(2,1)S(1)} %pad_bitcast_fusion, bf16[32,512]{1,0:T(8,128)(2,1)} %bitcast.101), kind=kLoop, calls=%fused_computation.83 | loop fusion | flops 81920 | bytes 122880 | tf_op jit(solution)/shard_map/broadcast_in_dim | solution.py:295
  1.7 2.3 %collective-permute-start.1 = (bf16[32,640]{1,0:T(8,128)(2,1)S(1)}, bf16[32,640]{1,0:T(8,128)(2,1)S(1)}, u32[]{:S(2)}, u32[]{:S(2)}) collective-permute-start(bf16[32,640]{1,0:T(8,128)(2,1)S(1)} %get-tuple-element.10), channel_id=1, source_target_pairs={{0,8},{1,9},{2,10},{3,11},{4,12},{5,13},{6,14},{7,15},{8,0},{9,1},... | collective-permute-start | bytes 122888 | tf_op jit(solution)/shard_map/ppermute | solution.py:244
  4.9 0.7 %select_reduce_fusion.1 = s32[64,4]{0,1:T(4,128)S(1)} fusion(s32[64,4]{0,1:T(4,128)} %bitcast.104, s32[64,4]{0,1:T(4,128)} %bitcast.102), kind=kLoop, calls=%fused_computation.40 | loop fusion | flops 2816 | bytes 3072 | tf_op jit(solution)/shard_map/reduce_sum | solution.py:289
  5.6 0.7 %fusion.15 = pred[64,4]{0,1:T(4,128)(4,1)S(1)} fusion(s32[64,4]{0,1:T(4,128)} %bitcast.103, pred[64,4]{0,1:T(4,128)(4,1)S(1)} %iota_compare_fusion.4), kind=kLoop, calls=%fused_computation.46 | loop fusion | flops 2816 | bytes 1536 | tf_op jit(solution)/shard_map/reduce_or | solution.py:290
  6.5 0.7 %fusion = bf16[9,128,144]{1,2,0:T(8,128)(2,1)S(1)} fusion(bf16[3,9,8,8]{3,2,1,0:T(8,128)(2,1)S(1)} %bitcast.76, pred[3,128,144]{1,2,0:T(8,128)(4,1)S(1)} %broadcast_compare_fusion.1, s32[144]{0:T(256)S(1)} %and_select_fusion.1, s32[128]{0:T(128)S(1)} %and_select_fusion), kind=kOutput, calls=%fused_computation.3 | convolution fusion | flops 9323008 | bytes 391616 | tf_op jit(solution)/shard_map/ro,xyoc->xyrc/dot_general | solution.py:188
  7.4 0.7 select_n.203.blk_ref
  8.5 1.1 %copy.47 = bf16[9,128,144]{2,1,0:T(8,128)(2,1)} copy(bf16[9,128,144]{1,2,0:T(8,128)(2,1)S(1)} %fusion) | data formatting | bytes 663552 | tf_op jit(solution)/shard_map/convert_element_type | solution.py:199
  9.6 0.8 %concatenate.24.blocks_ref = bf16[65,32,128]{2,1,0:T(8,128)(2,1)} pad(bf16[64,32,128]{2,1,0:T(8,128)(2,1)S(1)} %bitcast.86, bf16[]{:T(256)} %constant.149.clone.1), padding=0_1x0_0x0_0 | pad | bytes 1056770 | tf_op jit(solution)/shard_map/concatenate | solution.py:286
  11.7 3.8 %collective-permute-done.3 = bf16[2,2,32,640]{3,2,1,0:T(8,128)(2,1)S(1)} collective-permute-done((bf16[2,2,32,640]{3,2,1,0:T(8,128)(2,1)S(1)}, bf16[2,2,32,640]{3,2,1,0:T(8,128)(2,1)S(1)}, u32[]{:S(2)}, u32[]{:S(2)}) %collective-permute-start.3) | collective-permute-done | bytes 163872 | tf_op jit(solution)/shard_map/ppermute | solution.py:252
  15.6 2.7 %collective-permute-start.4 = (bf16[2,2,2,32,640]{4,3,2,1,0:T(8,128)(2,1)S(1)}, bf16[2,2,2,32,640]{4,3,2,1,0:T(8,128)(2,1)S(1)}, u32[]{:S(2)}, u32[]{:S(2)}) collective-permute-start(bf16[2,2,2,32,640]{4,3,2,1,0:T(8,128)(2,1)S(1)} %maximum_select_fusion.1), channel_id=1, source_target_pairs={{0,1},{1,0},{2,3},{3,2},{4,5},{5,4},{6,7},{7,6},{8,9},{9,8},{10,11... | collective-permute-start | bytes 983048 | tf_op jit(solution)/shard_map/ppermute | solution.py:252
  18.4 1.1 %collective-permute-done.4 = bf16[2,2,2,32,640]{4,3,2,1,0:T(8,128)(2,1)S(1)} collective-permute-done((bf16[2,2,2,32,640]{4,3,2,1,0:T(8,128)(2,1)S(1)}, bf16[2,2,2,32,640]{4,3,2,1,0:T(8,128)(2,1)S(1)}, u32[]{:S(2)}, u32[]{:S(2)}) %collective-permute-start.4) | collective-permute-done | bytes 327712 | tf_op jit(solution)/shard_map/ppermute | solution.py:252
  19.6 0.9 %maximum_select_fusion = bf16[2,2,2,2,32,640]{5,4,3,2,1,0:T(8,128)(2,1)} fusion(bf16[2,2,2,1,32,640]{5,4,3,2,1,0:T(8,128)(2,1)S(1)} %bitcast.95, bf16[2,2,2,1,32,640]{5,4,3,2,1,0:T(8,128)(2,1)S(1)} %copy_select_fusion, pred[]{:T(512)S(6)} %eq.127), kind=kLoop, calls=%fused_computation.10 | loop fusion | flops 983040 | bytes 1310721 | tf_op jit(solution)/shard_map/jit(_where)/select_n | solution.py:254
  20.5 4.1 %shard_map.91 = bf16[512,512]{1,0:T(8,128)(2,1)} custom-call(s32[256]{0:T(256)} %select_n.203.blk_ref, bf16[65,32,128]{2,1,0:T(8,128)(2,1)} %concatenate.24.blocks_ref, bf16[512,512]{1,0:T(8,128)(2,1)} %bitcast.94, bf16[16,32,640]{2,1,0:T(8,128)(2,1)} %bitcast.79), custom_call_target="tpu_custom_call" | custom-call | tf_op jit(solution)/shard_map/pallas_call | solution.py:121
  24.6 7.2 %all-to-all-start = ((bf16[16,32,512]{2,1,0:T(8,128)(2,1)}), bf16[16,32,512]{2,1,0:T(8,128)(2,1)S(1)}, u32[]{:S(2)}, u32[]{:S(2)}) async-start(bf16[16,32,512]{2,1,0:T(8,128)(2,1)} %bitcast.88), calls=%async_computation | async-start | bytes 1048576 | tf_op jit(solution)/shard_map/all_to_all | solution.py:299
  32.1 0.9 %slice.14 = bf16[16,32,128]{2,1,0:T(8,128)(2,1)S(1)} slice(bf16[16,32,640]{2,1,0:T(8,128)(2,1)} %bitcast.80), slice={[0:16], [0:32], [512:640]} | slice | bytes 262144 | tf_op jit(solution)/shard_map/slice | solution.py:307
  33.4 11.9 %all-to-all-done = bf16[16,32,512]{2,1,0:T(8,128)(2,1)S(1)} async-done(((bf16[16,32,512]{2,1,0:T(8,128)(2,1)}), bf16[16,32,512]{2,1,0:T(8,128)(2,1)S(1)}, u32[]{:S(2)}, u32[]{:S(2)}) %all-to-all-start) | async-done | bytes 524320 | tf_op jit(solution)/shard_map/all_to_all | solution.py:299
  46.1 3.6 %collective-permute-start.5 = (bf16[528,256]{1,0:T(8,128)(2,1)S(1)}, bf16[528,256]{1,0:T(8,128)(2,1)S(1)}, u32[]{:S(2)}, u32[]{:S(2)}) collective-permute-start(bf16[528,256]{1,0:T(8,128)(2,1)S(1)} %get-tuple-element.5), channel_id=1, source_target_pairs={{0,1},{1,2},{2,3},{3,4},{4,5},{5,6},{6,7},{7,8},{8,9},{9,10},{10,1... | collective-permute-start | bytes 811016 | tf_op jit(solution)/shard_map/ppermute | solution.py:226
  49.7 1.9 %collective-permute-start.6 = (bf16[528,256]{1,0:T(8,128)(2,1)S(1)}, bf16[528,256]{1,0:T(8,128)(2,1)S(1)}, u32[]{:S(2)}, u32[]{:S(2)}) collective-permute-start(bf16[528,256]{1,0:T(8,128)(2,1)S(1)} %get-tuple-element.6), channel_id=1, source_target_pairs={{1,0},{2,1},{3,2},{4,3},{5,4},{6,5},{7,6},{8,7},{9,8},{10,9},{11,1... | collective-permute-start | bytes 811016 | tf_op jit(solution)/shard_map/ppermute | solution.py:227
  52.3 1.3 %select_reduce_fusion = bf16[9,64,528]{2,1,0:T(8,128)(2,1)} fusion(f32[3,9,528]{2,1,0:T(8,128)S(1)} %convolution_bitcast_fusion, pred[3,64,528]{2,1,0:T(8,128)(4,1)S(1)} %broadcast_compare_fusion), kind=kLoop, calls=%fused_computation.1 | loop fusion | flops 1520640 | bytes 766656 | tf_op jit(solution)/shard_map/reduce_sum | solution.py:198
  53.6 4.8 %collective-permute-done.6 = bf16[528,256]{1,0:T(8,128)(2,1)S(1)} collective-permute-done((bf16[528,256]{1,0:T(8,128)(2,1)S(1)}, bf16[528,256]{1,0:T(8,128)(2,1)S(1)}, u32[]{:S(2)}, u32[]{:S(2)}) %collective-permute-start.6) | collective-permute-done | bytes 270368 | tf_op jit(solution)/shard_map/ppermute | solution.py:227
  58.4 1.1 %pad_maximum_fusion.refs_1_ = bf16[528,1024]{1,0:T(8,128)(2,1)} fusion(bf16[528,256]{1,0:T(8,128)(2,1)S(1)} %collective-permute-done.6, bf16[528,512]{1,0:T(8,128)(2,1)S(1)} %pad.10, bf16[528,256]{1,0:T(8,128)(2,1)S(1)} %collective-permute-done.5), kind=kLoop, calls=%fused_computation.9 | loop fusion | flops 3244032 | bytes 2162688 | tf_op jit(solution)/shard_map/concatenate | solution.py:228
  59.6 4.5 %shard_map.92.refs_0_ = bf16[528,768]{1,0:T(8,128)(2,1)} custom-call(s32[2]{0:T(128)} %add_convert_fusion.refs_0_, bf16[528,1024]{1,0:T(8,128)(2,1)} %pad_maximum_fusion.refs_1_, bf16[3,3,128,144]{3,2,1,0:T(8,128)(2,1)} %bitcast.85), custom_call_target="tpu_custom_call" | custom-call | tf_op jit(solution)/shard_map/pallas_call | solution.py:214
  64.0 3.2 %shard_map.93 = f32[4,64,128]{2,1,0:T(8,128)} custom-call(bf16[528,768]{1,0:T(8,128)(2,1)} %shard_map.92.refs_0_, bf16[3,3,64,528]{3,2,1,0:T(8,128)(2,1)} %bitcast.81), custom_call_target="tpu_custom_call" | custom-call | tf_op jit(solution)/shard_map/pallas_call | solution.py:214
  (53 shorter events, 5.1 us)
Async XLA Ops:
  0.0 6.4 %copy-start = (bf16[3,3,3,8,8]{4,3,2,1,0:T(8,128)(2,1)S(1)}, bf16[3,3,3,8,8]{4,3,2,1,0:T(8,128)(2,1)}, u32[]{:S(2)}) copy-start(bf16[3,3,3,8,8]{4,3,2,1,0:T(8,128)(2,1)} %param.16) | copy-start | bytes 10372
  0.0 8.0 %copy-start.1 = (bf16[1,32,8192]{2,1,0:T(8,128)(2,1)S(1)}, bf16[1,32,8192]{2,1,0:T(8,128)(2,1)}, u32[]{:S(2)}) copy-start(bf16[1,32,8192]{2,1,0:T(8,128)(2,1)} %param.9) | copy-start | bytes 1572868
  1.5 8.9 %collective-permute-start = (bf16[32,640]{1,0:T(8,128)(2,1)S(1)}, bf16[32,640]{1,0:T(8,128)(2,1)S(1)}, u32[]{:S(2)}, u32[]{:S(2)}) collective-permute-start(bf16[32,640]{1,0:T(8,128)(2,1)S(1)} %get-tuple-element.10), channel_id=1, source_target_pairs={{0,4},{1,5},{2,6},{3,7},{4,0},{5,1},{6,2},{7,3},{8,12},{9,13},{10,... | collective-permute-start | bytes 122888 | tf_op jit(solution)/shard_map/ppermute | solution.py:244
  1.7 8.8 %collective-permute-start.1 = (bf16[32,640]{1,0:T(8,128)(2,1)S(1)}, bf16[32,640]{1,0:T(8,128)(2,1)S(1)}, u32[]{:S(2)}, u32[]{:S(2)}) collective-permute-start(bf16[32,640]{1,0:T(8,128)(2,1)S(1)} %get-tuple-element.10), channel_id=1, source_target_pairs={{0,8},{1,9},{2,10},{3,11},{4,12},{5,13},{6,14},{7,15},{8,0},{9,1},... | collective-permute-start | bytes 122888 | tf_op jit(solution)/shard_map/ppermute | solution.py:244
  4.0 6.5 %collective-permute-start.2 = (bf16[32,640]{1,0:T(8,128)(2,1)S(1)}, bf16[32,640]{1,0:T(8,128)(2,1)S(1)}, u32[]{:S(2)}, u32[]{:S(2)}) collective-permute-start(bf16[32,640]{1,0:T(8,128)(2,1)S(1)} %get-tuple-element.10), channel_id=1, source_target_pairs={{0,12},{1,13},{2,14},{3,15},{4,8},{5,9},{6,10},{7,11},{8,4},{9,5},... | collective-permute-start | bytes 122888 | tf_op jit(solution)/shard_map/ppermute | solution.py:244
  8.2 1.4 %copy-start.2 = (bf16[3,3,3,8]{3,2,1,0:T(4,128)(2,1)S(1)}, bf16[3,3,3,8]{3,2,1,0:T(4,128)(2,1)}, u32[]{:S(2)}) copy-start(bf16[3,3,3,8]{3,2,1,0:T(4,128)(2,1)} %param.17) | copy-start | bytes 1300
  11.3 4.2 %collective-permute-start.3 = (bf16[2,2,32,640]{3,2,1,0:T(8,128)(2,1)S(1)}, bf16[2,2,32,640]{3,2,1,0:T(8,128)(2,1)S(1)}, u32[]{:S(2)}, u32[]{:S(2)}) collective-permute-start(bf16[2,2,32,640]{3,2,1,0:T(8,128)(2,1)S(1)} %broadcast_select_fusion), channel_id=1, source_target_pairs={{0,2},{1,3},{2,0},{3,1},{4,6},{5,7},{6,4},{7,5},{8,10},{9,11},{10,... | collective-permute-start | bytes 491528 | tf_op jit(solution)/shard_map/ppermute | solution.py:252
  15.6 4.0 %collective-permute-start.4 = (bf16[2,2,2,32,640]{4,3,2,1,0:T(8,128)(2,1)S(1)}, bf16[2,2,2,32,640]{4,3,2,1,0:T(8,128)(2,1)S(1)}, u32[]{:S(2)}, u32[]{:S(2)}) collective-permute-start(bf16[2,2,2,32,640]{4,3,2,1,0:T(8,128)(2,1)S(1)} %maximum_select_fusion.1), channel_id=1, source_target_pairs={{0,1},{1,0},{2,3},{3,2},{4,5},{5,4},{6,7},{7,6},{8,9},{9,8},{10,11... | collective-permute-start | bytes 983048 | tf_op jit(solution)/shard_map/ppermute | solution.py:252
  24.6 20.7 %all-to-all-start = ((bf16[16,32,512]{2,1,0:T(8,128)(2,1)}), bf16[16,32,512]{2,1,0:T(8,128)(2,1)S(1)}, u32[]{:S(2)}, u32[]{:S(2)}) async-start(bf16[16,32,512]{2,1,0:T(8,128)(2,1)} %bitcast.88), calls=%async_computation | async-start | bytes 1048576 | tf_op jit(solution)/shard_map/all_to_all | solution.py:299
  46.1 7.5 %collective-permute-start.5 = (bf16[528,256]{1,0:T(8,128)(2,1)S(1)}, bf16[528,256]{1,0:T(8,128)(2,1)S(1)}, u32[]{:S(2)}, u32[]{:S(2)}) collective-permute-start(bf16[528,256]{1,0:T(8,128)(2,1)S(1)} %get-tuple-element.5), channel_id=1, source_target_pairs={{0,1},{1,2},{2,3},{3,4},{4,5},{5,6},{6,7},{7,8},{8,9},{9,10},{10,1... | collective-permute-start | bytes 811016 | tf_op jit(solution)/shard_map/ppermute | solution.py:226
  49.7 8.7 %collective-permute-start.6 = (bf16[528,256]{1,0:T(8,128)(2,1)S(1)}, bf16[528,256]{1,0:T(8,128)(2,1)S(1)}, u32[]{:S(2)}, u32[]{:S(2)}) collective-permute-start(bf16[528,256]{1,0:T(8,128)(2,1)S(1)} %get-tuple-element.6), channel_id=1, source_target_pairs={{1,0},{2,1},{3,2},{4,3},{5,4},{6,5},{7,6},{8,7},{9,8},{10,9},{11,1... | collective-permute-start | bytes 811016 | tf_op jit(solution)/shard_map/ppermute | solution.py:227

commit v14 on v13

--- a/solution.py
+++ b/solution.py
@@ -135,11 +135,7 @@
     )(blk, blocks, table, refs)
 
 
-def conv_kernel(*refs, relu, rows, cols, groups, chunk):
-    if relu:
-        ends_ref, x_ref, m_ref, out_ref = refs
-    else:
-        x_ref, m_ref, out_ref = refs
+def conv_body(x_ref, m_ref, out_ref, ends_ref, *, relu, rows, cols, groups, chunk):
     width = rows * cols
     outs = m_ref.shape[2]
     depth = x_ref.shape[0] // groups - 2
@@ -199,24 +195,39 @@
     return mats.astype(kernel.dtype).reshape(3, 3, rows, cols)
 
 
-def conv_rows(framed, mats, relu, rows, cols, chunk, ends=None):
-    outs = mats.shape[2]
-    groups = mats.shape[3] // (chunk + 2)
+def conv_pair_kernel(
+    ends_ref, low_ref, vol_ref, high_ref, m1_ref, m2_ref, out_ref, framed, hidden, *, rows, cols, groups
+):
+    halo = low_ref.shape[1]
+    middle = vol_ref.shape[1]
+    framed[:, :halo] = low_ref[...]
+    framed[:, halo : halo + middle] = vol_ref[...]
+    framed[:, halo + middle :] = high_ref[...]
     depth = framed.shape[0] // groups - 2
-    if relu:
-        out_shape = jax.ShapeDtypeStruct(((depth + 2) * outs // chunk, rows * cols), jnp.bfloat16)
-    else:
-        out_shape = jax.ShapeDtypeStruct((rows, depth, cols), jnp.float32)
-    operands = (framed, mats) if ends is None else (ends, framed, mats)
-    in_specs = [pl.BlockSpec(memory_space=pltpu.VMEM), pl.BlockSpec(memory_space=pltpu.VMEM)]
-    if ends is not None:
-        in_specs = [pl.BlockSpec(memory_space=pltpu.SMEM)] + in_specs
+    first = m1_ref.shape[3] // groups - 2
+    conv_body(
+        framed, m1_ref, hidden, ends_ref, relu=True, rows=rows + 2, cols=cols, groups=groups, chunk=first
+    )
+    conv_body(
+        hidden, m2_ref, out_ref, None, relu=False, rows=rows, cols=cols, groups=groups, chunk=depth
+    )
+
+
+def conv_pair(ends, low, volume, high, first, second, rows, cols):
+    groups = second.shape[3] // (second.shape[2] + 2)
+    depth = volume.shape[0] // groups - 2
+    outs = first.shape[2] * depth // (first.shape[3] // groups - 2)
+    vmem = pl.BlockSpec(memory_space=pltpu.VMEM)
     return pl.pallas_call(
-        functools.partial(conv_kernel, relu=relu, rows=rows, cols=cols, groups=groups, chunk=chunk),
-        out_shape=out_shape,
-        in_specs=in_specs,
-        out_specs=pl.BlockSpec(memory_space=pltpu.VMEM),
-    )(*operands)
+        functools.partial(conv_pair_kernel, rows=rows, cols=cols, groups=groups),
+        out_shape=jax.ShapeDtypeStruct((rows, depth, cols), jnp.float32),
+        in_specs=[pl.BlockSpec(memory_space=pltpu.SMEM)] + [vmem] * 5,
+        out_specs=vmem,
+        scratch_shapes=[
+            pltpu.VMEM((volume.shape[0], volume.shape[1] + low.shape[1] + high.shape[1]), volume.dtype),
+            pltpu.VMEM(((depth + 2) * outs // depth, (rows + 2) * cols), jnp.bfloat16),
+        ],
+    )(ends, low, volume, high, first, second)
 
 
 def halo_cols(block, cols):
@@ -318,16 +329,21 @@
     count = lax.axis_size("view")
     place = lax.axis_index("view")
     ends = jnp.stack([place == 0, place == count - 1]).astype(jnp.int32)
-    hidden = conv_rows(
-        halo_cols(volume, 2 * columns),
+    count = lax.axis_size("view")
+    forward = [(i, i + 1) for i in range(count - 1)]
+    backward = [(target, source) for source, target in forward]
+    low = lax.ppermute(volume[:, volume.shape[1] - 2 * columns :], "view", forward)
+    high = lax.ppermute(volume[:, : 2 * columns], "view", backward)
+    scores = conv_pair(
+        ends,
+        low,
+        volume,
+        high,
         banded(kern_one, DEPTH // 4),
-        True,
-        TROWS + 2,
+        banded(kern_two, DEPTH),
+        TROWS,
         columns,
-        DEPTH // 4,
-        ends,
-    )
-    scores = conv_rows(hidden, banded(kern_two, DEPTH), False, TROWS, columns, DEPTH)
+    )
     return scores
 
 

time: 67.7 us -> 65.4 us (0.966)
  Pallas kernels: 11.8 us -> 10.1 us
  local copies, waits for them, and re-layouts: 5.26 us -> 6.81 us
  other arithmetic: 8.49 us -> 7.31 us
  waiting for transfers between devices: 21.7 us -> 20.8 us
    pallas_call x2 -> x1, Pallas kernels: 7.67 us -> 5.97 us  [conv_pair(): pl.pallas_call(functools.partial(conv_pair_kernel, rows=rows, cols=cols,...]
    concatenate x1 -> x0, other arithmetic: 1.14 us -> none  [halo_cols(): return jnp.concatenate([low, block, high], axis=1)]
    ppermute x3, starting transfers between devices: 2.65 us -> 3.49 us  [gather_view(): lax.ppermute(gathered, 'view', [(i, i ^ m * top) for i in range(count)])]
    ppermute x2, waiting for transfers between devices: 4.79 us -> 3.97 us  [the longest x1 3.97 us: body(): high = lax.ppermute(volume[:, :2 * columns], 'view', backward)]
    pad x1, local copies, waits for them, and re-layouts: 0.04 us -> 0.86 us  [body(): volume = jnp.pad(volume, ((GROUPS, GROUPS), (0, 0)))]
    unnamed x9 -> x13, local copies, waits for them, and re-layouts: 0.19 us -> 0.9 us
  transfers between devices with their start and end apart: 8 -> 8, of which waited for: 4 -> 4; matrix products, arithmetic and copies ran while one was open for 15% -> 17% of each run, Pallas kernels for 0% -> 0%
where the time goes in v14:
time: 65.4 us; the launch traced here: 64.9 us
  waiting for transfers between devices  20.8 us (32%)
  starting transfers between devices  18.4 us (28%)
  Pallas kernels  10.1 us (15%)
  other arithmetic  7.31 us (11%)
  local copies, waits for them, and re-layouts  6.81 us (10%)
  matrix products  1.23 us (2%)
    all_to_all x1, waiting for transfers between devices, body(): lax.all_to_all(corr_all.reshape(owners, cap * GROUPS, tpix), 'view', spli...  11.9 us
    all_to_all x1, starting transfers between devices, body(): lax.all_to_all(corr_all.reshape(owners, cap * GROUPS, tpix), 'view', spli...  6.51 us
    pallas_call x1, Pallas kernels, conv_pair(): pl.pallas_call(functools.partial(conv_pair_kernel, rows=rows, cols=cols,...  5.97 us
    ppermute x2, waiting for transfers between devices, gather_view(): lax.ppermute(gathered, 'view', [(i, i ^ stride) for i in range(count)])  4.89 us
    pallas_call x1, Pallas kernels, correlate(): pl.pallas_call(correlate_kernel, out_shape=jax.ShapeDtypeStruct((units *...  4.15 us
    ppermute x1, waiting for transfers between devices, body(): high = lax.ppermute(volume[:, :2 * columns], 'view', backward)  3.97 us
    ppermute x1, starting transfers between devices, body(): lax.ppermute(volume[:, volume.shape[1] - 2 * columns:], 'view', forward)  3.64 us
    ppermute x3, starting transfers between devices, gather_view(): lax.ppermute(gathered, 'view', [(i, i ^ m * top) for i in range(count)])  3.49 us
  transfers between devices with their start and end apart: 8, of which 4 were waited for; matrix products, arithmetic and copies ran while one was open for 17% of the time, Pallas kernels for 0%

profile of v14, /device:TPU:13, one launch (start us, length us, event | category | flops | bytes accessed | tf_op | source)
XLA Modules:
  0.0 64.9 jit_solution(5646782734661735744)
XLA Ops:
  0.7 0.8 %fusion.31 = (bf16[1,32,640]{2,1,0:T(8,128)(2,1)S(1)}, bf16[32,640]{1,0:T(8,128)(2,1)S(1)}) fusion(bf16[32,128]{1,0:T(8,128)(2,1)S(1)} %pad_bitcast_fusion, bf16[32,512]{1,0:T(8,128)(2,1)} %bitcast.101), kind=kLoop, calls=%fused_computation.82 | loop fusion | flops 81920 | bytes 122880 | tf_op jit(solution)/shard_map/broadcast_in_dim | solution.py:306
  1.5 1.3 %collective-permute-start.2 = (bf16[32,640]{1,0:T(8,128)(2,1)S(1)}, bf16[32,640]{1,0:T(8,128)(2,1)S(1)}, u32[]{:S(2)}, u32[]{:S(2)}) collective-permute-start(bf16[32,640]{1,0:T(8,128)(2,1)S(1)} %get-tuple-element.10), channel_id=1, source_target_pairs={{0,12},{1,13},{2,14},{3,15},{4,8},{5,9},{6,10},{7,11},{8,4},{9,5},... | collective-permute-start | bytes 122888 | tf_op jit(solution)/shard_map/ppermute | solution.py:255
  2.8 1.1 %collective-permute-start.1 = (bf16[32,640]{1,0:T(8,128)(2,1)S(1)}, bf16[32,640]{1,0:T(8,128)(2,1)S(1)}, u32[]{:S(2)}, u32[]{:S(2)}) collective-permute-start(bf16[32,640]{1,0:T(8,128)(2,1)S(1)} %get-tuple-element.10), channel_id=1, source_target_pairs={{0,8},{1,9},{2,10},{3,11},{4,12},{5,13},{6,14},{7,15},{8,0},{9,1},... | collective-permute-start | bytes 122888 | tf_op jit(solution)/shard_map/ppermute | solution.py:255
  3.8 1.1 %collective-permute-start = (bf16[32,640]{1,0:T(8,128)(2,1)S(1)}, bf16[32,640]{1,0:T(8,128)(2,1)S(1)}, u32[]{:S(2)}, u32[]{:S(2)}) collective-permute-start(bf16[32,640]{1,0:T(8,128)(2,1)S(1)} %get-tuple-element.10), channel_id=1, source_target_pairs={{0,4},{1,5},{2,6},{3,7},{4,0},{5,1},{6,2},{7,3},{8,12},{9,13},{10,... | collective-permute-start | bytes 122888 | tf_op jit(solution)/shard_map/ppermute | solution.py:255
  5.7 0.7 %fusion.15 = pred[64,4]{0,1:T(4,128)(4,1)S(1)} fusion(s32[64,4]{0,1:T(4,128)} %bitcast.102, pred[64,4]{0,1:T(4,128)(4,1)S(1)} %iota_compare_fusion.4), kind=kLoop, calls=%fused_computation.45 | loop fusion | flops 2816 | bytes 1536 | tf_op jit(solution)/shard_map/reduce_or | solution.py:301
  6.4 0.7 %select_reduce_fusion.1 = s32[64,4]{0,1:T(4,128)S(1)} fusion(s32[64,4]{0,1:T(4,128)} %bitcast.104, s32[64,4]{0,1:T(4,128)} %bitcast.103), kind=kLoop, calls=%fused_computation.39 | loop fusion | flops 2816 | bytes 3072 | tf_op jit(solution)/shard_map/reduce_sum | solution.py:300
  7.3 0.7 %fusion = bf16[9,128,144]{1,2,0:T(8,128)(2,1)S(1)} fusion(bf16[3,9,8,8]{3,2,1,0:T(8,128)(2,1)S(1)} %bitcast.76, pred[3,128,144]{1,2,0:T(8,128)(4,1)S(1)} %broadcast_compare_fusion.1, s32[144]{0:T(256)S(1)} %and_select_fusion.1, s32[128]{0:T(128)S(1)} %and_select_fusion), kind=kOutput, calls=%fused_computation.3 | convolution fusion | flops 9323008 | bytes 391616 | tf_op jit(solution)/shard_map/ro,xyoc->xyrc/dot_general | solution.py:184
  9.3 1.1 %copy.47 = bf16[9,128,144]{2,1,0:T(8,128)(2,1)} copy(bf16[9,128,144]{1,2,0:T(8,128)(2,1)S(1)} %fusion) | data formatting | bytes 663552 | tf_op jit(solution)/shard_map/convert_element_type | solution.py:195
  10.4 0.9 %concatenate.21.blocks_ref = bf16[65,32,128]{2,1,0:T(8,128)(2,1)} pad(bf16[64,32,128]{2,1,0:T(8,128)(2,1)S(1)} %bitcast.86, bf16[]{:T(256)} %constant.149.clone.1), padding=0_1x0_0x0_0 | pad | bytes 1056770 | tf_op jit(solution)/shard_map/concatenate | solution.py:297
  12.5 3.8 %collective-permute-done.3 = bf16[2,2,32,640]{3,2,1,0:T(8,128)(2,1)S(1)} collective-permute-done((bf16[2,2,32,640]{3,2,1,0:T(8,128)(2,1)S(1)}, bf16[2,2,32,640]{3,2,1,0:T(8,128)(2,1)S(1)}, u32[]{:S(2)}, u32[]{:S(2)}) %collective-permute-start.3) | collective-permute-done | bytes 163872 | tf_op jit(solution)/shard_map/ppermute | solution.py:263
  16.3 2.5 %collective-permute-start.4 = (bf16[2,2,2,32,640]{4,3,2,1,0:T(8,128)(2,1)S(1)}, bf16[2,2,2,32,640]{4,3,2,1,0:T(8,128)(2,1)S(1)}, u32[]{:S(2)}, u32[]{:S(2)}) collective-permute-start(bf16[2,2,2,32,640]{4,3,2,1,0:T(8,128)(2,1)S(1)} %maximum_select_fusion.1), channel_id=1, source_target_pairs={{0,1},{1,0},{2,3},{3,2},{4,5},{5,4},{6,7},{7,6},{8,9},{9,8},{10,11... | collective-permute-start | bytes 983048 | tf_op jit(solution)/shard_map/ppermute | solution.py:263
  18.9 1.1 %collective-permute-done.4 = bf16[2,2,2,32,640]{4,3,2,1,0:T(8,128)(2,1)S(1)} collective-permute-done((bf16[2,2,2,32,640]{4,3,2,1,0:T(8,128)(2,1)S(1)}, bf16[2,2,2,32,640]{4,3,2,1,0:T(8,128)(2,1)S(1)}, u32[]{:S(2)}, u32[]{:S(2)}) %collective-permute-start.4) | collective-permute-done | bytes 327712 | tf_op jit(solution)/shard_map/ppermute | solution.py:263
  20.1 0.9 %maximum_select_fusion = bf16[2,2,2,2,32,640]{5,4,3,2,1,0:T(8,128)(2,1)} fusion(bf16[2,2,2,1,32,640]{5,4,3,2,1,0:T(8,128)(2,1)S(1)} %bitcast.95, bf16[2,2,2,1,32,640]{5,4,3,2,1,0:T(8,128)(2,1)S(1)} %copy_select_fusion, pred[]{:T(512)S(6)} %eq.127), kind=kLoop, calls=%fused_computation.9 | loop fusion | flops 983040 | bytes 1310721 | tf_op jit(solution)/shard_map/jit(_where)/select_n | solution.py:265
  21.0 4.1 %shard_map.91 = bf16[512,512]{1,0:T(8,128)(2,1)} custom-call(s32[256]{0:T(256)} %select_n.203.blk_ref, bf16[65,32,128]{2,1,0:T(8,128)(2,1)} %concatenate.21.blocks_ref, bf16[512,512]{1,0:T(8,128)(2,1)} %bitcast.94, bf16[16,32,640]{2,1,0:T(8,128)(2,1)} %bitcast.79), custom_call_target="tpu_custom_call" | custom-call | tf_op jit(solution)/shard_map/pallas_call | solution.py:121
  25.1 6.5 %all-to-all-start = ((bf16[16,32,512]{2,1,0:T(8,128)(2,1)}), bf16[16,32,512]{2,1,0:T(8,128)(2,1)S(1)}, u32[]{:S(2)}, u32[]{:S(2)}) async-start(bf16[16,32,512]{2,1,0:T(8,128)(2,1)} %bitcast.88), calls=%async_computation | async-start | bytes 1048576 | tf_op jit(solution)/shard_map/all_to_all | solution.py:310
  31.9 0.9 %slice.14 = bf16[16,32,128]{2,1,0:T(8,128)(2,1)S(1)} slice(bf16[16,32,640]{2,1,0:T(8,128)(2,1)} %bitcast.80), slice={[0:16], [0:32], [512:640]} | slice | bytes 262144 | tf_op jit(solution)/shard_map/slice | solution.py:318
  33.3 11.9 %all-to-all-done = bf16[16,32,512]{2,1,0:T(8,128)(2,1)S(1)} async-done(((bf16[16,32,512]{2,1,0:T(8,128)(2,1)}), bf16[16,32,512]{2,1,0:T(8,128)(2,1)S(1)}, u32[]{:S(2)}, u32[]{:S(2)}) %all-to-all-start) | async-done | bytes 524320 | tf_op jit(solution)/shard_map/all_to_all | solution.py:310
  45.9 3.6 %collective-permute-start.5 = (bf16[528,256]{1,0:T(8,128)(2,1)S(1)}, bf16[528,256]{1,0:T(8,128)(2,1)S(1)}, u32[]{:S(2)}, u32[]{:S(2)}) collective-permute-start(bf16[528,256]{1,0:T(8,128)(2,1)S(1)} %get-tuple-element.6), channel_id=1, source_target_pairs={{0,1},{1,2},{2,3},{3,4},{4,5},{5,6},{6,7},{7,8},{8,9},{9,10},{10,1... | collective-permute-start | bytes 811016 | tf_op jit(solution)/shard_map/ppermute | solution.py:335
  49.6 1.9 %collective-permute-start.6 = (bf16[528,256]{1,0:T(8,128)(2,1)S(1)}, bf16[528,256]{1,0:T(8,128)(2,1)S(1)}, u32[]{:S(2)}, u32[]{:S(2)}) collective-permute-start(bf16[528,256]{1,0:T(8,128)(2,1)S(1)} %get-tuple-element.5), channel_id=1, source_target_pairs={{1,0},{2,1},{3,2},{4,3},{5,4},{6,5},{7,6},{8,7},{9,8},{10,9},{11,1... | collective-permute-start | bytes 811016 | tf_op jit(solution)/shard_map/ppermute | solution.py:336
  52.1 1.3 %select_reduce_fusion = bf16[9,64,528]{2,1,0:T(8,128)(2,1)} fusion(f32[3,9,528]{2,1,0:T(8,128)S(1)} %convolution_bitcast_fusion, pred[3,64,528]{2,1,0:T(8,128)(4,1)S(1)} %broadcast_compare_fusion), kind=kLoop, calls=%fused_computation.1 | loop fusion | flops 1520640 | bytes 766656 | tf_op jit(solution)/shard_map/reduce_sum | solution.py:194
  53.4 0.9 %pad.10.vol_ref = bf16[528,512]{1,0:T(8,128)(2,1)} pad(bf16[512,512]{1,0:T(8,128)(2,1)S(1)} %bitcast.78, bf16[]{:T(256)} %constant.149.clone.1), padding=8_8x0_0 | pad | bytes 1064962 | tf_op jit(solution)/shard_map/jit(_pad)/pad | solution.py:328
  54.3 4.0 %collective-permute-done.6.high_ref = bf16[528,256]{1,0:T(8,128)(2,1)S(1)} collective-permute-done((bf16[528,256]{1,0:T(8,128)(2,1)S(1)}, bf16[528,256]{1,0:T(8,128)(2,1)S(1)}, u32[]{:S(2)}, u32[]{:S(2)}) %collective-permute-start.6) | collective-permute-done | bytes 270368 | tf_op jit(solution)/shard_map/ppermute | solution.py:336
  58.3 0.7 %copy-done.3 = bf16[528,256]{1,0:T(8,128)(2,1)} copy-done((bf16[528,256]{1,0:T(8,128)(2,1)}, bf16[528,256]{1,0:T(8,128)(2,1)S(1)}, u32[]{:S(2)}) %copy-start.3) | copy-done | bytes 270360
  59.0 6.0 %shard_map.92 = f32[4,64,128]{2,1,0:T(8,128)} custom-call(s32[2]{0:T(128)} %add_convert_fusion.ends_ref, bf16[528,256]{1,0:T(8,128)(2,1)} %copy-done.2, bf16[528,512]{1,0:T(8,128)(2,1)} %pad.10.vol_ref, bf16[528,256]{1,0:T(8,128)(2,1)} %copy-done.3, bf16[3,3,128,144]{3,2,1,0:T(8,128)(2,1)} %bitcast.85, bf16[3,3,64,528]{3,2,1,0:T(8,128)(2,1)} %bitcast.81), custom_call_target="tpu_custom_call" | custom-call | tf_op jit(solution)/shard_map/pallas_call | solution.py:221
  (55 shorter events, 6.1 us)
Async XLA Ops:
  0.0 7.2 %copy-start = (bf16[3,3,3,8,8]{4,3,2,1,0:T(8,128)(2,1)S(1)}, bf16[3,3,3,8,8]{4,3,2,1,0:T(8,128)(2,1)}, u32[]{:S(2)}) copy-start(bf16[3,3,3,8,8]{4,3,2,1,0:T(8,128)(2,1)} %param.16) | copy-start | bytes 10372
  1.5 9.8 %collective-permute-start.2 = (bf16[32,640]{1,0:T(8,128)(2,1)S(1)}, bf16[32,640]{1,0:T(8,128)(2,1)S(1)}, u32[]{:S(2)}, u32[]{:S(2)}) collective-permute-start(bf16[32,640]{1,0:T(8,128)(2,1)S(1)} %get-tuple-element.10), channel_id=1, source_target_pairs={{0,12},{1,13},{2,14},{3,15},{4,8},{5,9},{6,10},{7,11},{8,4},{9,5},... | collective-permute-start | bytes 122888 | tf_op jit(solution)/shard_map/ppermute | solution.py:255
  2.8 8.5 %collective-permute-start.1 = (bf16[32,640]{1,0:T(8,128)(2,1)S(1)}, bf16[32,640]{1,0:T(8,128)(2,1)S(1)}, u32[]{:S(2)}, u32[]{:S(2)}) collective-permute-start(bf16[32,640]{1,0:T(8,128)(2,1)S(1)} %get-tuple-element.10), channel_id=1, source_target_pairs={{0,8},{1,9},{2,10},{3,11},{4,12},{5,13},{6,14},{7,15},{8,0},{9,1},... | collective-permute-start | bytes 122888 | tf_op jit(solution)/shard_map/ppermute | solution.py:255
  3.8 7.4 %collective-permute-start = (bf16[32,640]{1,0:T(8,128)(2,1)S(1)}, bf16[32,640]{1,0:T(8,128)(2,1)S(1)}, u32[]{:S(2)}, u32[]{:S(2)}) collective-permute-start(bf16[32,640]{1,0:T(8,128)(2,1)S(1)} %get-tuple-element.10), channel_id=1, source_target_pairs={{0,4},{1,5},{2,6},{3,7},{4,0},{5,1},{6,2},{7,3},{8,12},{9,13},{10,... | collective-permute-start | bytes 122888 | tf_op jit(solution)/shard_map/ppermute | solution.py:255
  7.2 1.6 %copy-start.1 = (bf16[1,32,8192]{2,1,0:T(8,128)(2,1)S(1)}, bf16[1,32,8192]{2,1,0:T(8,128)(2,1)}, u32[]{:S(2)}) copy-start(bf16[1,32,8192]{2,1,0:T(8,128)(2,1)} %param.9) | copy-start | bytes 1572868
  9.0 1.5 %copy-start.4 = (bf16[3,3,3,8]{3,2,1,0:T(4,128)(2,1)S(1)}, bf16[3,3,3,8]{3,2,1,0:T(4,128)(2,1)}, u32[]{:S(2)}) copy-start(bf16[3,3,3,8]{3,2,1,0:T(4,128)(2,1)} %param.17) | copy-start | bytes 1300
  12.0 4.2 %collective-permute-start.3 = (bf16[2,2,32,640]{3,2,1,0:T(8,128)(2,1)S(1)}, bf16[2,2,32,640]{3,2,1,0:T(8,128)(2,1)S(1)}, u32[]{:S(2)}, u32[]{:S(2)}) collective-permute-start(bf16[2,2,32,640]{3,2,1,0:T(8,128)(2,1)S(1)} %broadcast_select_fusion), channel_id=1, source_target_pairs={{0,2},{1,3},{2,0},{3,1},{4,6},{5,7},{6,4},{7,5},{8,10},{9,11},{10,... | collective-permute-start | bytes 491528 | tf_op jit(solution)/shard_map/ppermute | solution.py:263
  16.3 3.8 %collective-permute-start.4 = (bf16[2,2,2,32,640]{4,3,2,1,0:T(8,128)(2,1)S(1)}, bf16[2,2,2,32,640]{4,3,2,1,0:T(8,128)(2,1)S(1)}, u32[]{:S(2)}, u32[]{:S(2)}) collective-permute-start(bf16[2,2,2,32,640]{4,3,2,1,0:T(8,128)(2,1)S(1)} %maximum_select_fusion.1), channel_id=1, source_target_pairs={{0,1},{1,0},{2,3},{3,2},{4,5},{5,4},{6,7},{7,6},{8,9},{9,8},{10,11... | collective-permute-start | bytes 983048 | tf_op jit(solution)/shard_map/ppermute | solution.py:263
  25.1 20.1 %all-to-all-start = ((bf16[16,32,512]{2,1,0:T(8,128)(2,1)}), bf16[16,32,512]{2,1,0:T(8,128)(2,1)S(1)}, u32[]{:S(2)}, u32[]{:S(2)}) async-start(bf16[16,32,512]{2,1,0:T(8,128)(2,1)} %bitcast.88), calls=%async_computation | async-start | bytes 1048576 | tf_op jit(solution)/shard_map/all_to_all | solution.py:310
  45.9 8.4 %collective-permute-start.5 = (bf16[528,256]{1,0:T(8,128)(2,1)S(1)}, bf16[528,256]{1,0:T(8,128)(2,1)S(1)}, u32[]{:S(2)}, u32[]{:S(2)}) collective-permute-start(bf16[528,256]{1,0:T(8,128)(2,1)S(1)} %get-tuple-element.6), channel_id=1, source_target_pairs={{0,1},{1,2},{2,3},{3,4},{4,5},{5,6},{6,7},{7,8},{8,9},{9,10},{10,1... | collective-permute-start | bytes 811016 | tf_op jit(solution)/shard_map/ppermute | solution.py:335
  49.6 8.7 %collective-permute-start.6 = (bf16[528,256]{1,0:T(8,128)(2,1)S(1)}, bf16[528,256]{1,0:T(8,128)(2,1)S(1)}, u32[]{:S(2)}, u32[]{:S(2)}) collective-permute-start(bf16[528,256]{1,0:T(8,128)(2,1)S(1)} %get-tuple-element.5), channel_id=1, source_target_pairs={{1,0},{2,1},{3,2},{4,3},{5,4},{6,5},{7,6},{8,7},{9,8},{10,9},{11,1... | collective-permute-start | bytes 811016 | tf_op jit(solution)/shard_map/ppermute | solution.py:336
  54.3 4.0 %copy-start.2 = (bf16[528,256]{1,0:T(8,128)(2,1)}, bf16[528,256]{1,0:T(8,128)(2,1)S(1)}, u32[]{:S(2)}) copy-start(bf16[528,256]{1,0:T(8,128)(2,1)S(1)} %collective-permute-done.5.low_ref) | copy-start | bytes 811012
  58.3 0.7 %copy-start.3 = (bf16[528,256]{1,0:T(8,128)(2,1)}, bf16[528,256]{1,0:T(8,128)(2,1)S(1)}, u32[]{:S(2)}) copy-start(bf16[528,256]{1,0:T(8,128)(2,1)S(1)} %collective-permute-done.6.high_ref) | copy-start | bytes 811012

commit v15 on v14

--- a/solution.py
+++ b/solution.py
@@ -209,7 +209,15 @@
         framed, m1_ref, hidden, ends_ref, relu=True, rows=rows + 2, cols=cols, groups=groups, chunk=first
     )
     conv_body(
-        hidden, m2_ref, out_ref, None, relu=False, rows=rows, cols=cols, groups=groups, chunk=depth
+        hidden,
+        m2_ref,
+        out_ref,
+        None,
+        relu=False,
+        rows=rows,
+        cols=cols,
+        groups=groups,
+        chunk=m2_ref.shape[2],
     )
 
 
@@ -340,7 +348,7 @@
         volume,
         high,
         banded(kern_one, DEPTH // 4),
-        banded(kern_two, DEPTH),
+        banded(kern_two, DEPTH // 4),
         TROWS,
         columns,
     )

time: 65.4 us -> 64 us (0.979)
  local copies, waits for them, and re-layouts: 6.81 us -> 8.1 us
  waiting for transfers between devices: 20.8 us -> 19.7 us
  Pallas kernels: 10.1 us -> 9.03 us
  other arithmetic: 7.31 us -> 6.65 us
    unnamed x13 -> x11, local copies, waits for them, and re-layouts: 0.9 us -> 2.26 us
    ppermute x1, waiting for transfers between devices: 3.97 us -> 2.74 us  [body(): high = lax.ppermute(volume[:, :2 * columns], 'view', backward)]
    pallas_call x1, Pallas kernels: 5.97 us -> 4.88 us  [conv_pair(): pl.pallas_call(functools.partial(conv_pair_kernel, rows=rows, cols=cols,...]
    ppermute x3, starting transfers between devices: 3.49 us -> 2.65 us  [gather_view(): lax.ppermute(gathered, 'view', [(i, i ^ m * top) for i in range(count)])]
    reduce_sum x1, other arithmetic: 1.32 us -> 0.66 us  [banded(): mats = jnp.sum(jnp.where(band[:, None], tiles, 0.0), axis=0)]
where the time goes in v15:
time: 64 us; the launch traced here: 63.4 us
  waiting for transfers between devices  19.7 us (31%)
  starting transfers between devices  18.4 us (29%)
  Pallas kernels  9.03 us (14%)
  local copies, waits for them, and re-layouts  8.1 us (13%)
  other arithmetic  6.65 us (10%)
  matrix products  1.23 us (2%)
    all_to_all x1, waiting for transfers between devices, body(): lax.all_to_all(corr_all.reshape(owners, cap * GROUPS, tpix), 'view', spli...  12 us
    all_to_all x1, starting transfers between devices, body(): lax.all_to_all(corr_all.reshape(owners, cap * GROUPS, tpix), 'view', spli...  7.16 us
    ppermute x2, waiting for transfers between devices, gather_view(): lax.ppermute(gathered, 'view', [(i, i ^ stride) for i in range(count)])  4.99 us
    pallas_call x1, Pallas kernels, conv_pair(): pl.pallas_call(functools.partial(conv_pair_kernel, rows=rows, cols=cols,...  4.88 us
    pallas_call x1, Pallas kernels, correlate(): pl.pallas_call(correlate_kernel, out_shape=jax.ShapeDtypeStruct((units *...  4.15 us
    ppermute x1, starting transfers between devices, body(): lax.ppermute(volume[:, volume.shape[1] - 2 * columns:], 'view', forward)  3.63 us
    ppermute x2, starting transfers between devices, gather_view(): lax.ppermute(gathered, 'view', [(i, i ^ stride) for i in range(count)])  3.02 us
    ppermute x1, waiting for transfers between devices, body(): high = lax.ppermute(volume[:, :2 * columns], 'view', backward)  2.74 us
  transfers between devices with their start and end apart: 8, of which 4 were waited for; matrix products, arithmetic and copies ran while one was open for 17% of the time, Pallas kernels for 0%

profile of v15, /device:TPU:13, one launch (start us, length us, event | category | flops | bytes accessed | tf_op | source)
XLA Modules:
  0.0 63.4 jit_solution(12744961899380381162)
XLA Ops:
  0.0 0.7 %fusion.22 = bf16[64]{0:T(256)(128)(2,1)S(1)} fusion(s32[1,64]{1,0:T(1,128)} %param.15, s32[1,64]{1,0:T(1,128)} %param.14), kind=kLoop, calls=%fused_computation.65 | loop fusion | flops 192 | bytes 640 | tf_op jit(solution)/shard_map/convert_element_type | solution.py:311
  0.7 0.8 %fusion.24 = (bf16[1,32,640]{2,1,0:T(8,128)(2,1)S(1)}, bf16[32,640]{1,0:T(8,128)(2,1)S(1)}) fusion(bf16[32,128]{1,0:T(8,128)(2,1)S(1)} %pad_bitcast_fusion, bf16[32,512]{1,0:T(8,128)(2,1)} %bitcast.101), kind=kLoop, calls=%fused_computation.70 | loop fusion | flops 81920 | bytes 122880 | tf_op jit(solution)/shard_map/broadcast_in_dim | solution.py:314
  1.6 2.3 %collective-permute-start.1 = (bf16[32,640]{1,0:T(8,128)(2,1)S(1)}, bf16[32,640]{1,0:T(8,128)(2,1)S(1)}, u32[]{:S(2)}, u32[]{:S(2)}) collective-permute-start(bf16[32,640]{1,0:T(8,128)(2,1)S(1)} %get-tuple-element.10), channel_id=1, source_target_pairs={{0,8},{1,9},{2,10},{3,11},{4,12},{5,13},{6,14},{7,15},{8,0},{9,1},... | collective-permute-start | bytes 122888 | tf_op jit(solution)/shard_map/ppermute | solution.py:263
  4.8 0.7 %select_reduce_fusion.1 = s32[64,4]{0,1:T(4,128)S(1)} fusion(s32[64,4]{0,1:T(4,128)} %bitcast.104, s32[64,4]{0,1:T(4,128)} %bitcast.102), kind=kLoop, calls=%fused_computation.31 | loop fusion | flops 2816 | bytes 3072 | tf_op jit(solution)/shard_map/reduce_sum | solution.py:308
  5.6 0.7 %fusion.10 = pred[64,4]{0,1:T(4,128)(4,1)S(1)} fusion(s32[64,4]{0,1:T(4,128)} %bitcast.103, pred[64,4]{0,1:T(4,128)(4,1)S(1)} %iota_compare_fusion.3), kind=kLoop, calls=%fused_computation.37 | loop fusion | flops 2816 | bytes 1536 | tf_op jit(solution)/shard_map/reduce_or | solution.py:309
  6.5 0.7 %select_n.189.blk_ref = s32[256]{0:T(256)} reshape(s32[64,4]{1,0:T(8,128)S(1)} %copy.42) | data formatting | bytes 2048 | tf_op jit(solution)/shard_map/jit(_where)/select_n | solution.py:310
  7.2 1.2 %copy.54 = bf16[4,8,64,128]{3,2,1,0:T(8,128)(2,1)S(1)} copy(bf16[4,8,64,128]{3,1,2,0:T(8,128)(2,1)} %bitcast.90) | data formatting | bytes 1048576
  9.0 0.8 %concatenate.21.blocks_ref = bf16[65,32,128]{2,1,0:T(8,128)(2,1)} pad(bf16[64,32,128]{2,1,0:T(8,128)(2,1)S(1)} %bitcast.85, bf16[]{:T(256)} %constant.134.clone.1), padding=0_1x0_0x0_0 | pad | bytes 1056770 | tf_op jit(solution)/shard_map/concatenate | solution.py:305
  11.1 3.8 %collective-permute-done.3 = bf16[2,2,32,640]{3,2,1,0:T(8,128)(2,1)S(1)} collective-permute-done((bf16[2,2,32,640]{3,2,1,0:T(8,128)(2,1)S(1)}, bf16[2,2,32,640]{3,2,1,0:T(8,128)(2,1)S(1)}, u32[]{:S(2)}, u32[]{:S(2)}) %collective-permute-start.3) | collective-permute-done | bytes 163872 | tf_op jit(solution)/shard_map/ppermute | solution.py:271
  15.0 2.7 %collective-permute-start.4 = (bf16[2,2,2,32,640]{4,3,2,1,0:T(8,128)(2,1)S(1)}, bf16[2,2,2,32,640]{4,3,2,1,0:T(8,128)(2,1)S(1)}, u32[]{:S(2)}, u32[]{:S(2)}) collective-permute-start(bf16[2,2,2,32,640]{4,3,2,1,0:T(8,128)(2,1)S(1)} %maximum_select_fusion.1), channel_id=1, source_target_pairs={{0,1},{1,0},{2,3},{3,2},{4,5},{5,4},{6,7},{7,6},{8,9},{9,8},{10,11... | collective-permute-start | bytes 983048 | tf_op jit(solution)/shard_map/ppermute | solution.py:271
  17.8 1.1 %collective-permute-done.4 = bf16[2,2,2,32,640]{4,3,2,1,0:T(8,128)(2,1)S(1)} collective-permute-done((bf16[2,2,2,32,640]{4,3,2,1,0:T(8,128)(2,1)S(1)}, bf16[2,2,2,32,640]{4,3,2,1,0:T(8,128)(2,1)S(1)}, u32[]{:S(2)}, u32[]{:S(2)}) %collective-permute-start.4) | collective-permute-done | bytes 327712 | tf_op jit(solution)/shard_map/ppermute | solution.py:271
  19.0 0.9 %maximum_select_fusion = bf16[2,2,2,2,32,640]{5,4,3,2,1,0:T(8,128)(2,1)} fusion(bf16[2,2,2,1,32,640]{5,4,3,2,1,0:T(8,128)(2,1)S(1)} %bitcast.94, bf16[2,2,2,1,32,640]{5,4,3,2,1,0:T(8,128)(2,1)S(1)} %copy_select_fusion, pred[]{:T(512)S(6)} %eq.126), kind=kLoop, calls=%fused_computation.8 | loop fusion | flops 983040 | bytes 1310721 | tf_op jit(solution)/shard_map/jit(_where)/select_n | solution.py:273
  19.9 4.2 %shard_map.91 = bf16[512,512]{1,0:T(8,128)(2,1)} custom-call(s32[256]{0:T(256)} %select_n.189.blk_ref, bf16[65,32,128]{2,1,0:T(8,128)(2,1)} %concatenate.21.blocks_ref, bf16[512,512]{1,0:T(8,128)(2,1)} %bitcast.93, bf16[16,32,640]{2,1,0:T(8,128)(2,1)} %bitcast.79), custom_call_target="tpu_custom_call" | custom-call | tf_op jit(solution)/shard_map/pallas_call | solution.py:121
  24.0 7.2 %all-to-all-start = ((bf16[16,32,512]{2,1,0:T(8,128)(2,1)}), bf16[16,32,512]{2,1,0:T(8,128)(2,1)S(1)}, u32[]{:S(2)}, u32[]{:S(2)}) async-start(bf16[16,32,512]{2,1,0:T(8,128)(2,1)} %bitcast.87), calls=%async_computation | async-start | bytes 1048576 | tf_op jit(solution)/shard_map/all_to_all | solution.py:318
  31.4 0.9 %slice.14 = bf16[16,32,128]{2,1,0:T(8,128)(2,1)S(1)} slice(bf16[16,32,640]{2,1,0:T(8,128)(2,1)} %bitcast.80), slice={[0:16], [0:32], [512:640]} | slice | bytes 262144 | tf_op jit(solution)/shard_map/slice | solution.py:326
  32.8 12.0 %all-to-all-done = bf16[16,32,512]{2,1,0:T(8,128)(2,1)S(1)} async-done(((bf16[16,32,512]{2,1,0:T(8,128)(2,1)}), bf16[16,32,512]{2,1,0:T(8,128)(2,1)S(1)}, u32[]{:S(2)}, u32[]{:S(2)}) %all-to-all-start) | async-done | bytes 524320 | tf_op jit(solution)/shard_map/all_to_all | solution.py:318
  45.5 3.6 %collective-permute-start.5 = (bf16[528,256]{1,0:T(8,128)(2,1)S(1)}, bf16[528,256]{1,0:T(8,128)(2,1)S(1)}, u32[]{:S(2)}, u32[]{:S(2)}) collective-permute-start(bf16[528,256]{1,0:T(8,128)(2,1)S(1)} %get-tuple-element.6), channel_id=1, source_target_pairs={{0,1},{1,2},{2,3},{3,4},{4,5},{5,6},{6,7},{7,8},{8,9},{9,10},{10,1... | collective-permute-start | bytes 811016 | tf_op jit(solution)/shard_map/ppermute | solution.py:343
  49.1 1.9 %collective-permute-start.6 = (bf16[528,256]{1,0:T(8,128)(2,1)S(1)}, bf16[528,256]{1,0:T(8,128)(2,1)S(1)}, u32[]{:S(2)}, u32[]{:S(2)}) collective-permute-start(bf16[528,256]{1,0:T(8,128)(2,1)S(1)} %get-tuple-element.5), channel_id=1, source_target_pairs={{1,0},{2,1},{3,2},{4,3},{5,4},{6,5},{7,6},{8,7},{9,8},{10,9},{11,1... | collective-permute-start | bytes 811016 | tf_op jit(solution)/shard_map/ppermute | solution.py:344
  51.1 0.7 %fusion = bf16[9,128,144]{1,2,0:T(8,128)(2,1)S(1)} fusion(bf16[3,9,8,8]{3,2,1,0:T(8,128)(2,1)S(1)} %bitcast.76, pred[3,128,144]{1,2,0:T(8,128)(4,1)S(1)} %broadcast_compare_fusion, s32[144]{0:T(256)S(1)} %and_select_fusion.1, s32[128]{0:T(128)S(1)} %and_select_fusion), kind=kOutput, calls=%fused_computation.2 | convolution fusion | flops 9323008 | bytes 391616 | tf_op jit(solution)/shard_map/ro,xyoc->xyrc/dot_general | solution.py:184
  51.8 1.1 %copy.47 = bf16[9,128,144]{2,1,0:T(8,128)(2,1)} copy(bf16[9,128,144]{1,2,0:T(8,128)(2,1)S(1)} %fusion) | data formatting | bytes 663552 | tf_op jit(solution)/shard_map/convert_element_type | solution.py:195
  54.2 0.8 %pad.10.vol_ref = bf16[528,512]{1,0:T(8,128)(2,1)} pad(bf16[512,512]{1,0:T(8,128)(2,1)S(1)} %bitcast.78, bf16[]{:T(256)} %constant.134.clone.1), padding=8_8x0_0 | pad | bytes 1064962 | tf_op jit(solution)/shard_map/jit(_pad)/pad | solution.py:336
  55.1 2.7 %collective-permute-done.6.high_ref = bf16[528,256]{1,0:T(8,128)(2,1)S(1)} collective-permute-done((bf16[528,256]{1,0:T(8,128)(2,1)S(1)}, bf16[528,256]{1,0:T(8,128)(2,1)S(1)}, u32[]{:S(2)}, u32[]{:S(2)}) %collective-permute-start.6) | collective-permute-done | bytes 270368 | tf_op jit(solution)/shard_map/ppermute | solution.py:344
  57.8 0.7 %copy-done.2 = bf16[528,256]{1,0:T(8,128)(2,1)} copy-done((bf16[528,256]{1,0:T(8,128)(2,1)}, bf16[528,256]{1,0:T(8,128)(2,1)S(1)}, u32[]{:S(2)}) %copy-start.2) | copy-done | bytes 270360
  58.5 4.9 %shard_map.92 = f32[4,64,128]{2,1,0:T(8,128)} custom-call(s32[2]{0:T(128)} %add_convert_fusion.ends_ref, bf16[528,256]{1,0:T(8,128)(2,1)} %copy-done.1, bf16[528,512]{1,0:T(8,128)(2,1)} %pad.10.vol_ref, bf16[528,256]{1,0:T(8,128)(2,1)} %copy-done.2, bf16[3,3,128,144]{3,2,1,0:T(8,128)(2,1)} %bitcast.84, bf16[3,3,16,144]{3,2,1,0:T(8,128)(2,1)} %bitcast.95), custom_call_target="tpu_custom_call" | custom-call | tf_op jit(solution)/shard_map/pallas_call | solution.py:229
  (51 shorter events, 5.9 us)
Async XLA Ops:
  0.0 51.1 %copy-start = (bf16[3,3,3,8,8]{4,3,2,1,0:T(8,128)(2,1)S(1)}, bf16[3,3,3,8,8]{4,3,2,1,0:T(8,128)(2,1)}, u32[]{:S(2)}) copy-start(bf16[3,3,3,8,8]{4,3,2,1,0:T(8,128)(2,1)} %param.16) | copy-start | bytes 10372
  1.5 8.4 %collective-permute-start = (bf16[32,640]{1,0:T(8,128)(2,1)S(1)}, bf16[32,640]{1,0:T(8,128)(2,1)S(1)}, u32[]{:S(2)}, u32[]{:S(2)}) collective-permute-start(bf16[32,640]{1,0:T(8,128)(2,1)S(1)} %get-tuple-element.10), channel_id=1, source_target_pairs={{0,4},{1,5},{2,6},{3,7},{4,0},{5,1},{6,2},{7,3},{8,12},{9,13},{10,... | collective-permute-start | bytes 122888 | tf_op jit(solution)/shard_map/ppermute | solution.py:263
  1.6 8.2 %collective-permute-start.1 = (bf16[32,640]{1,0:T(8,128)(2,1)S(1)}, bf16[32,640]{1,0:T(8,128)(2,1)S(1)}, u32[]{:S(2)}, u32[]{:S(2)}) collective-permute-start(bf16[32,640]{1,0:T(8,128)(2,1)S(1)} %get-tuple-element.10), channel_id=1, source_target_pairs={{0,8},{1,9},{2,10},{3,11},{4,12},{5,13},{6,14},{7,15},{8,0},{9,1},... | collective-permute-start | bytes 122888 | tf_op jit(solution)/shard_map/ppermute | solution.py:263
  3.9 5.9 %collective-permute-start.2 = (bf16[32,640]{1,0:T(8,128)(2,1)S(1)}, bf16[32,640]{1,0:T(8,128)(2,1)S(1)}, u32[]{:S(2)}, u32[]{:S(2)}) collective-permute-start(bf16[32,640]{1,0:T(8,128)(2,1)S(1)} %get-tuple-element.10), channel_id=1, source_target_pairs={{0,12},{1,13},{2,14},{3,15},{4,8},{5,9},{6,10},{7,11},{8,4},{9,5},... | collective-permute-start | bytes 122888 | tf_op jit(solution)/shard_map/ppermute | solution.py:263
  8.3 0.7 %copy-start.3 = (bf16[3,3,3,8]{3,2,1,0:T(4,128)(2,1)S(1)}, bf16[3,3,3,8]{3,2,1,0:T(4,128)(2,1)}, u32[]{:S(2)}) copy-start(bf16[3,3,3,8]{3,2,1,0:T(4,128)(2,1)} %param.17) | copy-start | bytes 1300
  10.7 4.2 %collective-permute-start.3 = (bf16[2,2,32,640]{3,2,1,0:T(8,128)(2,1)S(1)}, bf16[2,2,32,640]{3,2,1,0:T(8,128)(2,1)S(1)}, u32[]{:S(2)}, u32[]{:S(2)}) collective-permute-start(bf16[2,2,32,640]{3,2,1,0:T(8,128)(2,1)S(1)} %broadcast_select_fusion), channel_id=1, source_target_pairs={{0,2},{1,3},{2,0},{3,1},{4,6},{5,7},{6,4},{7,5},{8,10},{9,11},{10,... | collective-permute-start | bytes 491528 | tf_op jit(solution)/shard_map/ppermute | solution.py:271
  15.0 4.0 %collective-permute-start.4 = (bf16[2,2,2,32,640]{4,3,2,1,0:T(8,128)(2,1)S(1)}, bf16[2,2,2,32,640]{4,3,2,1,0:T(8,128)(2,1)S(1)}, u32[]{:S(2)}, u32[]{:S(2)}) collective-permute-start(bf16[2,2,2,32,640]{4,3,2,1,0:T(8,128)(2,1)S(1)} %maximum_select_fusion.1), channel_id=1, source_target_pairs={{0,1},{1,0},{2,3},{3,2},{4,5},{5,4},{6,7},{7,6},{8,9},{9,8},{10,11... | collective-permute-start | bytes 983048 | tf_op jit(solution)/shard_map/ppermute | solution.py:271
  24.0 20.8 %all-to-all-start = ((bf16[16,32,512]{2,1,0:T(8,128)(2,1)}), bf16[16,32,512]{2,1,0:T(8,128)(2,1)S(1)}, u32[]{:S(2)}, u32[]{:S(2)}) async-start(bf16[16,32,512]{2,1,0:T(8,128)(2,1)} %bitcast.87), calls=%async_computation | async-start | bytes 1048576 | tf_op jit(solution)/shard_map/all_to_all | solution.py:318
  45.5 9.6 %collective-permute-start.5 = (bf16[528,256]{1,0:T(8,128)(2,1)S(1)}, bf16[528,256]{1,0:T(8,128)(2,1)S(1)}, u32[]{:S(2)}, u32[]{:S(2)}) collective-permute-start(bf16[528,256]{1,0:T(8,128)(2,1)S(1)} %get-tuple-element.6), channel_id=1, source_target_pairs={{0,1},{1,2},{2,3},{3,4},{4,5},{5,6},{6,7},{7,8},{8,9},{9,10},{10,1... | collective-permute-start | bytes 811016 | tf_op jit(solution)/shard_map/ppermute | solution.py:343
  49.1 8.7 %collective-permute-start.6 = (bf16[528,256]{1,0:T(8,128)(2,1)S(1)}, bf16[528,256]{1,0:T(8,128)(2,1)S(1)}, u32[]{:S(2)}, u32[]{:S(2)}) collective-permute-start(bf16[528,256]{1,0:T(8,128)(2,1)S(1)} %get-tuple-element.5), channel_id=1, source_target_pairs={{1,0},{2,1},{3,2},{4,3},{5,4},{6,5},{7,6},{8,7},{9,8},{10,9},{11,1... | collective-permute-start | bytes 811016 | tf_op jit(solution)/shard_map/ppermute | solution.py:344
  55.1 2.7 %copy-start.1 = (bf16[528,256]{1,0:T(8,128)(2,1)}, bf16[528,256]{1,0:T(8,128)(2,1)S(1)}, u32[]{:S(2)}) copy-start(bf16[528,256]{1,0:T(8,128)(2,1)S(1)} %collective-permute-done.5.low_ref) | copy-start | bytes 811012
  57.8 0.7 %copy-start.2 = (bf16[528,256]{1,0:T(8,128)(2,1)}, bf16[528,256]{1,0:T(8,128)(2,1)S(1)}, u32[]{:S(2)}) copy-start(bf16[528,256]{1,0:T(8,128)(2,1)S(1)} %collective-permute-done.6.high_ref) | copy-start | bytes 811012

commit v16 on v15

--- a/solution.py
+++ b/solution.py
@@ -312,6 +312,9 @@
 
     tag_block = jnp.pad(depth_code, (0, channels * 128 - units)).reshape(channels, 128)
     ref_all = gather_view(jnp.concatenate([ref_feat[0], tag_block], axis=1)[None])
+    ref_all, first, second = lax.optimization_barrier(
+        (ref_all, banded(kern_one, DEPTH // 4), banded(kern_two, DEPTH // 4))
+    )
     corr_all = correlate(
         blk, blocks, weight_table.reshape(slots * block_width, tpix), ref_all, units
     )
@@ -325,15 +328,15 @@
     depth_tags = lax.dynamic_slice_in_dim(
         ref_all[:, :, tpix:].reshape(owners, channels * 128), lax.axis_index("view") * cap, cap, axis=1
     ).reshape(owners * cap)
+    labels = jnp.arange(-1, DEPTH + 1).at[0].set(-2)
     onehot = (
-        depth_tags[None, :] == jnp.arange(DEPTH).astype(jnp.bfloat16)[:, None]
+        depth_tags[None, :] == labels.astype(jnp.bfloat16)[:, None]
     ).astype(jnp.bfloat16)
     summed = jnp.einsum("dn,ngp->dgp", onehot, arriving, preferred_element_type=jnp.float32)
     tallies = jnp.sum(onehot.astype(jnp.float32), axis=1)
     cost_volume = (summed / jnp.maximum(tallies, 1.0)[:, None, None]).astype(jnp.bfloat16)
     columns = tpix // TROWS
-    volume = cost_volume.reshape(DEPTH * GROUPS, TROWS * columns)
-    volume = jnp.pad(volume, ((GROUPS, GROUPS), (0, 0)))
+    volume = cost_volume.reshape((DEPTH + 2) * GROUPS, TROWS * columns)
     count = lax.axis_size("view")
     place = lax.axis_index("view")
     ends = jnp.stack([place == 0, place == count - 1]).astype(jnp.int32)
@@ -347,8 +350,8 @@
         low,
         volume,
         high,
-        banded(kern_one, DEPTH // 4),
-        banded(kern_two, DEPTH // 4),
+        first,
+        second,
         TROWS,
         columns,
     )

time: 64 us -> 66 us (1.031)
  waiting for transfers between devices: 19.7 us -> 23.4 us
  local copies, waits for them, and re-layouts: 8.1 us -> 6.54 us
    ppermute x1, waiting for transfers between devices: 2.74 us -> 5.27 us  [body(): high = lax.ppermute(volume[:, :2 * columns], 'view', backward)]
    pad x1 -> x0, local copies, waits for them, and re-layouts: 0.84 us -> none  [body(): volume = jnp.pad(volume, ((GROUPS, GROUPS), (0, 0)))]
    ppermute x1, waiting for transfers between devices: 0.01 us -> 0.82 us  [body(): lax.ppermute(volume[:, volume.shape[1] - 2 * columns:], 'view', forward)]
    unnamed x11 -> x13, local copies, waits for them, and re-layouts: 2.26 us -> 1.6 us
  transfers between devices with their start and end apart: 8 -> 8, of which waited for: 4 -> 5; matrix products, arithmetic and copies ran while one was open for 17% -> 15% of each run, Pallas kernels for 0% -> 0%
where the time goes in v16:
time: 66 us; the launch traced here: 65.4 us
  waiting for transfers between devices  23.4 us (35%)
  starting transfers between devices  18.4 us (28%)
  Pallas kernels  9.03 us (14%)
  other arithmetic  6.56 us (10%)
  local copies, waits for them, and re-layouts  6.54 us (10%)
  matrix products  1.31 us (2%)
    all_to_all x1, waiting for transfers between devices, body(): lax.all_to_all(corr_all.reshape(owners, cap * GROUPS, tpix), 'view', spli...  12.3 us
    all_to_all x1, starting transfers between devices, body(): lax.all_to_all(corr_all.reshape(owners, cap * GROUPS, tpix), 'view', spli...  7.14 us
    ppermute x1, waiting for transfers between devices, body(): high = lax.ppermute(volume[:, :2 * columns], 'view', backward)  5.27 us
    ppermute x2, waiting for transfers between devices, gather_view(): lax.ppermute(gathered, 'view', [(i, i ^ stride) for i in range(count)])  4.99 us
    pallas_call x1, Pallas kernels, conv_pair(): pl.pallas_call(functools.partial(conv_pair_kernel, rows=rows, cols=cols,...  4.88 us
    pallas_call x1, Pallas kernels, correlate(): pl.pallas_call(correlate_kernel, out_shape=jax.ShapeDtypeStruct((units *...  4.15 us
    ppermute x1, starting transfers between devices, body(): lax.ppermute(volume[:, volume.shape[1] - 2 * columns:], 'view', forward)  3.64 us
    ppermute x2, starting transfers between devices, gather_view(): lax.ppermute(gathered, 'view', [(i, i ^ stride) for i in range(count)])  3.02 us
  transfers between devices with their start and end apart: 8, of which 5 were waited for; matrix products, arithmetic and copies ran while one was open for 15% of the time, Pallas kernels for 0%

profile of v16, /device:TPU:13, one launch (start us, length us, event | category | flops | bytes accessed | tf_op | source)
XLA Modules:
  0.0 65.4 jit_solution(16478684616209339186)
XLA Ops:
  0.0 0.7 %fusion.22 = bf16[64]{0:T(256)(128)(2,1)S(1)} fusion(s32[1,64]{1,0:T(1,128)} %param.17, s32[1,64]{1,0:T(1,128)} %param.16), kind=kLoop, calls=%fused_computation.65 | loop fusion | flops 192 | bytes 640 | tf_op jit(solution)/shard_map/convert_element_type | solution.py:311
  0.7 0.8 %fusion.24 = (bf16[1,32,640]{2,1,0:T(8,128)(2,1)S(1)}, bf16[32,640]{1,0:T(8,128)(2,1)S(1)}) fusion(bf16[32,128]{1,0:T(8,128)(2,1)S(1)} %pad_bitcast_fusion, bf16[32,512]{1,0:T(8,128)(2,1)} %bitcast.101), kind=kLoop, calls=%fused_computation.71 | loop fusion | flops 81920 | bytes 122880 | tf_op jit(solution)/shard_map/broadcast_in_dim | solution.py:314
  1.6 2.3 %collective-permute-start.1 = (bf16[32,640]{1,0:T(8,128)(2,1)S(1)}, bf16[32,640]{1,0:T(8,128)(2,1)S(1)}, u32[]{:S(2)}, u32[]{:S(2)}) collective-permute-start(bf16[32,640]{1,0:T(8,128)(2,1)S(1)} %get-tuple-element.28), channel_id=1, source_target_pairs={{0,8},{1,9},{2,10},{3,11},{4,12},{5,13},{6,14},{7,15},{8,0},{9,1},... | collective-permute-start | bytes 122888 | tf_op jit(solution)/shard_map/ppermute | solution.py:263
  4.2 0.7 %copy.44 = bf16[3,3,3,8]{3,0,2,1:T(4,128)(2,1)S(1)} copy(bf16[3,3,3,8]{3,2,1,0:T(4,128)(2,1)} %param.19) | data formatting | bytes 864 | tf_op args[8]
  5.7 0.7 %select_reduce_fusion.1 = s32[64,4]{0,1:T(4,128)S(1)} fusion(s32[64,4]{0,1:T(4,128)} %bitcast.104, s32[64,4]{0,1:T(4,128)} %bitcast.102), kind=kLoop, calls=%fused_computation.28 | loop fusion | flops 2816 | bytes 3072 | tf_op jit(solution)/shard_map/reduce_sum | solution.py:308
  6.4 0.7 %fusion.10 = pred[64,4]{0,1:T(4,128)(4,1)S(1)} fusion(s32[64,4]{0,1:T(4,128)} %bitcast.103, pred[64,4]{0,1:T(4,128)(4,1)S(1)} %iota_compare_fusion.3), kind=kLoop, calls=%fused_computation.37 | loop fusion | flops 2816 | bytes 1536 | tf_op jit(solution)/shard_map/reduce_or | solution.py:309
  7.3 0.7 %select_reduce_fusion = bf16[9,16,144]{2,1,0:T(8,128)(2,1)} fusion(f32[3,9,144]{2,1,0:T(8,128)S(1)} %convolution_bitcast_fusion, pred[3,16,144]{2,1,0:T(8,128)(4,1)S(1)} %broadcast_compare_fusion.1), kind=kLoop, calls=%fused_computation.12 | loop fusion | flops 103680 | bytes 63936 | tf_op jit(solution)/shard_map/reduce_sum | solution.py:194
  7.9 0.7 %fusion = bf16[9,128,144]{1,2,0:T(8,128)(2,1)S(1)} fusion(bf16[3,9,8,8]{3,2,1,0:T(8,128)(2,1)S(1)} %bitcast.76, pred[3,128,144]{1,2,0:T(8,128)(4,1)S(1)} %broadcast_compare_fusion, s32[144]{0:T(256)S(1)} %and_select_fusion.1, s32[128]{0:T(128)S(1)} %get-tuple-element.29), kind=kOutput, calls=%fused_computation.2 | convolution fusion | flops 9323008 | bytes 391616 | tf_op jit(solution)/shard_map/ro,xyoc->xyrc/dot_general | solution.py:184
  8.8 1.1 %copy.43 = bf16[9,128,144]{2,1,0:T(8,128)(2,1)} copy(bf16[9,128,144]{1,2,0:T(8,128)(2,1)S(1)} %fusion) | data formatting | bytes 663552 | tf_op jit(solution)/shard_map/convert_element_type | solution.py:195
  11.1 0.9 %concatenate.23.blocks_ref = bf16[65,32,128]{2,1,0:T(8,128)(2,1)} pad(bf16[64,32,128]{2,1,0:T(8,128)(2,1)S(1)} %bitcast.85, bf16[]{:T(256)} %constant.159.clone.1), padding=0_1x0_0x0_0 | pad | bytes 1056770 | tf_op jit(solution)/shard_map/concatenate | solution.py:305
  13.2 3.8 %collective-permute-done.3 = bf16[2,2,32,640]{3,2,1,0:T(8,128)(2,1)S(1)} collective-permute-done((bf16[2,2,32,640]{3,2,1,0:T(8,128)(2,1)S(1)}, bf16[2,2,32,640]{3,2,1,0:T(8,128)(2,1)S(1)}, u32[]{:S(2)}, u32[]{:S(2)}) %collective-permute-start.3) | collective-permute-done | bytes 163872 | tf_op jit(solution)/shard_map/ppermute | solution.py:271
  17.1 2.7 %collective-permute-start.4 = (bf16[2,2,2,32,640]{4,3,2,1,0:T(8,128)(2,1)S(1)}, bf16[2,2,2,32,640]{4,3,2,1,0:T(8,128)(2,1)S(1)}, u32[]{:S(2)}, u32[]{:S(2)}) collective-permute-start(bf16[2,2,2,32,640]{4,3,2,1,0:T(8,128)(2,1)S(1)} %maximum_select_fusion.1), channel_id=1, source_target_pairs={{0,1},{1,0},{2,3},{3,2},{4,5},{5,4},{6,7},{7,6},{8,9},{9,8},{10,11... | collective-permute-start | bytes 983048 | tf_op jit(solution)/shard_map/ppermute | solution.py:271
  19.9 1.1 %collective-permute-done.4 = bf16[2,2,2,32,640]{4,3,2,1,0:T(8,128)(2,1)S(1)} collective-permute-done((bf16[2,2,2,32,640]{4,3,2,1,0:T(8,128)(2,1)S(1)}, bf16[2,2,2,32,640]{4,3,2,1,0:T(8,128)(2,1)S(1)}, u32[]{:S(2)}, u32[]{:S(2)}) %collective-permute-start.4) | collective-permute-done | bytes 327712 | tf_op jit(solution)/shard_map/ppermute | solution.py:271
  21.0 0.9 %maximum_select_fusion = bf16[2,2,2,2,32,640]{5,4,3,2,1,0:T(8,128)(2,1)} fusion(bf16[2,2,2,1,32,640]{5,4,3,2,1,0:T(8,128)(2,1)S(1)} %bitcast.94, bf16[2,2,2,1,32,640]{5,4,3,2,1,0:T(8,128)(2,1)S(1)} %copy_select_fusion, pred[]{:T(512)S(6)} %eq.126), kind=kLoop, calls=%fused_computation.8 | loop fusion | flops 983040 | bytes 1310721 | tf_op jit(solution)/shard_map/jit(_where)/select_n | solution.py:273
  22.0 4.1 %shard_map.91 = bf16[512,512]{1,0:T(8,128)(2,1)} custom-call(s32[256]{0:T(256)} %select_n.195.blk_ref, bf16[65,32,128]{2,1,0:T(8,128)(2,1)} %concatenate.23.blocks_ref, bf16[512,512]{1,0:T(8,128)(2,1)} %bitcast.93, bf16[16,32,640]{2,1,0:T(8,128)(2,1)} %bitcast.79), custom_call_target="tpu_custom_call" | custom-call | tf_op jit(solution)/shard_map/pallas_call | solution.py:121
  26.1 7.1 %all-to-all-start = ((bf16[16,32,512]{2,1,0:T(8,128)(2,1)}), bf16[16,32,512]{2,1,0:T(8,128)(2,1)S(1)}, u32[]{:S(2)}, u32[]{:S(2)}) async-start(bf16[16,32,512]{2,1,0:T(8,128)(2,1)} %bitcast.87), calls=%async_computation | async-start | bytes 1048576 | tf_op jit(solution)/shard_map/all_to_all | solution.py:321
  33.3 0.9 %slice.19 = bf16[16,32,128]{2,1,0:T(8,128)(2,1)S(1)} slice(bf16[16,32,640]{2,1,0:T(8,128)(2,1)} %bitcast.80), slice={[0:16], [0:32], [512:640]} | slice | bytes 262144 | tf_op jit(solution)/shard_map/slice | solution.py:329
  34.6 12.3 %all-to-all-done = bf16[16,32,512]{2,1,0:T(8,128)(2,1)S(1)} async-done(((bf16[16,32,512]{2,1,0:T(8,128)(2,1)}), bf16[16,32,512]{2,1,0:T(8,128)(2,1)S(1)}, u32[]{:S(2)}, u32[]{:S(2)}) %all-to-all-start) | async-done | bytes 524320 | tf_op jit(solution)/shard_map/all_to_all | solution.py:321
  47.5 3.6 %collective-permute-start.5 = (bf16[528,256]{1,0:T(8,128)(2,1)S(1)}, bf16[528,256]{1,0:T(8,128)(2,1)S(1)}, u32[]{:S(2)}, u32[]{:S(2)}) collective-permute-start(bf16[528,256]{1,0:T(8,128)(2,1)S(1)} %get-tuple-element.24), channel_id=1, source_target_pairs={{0,1},{1,2},{2,3},{3,4},{4,5},{5,6},{6,7},{7,8},{8,9},{9,10},{10,1... | collective-permute-start | bytes 811016 | tf_op jit(solution)/shard_map/ppermute | solution.py:346
  51.2 1.9 %collective-permute-start.6 = (bf16[528,256]{1,0:T(8,128)(2,1)S(1)}, bf16[528,256]{1,0:T(8,128)(2,1)S(1)}, u32[]{:S(2)}, u32[]{:S(2)}) collective-permute-start(bf16[528,256]{1,0:T(8,128)(2,1)S(1)} %get-tuple-element.23), channel_id=1, source_target_pairs={{1,0},{2,1},{3,2},{4,3},{5,4},{6,5},{7,6},{8,7},{9,8},{10,9},{11,1... | collective-permute-start | bytes 811016 | tf_op jit(solution)/shard_map/ppermute | solution.py:347
  53.8 0.8 %collective-permute-done.5.low_ref = bf16[528,256]{1,0:T(8,128)(2,1)S(1)} collective-permute-done((bf16[528,256]{1,0:T(8,128)(2,1)S(1)}, bf16[528,256]{1,0:T(8,128)(2,1)S(1)}, u32[]{:S(2)}, u32[]{:S(2)}) %collective-permute-start.5) | collective-permute-done | bytes 270368 | tf_op jit(solution)/shard_map/ppermute | solution.py:346
  54.6 5.3 %collective-permute-done.6.high_ref = bf16[528,256]{1,0:T(8,128)(2,1)S(1)} collective-permute-done((bf16[528,256]{1,0:T(8,128)(2,1)S(1)}, bf16[528,256]{1,0:T(8,128)(2,1)S(1)}, u32[]{:S(2)}, u32[]{:S(2)}) %collective-permute-start.6) | collective-permute-done | bytes 270368 | tf_op jit(solution)/shard_map/ppermute | solution.py:347
  59.9 0.7 %copy-done.4 = bf16[528,256]{1,0:T(8,128)(2,1)} copy-done((bf16[528,256]{1,0:T(8,128)(2,1)}, bf16[528,256]{1,0:T(8,128)(2,1)S(1)}, u32[]{:S(2)}) %copy-start.4) | copy-done | bytes 270360
  60.6 4.9 %shard_map.92 = f32[4,64,128]{2,1,0:T(8,128)} custom-call(s32[2]{0:T(128)} %add_convert_fusion.ends_ref, bf16[528,256]{1,0:T(8,128)(2,1)} %copy-done.3, bf16[528,512]{1,0:T(8,128)(2,1)} %bitcast.78, bf16[528,256]{1,0:T(8,128)(2,1)} %copy-done.4, bf16[3,3,128,144]{3,2,1,0:T(8,128)(2,1)} %bitcast.84, bf16[3,3,16,144]{3,2,1,0:T(8,128)(2,1)} %bitcast.95), custom_call_target="tpu_custom_call" | custom-call | tf_op jit(solution)/shard_map/pallas_call | solution.py:229
  (53 shorter events, 5.6 us)
Async XLA Ops:
  0.0 7.9 %copy-start = (bf16[3,3,3,8,8]{4,3,2,1,0:T(8,128)(2,1)S(1)}, bf16[3,3,3,8,8]{4,3,2,1,0:T(8,128)(2,1)}, u32[]{:S(2)}) copy-start(bf16[3,3,3,8,8]{4,3,2,1,0:T(8,128)(2,1)} %param.18) | copy-start | bytes 10372
  1.5 10.5 %collective-permute-start = (bf16[32,640]{1,0:T(8,128)(2,1)S(1)}, bf16[32,640]{1,0:T(8,128)(2,1)S(1)}, u32[]{:S(2)}, u32[]{:S(2)}) collective-permute-start(bf16[32,640]{1,0:T(8,128)(2,1)S(1)} %get-tuple-element.28), channel_id=1, source_target_pairs={{0,4},{1,5},{2,6},{3,7},{4,0},{5,1},{6,2},{7,3},{8,12},{9,13},{10,... | collective-permute-start | bytes 122888 | tf_op jit(solution)/shard_map/ppermute | solution.py:263
  1.6 10.3 %collective-permute-start.1 = (bf16[32,640]{1,0:T(8,128)(2,1)S(1)}, bf16[32,640]{1,0:T(8,128)(2,1)S(1)}, u32[]{:S(2)}, u32[]{:S(2)}) collective-permute-start(bf16[32,640]{1,0:T(8,128)(2,1)S(1)} %get-tuple-element.28), channel_id=1, source_target_pairs={{0,8},{1,9},{2,10},{3,11},{4,12},{5,13},{6,14},{7,15},{8,0},{9,1},... | collective-permute-start | bytes 122888 | tf_op jit(solution)/shard_map/ppermute | solution.py:263
  3.9 8.0 %collective-permute-start.2 = (bf16[32,640]{1,0:T(8,128)(2,1)S(1)}, bf16[32,640]{1,0:T(8,128)(2,1)S(1)}, u32[]{:S(2)}, u32[]{:S(2)}) collective-permute-start(bf16[32,640]{1,0:T(8,128)(2,1)S(1)} %get-tuple-element.28), channel_id=1, source_target_pairs={{0,12},{1,13},{2,14},{3,15},{4,8},{5,9},{6,10},{7,11},{8,4},{9,5},... | collective-permute-start | bytes 122888 | tf_op jit(solution)/shard_map/ppermute | solution.py:263
  8.7 1.9 %copy-start.2 = (bf16[1,32,8192]{2,1,0:T(8,128)(2,1)S(1)}, bf16[1,32,8192]{2,1,0:T(8,128)(2,1)}, u32[]{:S(2)}) copy-start(bf16[1,32,8192]{2,1,0:T(8,128)(2,1)} %param.11) | copy-start | bytes 1572868
  12.8 4.2 %collective-permute-start.3 = (bf16[2,2,32,640]{3,2,1,0:T(8,128)(2,1)S(1)}, bf16[2,2,32,640]{3,2,1,0:T(8,128)(2,1)S(1)}, u32[]{:S(2)}, u32[]{:S(2)}) collective-permute-start(bf16[2,2,32,640]{3,2,1,0:T(8,128)(2,1)S(1)} %broadcast_select_fusion), channel_id=1, source_target_pairs={{0,2},{1,3},{2,0},{3,1},{4,6},{5,7},{6,4},{7,5},{8,10},{9,11},{10,... | collective-permute-start | bytes 491528 | tf_op jit(solution)/shard_map/ppermute | solution.py:271
  17.1 4.0 %collective-permute-start.4 = (bf16[2,2,2,32,640]{4,3,2,1,0:T(8,128)(2,1)S(1)}, bf16[2,2,2,32,640]{4,3,2,1,0:T(8,128)(2,1)S(1)}, u32[]{:S(2)}, u32[]{:S(2)}) collective-permute-start(bf16[2,2,2,32,640]{4,3,2,1,0:T(8,128)(2,1)S(1)} %maximum_select_fusion.1), channel_id=1, source_target_pairs={{0,1},{1,0},{2,3},{3,2},{4,5},{5,4},{6,7},{7,6},{8,9},{9,8},{10,11... | collective-permute-start | bytes 983048 | tf_op jit(solution)/shard_map/ppermute | solution.py:271
  26.1 20.7 %all-to-all-start = ((bf16[16,32,512]{2,1,0:T(8,128)(2,1)}), bf16[16,32,512]{2,1,0:T(8,128)(2,1)S(1)}, u32[]{:S(2)}, u32[]{:S(2)}) async-start(bf16[16,32,512]{2,1,0:T(8,128)(2,1)} %bitcast.87), calls=%async_computation | async-start | bytes 1048576 | tf_op jit(solution)/shard_map/all_to_all | solution.py:321
  47.5 12.4 %copy-start.1 = (bf16[66,8,512]{2,1,0:T(8,128)(2,1)}, bf16[66,8,512]{2,1,0:T(8,128)(2,1)S(1)}, u32[]{:S(2)}) copy-start(bf16[66,8,512]{2,1,0:T(8,128)(2,1)S(1)} %copy.64) | copy-start | bytes 1622020
  47.5 7.1 %collective-permute-start.5 = (bf16[528,256]{1,0:T(8,128)(2,1)S(1)}, bf16[528,256]{1,0:T(8,128)(2,1)S(1)}, u32[]{:S(2)}, u32[]{:S(2)}) collective-permute-start(bf16[528,256]{1,0:T(8,128)(2,1)S(1)} %get-tuple-element.24), channel_id=1, source_target_pairs={{0,1},{1,2},{2,3},{3,4},{4,5},{5,6},{6,7},{7,8},{8,9},{9,10},{10,1... | collective-permute-start | bytes 811016 | tf_op jit(solution)/shard_map/ppermute | solution.py:346
  51.2 8.7 %collective-permute-start.6 = (bf16[528,256]{1,0:T(8,128)(2,1)S(1)}, bf16[528,256]{1,0:T(8,128)(2,1)S(1)}, u32[]{:S(2)}, u32[]{:S(2)}) collective-permute-start(bf16[528,256]{1,0:T(8,128)(2,1)S(1)} %get-tuple-element.23), channel_id=1, source_target_pairs={{1,0},{2,1},{3,2},{4,3},{5,4},{6,5},{7,6},{8,7},{9,8},{10,9},{11,1... | collective-permute-start | bytes 811016 | tf_op jit(solution)/shard_map/ppermute | solution.py:347
  54.6 5.3 %copy-start.3 = (bf16[528,256]{1,0:T(8,128)(2,1)}, bf16[528,256]{1,0:T(8,128)(2,1)S(1)}, u32[]{:S(2)}) copy-start(bf16[528,256]{1,0:T(8,128)(2,1)S(1)} %collective-permute-done.5.low_ref) | copy-start | bytes 811012
  59.9 0.7 %copy-start.4 = (bf16[528,256]{1,0:T(8,128)(2,1)}, bf16[528,256]{1,0:T(8,128)(2,1)S(1)}, u32[]{:S(2)}) copy-start(bf16[528,256]{1,0:T(8,128)(2,1)S(1)} %collective-permute-done.6.high_ref) | copy-start | bytes 811012

commit v17 on v15

--- a/solution.py
+++ b/solution.py
@@ -325,15 +325,15 @@
     depth_tags = lax.dynamic_slice_in_dim(
         ref_all[:, :, tpix:].reshape(owners, channels * 128), lax.axis_index("view") * cap, cap, axis=1
     ).reshape(owners * cap)
+    labels = jnp.arange(-1, DEPTH + 1).at[0].set(-2)
     onehot = (
-        depth_tags[None, :] == jnp.arange(DEPTH).astype(jnp.bfloat16)[:, None]
+        depth_tags[None, :] == labels.astype(jnp.bfloat16)[:, None]
     ).astype(jnp.bfloat16)
     summed = jnp.einsum("dn,ngp->dgp", onehot, arriving, preferred_element_type=jnp.float32)
     tallies = jnp.sum(onehot.astype(jnp.float32), axis=1)
     cost_volume = (summed / jnp.maximum(tallies, 1.0)[:, None, None]).astype(jnp.bfloat16)
     columns = tpix // TROWS
-    volume = cost_volume.reshape(DEPTH * GROUPS, TROWS * columns)
-    volume = jnp.pad(volume, ((GROUPS, GROUPS), (0, 0)))
+    volume = cost_volume.reshape((DEPTH + 2) * GROUPS, TROWS * columns)
     count = lax.axis_size("view")
     place = lax.axis_index("view")
     ends = jnp.stack([place == 0, place == count - 1]).astype(jnp.int32)

time: 64 us -> 63.9 us (level)
  waiting for transfers between devices: 19.7 us -> 20.7 us
  local copies, waits for them, and re-layouts: 8.1 us -> 7.15 us
    ppermute x1, waiting for transfers between devices: 2.74 us -> 3.62 us  [body(): high = lax.ppermute(volume[:, :2 * columns], 'view', backward)]
    pad x1 -> x0, local copies, waits for them, and re-layouts: 0.84 us -> none  [body(): volume = jnp.pad(volume, ((GROUPS, GROUPS), (0, 0)))]
    unnamed x11 -> x13, local copies, waits for them, and re-layouts: 2.26 us -> 2.24 us
  transfers between devices with their start and end apart: 8 -> 8, of which waited for: 4 -> 4; matrix products, arithmetic and copies ran while one was open for 17% -> 16% of each run, Pallas kernels for 0% -> 0%
where the time goes in v17:
time: 63.9 us; the launch traced here: 63.3 us
  waiting for transfers between devices  20.7 us (32%)
  starting transfers between devices  18.4 us (29%)
  Pallas kernels  9.02 us (14%)
  local copies, waits for them, and re-layouts  7.15 us (11%)
  other arithmetic  6.5 us (10%)
  matrix products  1.31 us (2%)
    all_to_all x1, waiting for transfers between devices, body(): lax.all_to_all(corr_all.reshape(owners, cap * GROUPS, tpix), 'view', spli...  12.1 us
    all_to_all x1, starting transfers between devices, body(): lax.all_to_all(corr_all.reshape(owners, cap * GROUPS, tpix), 'view', spli...  7.14 us
    ppermute x2, waiting for transfers between devices, gather_view(): lax.ppermute(gathered, 'view', [(i, i ^ stride) for i in range(count)])  4.99 us
    pallas_call x1, Pallas kernels, conv_pair(): pl.pallas_call(functools.partial(conv_pair_kernel, rows=rows, cols=cols,...  4.88 us
    pallas_call x1, Pallas kernels, correlate(): pl.pallas_call(correlate_kernel, out_shape=jax.ShapeDtypeStruct((units *...  4.14 us
    ppermute x1, starting transfers between devices, body(): lax.ppermute(volume[:, volume.shape[1] - 2 * columns:], 'view', forward)  3.64 us
    ppermute x1, waiting for transfers between devices, body(): high = lax.ppermute(volume[:, :2 * columns], 'view', backward)  3.62 us
    ppermute x2, starting transfers between devices, gather_view(): lax.ppermute(gathered, 'view', [(i, i ^ stride) for i in range(count)])  3.02 us
  transfers between devices with their start and end apart: 8, of which 4 were waited for; matrix products, arithmetic and copies ran while one was open for 16% of the time, Pallas kernels for 0%

profile of v17, /device:TPU:13, one launch (start us, length us, event | category | flops | bytes accessed | tf_op | source)
XLA Modules:
  0.0 63.3 jit_solution(12534658052605182955)
XLA Ops:
  0.0 0.7 %fusion.22 = bf16[64]{0:T(256)(128)(2,1)S(1)} fusion(s32[1,64]{1,0:T(1,128)} %param.17, s32[1,64]{1,0:T(1,128)} %param.16), kind=kLoop, calls=%fused_computation.65 | loop fusion | flops 192 | bytes 640 | tf_op jit(solution)/shard_map/convert_element_type | solution.py:311
  0.7 0.8 %fusion.24 = (bf16[1,32,640]{2,1,0:T(8,128)(2,1)S(1)}, bf16[32,640]{1,0:T(8,128)(2,1)S(1)}) fusion(bf16[32,128]{1,0:T(8,128)(2,1)S(1)} %pad_bitcast_fusion, bf16[32,512]{1,0:T(8,128)(2,1)} %bitcast.101), kind=kLoop, calls=%fused_computation.71 | loop fusion | flops 81920 | bytes 122880 | tf_op jit(solution)/shard_map/broadcast_in_dim | solution.py:314
  1.6 2.3 %collective-permute-start.1 = (bf16[32,640]{1,0:T(8,128)(2,1)S(1)}, bf16[32,640]{1,0:T(8,128)(2,1)S(1)}, u32[]{:S(2)}, u32[]{:S(2)}) collective-permute-start(bf16[32,640]{1,0:T(8,128)(2,1)S(1)} %get-tuple-element.22), channel_id=1, source_target_pairs={{0,8},{1,9},{2,10},{3,11},{4,12},{5,13},{6,14},{7,15},{8,0},{9,1},... | collective-permute-start | bytes 122888 | tf_op jit(solution)/shard_map/ppermute | solution.py:263
  4.8 0.7 %select_reduce_fusion.1 = s32[64,4]{0,1:T(4,128)S(1)} fusion(s32[64,4]{0,1:T(4,128)} %bitcast.104, s32[64,4]{0,1:T(4,128)} %bitcast.102), kind=kLoop, calls=%fused_computation.31 | loop fusion | flops 2816 | bytes 3072 | tf_op jit(solution)/shard_map/reduce_sum | solution.py:308
  5.5 0.7 %fusion.10 = pred[64,4]{0,1:T(4,128)(4,1)S(1)} fusion(s32[64,4]{0,1:T(4,128)} %bitcast.103, pred[64,4]{0,1:T(4,128)(4,1)S(1)} %iota_compare_fusion.3), kind=kLoop, calls=%fused_computation.37 | loop fusion | flops 2816 | bytes 1536 | tf_op jit(solution)/shard_map/reduce_or | solution.py:309
  6.5 0.7 %select_n.189.blk_ref = s32[256]{0:T(256)} reshape(s32[64,4]{1,0:T(8,128)S(1)} %copy.42) | data formatting | bytes 2048 | tf_op jit(solution)/shard_map/jit(_where)/select_n | solution.py:310
  7.2 1.2 %copy.54 = bf16[4,8,64,128]{3,2,1,0:T(8,128)(2,1)S(1)} copy(bf16[4,8,64,128]{3,1,2,0:T(8,128)(2,1)} %bitcast.90) | data formatting | bytes 1048576
  9.0 0.8 %concatenate.23.blocks_ref = bf16[65,32,128]{2,1,0:T(8,128)(2,1)} pad(bf16[64,32,128]{2,1,0:T(8,128)(2,1)S(1)} %bitcast.85, bf16[]{:T(256)} %constant.159.clone.1), padding=0_1x0_0x0_0 | pad | bytes 1056770 | tf_op jit(solution)/shard_map/concatenate | solution.py:305
  11.1 3.8 %collective-permute-done.3 = bf16[2,2,32,640]{3,2,1,0:T(8,128)(2,1)S(1)} collective-permute-done((bf16[2,2,32,640]{3,2,1,0:T(8,128)(2,1)S(1)}, bf16[2,2,32,640]{3,2,1,0:T(8,128)(2,1)S(1)}, u32[]{:S(2)}, u32[]{:S(2)}) %collective-permute-start.3) | collective-permute-done | bytes 163872 | tf_op jit(solution)/shard_map/ppermute | solution.py:271
  15.0 2.7 %collective-permute-start.4 = (bf16[2,2,2,32,640]{4,3,2,1,0:T(8,128)(2,1)S(1)}, bf16[2,2,2,32,640]{4,3,2,1,0:T(8,128)(2,1)S(1)}, u32[]{:S(2)}, u32[]{:S(2)}) collective-permute-start(bf16[2,2,2,32,640]{4,3,2,1,0:T(8,128)(2,1)S(1)} %maximum_select_fusion.1), channel_id=1, source_target_pairs={{0,1},{1,0},{2,3},{3,2},{4,5},{5,4},{6,7},{7,6},{8,9},{9,8},{10,11... | collective-permute-start | bytes 983048 | tf_op jit(solution)/shard_map/ppermute | solution.py:271
  17.8 1.1 %collective-permute-done.4 = bf16[2,2,2,32,640]{4,3,2,1,0:T(8,128)(2,1)S(1)} collective-permute-done((bf16[2,2,2,32,640]{4,3,2,1,0:T(8,128)(2,1)S(1)}, bf16[2,2,2,32,640]{4,3,2,1,0:T(8,128)(2,1)S(1)}, u32[]{:S(2)}, u32[]{:S(2)}) %collective-permute-start.4) | collective-permute-done | bytes 327712 | tf_op jit(solution)/shard_map/ppermute | solution.py:271
  19.0 0.9 %maximum_select_fusion = bf16[2,2,2,2,32,640]{5,4,3,2,1,0:T(8,128)(2,1)} fusion(bf16[2,2,2,1,32,640]{5,4,3,2,1,0:T(8,128)(2,1)S(1)} %bitcast.94, bf16[2,2,2,1,32,640]{5,4,3,2,1,0:T(8,128)(2,1)S(1)} %copy_select_fusion, pred[]{:T(512)S(6)} %eq.126), kind=kLoop, calls=%fused_computation.8 | loop fusion | flops 983040 | bytes 1310721 | tf_op jit(solution)/shard_map/jit(_where)/select_n | solution.py:273
  19.9 4.1 %shard_map.91 = bf16[512,512]{1,0:T(8,128)(2,1)} custom-call(s32[256]{0:T(256)} %select_n.189.blk_ref, bf16[65,32,128]{2,1,0:T(8,128)(2,1)} %concatenate.23.blocks_ref, bf16[512,512]{1,0:T(8,128)(2,1)} %bitcast.93, bf16[16,32,640]{2,1,0:T(8,128)(2,1)} %bitcast.79), custom_call_target="tpu_custom_call" | custom-call | tf_op jit(solution)/shard_map/pallas_call | solution.py:121
  24.0 7.1 %all-to-all-start = ((bf16[16,32,512]{2,1,0:T(8,128)(2,1)}), bf16[16,32,512]{2,1,0:T(8,128)(2,1)S(1)}, u32[]{:S(2)}, u32[]{:S(2)}) async-start(bf16[16,32,512]{2,1,0:T(8,128)(2,1)} %bitcast.87), calls=%async_computation | async-start | bytes 1048576 | tf_op jit(solution)/shard_map/all_to_all | solution.py:318
  31.4 0.9 %slice.24 = bf16[16,32,128]{2,1,0:T(8,128)(2,1)S(1)} slice(bf16[16,32,640]{2,1,0:T(8,128)(2,1)} %bitcast.80), slice={[0:16], [0:32], [512:640]} | slice | bytes 262144 | tf_op jit(solution)/shard_map/slice | solution.py:326
  32.7 12.1 %all-to-all-done = bf16[16,32,512]{2,1,0:T(8,128)(2,1)S(1)} async-done(((bf16[16,32,512]{2,1,0:T(8,128)(2,1)}), bf16[16,32,512]{2,1,0:T(8,128)(2,1)S(1)}, u32[]{:S(2)}, u32[]{:S(2)}) %all-to-all-start) | async-done | bytes 524320 | tf_op jit(solution)/shard_map/all_to_all | solution.py:318
  45.4 3.6 %collective-permute-start.5 = (bf16[528,256]{1,0:T(8,128)(2,1)S(1)}, bf16[528,256]{1,0:T(8,128)(2,1)S(1)}, u32[]{:S(2)}, u32[]{:S(2)}) collective-permute-start(bf16[528,256]{1,0:T(8,128)(2,1)S(1)} %get-tuple-element.18), channel_id=1, source_target_pairs={{0,1},{1,2},{2,3},{3,4},{4,5},{5,6},{6,7},{7,8},{8,9},{9,10},{10,1... | collective-permute-start | bytes 811016 | tf_op jit(solution)/shard_map/ppermute | solution.py:343
  49.1 1.9 %collective-permute-start.6 = (bf16[528,256]{1,0:T(8,128)(2,1)S(1)}, bf16[528,256]{1,0:T(8,128)(2,1)S(1)}, u32[]{:S(2)}, u32[]{:S(2)}) collective-permute-start(bf16[528,256]{1,0:T(8,128)(2,1)S(1)} %get-tuple-element.17), channel_id=1, source_target_pairs={{1,0},{2,1},{3,2},{4,3},{5,4},{6,5},{7,6},{8,7},{9,8},{10,9},{11,1... | collective-permute-start | bytes 811016 | tf_op jit(solution)/shard_map/ppermute | solution.py:344
  51.0 0.7 %fusion = bf16[9,128,144]{1,2,0:T(8,128)(2,1)S(1)} fusion(bf16[3,9,8,8]{3,2,1,0:T(8,128)(2,1)S(1)} %bitcast.76, pred[3,128,144]{1,2,0:T(8,128)(4,1)S(1)} %broadcast_compare_fusion, s32[144]{0:T(256)S(1)} %and_select_fusion.1, s32[128]{0:T(128)S(1)} %get-tuple-element.23), kind=kOutput, calls=%fused_computation.2 | convolution fusion | flops 9323008 | bytes 391616 | tf_op jit(solution)/shard_map/ro,xyoc->xyrc/dot_general | solution.py:184
  51.8 1.1 %copy.47 = bf16[9,128,144]{2,1,0:T(8,128)(2,1)} copy(bf16[9,128,144]{1,2,0:T(8,128)(2,1)S(1)} %fusion) | data formatting | bytes 663552 | tf_op jit(solution)/shard_map/convert_element_type | solution.py:195
  53.5 0.7 %select_reduce_fusion = bf16[9,16,144]{2,1,0:T(8,128)(2,1)} fusion(f32[3,9,144]{2,1,0:T(8,128)S(1)} %convolution_bitcast_fusion, pred[3,16,144]{2,1,0:T(8,128)(4,1)S(1)} %broadcast_compare_fusion.1), kind=kLoop, calls=%fused_computation.12 | loop fusion | flops 103680 | bytes 63936 | tf_op jit(solution)/shard_map/reduce_sum | solution.py:194
  54.1 3.6 %collective-permute-done.6.high_ref = bf16[528,256]{1,0:T(8,128)(2,1)S(1)} collective-permute-done((bf16[528,256]{1,0:T(8,128)(2,1)S(1)}, bf16[528,256]{1,0:T(8,128)(2,1)S(1)}, u32[]{:S(2)}, u32[]{:S(2)}) %collective-permute-start.6) | collective-permute-done | bytes 270368 | tf_op jit(solution)/shard_map/ppermute | solution.py:344
  57.8 0.7 %copy-done.3 = bf16[528,256]{1,0:T(8,128)(2,1)} copy-done((bf16[528,256]{1,0:T(8,128)(2,1)}, bf16[528,256]{1,0:T(8,128)(2,1)S(1)}, u32[]{:S(2)}) %copy-start.3) | copy-done | bytes 270360
  58.5 4.9 %shard_map.92 = f32[4,64,128]{2,1,0:T(8,128)} custom-call(s32[2]{0:T(128)} %add_convert_fusion.ends_ref, bf16[528,256]{1,0:T(8,128)(2,1)} %copy-done.2, bf16[528,512]{1,0:T(8,128)(2,1)} %bitcast.78, bf16[528,256]{1,0:T(8,128)(2,1)} %copy-done.3, bf16[3,3,128,144]{3,2,1,0:T(8,128)(2,1)} %bitcast.84, bf16[3,3,16,144]{3,2,1,0:T(8,128)(2,1)} %bitcast.95), custom_call_target="tpu_custom_call" | custom-call | tf_op jit(solution)/shard_map/pallas_call | solution.py:229
  (53 shorter events, 5.1 us)
Async XLA Ops:
  0.0 51.0 %copy-start = (bf16[3,3,3,8,8]{4,3,2,1,0:T(8,128)(2,1)S(1)}, bf16[3,3,3,8,8]{4,3,2,1,0:T(8,128)(2,1)}, u32[]{:S(2)}) copy-start(bf16[3,3,3,8,8]{4,3,2,1,0:T(8,128)(2,1)} %param.18) | copy-start | bytes 10372
  1.5 8.4 %collective-permute-start = (bf16[32,640]{1,0:T(8,128)(2,1)S(1)}, bf16[32,640]{1,0:T(8,128)(2,1)S(1)}, u32[]{:S(2)}, u32[]{:S(2)}) collective-permute-start(bf16[32,640]{1,0:T(8,128)(2,1)S(1)} %get-tuple-element.22), channel_id=1, source_target_pairs={{0,4},{1,5},{2,6},{3,7},{4,0},{5,1},{6,2},{7,3},{8,12},{9,13},{10,... | collective-permute-start | bytes 122888 | tf_op jit(solution)/shard_map/ppermute | solution.py:263
  1.6 8.2 %collective-permute-start.1 = (bf16[32,640]{1,0:T(8,128)(2,1)S(1)}, bf16[32,640]{1,0:T(8,128)(2,1)S(1)}, u32[]{:S(2)}, u32[]{:S(2)}) collective-permute-start(bf16[32,640]{1,0:T(8,128)(2,1)S(1)} %get-tuple-element.22), channel_id=1, source_target_pairs={{0,8},{1,9},{2,10},{3,11},{4,12},{5,13},{6,14},{7,15},{8,0},{9,1},... | collective-permute-start | bytes 122888 | tf_op jit(solution)/shard_map/ppermute | solution.py:263
  3.9 5.9 %collective-permute-start.2 = (bf16[32,640]{1,0:T(8,128)(2,1)S(1)}, bf16[32,640]{1,0:T(8,128)(2,1)S(1)}, u32[]{:S(2)}, u32[]{:S(2)}) collective-permute-start(bf16[32,640]{1,0:T(8,128)(2,1)S(1)} %get-tuple-element.22), channel_id=1, source_target_pairs={{0,12},{1,13},{2,14},{3,15},{4,8},{5,9},{6,10},{7,11},{8,4},{9,5},... | collective-permute-start | bytes 122888 | tf_op jit(solution)/shard_map/ppermute | solution.py:263
  8.3 0.7 %copy-start.4 = (bf16[3,3,3,8]{3,2,1,0:T(4,128)(2,1)S(1)}, bf16[3,3,3,8]{3,2,1,0:T(4,128)(2,1)}, u32[]{:S(2)}) copy-start(bf16[3,3,3,8]{3,2,1,0:T(4,128)(2,1)} %param.19) | copy-start | bytes 1300
  10.7 4.2 %collective-permute-start.3 = (bf16[2,2,32,640]{3,2,1,0:T(8,128)(2,1)S(1)}, bf16[2,2,32,640]{3,2,1,0:T(8,128)(2,1)S(1)}, u32[]{:S(2)}, u32[]{:S(2)}) collective-permute-start(bf16[2,2,32,640]{3,2,1,0:T(8,128)(2,1)S(1)} %broadcast_select_fusion), channel_id=1, source_target_pairs={{0,2},{1,3},{2,0},{3,1},{4,6},{5,7},{6,4},{7,5},{8,10},{9,11},{10,... | collective-permute-start | bytes 491528 | tf_op jit(solution)/shard_map/ppermute | solution.py:271
  15.0 4.0 %collective-permute-start.4 = (bf16[2,2,2,32,640]{4,3,2,1,0:T(8,128)(2,1)S(1)}, bf16[2,2,2,32,640]{4,3,2,1,0:T(8,128)(2,1)S(1)}, u32[]{:S(2)}, u32[]{:S(2)}) collective-permute-start(bf16[2,2,2,32,640]{4,3,2,1,0:T(8,128)(2,1)S(1)} %maximum_select_fusion.1), channel_id=1, source_target_pairs={{0,1},{1,0},{2,3},{3,2},{4,5},{5,4},{6,7},{7,6},{8,9},{9,8},{10,11... | collective-permute-start | bytes 983048 | tf_op jit(solution)/shard_map/ppermute | solution.py:271
  24.0 20.7 %all-to-all-start = ((bf16[16,32,512]{2,1,0:T(8,128)(2,1)}), bf16[16,32,512]{2,1,0:T(8,128)(2,1)S(1)}, u32[]{:S(2)}, u32[]{:S(2)}) async-start(bf16[16,32,512]{2,1,0:T(8,128)(2,1)} %bitcast.87), calls=%async_computation | async-start | bytes 1048576 | tf_op jit(solution)/shard_map/all_to_all | solution.py:318
  45.4 6.4 %copy-start.1 = (bf16[66,8,512]{2,1,0:T(8,128)(2,1)}, bf16[66,8,512]{2,1,0:T(8,128)(2,1)S(1)}, u32[]{:S(2)}) copy-start(bf16[66,8,512]{2,1,0:T(8,128)(2,1)S(1)} %copy.64) | copy-start | bytes 1622020
  45.4 8.7 %collective-permute-start.5 = (bf16[528,256]{1,0:T(8,128)(2,1)S(1)}, bf16[528,256]{1,0:T(8,128)(2,1)S(1)}, u32[]{:S(2)}, u32[]{:S(2)}) collective-permute-start(bf16[528,256]{1,0:T(8,128)(2,1)S(1)} %get-tuple-element.18), channel_id=1, source_target_pairs={{0,1},{1,2},{2,3},{3,4},{4,5},{5,6},{6,7},{7,8},{8,9},{9,10},{10,1... | collective-permute-start | bytes 811016 | tf_op jit(solution)/shard_map/ppermute | solution.py:343
  49.1 8.7 %collective-permute-start.6 = (bf16[528,256]{1,0:T(8,128)(2,1)S(1)}, bf16[528,256]{1,0:T(8,128)(2,1)S(1)}, u32[]{:S(2)}, u32[]{:S(2)}) collective-permute-start(bf16[528,256]{1,0:T(8,128)(2,1)S(1)} %get-tuple-element.17), channel_id=1, source_target_pairs={{1,0},{2,1},{3,2},{4,3},{5,4},{6,5},{7,6},{8,7},{9,8},{10,9},{11,1... | collective-permute-start | bytes 811016 | tf_op jit(solution)/shard_map/ppermute | solution.py:344
  54.1 3.6 %copy-start.2 = (bf16[528,256]{1,0:T(8,128)(2,1)}, bf16[528,256]{1,0:T(8,128)(2,1)S(1)}, u32[]{:S(2)}) copy-start(bf16[528,256]{1,0:T(8,128)(2,1)S(1)} %collective-permute-done.5.low_ref) | copy-start | bytes 811012
  57.8 0.7 %copy-start.3 = (bf16[528,256]{1,0:T(8,128)(2,1)}, bf16[528,256]{1,0:T(8,128)(2,1)S(1)}, u32[]{:S(2)}) copy-start(bf16[528,256]{1,0:T(8,128)(2,1)S(1)} %collective-permute-done.6.high_ref) | copy-start | bytes 811012

commit v18 on v17

--- a/solution.py
+++ b/solution.py
@@ -179,11 +179,8 @@
         outs = kernel.shape[4]
         rows = chunk * outs
         row = lax.iota(jnp.int32, rows)
-        pick = (row[:, None] % outs == jnp.arange(outs)[None, :]).astype(kernel.dtype)
         lanes = jnp.einsum("xyio,ic->xyoc", taps, spread, preferred_element_type=jnp.float32)
-        tiles = jnp.einsum(
-            "ro,xyoc->xyrc", pick, lanes.astype(kernel.dtype), preferred_element_type=jnp.float32
-        )
+        tiles = jnp.broadcast_to(lanes[:, :, None], (3, 9, chunk, outs, cols)).reshape(3, 9, rows, cols)
         depth_of_row = row // outs
     else:
         rows = chunk

time: 63.9 us -> 65.5 us (1.025)
  waiting for transfers between devices: 20.7 us -> 22.1 us
  other arithmetic: 6.5 us -> 7.87 us
    ppermute x1, waiting for transfers between devices: 3.62 us -> 4.88 us  [body(): high = lax.ppermute(volume[:, :2 * columns], 'view', backward)]
    reduce_sum x1 -> x2, other arithmetic: 0.67 us -> 1.89 us  [banded(): mats = jnp.sum(jnp.where(band[:, None], tiles, 0.0), axis=0)]
    convert_element_type x1 -> x0, local copies, waits for them, and re-layouts: 1.07 us -> none  [banded(): return mats.astype(kernel.dtype).reshape(3, 3, rows, cols)]
    reshape x0 -> x1, local copies, waits for them, and re-layouts: none -> 1.05 us  [banded(): taps = kernel.reshape((3, 9) + kernel.shape[3:])]
    unnamed x13 -> x11, local copies, waits for them, and re-layouts: 2.24 us -> 1.58 us
where the time goes in v18:
time: 65.5 us; the launch traced here: 64.9 us
  waiting for transfers between devices  22.1 us (34%)
  starting transfers between devices  18.4 us (28%)
  Pallas kernels  9.02 us (14%)
  other arithmetic  7.87 us (12%)
  local copies, waits for them, and re-layouts  6.58 us (10%)
  matrix products  0.81 us (1%)
    all_to_all x1, waiting for transfers between devices, body(): lax.all_to_all(corr_all.reshape(owners, cap * GROUPS, tpix), 'view', spli...  12.2 us
    all_to_all x1, starting transfers between devices, body(): lax.all_to_all(corr_all.reshape(owners, cap * GROUPS, tpix), 'view', spli...  7.15 us
    ppermute x2, waiting for transfers between devices, gather_view(): lax.ppermute(gathered, 'view', [(i, i ^ stride) for i in range(count)])  4.99 us
    ppermute x1, waiting for transfers between devices, body(): high = lax.ppermute(volume[:, :2 * columns], 'view', backward)  4.88 us
    pallas_call x1, Pallas kernels, conv_pair(): pl.pallas_call(functools.partial(conv_pair_kernel, rows=rows, cols=cols,...  4.88 us
    pallas_call x1, Pallas kernels, correlate(): pl.pallas_call(correlate_kernel, out_shape=jax.ShapeDtypeStruct((units *...  4.14 us
    ppermute x1, starting transfers between devices, body(): lax.ppermute(volume[:, volume.shape[1] - 2 * columns:], 'view', forward)  3.64 us
    ppermute x2, starting transfers between devices, gather_view(): lax.ppermute(gathered, 'view', [(i, i ^ stride) for i in range(count)])  3.02 us
  transfers between devices with their start and end apart: 8, of which 4 were waited for; matrix products, arithmetic and copies ran while one was open for 16% of the time, Pallas kernels for 0%

profile of v18, /device:TPU:13, one launch (start us, length us, event | category | flops | bytes accessed | tf_op | source)
XLA Modules:
  0.0 64.9 jit_solution(7376963174053470594)
XLA Ops:
  0.0 0.7 %fusion.16 = bf16[64]{0:T(256)(128)(2,1)S(1)} fusion(s32[1,64]{1,0:T(1,128)} %param.17, s32[1,64]{1,0:T(1,128)} %param.16), kind=kLoop, calls=%fused_computation.60 | loop fusion | flops 192 | bytes 640 | tf_op jit(solution)/shard_map/convert_element_type | solution.py:308
  0.7 0.8 %fusion.18 = (bf16[1,32,640]{2,1,0:T(8,128)(2,1)S(1)}, bf16[32,640]{1,0:T(8,128)(2,1)S(1)}) fusion(bf16[32,128]{1,0:T(8,128)(2,1)S(1)} %pad_bitcast_fusion, bf16[32,512]{1,0:T(8,128)(2,1)} %bitcast.89), kind=kLoop, calls=%fused_computation.66 | loop fusion | flops 81920 | bytes 122880 | tf_op jit(solution)/shard_map/broadcast_in_dim | solution.py:311
  1.7 2.3 %collective-permute-start.1 = (bf16[32,640]{1,0:T(8,128)(2,1)S(1)}, bf16[32,640]{1,0:T(8,128)(2,1)S(1)}, u32[]{:S(2)}, u32[]{:S(2)}) collective-permute-start(bf16[32,640]{1,0:T(8,128)(2,1)S(1)} %get-tuple-element.22), channel_id=1, source_target_pairs={{0,8},{1,9},{2,10},{3,11},{4,12},{5,13},{6,14},{7,15},{8,0},{9,1},... | collective-permute-start | bytes 122888 | tf_op jit(solution)/shard_map/ppermute | solution.py:260
  4.9 0.7 %select_reduce_fusion.2 = s32[64,4]{0,1:T(4,128)S(1)} fusion(s32[64,4]{0,1:T(4,128)} %bitcast.92, s32[64,4]{0,1:T(4,128)} %bitcast.90), kind=kLoop, calls=%fused_computation.34 | loop fusion | flops 2816 | bytes 3072 | tf_op jit(solution)/shard_map/reduce_sum | solution.py:305
  5.6 0.7 %fusion.9 = pred[64,4]{0,1:T(4,128)(4,1)S(1)} fusion(s32[64,4]{0,1:T(4,128)} %bitcast.91, pred[64,4]{0,1:T(4,128)(4,1)S(1)} %iota_compare_fusion.2), kind=kLoop, calls=%fused_computation.41 | loop fusion | flops 2816 | bytes 1536 | tf_op jit(solution)/shard_map/reduce_or | solution.py:306
  6.3 1.0 %copy.38 = bf16[3,9,8,8]{1,2,3,0:T(8,128)(2,1)S(1)} copy(bf16[3,9,8,8]{3,2,1,0:T(8,128)(2,1)} %bitcast.84) | data formatting | bytes 6912 | tf_op jit(solution)/shard_map/reshape | solution.py:175
  7.3 0.7 %copy.40 = bf16[3,3,3,8]{3,0,2,1:T(4,128)(2,1)S(1)} copy(bf16[3,3,3,8]{3,2,1,0:T(4,128)(2,1)} %param.19) | data formatting | bytes 864 | tf_op args[8]
  8.5 0.7 %select_reduce_fusion.1 = bf16[9,16,144]{2,1,0:T(8,128)(2,1)} fusion(f32[3,9,144]{2,1,0:T(8,128)S(1)} %convolution_bitcast_fusion.1, pred[3,16,144]{2,1,0:T(8,128)(4,1)S(1)} %broadcast_compare_fusion.1), kind=kLoop, calls=%fused_computation.10 | loop fusion | flops 103680 | bytes 63936 | tf_op jit(solution)/shard_map/reduce_sum | solution.py:191
  9.3 0.7 %select_n.180.blk_ref = s32[256]{0:T(256)} reshape(s32[64,4]{1,0:T(8,128)S(1)} %copy.34) | data formatting | bytes 2048 | tf_op jit(solution)/shard_map/jit(_where)/select_n | solution.py:307
  10.6 0.8 %concatenate.23.blocks_ref = bf16[65,32,128]{2,1,0:T(8,128)(2,1)} pad(bf16[64,32,128]{2,1,0:T(8,128)(2,1)S(1)} %bitcast.72, bf16[]{:T(256)} %constant.153.clone.1), padding=0_1x0_0x0_0 | pad | bytes 1056770 | tf_op jit(solution)/shard_map/concatenate | solution.py:302
  12.6 3.8 %collective-permute-done.3 = bf16[2,2,32,640]{3,2,1,0:T(8,128)(2,1)S(1)} collective-permute-done((bf16[2,2,32,640]{3,2,1,0:T(8,128)(2,1)S(1)}, bf16[2,2,32,640]{3,2,1,0:T(8,128)(2,1)S(1)}, u32[]{:S(2)}, u32[]{:S(2)}) %collective-permute-start.3) | collective-permute-done | bytes 163872 | tf_op jit(solution)/shard_map/ppermute | solution.py:268
  16.5 2.7 %collective-permute-start.4 = (bf16[2,2,2,32,640]{4,3,2,1,0:T(8,128)(2,1)S(1)}, bf16[2,2,2,32,640]{4,3,2,1,0:T(8,128)(2,1)S(1)}, u32[]{:S(2)}, u32[]{:S(2)}) collective-permute-start(bf16[2,2,2,32,640]{4,3,2,1,0:T(8,128)(2,1)S(1)} %maximum_select_fusion.1), channel_id=1, source_target_pairs={{0,1},{1,0},{2,3},{3,2},{4,5},{5,4},{6,7},{7,6},{8,9},{9,8},{10,11... | collective-permute-start | bytes 983048 | tf_op jit(solution)/shard_map/ppermute | solution.py:268
  19.4 1.1 %collective-permute-done.4 = bf16[2,2,2,32,640]{4,3,2,1,0:T(8,128)(2,1)S(1)} collective-permute-done((bf16[2,2,2,32,640]{4,3,2,1,0:T(8,128)(2,1)S(1)}, bf16[2,2,2,32,640]{4,3,2,1,0:T(8,128)(2,1)S(1)}, u32[]{:S(2)}, u32[]{:S(2)}) %collective-permute-start.4) | collective-permute-done | bytes 327712 | tf_op jit(solution)/shard_map/ppermute | solution.py:268
  20.5 0.9 %maximum_select_fusion = bf16[2,2,2,2,32,640]{5,4,3,2,1,0:T(8,128)(2,1)} fusion(bf16[2,2,2,1,32,640]{5,4,3,2,1,0:T(8,128)(2,1)S(1)} %bitcast.81, bf16[2,2,2,1,32,640]{5,4,3,2,1,0:T(8,128)(2,1)S(1)} %copy_select_fusion, pred[]{:T(512)S(6)} %eq.111), kind=kLoop, calls=%fused_computation.6 | loop fusion | flops 983040 | bytes 1310721 | tf_op jit(solution)/shard_map/jit(_where)/select_n | solution.py:270
  21.5 4.1 %shard_map.91 = bf16[512,512]{1,0:T(8,128)(2,1)} custom-call(s32[256]{0:T(256)} %select_n.180.blk_ref, bf16[65,32,128]{2,1,0:T(8,128)(2,1)} %concatenate.23.blocks_ref, bf16[512,512]{1,0:T(8,128)(2,1)} %bitcast.80, bf16[16,32,640]{2,1,0:T(8,128)(2,1)} %bitcast.66), custom_call_target="tpu_custom_call" | custom-call | tf_op jit(solution)/shard_map/pallas_call | solution.py:121
  25.6 7.2 %all-to-all-start = ((bf16[16,32,512]{2,1,0:T(8,128)(2,1)}), bf16[16,32,512]{2,1,0:T(8,128)(2,1)S(1)}, u32[]{:S(2)}, u32[]{:S(2)}) async-start(bf16[16,32,512]{2,1,0:T(8,128)(2,1)} %bitcast.74), calls=%async_computation | async-start | bytes 1048576 | tf_op jit(solution)/shard_map/all_to_all | solution.py:315
  32.9 0.9 %slice.24 = bf16[16,32,128]{2,1,0:T(8,128)(2,1)S(1)} slice(bf16[16,32,640]{2,1,0:T(8,128)(2,1)} %bitcast.67), slice={[0:16], [0:32], [512:640]} | slice | bytes 262144 | tf_op jit(solution)/shard_map/slice | solution.py:323
  34.2 12.2 %all-to-all-done = bf16[16,32,512]{2,1,0:T(8,128)(2,1)S(1)} async-done(((bf16[16,32,512]{2,1,0:T(8,128)(2,1)}), bf16[16,32,512]{2,1,0:T(8,128)(2,1)S(1)}, u32[]{:S(2)}, u32[]{:S(2)}) %all-to-all-start) | async-done | bytes 524320 | tf_op jit(solution)/shard_map/all_to_all | solution.py:315
  47.0 3.6 %collective-permute-start.5 = (bf16[528,256]{1,0:T(8,128)(2,1)S(1)}, bf16[528,256]{1,0:T(8,128)(2,1)S(1)}, u32[]{:S(2)}, u32[]{:S(2)}) collective-permute-start(bf16[528,256]{1,0:T(8,128)(2,1)S(1)} %get-tuple-element.18), channel_id=1, source_target_pairs={{0,1},{1,2},{2,3},{3,4},{4,5},{5,6},{6,7},{7,8},{8,9},{9,10},{10,1... | collective-permute-start | bytes 811016 | tf_op jit(solution)/shard_map/ppermute | solution.py:340
  50.7 1.9 %collective-permute-start.6 = (bf16[528,256]{1,0:T(8,128)(2,1)S(1)}, bf16[528,256]{1,0:T(8,128)(2,1)S(1)}, u32[]{:S(2)}, u32[]{:S(2)}) collective-permute-start(bf16[528,256]{1,0:T(8,128)(2,1)S(1)} %get-tuple-element.17), channel_id=1, source_target_pairs={{1,0},{2,1},{3,2},{4,3},{5,4},{6,5},{7,6},{8,7},{9,8},{10,9},{11,1... | collective-permute-start | bytes 811016 | tf_op jit(solution)/shard_map/ppermute | solution.py:341
  53.2 1.2 %select_reduce_fusion = bf16[9,16,8,144]{3,2,1,0:T(8,128)(2,1)} fusion(f32[3,9,8,144]{3,2,1,0:T(8,128)S(1)} %copy.39, pred[3,16,8,144]{3,2,1,0:T(8,128)(4,1)S(1)} %broadcast_compare_fusion), kind=kLoop, calls=%fused_computation.1 | loop fusion | flops 829440 | bytes 511488 | tf_op jit(solution)/shard_map/reduce_sum | solution.py:191
  54.5 4.9 %collective-permute-done.6.high_ref = bf16[528,256]{1,0:T(8,128)(2,1)S(1)} collective-permute-done((bf16[528,256]{1,0:T(8,128)(2,1)S(1)}, bf16[528,256]{1,0:T(8,128)(2,1)S(1)}, u32[]{:S(2)}, u32[]{:S(2)}) %collective-permute-start.6) | collective-permute-done | bytes 270368 | tf_op jit(solution)/shard_map/ppermute | solution.py:341
  59.3 0.7 %copy-done.3 = bf16[528,256]{1,0:T(8,128)(2,1)} copy-done((bf16[528,256]{1,0:T(8,128)(2,1)}, bf16[528,256]{1,0:T(8,128)(2,1)S(1)}, u32[]{:S(2)}) %copy-start.3) | copy-done | bytes 270360
  60.0 4.9 %shard_map.92 = f32[4,64,128]{2,1,0:T(8,128)} custom-call(s32[2]{0:T(128)} %add_convert_fusion.ends_ref, bf16[528,256]{1,0:T(8,128)(2,1)} %copy-done.2, bf16[528,512]{1,0:T(8,128)(2,1)} %bitcast.65, bf16[528,256]{1,0:T(8,128)(2,1)} %copy-done.3, bf16[3,3,128,144]{3,2,1,0:T(8,128)(2,1)} %bitcast.71, bf16[3,3,16,144]{3,2,1,0:T(8,128)(2,1)} %bitcast.82), custom_call_target="tpu_custom_call" | custom-call | tf_op jit(solution)/shard_map/pallas_call | solution.py:226
  (53 shorter events, 5.3 us)
Async XLA Ops:
  0.0 10.0 %copy-start.1 = (bf16[1,32,8192]{2,1,0:T(8,128)(2,1)S(1)}, bf16[1,32,8192]{2,1,0:T(8,128)(2,1)}, u32[]{:S(2)}) copy-start(bf16[1,32,8192]{2,1,0:T(8,128)(2,1)} %param.11) | copy-start | bytes 1572868
  1.5 9.9 %collective-permute-start = (bf16[32,640]{1,0:T(8,128)(2,1)S(1)}, bf16[32,640]{1,0:T(8,128)(2,1)S(1)}, u32[]{:S(2)}, u32[]{:S(2)}) collective-permute-start(bf16[32,640]{1,0:T(8,128)(2,1)S(1)} %get-tuple-element.22), channel_id=1, source_target_pairs={{0,4},{1,5},{2,6},{3,7},{4,0},{5,1},{6,2},{7,3},{8,12},{9,13},{10,... | collective-permute-start | bytes 122888 | tf_op jit(solution)/shard_map/ppermute | solution.py:260
  1.7 9.8 %collective-permute-start.1 = (bf16[32,640]{1,0:T(8,128)(2,1)S(1)}, bf16[32,640]{1,0:T(8,128)(2,1)S(1)}, u32[]{:S(2)}, u32[]{:S(2)}) collective-permute-start(bf16[32,640]{1,0:T(8,128)(2,1)S(1)} %get-tuple-element.22), channel_id=1, source_target_pairs={{0,8},{1,9},{2,10},{3,11},{4,12},{5,13},{6,14},{7,15},{8,0},{9,1},... | collective-permute-start | bytes 122888 | tf_op jit(solution)/shard_map/ppermute | solution.py:260
  4.0 7.4 %collective-permute-start.2 = (bf16[32,640]{1,0:T(8,128)(2,1)S(1)}, bf16[32,640]{1,0:T(8,128)(2,1)S(1)}, u32[]{:S(2)}, u32[]{:S(2)}) collective-permute-start(bf16[32,640]{1,0:T(8,128)(2,1)S(1)} %get-tuple-element.22), channel_id=1, source_target_pairs={{0,12},{1,13},{2,14},{3,15},{4,8},{5,9},{6,10},{7,11},{8,4},{9,5},... | collective-permute-start | bytes 122888 | tf_op jit(solution)/shard_map/ppermute | solution.py:260
  12.3 4.2 %collective-permute-start.3 = (bf16[2,2,32,640]{3,2,1,0:T(8,128)(2,1)S(1)}, bf16[2,2,32,640]{3,2,1,0:T(8,128)(2,1)S(1)}, u32[]{:S(2)}, u32[]{:S(2)}) collective-permute-start(bf16[2,2,32,640]{3,2,1,0:T(8,128)(2,1)S(1)} %broadcast_select_fusion), channel_id=1, source_target_pairs={{0,2},{1,3},{2,0},{3,1},{4,6},{5,7},{6,4},{7,5},{8,10},{9,11},{10,... | collective-permute-start | bytes 491528 | tf_op jit(solution)/shard_map/ppermute | solution.py:268
  16.5 4.0 %collective-permute-start.4 = (bf16[2,2,2,32,640]{4,3,2,1,0:T(8,128)(2,1)S(1)}, bf16[2,2,2,32,640]{4,3,2,1,0:T(8,128)(2,1)S(1)}, u32[]{:S(2)}, u32[]{:S(2)}) collective-permute-start(bf16[2,2,2,32,640]{4,3,2,1,0:T(8,128)(2,1)S(1)} %maximum_select_fusion.1), channel_id=1, source_target_pairs={{0,1},{1,0},{2,3},{3,2},{4,5},{5,4},{6,7},{7,6},{8,9},{9,8},{10,11... | collective-permute-start | bytes 983048 | tf_op jit(solution)/shard_map/ppermute | solution.py:268
  25.6 20.7 %all-to-all-start = ((bf16[16,32,512]{2,1,0:T(8,128)(2,1)}), bf16[16,32,512]{2,1,0:T(8,128)(2,1)S(1)}, u32[]{:S(2)}, u32[]{:S(2)}) async-start(bf16[16,32,512]{2,1,0:T(8,128)(2,1)} %bitcast.74), calls=%async_computation | async-start | bytes 1048576 | tf_op jit(solution)/shard_map/all_to_all | solution.py:315
  46.9 7.5 %copy-start = (bf16[66,8,512]{2,1,0:T(8,128)(2,1)}, bf16[66,8,512]{2,1,0:T(8,128)(2,1)S(1)}, u32[]{:S(2)}) copy-start(bf16[66,8,512]{2,1,0:T(8,128)(2,1)S(1)} %copy.54) | copy-start | bytes 1622020
  47.0 7.4 %collective-permute-start.5 = (bf16[528,256]{1,0:T(8,128)(2,1)S(1)}, bf16[528,256]{1,0:T(8,128)(2,1)S(1)}, u32[]{:S(2)}, u32[]{:S(2)}) collective-permute-start(bf16[528,256]{1,0:T(8,128)(2,1)S(1)} %get-tuple-element.18), channel_id=1, source_target_pairs={{0,1},{1,2},{2,3},{3,4},{4,5},{5,6},{6,7},{7,8},{8,9},{9,10},{10,1... | collective-permute-start | bytes 811016 | tf_op jit(solution)/shard_map/ppermute | solution.py:340
  50.7 8.7 %collective-permute-start.6 = (bf16[528,256]{1,0:T(8,128)(2,1)S(1)}, bf16[528,256]{1,0:T(8,128)(2,1)S(1)}, u32[]{:S(2)}, u32[]{:S(2)}) collective-permute-start(bf16[528,256]{1,0:T(8,128)(2,1)S(1)} %get-tuple-element.17), channel_id=1, source_target_pairs={{1,0},{2,1},{3,2},{4,3},{5,4},{6,5},{7,6},{8,7},{9,8},{10,9},{11,1... | collective-permute-start | bytes 811016 | tf_op jit(solution)/shard_map/ppermute | solution.py:341
  54.4 4.9 %copy-start.2 = (bf16[528,256]{1,0:T(8,128)(2,1)}, bf16[528,256]{1,0:T(8,128)(2,1)S(1)}, u32[]{:S(2)}) copy-start(bf16[528,256]{1,0:T(8,128)(2,1)S(1)} %collective-permute-done.5.low_ref) | copy-start | bytes 811012
  59.3 0.7 %copy-start.3 = (bf16[528,256]{1,0:T(8,128)(2,1)}, bf16[528,256]{1,0:T(8,128)(2,1)S(1)}, u32[]{:S(2)}) copy-start(bf16[528,256]{1,0:T(8,128)(2,1)S(1)} %collective-permute-done.6.high_ref) | copy-start | bytes 811012

commit v19 on v18

--- a/solution.py
+++ b/solution.py
@@ -312,6 +312,9 @@
     corr_all = correlate(
         blk, blocks, weight_table.reshape(slots * block_width, tpix), ref_all, units
     )
+    corr_all, kern_one, kern_two = lax.optimization_barrier((corr_all, kern_one, kern_two))
+    first = banded(kern_one, DEPTH // 4)
+    second = banded(kern_two, DEPTH // 4)
     arriving = lax.all_to_all(
         corr_all.reshape(owners, cap * GROUPS, tpix),
         "view",
@@ -344,8 +347,8 @@
         low,
         volume,
         high,
-        banded(kern_one, DEPTH // 4),
-        banded(kern_two, DEPTH // 4),
+        first,
+        second,
         TROWS,
         columns,
     )

time: 65.5 us -> 62.8 us (0.959)
  local copies, waits for them, and re-layouts: 6.58 us -> 4.72 us
  waiting for transfers between devices: 22.1 us -> 21.2 us
    reshape x1 -> x0, local copies, waits for them, and re-layouts: 1.05 us -> none  [banded(): taps = kernel.reshape((3, 9) + kernel.shape[3:])]
    all_to_all x1, waiting for transfers between devices: 12.2 us -> 11.4 us  [body(): lax.all_to_all(corr_all.reshape(owners, cap * GROUPS, tpix), 'view', spli...]
    unnamed x11 -> x14, local copies, waits for them, and re-layouts: 1.58 us -> 0.88 us
  transfers between devices with their start and end apart: 8 -> 8, of which waited for: 4 -> 4; matrix products, arithmetic and copies ran while one was open for 16% -> 14% of each run, Pallas kernels for 0% -> 0%
where the time goes in v19:
time: 62.8 us; the launch traced here: 62.3 us
  waiting for transfers between devices  21.2 us (34%)
  starting transfers between devices  18.5 us (29%)
  Pallas kernels  9.01 us (14%)
  other arithmetic  7.8 us (12%)
  local copies, waits for them, and re-layouts  4.72 us (8%)
  matrix products  0.78 us (1%)
    all_to_all x1, waiting for transfers between devices, body(): lax.all_to_all(corr_all.reshape(owners, cap * GROUPS, tpix), 'view', spli...  11.4 us
    all_to_all x1, starting transfers between devices, body(): lax.all_to_all(corr_all.reshape(owners, cap * GROUPS, tpix), 'view', spli...  7.29 us
    ppermute x2, waiting for transfers between devices, gather_view(): lax.ppermute(gathered, 'view', [(i, i ^ stride) for i in range(count)])  4.99 us
    pallas_call x1, Pallas kernels, conv_pair(): pl.pallas_call(functools.partial(conv_pair_kernel, rows=rows, cols=cols,...  4.88 us
    ppermute x1, waiting for transfers between devices, body(): high = lax.ppermute(volume[:, :2 * columns], 'view', backward)  4.85 us
    pallas_call x1, Pallas kernels, correlate(): pl.pallas_call(correlate_kernel, out_shape=jax.ShapeDtypeStruct((units *...  4.13 us
    ppermute x1, starting transfers between devices, body(): lax.ppermute(volume[:, volume.shape[1] - 2 * columns:], 'view', forward)  3.64 us
    ppermute x2, starting transfers between devices, gather_view(): lax.ppermute(gathered, 'view', [(i, i ^ stride) for i in range(count)])  3.02 us
  transfers between devices with their start and end apart: 8, of which 4 were waited for; matrix products, arithmetic and copies ran while one was open for 14% of the time, Pallas kernels for 0%

profile of v19, /device:TPU:13, one launch (start us, length us, event | category | flops | bytes accessed | tf_op | source)
XLA Modules:
  0.0 62.3 jit_solution(11317454791692427808)
XLA Ops:
  0.0 0.7 %fusion.18 = bf16[64]{0:T(256)(128)(2,1)S(1)} fusion(s32[1,64]{1,0:T(1,128)} %param.17, s32[1,64]{1,0:T(1,128)} %param.16), kind=kLoop, calls=%fused_computation.60 | loop fusion | flops 192 | bytes 640 | tf_op jit(solution)/shard_map/convert_element_type | solution.py:308
  0.7 0.8 %fusion.20 = (bf16[1,32,640]{2,1,0:T(8,128)(2,1)S(1)}, bf16[32,640]{1,0:T(8,128)(2,1)S(1)}) fusion(bf16[32,128]{1,0:T(8,128)(2,1)S(1)} %pad_bitcast_fusion, bf16[32,512]{1,0:T(8,128)(2,1)} %bitcast.85), kind=kLoop, calls=%fused_computation.66 | loop fusion | flops 81920 | bytes 122880 | tf_op jit(solution)/shard_map/broadcast_in_dim | solution.py:311
  1.7 2.3 %collective-permute-start.1 = (bf16[32,640]{1,0:T(8,128)(2,1)S(1)}, bf16[32,640]{1,0:T(8,128)(2,1)S(1)}, u32[]{:S(2)}, u32[]{:S(2)}) collective-permute-start(bf16[32,640]{1,0:T(8,128)(2,1)S(1)} %get-tuple-element.28), channel_id=1, source_target_pairs={{0,8},{1,9},{2,10},{3,11},{4,12},{5,13},{6,14},{7,15},{8,0},{9,1},... | collective-permute-start | bytes 122888 | tf_op jit(solution)/shard_map/ppermute | solution.py:260
  4.2 0.7 %iota_compare_fusion.2 = pred[64,4]{0,1:T(4,128)(4,1)S(1)} fusion(s32[64]{0:T(128)} %bitcast.89), kind=kLoop, calls=%fused_computation.51 | loop fusion | flops 256 | bytes 512 | tf_op jit(solution)/shard_map/lt | solution.py:304
  4.9 0.7 %select_reduce_fusion.2 = s32[64,4]{0,1:T(4,128)S(1)} fusion(s32[64,4]{0,1:T(4,128)} %bitcast.88, s32[64,4]{0,1:T(4,128)} %bitcast.86), kind=kLoop, calls=%fused_computation.33 | loop fusion | flops 2816 | bytes 3072 | tf_op jit(solution)/shard_map/reduce_sum | solution.py:305
  5.6 0.7 %fusion.10 = pred[64,4]{0,1:T(4,128)(4,1)S(1)} fusion(s32[64,4]{0,1:T(4,128)} %bitcast.87, pred[64,4]{0,1:T(4,128)(4,1)S(1)} %iota_compare_fusion.2), kind=kLoop, calls=%fused_computation.40 | loop fusion | flops 2816 | bytes 1536 | tf_op jit(solution)/shard_map/reduce_or | solution.py:306
  6.7 0.7 %select_n.180.blk_ref = s32[256]{0:T(256)} reshape(s32[64,4]{1,0:T(8,128)S(1)} %copy.32) | data formatting | bytes 2048 | tf_op jit(solution)/shard_map/jit(_where)/select_n | solution.py:307
  7.9 0.8 %concatenate.23.blocks_ref = bf16[65,32,128]{2,1,0:T(8,128)(2,1)} pad(bf16[64,32,128]{2,1,0:T(8,128)(2,1)S(1)} %bitcast.69, bf16[]{:T(256)} %constant.153.clone.1), padding=0_1x0_0x0_0 | pad | bytes 1056770 | tf_op jit(solution)/shard_map/concatenate | solution.py:302
  9.9 3.8 %collective-permute-done.3 = bf16[2,2,32,640]{3,2,1,0:T(8,128)(2,1)S(1)} collective-permute-done((bf16[2,2,32,640]{3,2,1,0:T(8,128)(2,1)S(1)}, bf16[2,2,32,640]{3,2,1,0:T(8,128)(2,1)S(1)}, u32[]{:S(2)}, u32[]{:S(2)}) %collective-permute-start.3) | collective-permute-done | bytes 163872 | tf_op jit(solution)/shard_map/ppermute | solution.py:268
  13.8 2.7 %collective-permute-start.4 = (bf16[2,2,2,32,640]{4,3,2,1,0:T(8,128)(2,1)S(1)}, bf16[2,2,2,32,640]{4,3,2,1,0:T(8,128)(2,1)S(1)}, u32[]{:S(2)}, u32[]{:S(2)}) collective-permute-start(bf16[2,2,2,32,640]{4,3,2,1,0:T(8,128)(2,1)S(1)} %maximum_select_fusion.1), channel_id=1, source_target_pairs={{0,1},{1,0},{2,3},{3,2},{4,5},{5,4},{6,7},{7,6},{8,9},{9,8},{10,11... | collective-permute-start | bytes 983048 | tf_op jit(solution)/shard_map/ppermute | solution.py:268
  16.7 1.1 %collective-permute-done.4 = bf16[2,2,2,32,640]{4,3,2,1,0:T(8,128)(2,1)S(1)} collective-permute-done((bf16[2,2,2,32,640]{4,3,2,1,0:T(8,128)(2,1)S(1)}, bf16[2,2,2,32,640]{4,3,2,1,0:T(8,128)(2,1)S(1)}, u32[]{:S(2)}, u32[]{:S(2)}) %collective-permute-start.4) | collective-permute-done | bytes 327712 | tf_op jit(solution)/shard_map/ppermute | solution.py:268
  17.8 0.9 %maximum_select_fusion = bf16[2,2,2,2,32,640]{5,4,3,2,1,0:T(8,128)(2,1)} fusion(bf16[2,2,2,1,32,640]{5,4,3,2,1,0:T(8,128)(2,1)S(1)} %bitcast.78, bf16[2,2,2,1,32,640]{5,4,3,2,1,0:T(8,128)(2,1)S(1)} %copy_select_fusion, pred[]{:T(512)S(6)} %eq.111), kind=kLoop, calls=%fused_computation.4 | loop fusion | flops 983040 | bytes 1310721 | tf_op jit(solution)/shard_map/jit(_where)/select_n | solution.py:270
  18.7 4.1 %shard_map.91 = bf16[512,512]{1,0:T(8,128)(2,1)} custom-call(s32[256]{0:T(256)} %select_n.180.blk_ref, bf16[65,32,128]{2,1,0:T(8,128)(2,1)} %concatenate.23.blocks_ref, bf16[512,512]{1,0:T(8,128)(2,1)} %bitcast.77, bf16[16,32,640]{2,1,0:T(8,128)(2,1)} %bitcast.63), custom_call_target="tpu_custom_call" | custom-call | tf_op jit(solution)/shard_map/pallas_call | solution.py:121
  22.9 7.3 %all-to-all-start = ((bf16[16,32,512]{2,1,0:T(8,128)(2,1)}), bf16[16,32,512]{2,1,0:T(8,128)(2,1)S(1)}, u32[]{:S(2)}, u32[]{:S(2)}) async-start(bf16[16,32,512]{2,1,0:T(8,128)(2,1)} %bitcast.71), calls=%async_computation | async-start | bytes 1048576 | tf_op jit(solution)/shard_map/all_to_all | solution.py:318
  30.2 0.6 add_convert_fusion.ends_ref
  30.7 0.9 %slice.24 = bf16[16,32,128]{2,1,0:T(8,128)(2,1)S(1)} slice(bf16[16,32,640]{2,1,0:T(8,128)(2,1)} %bitcast.64), slice={[0:16], [0:32], [512:640]} | slice | bytes 262144 | tf_op jit(solution)/shard_map/slice | solution.py:326
  32.4 11.4 %all-to-all-done = bf16[16,32,512]{2,1,0:T(8,128)(2,1)S(1)} async-done(((bf16[16,32,512]{2,1,0:T(8,128)(2,1)}), bf16[16,32,512]{2,1,0:T(8,128)(2,1)S(1)}, u32[]{:S(2)}, u32[]{:S(2)}) %all-to-all-start) | async-done | bytes 524320 | tf_op jit(solution)/shard_map/all_to_all | solution.py:318
  44.4 3.6 %collective-permute-start.5 = (bf16[528,256]{1,0:T(8,128)(2,1)S(1)}, bf16[528,256]{1,0:T(8,128)(2,1)S(1)}, u32[]{:S(2)}, u32[]{:S(2)}) collective-permute-start(bf16[528,256]{1,0:T(8,128)(2,1)S(1)} %get-tuple-element.24), channel_id=1, source_target_pairs={{0,1},{1,2},{2,3},{3,4},{4,5},{5,6},{6,7},{7,8},{8,9},{9,10},{10,1... | collective-permute-start | bytes 811016 | tf_op jit(solution)/shard_map/ppermute | solution.py:343
  48.1 1.9 %collective-permute-start.6 = (bf16[528,256]{1,0:T(8,128)(2,1)S(1)}, bf16[528,256]{1,0:T(8,128)(2,1)S(1)}, u32[]{:S(2)}, u32[]{:S(2)}) collective-permute-start(bf16[528,256]{1,0:T(8,128)(2,1)S(1)} %get-tuple-element.23), channel_id=1, source_target_pairs={{1,0},{2,1},{3,2},{4,3},{5,4},{6,5},{7,6},{8,7},{9,8},{10,9},{11,1... | collective-permute-start | bytes 811016 | tf_op jit(solution)/shard_map/ppermute | solution.py:344
  50.0 0.7 %select_reduce_fusion.1 = bf16[9,16,144]{2,1,0:T(8,128)(2,1)} fusion(f32[3,9,144]{2,1,0:T(8,128)S(1)} %fusion.2, pred[3,16,144]{2,1,0:T(8,128)(4,1)S(1)} %broadcast_compare_fusion.1), kind=kLoop, calls=%fused_computation.8 | loop fusion | flops 103680 | bytes 63936 | tf_op jit(solution)/shard_map/reduce_sum | solution.py:191
  50.7 1.2 %select_reduce_fusion = bf16[9,16,8,144]{3,2,1,0:T(8,128)(2,1)} fusion(f32[3,9,8,144]{3,2,1,0:T(8,128)S(1)} %fusion.11, pred[3,16,8,144]{3,2,1,0:T(8,128)(4,1)S(1)} %broadcast_compare_fusion), kind=kLoop, calls=%fused_computation.1 | loop fusion | flops 829440 | bytes 511488 | tf_op jit(solution)/shard_map/reduce_sum | solution.py:191
  51.9 4.9 %collective-permute-done.6.high_ref = bf16[528,256]{1,0:T(8,128)(2,1)S(1)} collective-permute-done((bf16[528,256]{1,0:T(8,128)(2,1)S(1)}, bf16[528,256]{1,0:T(8,128)(2,1)S(1)}, u32[]{:S(2)}, u32[]{:S(2)}) %collective-permute-start.6) | collective-permute-done | bytes 270368 | tf_op jit(solution)/shard_map/ppermute | solution.py:344
  56.7 0.7 %copy-done.4 = bf16[528,256]{1,0:T(8,128)(2,1)} copy-done((bf16[528,256]{1,0:T(8,128)(2,1)}, bf16[528,256]{1,0:T(8,128)(2,1)S(1)}, u32[]{:S(2)}) %copy-start.4) | copy-done | bytes 270360
  57.4 4.9 %shard_map.92 = f32[4,64,128]{2,1,0:T(8,128)} custom-call(s32[2]{0:T(128)} %add_convert_fusion.ends_ref, bf16[528,256]{1,0:T(8,128)(2,1)} %copy-done.3, bf16[528,512]{1,0:T(8,128)(2,1)} %bitcast.62, bf16[528,256]{1,0:T(8,128)(2,1)} %copy-done.4, bf16[3,3,128,144]{3,2,1,0:T(8,128)(2,1)} %bitcast.68, bf16[3,3,16,144]{3,2,1,0:T(8,128)(2,1)} %bitcast.79), custom_call_target="tpu_custom_call" | custom-call | tf_op jit(solution)/shard_map/pallas_call | solution.py:226
  (55 shorter events, 3.9 us)
Async XLA Ops:
  0.0 32.2 %copy-start = (bf16[3,3,3,8,8]{4,3,2,1,0:T(8,128)(2,1)S(1)}, bf16[3,3,3,8,8]{4,3,2,1,0:T(8,128)(2,1)}, u32[]{:S(2)}) copy-start(bf16[3,3,3,8,8]{4,3,2,1,0:T(8,128)(2,1)} %param.18) | copy-start | bytes 10372
  0.0 7.4 %copy-start.2 = (bf16[1,32,8192]{2,1,0:T(8,128)(2,1)S(1)}, bf16[1,32,8192]{2,1,0:T(8,128)(2,1)}, u32[]{:S(2)}) copy-start(bf16[1,32,8192]{2,1,0:T(8,128)(2,1)} %param.11) | copy-start | bytes 1572868
  1.5 7.2 %collective-permute-start = (bf16[32,640]{1,0:T(8,128)(2,1)S(1)}, bf16[32,640]{1,0:T(8,128)(2,1)S(1)}, u32[]{:S(2)}, u32[]{:S(2)}) collective-permute-start(bf16[32,640]{1,0:T(8,128)(2,1)S(1)} %get-tuple-element.28), channel_id=1, source_target_pairs={{0,4},{1,5},{2,6},{3,7},{4,0},{5,1},{6,2},{7,3},{8,12},{9,13},{10,... | collective-permute-start | bytes 122888 | tf_op jit(solution)/shard_map/ppermute | solution.py:260
  1.7 7.0 %collective-permute-start.1 = (bf16[32,640]{1,0:T(8,128)(2,1)S(1)}, bf16[32,640]{1,0:T(8,128)(2,1)S(1)}, u32[]{:S(2)}, u32[]{:S(2)}) collective-permute-start(bf16[32,640]{1,0:T(8,128)(2,1)S(1)} %get-tuple-element.28), channel_id=1, source_target_pairs={{0,8},{1,9},{2,10},{3,11},{4,12},{5,13},{6,14},{7,15},{8,0},{9,1},... | collective-permute-start | bytes 122888 | tf_op jit(solution)/shard_map/ppermute | solution.py:260
  4.0 4.7 %collective-permute-start.2 = (bf16[32,640]{1,0:T(8,128)(2,1)S(1)}, bf16[32,640]{1,0:T(8,128)(2,1)S(1)}, u32[]{:S(2)}, u32[]{:S(2)}) collective-permute-start(bf16[32,640]{1,0:T(8,128)(2,1)S(1)} %get-tuple-element.28), channel_id=1, source_target_pairs={{0,12},{1,13},{2,14},{3,15},{4,8},{5,9},{6,10},{7,11},{8,4},{9,5},... | collective-permute-start | bytes 122888 | tf_op jit(solution)/shard_map/ppermute | solution.py:260
  9.5 4.2 %collective-permute-start.3 = (bf16[2,2,32,640]{3,2,1,0:T(8,128)(2,1)S(1)}, bf16[2,2,32,640]{3,2,1,0:T(8,128)(2,1)S(1)}, u32[]{:S(2)}, u32[]{:S(2)}) collective-permute-start(bf16[2,2,32,640]{3,2,1,0:T(8,128)(2,1)S(1)} %broadcast_select_fusion), channel_id=1, source_target_pairs={{0,2},{1,3},{2,0},{3,1},{4,6},{5,7},{6,4},{7,5},{8,10},{9,11},{10,... | collective-permute-start | bytes 491528 | tf_op jit(solution)/shard_map/ppermute | solution.py:268
  13.8 4.0 %collective-permute-start.4 = (bf16[2,2,2,32,640]{4,3,2,1,0:T(8,128)(2,1)S(1)}, bf16[2,2,2,32,640]{4,3,2,1,0:T(8,128)(2,1)S(1)}, u32[]{:S(2)}, u32[]{:S(2)}) collective-permute-start(bf16[2,2,2,32,640]{4,3,2,1,0:T(8,128)(2,1)S(1)} %maximum_select_fusion.1), channel_id=1, source_target_pairs={{0,1},{1,0},{2,3},{3,2},{4,5},{5,4},{6,7},{7,6},{8,9},{9,8},{10,11... | collective-permute-start | bytes 983048 | tf_op jit(solution)/shard_map/ppermute | solution.py:268
  22.9 9.1 %copy-start.5 = (bf16[3,3,3,8]{3,2,1,0:T(4,128)(2,1)S(1)}, bf16[3,3,3,8]{3,2,1,0:T(4,128)(2,1)}, u32[]{:S(2)}) copy-start(bf16[3,3,3,8]{3,2,1,0:T(4,128)(2,1)} %param.19) | copy-start | bytes 1300
  22.9 20.9 %all-to-all-start = ((bf16[16,32,512]{2,1,0:T(8,128)(2,1)}), bf16[16,32,512]{2,1,0:T(8,128)(2,1)S(1)}, u32[]{:S(2)}, u32[]{:S(2)}) async-start(bf16[16,32,512]{2,1,0:T(8,128)(2,1)} %bitcast.71), calls=%async_computation | async-start | bytes 1048576 | tf_op jit(solution)/shard_map/all_to_all | solution.py:318
  44.4 7.5 %copy-start.1 = (bf16[66,8,512]{2,1,0:T(8,128)(2,1)}, bf16[66,8,512]{2,1,0:T(8,128)(2,1)S(1)}, u32[]{:S(2)}) copy-start(bf16[66,8,512]{2,1,0:T(8,128)(2,1)S(1)} %copy.52) | copy-start | bytes 1622020
  44.4 7.5 %collective-permute-start.5 = (bf16[528,256]{1,0:T(8,128)(2,1)S(1)}, bf16[528,256]{1,0:T(8,128)(2,1)S(1)}, u32[]{:S(2)}, u32[]{:S(2)}) collective-permute-start(bf16[528,256]{1,0:T(8,128)(2,1)S(1)} %get-tuple-element.24), channel_id=1, source_target_pairs={{0,1},{1,2},{2,3},{3,4},{4,5},{5,6},{6,7},{7,8},{8,9},{9,10},{10,1... | collective-permute-start | bytes 811016 | tf_op jit(solution)/shard_map/ppermute | solution.py:343
  48.1 8.7 %collective-permute-start.6 = (bf16[528,256]{1,0:T(8,128)(2,1)S(1)}, bf16[528,256]{1,0:T(8,128)(2,1)S(1)}, u32[]{:S(2)}, u32[]{:S(2)}) collective-permute-start(bf16[528,256]{1,0:T(8,128)(2,1)S(1)} %get-tuple-element.23), channel_id=1, source_target_pairs={{1,0},{2,1},{3,2},{4,3},{5,4},{6,5},{7,6},{8,7},{9,8},{10,9},{11,1... | collective-permute-start | bytes 811016 | tf_op jit(solution)/shard_map/ppermute | solution.py:344
  51.9 4.9 %copy-start.3 = (bf16[528,256]{1,0:T(8,128)(2,1)}, bf16[528,256]{1,0:T(8,128)(2,1)S(1)}, u32[]{:S(2)}) copy-start(bf16[528,256]{1,0:T(8,128)(2,1)S(1)} %collective-permute-done.5.low_ref) | copy-start | bytes 811012
  56.7 0.7 %copy-start.4 = (bf16[528,256]{1,0:T(8,128)(2,1)}, bf16[528,256]{1,0:T(8,128)(2,1)S(1)}, u32[]{:S(2)}) copy-start(bf16[528,256]{1,0:T(8,128)(2,1)S(1)} %collective-permute-done.6.high_ref) | copy-start | bytes 811012

commit v20 on v19

--- a/solution.py
+++ b/solution.py
@@ -322,6 +322,7 @@
         concat_axis=0,
         tiled=True,
     ).reshape(owners * cap, GROUPS, tpix)
+    arriving, first, second = lax.optimization_barrier((arriving, first, second))
     depth_tags = lax.dynamic_slice_in_dim(
         ref_all[:, :, tpix:].reshape(owners, channels * 128), lax.axis_index("view") * cap, cap, axis=1
     ).reshape(owners * cap)

time: 62.8 us -> 62.3 us (level)
  the two profiles are of different devices: /device:TPU:13 before, /device:TPU:1 now
where the time goes in v20:
time: 62.3 us; the launch traced here: 61.9 us
  starting transfers between devices  20.2 us (32%)
  waiting for transfers between devices  20.1 us (32%)
  Pallas kernels  9 us (14%)
  other arithmetic  7.07 us (11%)
  local copies, waits for them, and re-layouts  4.47 us (7%)
  matrix products  0.77 us (1%)
    all_to_all x1, waiting for transfers between devices, body(): lax.all_to_all(corr_all.reshape(owners, cap * GROUPS, tpix), 'view', spli...  11.7 us
    all_to_all x1, starting transfers between devices, body(): lax.all_to_all(corr_all.reshape(owners, cap * GROUPS, tpix), 'view', spli...  5.37 us
    pallas_call x1, Pallas kernels, conv_pair(): pl.pallas_call(functools.partial(conv_pair_kernel, rows=rows, cols=cols,...  4.88 us
    ppermute x2, starting transfers between devices, gather_view(): lax.ppermute(gathered, 'view', [(i, i ^ stride) for i in range(count)])  4.8 us
    ppermute x3, starting transfers between devices, gather_view(): lax.ppermute(gathered, 'view', [(i, i ^ m * top) for i in range(count)])  4.44 us
    pallas_call x1, Pallas kernels, correlate(): pl.pallas_call(correlate_kernel, out_shape=jax.ShapeDtypeStruct((units *...  4.11 us
    ppermute x2, waiting for transfers between devices, gather_view(): lax.ppermute(gathered, 'view', [(i, i ^ stride) for i in range(count)])  3.98 us
    ppermute x1, starting transfers between devices, body(): lax.ppermute(volume[:, volume.shape[1] - 2 * columns:], 'view', forward)  3.16 us
  transfers between devices with their start and end apart: 8, of which 6 were waited for; matrix products, arithmetic and copies ran while one was open for 12% of the time, Pallas kernels for 0%

profile of v20, /device:TPU:1, one launch (start us, length us, event | category | flops | bytes accessed | tf_op | source)
XLA Modules:
  0.0 61.9 jit_solution(10946035821479272057)
XLA Ops:
  0.0 0.7 %fusion.18 = bf16[64]{0:T(256)(128)(2,1)S(1)} fusion(s32[1,64]{1,0:T(1,128)} %param.17, s32[1,64]{1,0:T(1,128)} %param.16), kind=kLoop, calls=%fused_computation.60 | loop fusion | flops 192 | bytes 640 | tf_op jit(solution)/shard_map/convert_element_type | solution.py:308
  0.7 0.8 %fusion.20 = (bf16[1,32,640]{2,1,0:T(8,128)(2,1)S(1)}, bf16[32,640]{1,0:T(8,128)(2,1)S(1)}) fusion(bf16[32,128]{1,0:T(8,128)(2,1)S(1)} %pad_bitcast_fusion, bf16[32,512]{1,0:T(8,128)(2,1)} %bitcast.85), kind=kLoop, calls=%fused_computation.66 | loop fusion | flops 81920 | bytes 122880 | tf_op jit(solution)/shard_map/broadcast_in_dim | solution.py:311
  1.5 3.1 %collective-permute-start.1 = (bf16[32,640]{1,0:T(8,128)(2,1)S(1)}, bf16[32,640]{1,0:T(8,128)(2,1)S(1)}, u32[]{:S(2)}, u32[]{:S(2)}) collective-permute-start(bf16[32,640]{1,0:T(8,128)(2,1)S(1)} %get-tuple-element.34), channel_id=1, source_target_pairs={{0,8},{1,9},{2,10},{3,11},{4,12},{5,13},{6,14},{7,15},{8,0},{9,1},... | collective-permute-start | bytes 122888 | tf_op jit(solution)/shard_map/ppermute | solution.py:260
  4.7 1.3 %collective-permute-start = (bf16[32,640]{1,0:T(8,128)(2,1)S(1)}, bf16[32,640]{1,0:T(8,128)(2,1)S(1)}, u32[]{:S(2)}, u32[]{:S(2)}) collective-permute-start(bf16[32,640]{1,0:T(8,128)(2,1)S(1)} %get-tuple-element.34), channel_id=1, source_target_pairs={{0,4},{1,5},{2,6},{3,7},{4,0},{5,1},{6,2},{7,3},{8,12},{9,13},{10,... | collective-permute-start | bytes 122888 | tf_op jit(solution)/shard_map/ppermute | solution.py:260
  6.7 0.7 %fusion.10 = pred[64,4]{0,1:T(4,128)(4,1)S(1)} fusion(s32[64,4]{0,1:T(4,128)} %bitcast.86, pred[64,4]{0,1:T(4,128)(4,1)S(1)} %iota_compare_fusion.2), kind=kLoop, calls=%fused_computation.40 | loop fusion | flops 2816 | bytes 1536 | tf_op jit(solution)/shard_map/reduce_or | solution.py:306
  7.4 0.7 %select_reduce_fusion.2 = s32[64,4]{0,1:T(4,128)S(1)} fusion(s32[64,4]{0,1:T(4,128)} %bitcast.88, s32[64,4]{0,1:T(4,128)} %bitcast.87), kind=kLoop, calls=%fused_computation.33 | loop fusion | flops 2816 | bytes 3072 | tf_op jit(solution)/shard_map/reduce_sum | solution.py:305
  8.5 0.7 %select_n.180.blk_ref = s32[256]{0:T(256)} reshape(s32[64,4]{1,0:T(8,128)S(1)} %copy.32) | data formatting | bytes 2048 | tf_op jit(solution)/shard_map/jit(_where)/select_n | solution.py:307
  9.7 0.9 %concatenate.23.blocks_ref = bf16[65,32,128]{2,1,0:T(8,128)(2,1)} pad(bf16[64,32,128]{2,1,0:T(8,128)(2,1)S(1)} %bitcast.69, bf16[]{:T(256)} %constant.153.clone.1), padding=0_1x0_0x0_0 | pad | bytes 1056770 | tf_op jit(solution)/shard_map/concatenate | solution.py:302
  11.5 1.3 %collective-permute-start.3 = (bf16[2,2,32,640]{3,2,1,0:T(8,128)(2,1)S(1)}, bf16[2,2,32,640]{3,2,1,0:T(8,128)(2,1)S(1)}, u32[]{:S(2)}, u32[]{:S(2)}) collective-permute-start(bf16[2,2,32,640]{3,2,1,0:T(8,128)(2,1)S(1)} %broadcast_select_fusion), channel_id=1, source_target_pairs={{0,2},{1,3},{2,0},{3,1},{4,6},{5,7},{6,4},{7,5},{8,10},{9,11},{10,... | collective-permute-start | bytes 491528 | tf_op jit(solution)/shard_map/ppermute | solution.py:268
  12.9 2.8 %collective-permute-done.3 = bf16[2,2,32,640]{3,2,1,0:T(8,128)(2,1)S(1)} collective-permute-done((bf16[2,2,32,640]{3,2,1,0:T(8,128)(2,1)S(1)}, bf16[2,2,32,640]{3,2,1,0:T(8,128)(2,1)S(1)}, u32[]{:S(2)}, u32[]{:S(2)}) %collective-permute-start.3) | collective-permute-done | bytes 163872 | tf_op jit(solution)/shard_map/ppermute | solution.py:268
  15.8 3.5 %collective-permute-start.4 = (bf16[2,2,2,32,640]{4,3,2,1,0:T(8,128)(2,1)S(1)}, bf16[2,2,2,32,640]{4,3,2,1,0:T(8,128)(2,1)S(1)}, u32[]{:S(2)}, u32[]{:S(2)}) collective-permute-start(bf16[2,2,2,32,640]{4,3,2,1,0:T(8,128)(2,1)S(1)} %maximum_select_fusion.1), channel_id=1, source_target_pairs={{0,1},{1,0},{2,3},{3,2},{4,5},{5,4},{6,7},{7,6},{8,9},{9,8},{10,11... | collective-permute-start | bytes 983048 | tf_op jit(solution)/shard_map/ppermute | solution.py:268
  19.4 1.1 %collective-permute-done.4 = bf16[2,2,2,32,640]{4,3,2,1,0:T(8,128)(2,1)S(1)} collective-permute-done((bf16[2,2,2,32,640]{4,3,2,1,0:T(8,128)(2,1)S(1)}, bf16[2,2,2,32,640]{4,3,2,1,0:T(8,128)(2,1)S(1)}, u32[]{:S(2)}, u32[]{:S(2)}) %collective-permute-start.4) | collective-permute-done | bytes 327712 | tf_op jit(solution)/shard_map/ppermute | solution.py:268
  21.5 4.1 %shard_map.91 = bf16[512,512]{1,0:T(8,128)(2,1)} custom-call(s32[256]{0:T(256)} %select_n.180.blk_ref, bf16[65,32,128]{2,1,0:T(8,128)(2,1)} %concatenate.23.blocks_ref, bf16[512,512]{1,0:T(8,128)(2,1)} %bitcast.77, bf16[16,32,640]{2,1,0:T(8,128)(2,1)} %bitcast.64), custom_call_target="tpu_custom_call" | custom-call | tf_op jit(solution)/shard_map/pallas_call | solution.py:121
  25.6 5.4 %all-to-all-start = ((bf16[16,32,512]{2,1,0:T(8,128)(2,1)}), bf16[16,32,512]{2,1,0:T(8,128)(2,1)S(1)}, u32[]{:S(2)}, u32[]{:S(2)}) async-start(bf16[16,32,512]{2,1,0:T(8,128)(2,1)} %bitcast.71), calls=%async_computation | async-start | bytes 1048576 | tf_op jit(solution)/shard_map/all_to_all | solution.py:318
  31.2 0.7 %select_reduce_fusion.1 = bf16[9,16,144]{2,1,0:T(8,128)(2,1)} fusion(f32[3,9,144]{2,1,0:T(8,128)S(1)} %fusion.2, pred[3,16,144]{2,1,0:T(8,128)(4,1)S(1)} %broadcast_compare_fusion.1), kind=kLoop, calls=%fused_computation.8 | loop fusion | flops 103680 | bytes 63936 | tf_op jit(solution)/shard_map/reduce_sum | solution.py:191
  32.1 1.2 %select_reduce_fusion = bf16[9,16,8,144]{3,2,1,0:T(8,128)(2,1)} fusion(f32[3,9,8,144]{3,2,1,0:T(8,128)S(1)} %fusion.11, pred[3,16,8,144]{3,2,1,0:T(8,128)(4,1)S(1)} %broadcast_compare_fusion), kind=kLoop, calls=%fused_computation.1 | loop fusion | flops 829440 | bytes 511488 | tf_op jit(solution)/shard_map/reduce_sum | solution.py:191
  33.4 11.7 %all-to-all-done = bf16[16,32,512]{2,1,0:T(8,128)(2,1)S(1)} async-done(((bf16[16,32,512]{2,1,0:T(8,128)(2,1)}), bf16[16,32,512]{2,1,0:T(8,128)(2,1)S(1)}, u32[]{:S(2)}, u32[]{:S(2)}) %all-to-all-start) | async-done | bytes 524320 | tf_op jit(solution)/shard_map/all_to_all | solution.py:318
  45.7 2.4 %collective-permute-start.6 = (bf16[528,256]{1,0:T(8,128)(2,1)S(1)}, bf16[528,256]{1,0:T(8,128)(2,1)S(1)}, u32[]{:S(2)}, u32[]{:S(2)}) collective-permute-start(bf16[528,256]{1,0:T(8,128)(2,1)S(1)} %get-tuple-element.29), channel_id=1, source_target_pairs={{1,0},{2,1},{3,2},{4,3},{5,4},{6,5},{7,6},{8,7},{9,8},{10,9},{11,1... | collective-permute-start | bytes 811016 | tf_op jit(solution)/shard_map/ppermute | solution.py:345
  48.1 3.2 %collective-permute-start.5 = (bf16[528,256]{1,0:T(8,128)(2,1)S(1)}, bf16[528,256]{1,0:T(8,128)(2,1)S(1)}, u32[]{:S(2)}, u32[]{:S(2)}) collective-permute-start(bf16[528,256]{1,0:T(8,128)(2,1)S(1)} %get-tuple-element.30), channel_id=1, source_target_pairs={{0,1},{1,2},{2,3},{3,4},{4,5},{5,6},{6,7},{7,8},{8,9},{9,10},{10,1... | collective-permute-start | bytes 811016 | tf_op jit(solution)/shard_map/ppermute | solution.py:344
  51.3 0.7 %add_convert_fusion.ends_ref = s32[2]{0:T(128)} fusion(pred[1]{0:T(512)(128)(4,1)} %bitcast.1, pred[1]{0:T(512)(128)(4,1)} %bitcast), kind=kLoop, calls=%fused_computation.52 | loop fusion | flops 4 | bytes 10 | tf_op jit(solution)/shard_map/convert_element_type | solution.py:340
  52.0 1.5 %collective-permute-done.6.high_ref = bf16[528,256]{1,0:T(8,128)(2,1)S(1)} collective-permute-done((bf16[528,256]{1,0:T(8,128)(2,1)S(1)}, bf16[528,256]{1,0:T(8,128)(2,1)S(1)}, u32[]{:S(2)}, u32[]{:S(2)}) %collective-permute-start.6) | collective-permute-done | bytes 270368 | tf_op jit(solution)/shard_map/ppermute | solution.py:345
  53.5 2.8 %collective-permute-done.5.low_ref = bf16[528,256]{1,0:T(8,128)(2,1)S(1)} collective-permute-done((bf16[528,256]{1,0:T(8,128)(2,1)S(1)}, bf16[528,256]{1,0:T(8,128)(2,1)S(1)}, u32[]{:S(2)}, u32[]{:S(2)}) %collective-permute-start.5) | collective-permute-done | bytes 270368 | tf_op jit(solution)/shard_map/ppermute | solution.py:344
  56.3 0.7 %copy-done.5 = bf16[528,256]{1,0:T(8,128)(2,1)} copy-done((bf16[528,256]{1,0:T(8,128)(2,1)}, bf16[528,256]{1,0:T(8,128)(2,1)S(1)}, u32[]{:S(2)}) %copy-start.5) | copy-done | bytes 270360
  57.0 4.9 %shard_map.92 = f32[4,64,128]{2,1,0:T(8,128)} custom-call(s32[2]{0:T(128)} %add_convert_fusion.ends_ref, bf16[528,256]{1,0:T(8,128)(2,1)} %copy-done.5, bf16[528,512]{1,0:T(8,128)(2,1)} %bitcast.62, bf16[528,256]{1,0:T(8,128)(2,1)} %copy-done.4, bf16[3,3,128,144]{3,2,1,0:T(8,128)(2,1)} %bitcast.68, bf16[3,3,16,144]{3,2,1,0:T(8,128)(2,1)} %bitcast.79), custom_call_target="tpu_custom_call" | custom-call | tf_op jit(solution)/shard_map/pallas_call | solution.py:226
  (57 shorter events, 4.7 us)
Async XLA Ops:
  0.0 31.9 %copy-start = (bf16[3,3,3,8,8]{4,3,2,1,0:T(8,128)(2,1)S(1)}, bf16[3,3,3,8,8]{4,3,2,1,0:T(8,128)(2,1)}, u32[]{:S(2)}) copy-start(bf16[3,3,3,8,8]{4,3,2,1,0:T(8,128)(2,1)} %param.18) | copy-start | bytes 10372
  0.0 9.2 %copy-start.3 = (bf16[1,32,8192]{2,1,0:T(8,128)(2,1)S(1)}, bf16[1,32,8192]{2,1,0:T(8,128)(2,1)}, u32[]{:S(2)}) copy-start(bf16[1,32,8192]{2,1,0:T(8,128)(2,1)} %param.11) | copy-start | bytes 1572868
  1.5 9.0 %collective-permute-start.1 = (bf16[32,640]{1,0:T(8,128)(2,1)S(1)}, bf16[32,640]{1,0:T(8,128)(2,1)S(1)}, u32[]{:S(2)}, u32[]{:S(2)}) collective-permute-start(bf16[32,640]{1,0:T(8,128)(2,1)S(1)} %get-tuple-element.34), channel_id=1, source_target_pairs={{0,8},{1,9},{2,10},{3,11},{4,12},{5,13},{6,14},{7,15},{8,0},{9,1},... | collective-permute-start | bytes 122888 | tf_op jit(solution)/shard_map/ppermute | solution.py:260
  4.7 5.9 %collective-permute-start = (bf16[32,640]{1,0:T(8,128)(2,1)S(1)}, bf16[32,640]{1,0:T(8,128)(2,1)S(1)}, u32[]{:S(2)}, u32[]{:S(2)}) collective-permute-start(bf16[32,640]{1,0:T(8,128)(2,1)S(1)} %get-tuple-element.34), channel_id=1, source_target_pairs={{0,4},{1,5},{2,6},{3,7},{4,0},{5,1},{6,2},{7,3},{8,12},{9,13},{10,... | collective-permute-start | bytes 122888 | tf_op jit(solution)/shard_map/ppermute | solution.py:260
  5.9 4.8 %collective-permute-start.2 = (bf16[32,640]{1,0:T(8,128)(2,1)S(1)}, bf16[32,640]{1,0:T(8,128)(2,1)S(1)}, u32[]{:S(2)}, u32[]{:S(2)}) collective-permute-start(bf16[32,640]{1,0:T(8,128)(2,1)S(1)} %get-tuple-element.34), channel_id=1, source_target_pairs={{0,12},{1,13},{2,14},{3,15},{4,8},{5,9},{6,10},{7,11},{8,4},{9,5},... | collective-permute-start | bytes 122888 | tf_op jit(solution)/shard_map/ppermute | solution.py:260
  11.5 4.2 %collective-permute-start.3 = (bf16[2,2,32,640]{3,2,1,0:T(8,128)(2,1)S(1)}, bf16[2,2,32,640]{3,2,1,0:T(8,128)(2,1)S(1)}, u32[]{:S(2)}, u32[]{:S(2)}) collective-permute-start(bf16[2,2,32,640]{3,2,1,0:T(8,128)(2,1)S(1)} %broadcast_select_fusion), channel_id=1, source_target_pairs={{0,2},{1,3},{2,0},{3,1},{4,6},{5,7},{6,4},{7,5},{8,10},{9,11},{10,... | collective-permute-start | bytes 491528 | tf_op jit(solution)/shard_map/ppermute | solution.py:268
  15.8 4.7 %collective-permute-start.4 = (bf16[2,2,2,32,640]{4,3,2,1,0:T(8,128)(2,1)S(1)}, bf16[2,2,2,32,640]{4,3,2,1,0:T(8,128)(2,1)S(1)}, u32[]{:S(2)}, u32[]{:S(2)}) collective-permute-start(bf16[2,2,2,32,640]{4,3,2,1,0:T(8,128)(2,1)S(1)} %maximum_select_fusion.1), channel_id=1, source_target_pairs={{0,1},{1,0},{2,3},{3,2},{4,5},{5,4},{6,7},{7,6},{8,9},{9,8},{10,11... | collective-permute-start | bytes 983048 | tf_op jit(solution)/shard_map/ppermute | solution.py:268
  20.6 0.8 %copy-start.2 = (bf16[2,2,2,2,32,640]{5,4,3,2,1,0:T(8,128)(2,1)}, bf16[2,2,2,2,32,640]{5,4,3,2,1,0:T(8,128)(2,1)S(1)}, u32[]{:S(2)}) copy-start(bf16[2,2,2,2,32,640]{5,4,3,2,1,0:T(8,128)(2,1)S(1)} %maximum_select_fusion) | copy-start | bytes 1966084
  25.6 5.4 %copy-start.6 = (bf16[3,3,3,8]{3,2,1,0:T(4,128)(2,1)S(1)}, bf16[3,3,3,8]{3,2,1,0:T(4,128)(2,1)}, u32[]{:S(2)}) copy-start(bf16[3,3,3,8]{3,2,1,0:T(4,128)(2,1)} %param.19) | copy-start | bytes 1300
  25.6 19.4 %all-to-all-start = ((bf16[16,32,512]{2,1,0:T(8,128)(2,1)}), bf16[16,32,512]{2,1,0:T(8,128)(2,1)S(1)}, u32[]{:S(2)}, u32[]{:S(2)}) async-start(bf16[16,32,512]{2,1,0:T(8,128)(2,1)} %bitcast.71), calls=%async_computation | async-start | bytes 1048576 | tf_op jit(solution)/shard_map/all_to_all | solution.py:318
  45.7 10.6 %copy-start.1 = (bf16[66,8,512]{2,1,0:T(8,128)(2,1)}, bf16[66,8,512]{2,1,0:T(8,128)(2,1)S(1)}, u32[]{:S(2)}) copy-start(bf16[66,8,512]{2,1,0:T(8,128)(2,1)S(1)} %copy.52) | copy-start | bytes 1622020
  45.7 7.8 %collective-permute-start.6 = (bf16[528,256]{1,0:T(8,128)(2,1)S(1)}, bf16[528,256]{1,0:T(8,128)(2,1)S(1)}, u32[]{:S(2)}, u32[]{:S(2)}) collective-permute-start(bf16[528,256]{1,0:T(8,128)(2,1)S(1)} %get-tuple-element.29), channel_id=1, source_target_pairs={{1,0},{2,1},{3,2},{4,3},{5,4},{6,5},{7,6},{8,7},{9,8},{10,9},{11,1... | collective-permute-start | bytes 811016 | tf_op jit(solution)/shard_map/ppermute | solution.py:345
  48.1 8.1 %collective-permute-start.5 = (bf16[528,256]{1,0:T(8,128)(2,1)S(1)}, bf16[528,256]{1,0:T(8,128)(2,1)S(1)}, u32[]{:S(2)}, u32[]{:S(2)}) collective-permute-start(bf16[528,256]{1,0:T(8,128)(2,1)S(1)} %get-tuple-element.30), channel_id=1, source_target_pairs={{0,1},{1,2},{2,3},{3,4},{4,5},{5,6},{6,7},{7,8},{8,9},{9,10},{10,1... | collective-permute-start | bytes 811016 | tf_op jit(solution)/shard_map/ppermute | solution.py:344
  53.5 2.8 %copy-start.4 = (bf16[528,256]{1,0:T(8,128)(2,1)}, bf16[528,256]{1,0:T(8,128)(2,1)S(1)}, u32[]{:S(2)}) copy-start(bf16[528,256]{1,0:T(8,128)(2,1)S(1)} %collective-permute-done.6.high_ref) | copy-start | bytes 811012
  56.3 0.7 %copy-start.5 = (bf16[528,256]{1,0:T(8,128)(2,1)}, bf16[528,256]{1,0:T(8,128)(2,1)S(1)}, u32[]{:S(2)}) copy-start(bf16[528,256]{1,0:T(8,128)(2,1)S(1)} %collective-permute-done.5.low_ref) | copy-start | bytes 811012

commit v21 on v20

--- a/solution.py
+++ b/solution.py
@@ -73,13 +73,13 @@
     return carried
 
 
-def correlate_kernel(blk_ref, blocks_ref, table_ref, ref_ref, out_ref, arranged, products):
+def correlate_kernel(blk_ref, bit_ref, blocks_ref, table_ref, ref_ref, partner_ref, out_ref, arranged, products, *, pairs):
     chunk = 16
     slots = table_ref.shape[0] // blocks_ref.shape[2]
     width = blocks_ref.shape[2]
     channels = blocks_ref.shape[1]
     units = out_ref.shape[0] // GROUPS
-    cap = units // ref_ref.shape[0]
+    cap = units // (ref_ref.shape[0] * (2 if pairs else 1))
     group_size = channels // GROUPS
     rows = chunk * channels
 
@@ -95,7 +95,13 @@
         lanes = products.shape[0]
         for u in range(chunk):
             unit = c * chunk + u
-            tile = ref_ref[unit // cap].astype(jnp.float32)
+            if pairs:
+                owner = unit // cap
+                tile = jnp.where(
+                    owner % 2 == bit_ref[0], ref_ref[owner // 2], partner_ref[owner // 2]
+                ).astype(jnp.float32)
+            else:
+                tile = ref_ref[unit // cap].astype(jnp.float32)
             for j in range(lanes):
                 products[j, u * channels : (u + 1) * channels, :] = (
                     warped[u * channels : (u + 1) * channels, j * 128 : (j + 1) * 128]
@@ -114,15 +120,19 @@
     lax.fori_loop(0, units // chunk, step, 0, unroll=2)
 
 
-def correlate(blk, blocks, table, refs, units):
-    channels, width = blocks.shape[1], blocks.shape[2]
+def correlate(blk, blocks, table, mine, partner, bit, units):
+    channels = blocks.shape[1]
     tpix = table.shape[1]
     chunk = 16
+    pairs = bit is not None
+    bits = jnp.reshape(bit if pairs else 0, (1,)).astype(jnp.int32)
     return pl.pallas_call(
-        correlate_kernel,
+        functools.partial(correlate_kernel, pairs=pairs),
         out_shape=jax.ShapeDtypeStruct((units * GROUPS, tpix), jnp.bfloat16),
         in_specs=[
             pl.BlockSpec(memory_space=pltpu.SMEM),
+            pl.BlockSpec(memory_space=pltpu.SMEM),
+            pl.BlockSpec(memory_space=pltpu.VMEM),
             pl.BlockSpec(memory_space=pltpu.VMEM),
             pl.BlockSpec(memory_space=pltpu.VMEM),
             pl.BlockSpec(memory_space=pltpu.VMEM),
@@ -132,7 +142,7 @@
             pltpu.VMEM((chunk * channels, table.shape[0]), jnp.bfloat16),
             pltpu.VMEM((tpix // 128, chunk * channels, 128), jnp.float32),
         ],
-    )(blk, blocks, table, refs)
+    )(blk, bits, blocks, table, mine, partner)
 
 
 def conv_body(x_ref, m_ref, out_ref, ends_ref, *, relu, rows, cols, groups, chunk):
@@ -244,12 +254,13 @@
     return jnp.concatenate([low, block, high], axis=1)
 
 
-def gather_view(block):
+def gather_view(block, split=False):
     count = lax.axis_size("view")
-    if count & (count - 1):
-        return lax.all_to_all(
+    if count & (count - 1) or (split and count < 8):
+        whole = lax.all_to_all(
             jnp.broadcast_to(block, (count,) + block.shape[1:]), "view", 0, 0, tiled=True
         )
+        return (whole, whole, None) if split else whole
     index = lax.axis_index("view")
     gathered = block[0]
     level = 0
@@ -266,6 +277,9 @@
         stride = top // 2
     while stride >= 1:
         other = lax.ppermute(gathered, "view", [(i, i ^ stride) for i in range(count)])
+        if split and stride == 1:
+            half = (count // 2,) + block.shape[1:]
+            return gathered.reshape(half), other.reshape(half), index % 2
         low = (index // stride) % 2 == 0
         gathered = jnp.where(
             low, jnp.stack([gathered, other], axis=level), jnp.stack([other, gathered], axis=level)
@@ -308,9 +322,11 @@
     depth_code = jnp.where(counts > 0, depth_plane[0], -1).astype(jnp.bfloat16)
 
     tag_block = jnp.pad(depth_code, (0, channels * 128 - units)).reshape(channels, 128)
-    ref_all = gather_view(jnp.concatenate([ref_feat[0], tag_block], axis=1)[None])
+    mine, partner, bit = gather_view(
+        jnp.concatenate([ref_feat[0], tag_block], axis=1)[None], split=True
+    )
     corr_all = correlate(
-        blk, blocks, weight_table.reshape(slots * block_width, tpix), ref_all, units
+        blk, blocks, weight_table.reshape(slots * block_width, tpix), mine, partner, bit, units
     )
     corr_all, kern_one, kern_two = lax.optimization_barrier((corr_all, kern_one, kern_two))
     first = banded(kern_one, DEPTH // 4)
@@ -323,8 +339,15 @@
         tiled=True,
     ).reshape(owners * cap, GROUPS, tpix)
     arriving, first, second = lax.optimization_barrier((arriving, first, second))
+    if bit is None:
+        tag_rows = mine[:, :, tpix:]
+    else:
+        own, other = mine[:, :, tpix:], partner[:, :, tpix:]
+        tag_rows = jnp.where(
+            bit == 0, jnp.stack([own, other], axis=1), jnp.stack([other, own], axis=1)
+        )
     depth_tags = lax.dynamic_slice_in_dim(
-        ref_all[:, :, tpix:].reshape(owners, channels * 128), lax.axis_index("view") * cap, cap, axis=1
+        tag_rows.reshape(owners, channels * 128), lax.axis_index("view") * cap, cap, axis=1
     ).reshape(owners * cap)
     labels = jnp.arange(-1, DEPTH + 1).at[0].set(-2)
     onehot = (

time: 62.3 us -> 62 us (level)
    unnamed x16 -> x18, local copies, waits for them, and re-layouts: 1.47 us -> 1.32 us
where the time goes in v21:
time: 62 us; the launch traced here: 61.6 us
  waiting for transfers between devices  20.3 us (33%)
  starting transfers between devices  20.1 us (32%)
  Pallas kernels  9.03 us (15%)
  other arithmetic  6.79 us (11%)
  local copies, waits for them, and re-layouts  4.29 us (7%)
  matrix products  0.77 us (1%)
    all_to_all x1, waiting for transfers between devices, body(): lax.all_to_all(corr_all.reshape(owners, cap * GROUPS, tpix), 'view', spli...  11.7 us
    all_to_all x1, starting transfers between devices, body(): lax.all_to_all(corr_all.reshape(owners, cap * GROUPS, tpix), 'view', spli...  5.34 us
    pallas_call x1, Pallas kernels, conv_pair(): pl.pallas_call(functools.partial(conv_pair_kernel, rows=rows, cols=cols,...  4.88 us
    ppermute x2, starting transfers between devices, gather_view(): lax.ppermute(gathered, 'view', [(i, i ^ stride) for i in range(count)])  4.8 us
    ppermute x3, starting transfers between devices, gather_view(): lax.ppermute(gathered, 'view', [(i, i ^ m * top) for i in range(count)])  4.44 us
    pallas_call x1, Pallas kernels, correlate(): pl.pallas_call(functools.partial(correlate_kernel, pairs=pairs), out_shap...  4.15 us
    ppermute x2, waiting for transfers between devices, gather_view(): lax.ppermute(gathered, 'view', [(i, i ^ stride) for i in range(count)])  4.07 us
    ppermute x1, starting transfers between devices, body(): lax.ppermute(volume[:, volume.shape[1] - 2 * columns:], 'view', forward)  3.16 us
  transfers between devices with their start and end apart: 8, of which 6 were waited for; matrix products, arithmetic and copies ran while one was open for 12% of the time, Pallas kernels for 0%

profile of v21, /device:TPU:1, one launch (start us, length us, event | category | flops | bytes accessed | tf_op | source)
XLA Modules:
  0.0 61.6 jit_solution(11973580186580673519)
XLA Ops:
  0.0 0.7 %fusion.18 = bf16[64]{0:T(256)(128)(2,1)S(1)} fusion(s32[1,64]{1,0:T(1,128)} %param.17, s32[1,64]{1,0:T(1,128)} %param.16), kind=kLoop, calls=%fused_computation.59 | loop fusion | flops 192 | bytes 640 | tf_op jit(solution)/shard_map/convert_element_type | solution.py:322
  0.7 0.8 %fusion.20 = (bf16[1,32,640]{2,1,0:T(8,128)(2,1)S(1)}, bf16[32,640]{1,0:T(8,128)(2,1)S(1)}) fusion(bf16[32,128]{1,0:T(8,128)(2,1)S(1)} %pad_bitcast_fusion, bf16[32,512]{1,0:T(8,128)(2,1)} %bitcast.87), kind=kLoop, calls=%fused_computation.65 | loop fusion | flops 81920 | bytes 122880 | tf_op jit(solution)/shard_map/broadcast_in_dim | solution.py:326
  1.5 3.1 %collective-permute-start.1 = (bf16[32,640]{1,0:T(8,128)(2,1)S(1)}, bf16[32,640]{1,0:T(8,128)(2,1)S(1)}, u32[]{:S(2)}, u32[]{:S(2)}) collective-permute-start(bf16[32,640]{1,0:T(8,128)(2,1)S(1)} %get-tuple-element.32), channel_id=1, source_target_pairs={{0,8},{1,9},{2,10},{3,11},{4,12},{5,13},{6,14},{7,15},{8,0},{9,1},... | collective-permute-start | bytes 122888 | tf_op jit(solution)/shard_map/ppermute | solution.py:271
  4.7 1.3 %collective-permute-start = (bf16[32,640]{1,0:T(8,128)(2,1)S(1)}, bf16[32,640]{1,0:T(8,128)(2,1)S(1)}, u32[]{:S(2)}, u32[]{:S(2)}) collective-permute-start(bf16[32,640]{1,0:T(8,128)(2,1)S(1)} %get-tuple-element.32), channel_id=1, source_target_pairs={{0,4},{1,5},{2,6},{3,7},{4,0},{5,1},{6,2},{7,3},{8,12},{9,13},{10,... | collective-permute-start | bytes 122888 | tf_op jit(solution)/shard_map/ppermute | solution.py:271
  6.0 0.7 %iota_compare_fusion.2 = pred[64,4]{0,1:T(4,128)(4,1)S(1)} fusion(s32[64]{0:T(128)} %bitcast.91), kind=kLoop, calls=%fused_computation.50 | loop fusion | flops 256 | bytes 512 | tf_op jit(solution)/shard_map/lt | solution.py:318
  6.7 0.7 %fusion.10 = pred[64,4]{0,1:T(4,128)(4,1)S(1)} fusion(s32[64,4]{0,1:T(4,128)} %bitcast.88, pred[64,4]{0,1:T(4,128)(4,1)S(1)} %iota_compare_fusion.2), kind=kLoop, calls=%fused_computation.39 | loop fusion | flops 2816 | bytes 1536 | tf_op jit(solution)/shard_map/reduce_or | solution.py:320
  7.4 0.7 %select_reduce_fusion.2 = s32[64,4]{0,1:T(4,128)S(1)} fusion(s32[64,4]{0,1:T(4,128)} %bitcast.90, s32[64,4]{0,1:T(4,128)} %bitcast.89), kind=kLoop, calls=%fused_computation.32 | loop fusion | flops 2816 | bytes 3072 | tf_op jit(solution)/shard_map/reduce_sum | solution.py:319
  8.5 0.7 %select_n.162.blk_ref = s32[256]{0:T(256)} reshape(s32[64,4]{1,0:T(8,128)S(1)} %copy.28) | data formatting | bytes 2048 | tf_op jit(solution)/shard_map/jit(_where)/select_n | solution.py:321
  9.6 0.8 %concatenate.9.blocks_ref = bf16[65,32,128]{2,1,0:T(8,128)(2,1)} pad(bf16[64,32,128]{2,1,0:T(8,128)(2,1)S(1)} %bitcast.68, bf16[]{:T(256)} %constant.144.clone.1), padding=0_1x0_0x0_0 | pad | bytes 1056770 | tf_op jit(solution)/shard_map/concatenate | solution.py:316
  11.4 1.3 %collective-permute-start.3 = (bf16[2,2,32,640]{3,2,1,0:T(8,128)(2,1)S(1)}, bf16[2,2,32,640]{3,2,1,0:T(8,128)(2,1)S(1)}, u32[]{:S(2)}, u32[]{:S(2)}) collective-permute-start(bf16[2,2,32,640]{3,2,1,0:T(8,128)(2,1)S(1)} %broadcast_select_fusion), channel_id=1, source_target_pairs={{0,2},{1,3},{2,0},{3,1},{4,6},{5,7},{6,4},{7,5},{8,10},{9,11},{10,... | collective-permute-start | bytes 491528 | tf_op jit(solution)/shard_map/ppermute | solution.py:279
  12.8 2.8 %collective-permute-done.3 = bf16[2,2,32,640]{3,2,1,0:T(8,128)(2,1)S(1)} collective-permute-done((bf16[2,2,32,640]{3,2,1,0:T(8,128)(2,1)S(1)}, bf16[2,2,32,640]{3,2,1,0:T(8,128)(2,1)S(1)}, u32[]{:S(2)}, u32[]{:S(2)}) %collective-permute-start.3) | collective-permute-done | bytes 163872 | tf_op jit(solution)/shard_map/ppermute | solution.py:279
  15.7 3.5 %collective-permute-start.4 = (bf16[2,2,2,32,640]{4,3,2,1,0:T(8,128)(2,1)S(1)}, bf16[2,2,2,32,640]{4,3,2,1,0:T(8,128)(2,1)S(1)}, u32[]{:S(2)}, u32[]{:S(2)}) collective-permute-start(bf16[2,2,2,32,640]{4,3,2,1,0:T(8,128)(2,1)S(1)} %maximum_select_fusion), channel_id=1, source_target_pairs={{0,1},{1,0},{2,3},{3,2},{4,5},{5,4},{6,7},{7,6},{8,9},{9,8},{10,11... | collective-permute-start | bytes 983048 | tf_op jit(solution)/shard_map/ppermute | solution.py:279
  19.2 1.2 %collective-permute-done.4 = bf16[2,2,2,32,640]{4,3,2,1,0:T(8,128)(2,1)S(1)} collective-permute-done((bf16[2,2,2,32,640]{4,3,2,1,0:T(8,128)(2,1)S(1)}, bf16[2,2,2,32,640]{4,3,2,1,0:T(8,128)(2,1)S(1)}, u32[]{:S(2)}, u32[]{:S(2)}) %collective-permute-start.4) | collective-permute-done | bytes 327712 | tf_op jit(solution)/shard_map/ppermute | solution.py:279
  21.2 4.1 %shard_map.91 = bf16[512,512]{1,0:T(8,128)(2,1)} custom-call(s32[256]{0:T(256)} %select_n.162.blk_ref, s32[1]{0:T(128)} %bitcast.22.bit_ref, bf16[65,32,128]{2,1,0:T(8,128)(2,1)} %concatenate.9.blocks_ref, bf16[512,512]{1,0:T(8,128)(2,1)} %bitcast.74, bf16[8,32,640]{2,1,0:T(8,128)(2,1)} %bitcast.71, bf16[8,32,640]{2,1,0:T(8,128)(2,1)} %bitcast.79), custom_call_target="tpu_custom_call" | custom-call | tf_op jit(solution)/shard_map/pallas_call | solution.py:129
  25.3 5.3 %all-to-all-start = ((bf16[16,32,512]{2,1,0:T(8,128)(2,1)}), bf16[16,32,512]{2,1,0:T(8,128)(2,1)S(1)}, u32[]{:S(2)}, u32[]{:S(2)}) async-start(bf16[16,32,512]{2,1,0:T(8,128)(2,1)} %bitcast.67), calls=%async_computation | async-start | bytes 1048576 | tf_op jit(solution)/shard_map/all_to_all | solution.py:334
  30.9 0.7 %select_reduce_fusion.1 = bf16[9,16,144]{2,1,0:T(8,128)(2,1)} fusion(f32[3,9,144]{2,1,0:T(8,128)S(1)} %fusion.2, pred[3,16,144]{2,1,0:T(8,128)(4,1)S(1)} %broadcast_compare_fusion.1), kind=kLoop, calls=%fused_computation.7 | loop fusion | flops 103680 | bytes 63936 | tf_op jit(solution)/shard_map/reduce_sum | solution.py:201
  31.8 1.2 %select_reduce_fusion = bf16[9,16,8,144]{3,2,1,0:T(8,128)(2,1)} fusion(f32[3,9,8,144]{3,2,1,0:T(8,128)S(1)} %fusion.11, pred[3,16,8,144]{3,2,1,0:T(8,128)(4,1)S(1)} %broadcast_compare_fusion), kind=kLoop, calls=%fused_computation.1 | loop fusion | flops 829440 | bytes 511488 | tf_op jit(solution)/shard_map/reduce_sum | solution.py:201
  33.0 11.7 %all-to-all-done = bf16[16,32,512]{2,1,0:T(8,128)(2,1)S(1)} async-done(((bf16[16,32,512]{2,1,0:T(8,128)(2,1)}), bf16[16,32,512]{2,1,0:T(8,128)(2,1)S(1)}, u32[]{:S(2)}, u32[]{:S(2)}) %all-to-all-start) | async-done | bytes 524320 | tf_op jit(solution)/shard_map/all_to_all | solution.py:334
  45.4 2.4 %collective-permute-start.6 = (bf16[528,256]{1,0:T(8,128)(2,1)S(1)}, bf16[528,256]{1,0:T(8,128)(2,1)S(1)}, u32[]{:S(2)}, u32[]{:S(2)}) collective-permute-start(bf16[528,256]{1,0:T(8,128)(2,1)S(1)} %get-tuple-element.29), channel_id=1, source_target_pairs={{1,0},{2,1},{3,2},{4,3},{5,4},{6,5},{7,6},{8,7},{9,8},{10,9},{11,1... | collective-permute-start | bytes 811016 | tf_op jit(solution)/shard_map/ppermute | solution.py:368
  47.8 3.2 %collective-permute-start.5 = (bf16[528,256]{1,0:T(8,128)(2,1)S(1)}, bf16[528,256]{1,0:T(8,128)(2,1)S(1)}, u32[]{:S(2)}, u32[]{:S(2)}) collective-permute-start(bf16[528,256]{1,0:T(8,128)(2,1)S(1)} %get-tuple-element.30), channel_id=1, source_target_pairs={{0,1},{1,2},{2,3},{3,4},{4,5},{5,6},{6,7},{7,8},{8,9},{9,10},{10,1... | collective-permute-start | bytes 811016 | tf_op jit(solution)/shard_map/ppermute | solution.py:367
  51.7 1.5 %collective-permute-done.6.high_ref = bf16[528,256]{1,0:T(8,128)(2,1)S(1)} collective-permute-done((bf16[528,256]{1,0:T(8,128)(2,1)S(1)}, bf16[528,256]{1,0:T(8,128)(2,1)S(1)}, u32[]{:S(2)}, u32[]{:S(2)}) %collective-permute-start.6) | collective-permute-done | bytes 270368 | tf_op jit(solution)/shard_map/ppermute | solution.py:368
  53.2 2.8 %collective-permute-done.5.low_ref = bf16[528,256]{1,0:T(8,128)(2,1)S(1)} collective-permute-done((bf16[528,256]{1,0:T(8,128)(2,1)S(1)}, bf16[528,256]{1,0:T(8,128)(2,1)S(1)}, u32[]{:S(2)}, u32[]{:S(2)}) %collective-permute-start.5) | collective-permute-done | bytes 270368 | tf_op jit(solution)/shard_map/ppermute | solution.py:367
  56.0 0.7 %copy-done.6 = bf16[528,256]{1,0:T(8,128)(2,1)} copy-done((bf16[528,256]{1,0:T(8,128)(2,1)}, bf16[528,256]{1,0:T(8,128)(2,1)S(1)}, u32[]{:S(2)}) %copy-start.6) | copy-done | bytes 270360
  56.7 4.9 %shard_map.92 = f32[4,64,128]{2,1,0:T(8,128)} custom-call(s32[2]{0:T(128)} %add_convert_fusion.ends_ref, bf16[528,256]{1,0:T(8,128)(2,1)} %copy-done.6, bf16[528,512]{1,0:T(8,128)(2,1)} %bitcast.65, bf16[528,256]{1,0:T(8,128)(2,1)} %copy-done.5, bf16[3,3,128,144]{3,2,1,0:T(8,128)(2,1)} %bitcast.66, bf16[3,3,16,144]{3,2,1,0:T(8,128)(2,1)} %bitcast.80), custom_call_target="tpu_custom_call" | custom-call | tf_op jit(solution)/shard_map/pallas_call | solution.py:236
  (58 shorter events, 4.4 us)
Async XLA Ops:
  0.0 31.6 %copy-start = (bf16[3,3,3,8,8]{4,3,2,1,0:T(8,128)(2,1)S(1)}, bf16[3,3,3,8,8]{4,3,2,1,0:T(8,128)(2,1)}, u32[]{:S(2)}) copy-start(bf16[3,3,3,8,8]{4,3,2,1,0:T(8,128)(2,1)} %param.18) | copy-start | bytes 10372
  0.0 9.2 %copy-start.3 = (bf16[1,32,8192]{2,1,0:T(8,128)(2,1)S(1)}, bf16[1,32,8192]{2,1,0:T(8,128)(2,1)}, u32[]{:S(2)}) copy-start(bf16[1,32,8192]{2,1,0:T(8,128)(2,1)} %param.11) | copy-start | bytes 1572868
  1.5 9.0 %collective-permute-start.1 = (bf16[32,640]{1,0:T(8,128)(2,1)S(1)}, bf16[32,640]{1,0:T(8,128)(2,1)S(1)}, u32[]{:S(2)}, u32[]{:S(2)}) collective-permute-start(bf16[32,640]{1,0:T(8,128)(2,1)S(1)} %get-tuple-element.32), channel_id=1, source_target_pairs={{0,8},{1,9},{2,10},{3,11},{4,12},{5,13},{6,14},{7,15},{8,0},{9,1},... | collective-permute-start | bytes 122888 | tf_op jit(solution)/shard_map/ppermute | solution.py:271
  4.7 5.8 %collective-permute-start = (bf16[32,640]{1,0:T(8,128)(2,1)S(1)}, bf16[32,640]{1,0:T(8,128)(2,1)S(1)}, u32[]{:S(2)}, u32[]{:S(2)}) collective-permute-start(bf16[32,640]{1,0:T(8,128)(2,1)S(1)} %get-tuple-element.32), channel_id=1, source_target_pairs={{0,4},{1,5},{2,6},{3,7},{4,0},{5,1},{6,2},{7,3},{8,12},{9,13},{10,... | collective-permute-start | bytes 122888 | tf_op jit(solution)/shard_map/ppermute | solution.py:271
  5.9 4.8 %collective-permute-start.2 = (bf16[32,640]{1,0:T(8,128)(2,1)S(1)}, bf16[32,640]{1,0:T(8,128)(2,1)S(1)}, u32[]{:S(2)}, u32[]{:S(2)}) collective-permute-start(bf16[32,640]{1,0:T(8,128)(2,1)S(1)} %get-tuple-element.32), channel_id=1, source_target_pairs={{0,12},{1,13},{2,14},{3,15},{4,8},{5,9},{6,10},{7,11},{8,4},{9,5},... | collective-permute-start | bytes 122888 | tf_op jit(solution)/shard_map/ppermute | solution.py:271
  11.4 4.2 %collective-permute-start.3 = (bf16[2,2,32,640]{3,2,1,0:T(8,128)(2,1)S(1)}, bf16[2,2,32,640]{3,2,1,0:T(8,128)(2,1)S(1)}, u32[]{:S(2)}, u32[]{:S(2)}) collective-permute-start(bf16[2,2,32,640]{3,2,1,0:T(8,128)(2,1)S(1)} %broadcast_select_fusion), channel_id=1, source_target_pairs={{0,2},{1,3},{2,0},{3,1},{4,6},{5,7},{6,4},{7,5},{8,10},{9,11},{10,... | collective-permute-start | bytes 491528 | tf_op jit(solution)/shard_map/ppermute | solution.py:279
  15.7 5.1 %copy-start.2 = (bf16[2,2,2,32,640]{4,3,2,1,0:T(8,128)(2,1)}, bf16[2,2,2,32,640]{4,3,2,1,0:T(8,128)(2,1)S(1)}, u32[]{:S(2)}) copy-start(bf16[2,2,2,32,640]{4,3,2,1,0:T(8,128)(2,1)S(1)} %maximum_select_fusion) | copy-start | bytes 983044
  15.7 4.7 %collective-permute-start.4 = (bf16[2,2,2,32,640]{4,3,2,1,0:T(8,128)(2,1)S(1)}, bf16[2,2,2,32,640]{4,3,2,1,0:T(8,128)(2,1)S(1)}, u32[]{:S(2)}, u32[]{:S(2)}) collective-permute-start(bf16[2,2,2,32,640]{4,3,2,1,0:T(8,128)(2,1)S(1)} %maximum_select_fusion), channel_id=1, source_target_pairs={{0,1},{1,0},{2,3},{3,2},{4,5},{5,4},{6,7},{7,6},{8,9},{9,8},{10,11... | collective-permute-start | bytes 983048 | tf_op jit(solution)/shard_map/ppermute | solution.py:279
  20.5 0.7 %copy-start.4 = (bf16[2,2,2,32,640]{4,3,2,1,0:T(8,128)(2,1)}, bf16[2,2,2,32,640]{4,3,2,1,0:T(8,128)(2,1)S(1)}, u32[]{:S(2)}) copy-start(bf16[2,2,2,32,640]{4,3,2,1,0:T(8,128)(2,1)S(1)} %collective-permute-done.4) | copy-start | bytes 983044
  25.3 5.3 %copy-start.7 = (bf16[3,3,3,8]{3,2,1,0:T(4,128)(2,1)S(1)}, bf16[3,3,3,8]{3,2,1,0:T(4,128)(2,1)}, u32[]{:S(2)}) copy-start(bf16[3,3,3,8]{3,2,1,0:T(4,128)(2,1)} %param.19) | copy-start | bytes 1300
  25.3 19.4 %all-to-all-start = ((bf16[16,32,512]{2,1,0:T(8,128)(2,1)}), bf16[16,32,512]{2,1,0:T(8,128)(2,1)S(1)}, u32[]{:S(2)}, u32[]{:S(2)}) async-start(bf16[16,32,512]{2,1,0:T(8,128)(2,1)} %bitcast.67), calls=%async_computation | async-start | bytes 1048576 | tf_op jit(solution)/shard_map/all_to_all | solution.py:334
  45.4 10.6 %copy-start.1 = (bf16[66,8,512]{2,1,0:T(8,128)(2,1)}, bf16[66,8,512]{2,1,0:T(8,128)(2,1)S(1)}, u32[]{:S(2)}) copy-start(bf16[66,8,512]{2,1,0:T(8,128)(2,1)S(1)} %copy.46) | copy-start | bytes 1622020
  45.4 7.8 %collective-permute-start.6 = (bf16[528,256]{1,0:T(8,128)(2,1)S(1)}, bf16[528,256]{1,0:T(8,128)(2,1)S(1)}, u32[]{:S(2)}, u32[]{:S(2)}) collective-permute-start(bf16[528,256]{1,0:T(8,128)(2,1)S(1)} %get-tuple-element.29), channel_id=1, source_target_pairs={{1,0},{2,1},{3,2},{4,3},{5,4},{6,5},{7,6},{8,7},{9,8},{10,9},{11,1... | collective-permute-start | bytes 811016 | tf_op jit(solution)/shard_map/ppermute | solution.py:368
  47.8 8.1 %collective-permute-start.5 = (bf16[528,256]{1,0:T(8,128)(2,1)S(1)}, bf16[528,256]{1,0:T(8,128)(2,1)S(1)}, u32[]{:S(2)}, u32[]{:S(2)}) collective-permute-start(bf16[528,256]{1,0:T(8,128)(2,1)S(1)} %get-tuple-element.30), channel_id=1, source_target_pairs={{0,1},{1,2},{2,3},{3,4},{4,5},{5,6},{6,7},{7,8},{8,9},{9,10},{10,1... | collective-permute-start | bytes 811016 | tf_op jit(solution)/shard_map/ppermute | solution.py:367
  53.2 2.8 %copy-start.5 = (bf16[528,256]{1,0:T(8,128)(2,1)}, bf16[528,256]{1,0:T(8,128)(2,1)S(1)}, u32[]{:S(2)}) copy-start(bf16[528,256]{1,0:T(8,128)(2,1)S(1)} %collective-permute-done.6.high_ref) | copy-start | bytes 811012
  56.0 0.7 %copy-start.6 = (bf16[528,256]{1,0:T(8,128)(2,1)}, bf16[528,256]{1,0:T(8,128)(2,1)S(1)}, u32[]{:S(2)}) copy-start(bf16[528,256]{1,0:T(8,128)(2,1)S(1)} %collective-permute-done.5.low_ref) | copy-start | bytes 811012

commit v22 on v20

--- a/solution.py
+++ b/solution.py
@@ -74,7 +74,7 @@
 
 
 def correlate_kernel(blk_ref, blocks_ref, table_ref, ref_ref, out_ref, arranged, products):
-    chunk = 16
+    chunk = 32
     slots = table_ref.shape[0] // blocks_ref.shape[2]
     width = blocks_ref.shape[2]
     channels = blocks_ref.shape[1]
@@ -111,13 +111,13 @@
             ).astype(out_ref.dtype)
         return carry
 
-    lax.fori_loop(0, units // chunk, step, 0, unroll=2)
+    lax.fori_loop(0, units // chunk, step, 0, unroll=True)
 
 
 def correlate(blk, blocks, table, refs, units):
     channels, width = blocks.shape[1], blocks.shape[2]
     tpix = table.shape[1]
-    chunk = 16
+    chunk = 32
     return pl.pallas_call(
         correlate_kernel,
         out_shape=jax.ShapeDtypeStruct((units * GROUPS, tpix), jnp.bfloat16),

time: 62.3 us -> 62 us (level)
  no operation moved by 1% of the time
where the time goes in v22:
time: 62 us; the launch traced here: 61.6 us
  starting transfers between devices  20.2 us (33%)
  waiting for transfers between devices  20.1 us (32%)
  Pallas kernels  8.69 us (14%)
  other arithmetic  7.07 us (11%)
  local copies, waits for them, and re-layouts  4.47 us (7%)
  matrix products  0.77 us (1%)
    all_to_all x1, waiting for transfers between devices, body(): lax.all_to_all(corr_all.reshape(owners, cap * GROUPS, tpix), 'view', spli...  11.7 us
    all_to_all x1, starting transfers between devices, body(): lax.all_to_all(corr_all.reshape(owners, cap * GROUPS, tpix), 'view', spli...  5.38 us
    pallas_call x1, Pallas kernels, conv_pair(): pl.pallas_call(functools.partial(conv_pair_kernel, rows=rows, cols=cols,...  4.88 us
    ppermute x2, starting transfers between devices, gather_view(): lax.ppermute(gathered, 'view', [(i, i ^ stride) for i in range(count)])  4.8 us
    ppermute x3, starting transfers between devices, gather_view(): lax.ppermute(gathered, 'view', [(i, i ^ m * top) for i in range(count)])  4.44 us
    ppermute x2, waiting for transfers between devices, gather_view(): lax.ppermute(gathered, 'view', [(i, i ^ stride) for i in range(count)])  3.98 us
    pallas_call x1, Pallas kernels, correlate(): pl.pallas_call(correlate_kernel, out_shape=jax.ShapeDtypeStruct((units *...  3.81 us
    ppermute x1, starting transfers between devices, body(): lax.ppermute(volume[:, volume.shape[1] - 2 * columns:], 'view', forward)  3.16 us
  transfers between devices with their start and end apart: 8, of which 6 were waited for; matrix products, arithmetic and copies ran while one was open for 12% of the time, Pallas kernels for 0%

profile of v22, /device:TPU:1, one launch (start us, length us, event | category | flops | bytes accessed | tf_op | source)
XLA Modules:
  0.0 61.6 jit_solution(6888113769972511037)
XLA Ops:
  0.0 0.7 %fusion.18 = bf16[64]{0:T(256)(128)(2,1)S(1)} fusion(s32[1,64]{1,0:T(1,128)} %param.17, s32[1,64]{1,0:T(1,128)} %param.16), kind=kLoop, calls=%fused_computation.60 | loop fusion | flops 192 | bytes 640 | tf_op jit(solution)/shard_map/convert_element_type | solution.py:308
  0.7 0.8 %fusion.20 = (bf16[1,32,640]{2,1,0:T(8,128)(2,1)S(1)}, bf16[32,640]{1,0:T(8,128)(2,1)S(1)}) fusion(bf16[32,128]{1,0:T(8,128)(2,1)S(1)} %pad_bitcast_fusion, bf16[32,512]{1,0:T(8,128)(2,1)} %bitcast.85), kind=kLoop, calls=%fused_computation.66 | loop fusion | flops 81920 | bytes 122880 | tf_op jit(solution)/shard_map/broadcast_in_dim | solution.py:311
  1.5 3.1 %collective-permute-start.1 = (bf16[32,640]{1,0:T(8,128)(2,1)S(1)}, bf16[32,640]{1,0:T(8,128)(2,1)S(1)}, u32[]{:S(2)}, u32[]{:S(2)}) collective-permute-start(bf16[32,640]{1,0:T(8,128)(2,1)S(1)} %get-tuple-element.34), channel_id=1, source_target_pairs={{0,8},{1,9},{2,10},{3,11},{4,12},{5,13},{6,14},{7,15},{8,0},{9,1},... | collective-permute-start | bytes 122888 | tf_op jit(solution)/shard_map/ppermute | solution.py:260
  4.7 1.3 %collective-permute-start = (bf16[32,640]{1,0:T(8,128)(2,1)S(1)}, bf16[32,640]{1,0:T(8,128)(2,1)S(1)}, u32[]{:S(2)}, u32[]{:S(2)}) collective-permute-start(bf16[32,640]{1,0:T(8,128)(2,1)S(1)} %get-tuple-element.34), channel_id=1, source_target_pairs={{0,4},{1,5},{2,6},{3,7},{4,0},{5,1},{6,2},{7,3},{8,12},{9,13},{10,... | collective-permute-start | bytes 122888 | tf_op jit(solution)/shard_map/ppermute | solution.py:260
  6.7 0.7 %fusion.10 = pred[64,4]{0,1:T(4,128)(4,1)S(1)} fusion(s32[64,4]{0,1:T(4,128)} %bitcast.86, pred[64,4]{0,1:T(4,128)(4,1)S(1)} %iota_compare_fusion.2), kind=kLoop, calls=%fused_computation.40 | loop fusion | flops 2816 | bytes 1536 | tf_op jit(solution)/shard_map/reduce_or | solution.py:306
  7.4 0.7 %select_reduce_fusion.2 = s32[64,4]{0,1:T(4,128)S(1)} fusion(s32[64,4]{0,1:T(4,128)} %bitcast.88, s32[64,4]{0,1:T(4,128)} %bitcast.87), kind=kLoop, calls=%fused_computation.33 | loop fusion | flops 2816 | bytes 3072 | tf_op jit(solution)/shard_map/reduce_sum | solution.py:305
  8.5 0.7 %select_n.180.blk_ref = s32[256]{0:T(256)} reshape(s32[64,4]{1,0:T(8,128)S(1)} %copy.32) | data formatting | bytes 2048 | tf_op jit(solution)/shard_map/jit(_where)/select_n | solution.py:307
  9.7 0.9 %concatenate.23.blocks_ref = bf16[65,32,128]{2,1,0:T(8,128)(2,1)} pad(bf16[64,32,128]{2,1,0:T(8,128)(2,1)S(1)} %bitcast.69, bf16[]{:T(256)} %constant.153.clone.1), padding=0_1x0_0x0_0 | pad | bytes 1056770 | tf_op jit(solution)/shard_map/concatenate | solution.py:302
  11.5 1.3 %collective-permute-start.3 = (bf16[2,2,32,640]{3,2,1,0:T(8,128)(2,1)S(1)}, bf16[2,2,32,640]{3,2,1,0:T(8,128)(2,1)S(1)}, u32[]{:S(2)}, u32[]{:S(2)}) collective-permute-start(bf16[2,2,32,640]{3,2,1,0:T(8,128)(2,1)S(1)} %broadcast_select_fusion), channel_id=1, source_target_pairs={{0,2},{1,3},{2,0},{3,1},{4,6},{5,7},{6,4},{7,5},{8,10},{9,11},{10,... | collective-permute-start | bytes 491528 | tf_op jit(solution)/shard_map/ppermute | solution.py:268
  12.9 2.8 %collective-permute-done.3 = bf16[2,2,32,640]{3,2,1,0:T(8,128)(2,1)S(1)} collective-permute-done((bf16[2,2,32,640]{3,2,1,0:T(8,128)(2,1)S(1)}, bf16[2,2,32,640]{3,2,1,0:T(8,128)(2,1)S(1)}, u32[]{:S(2)}, u32[]{:S(2)}) %collective-permute-start.3) | collective-permute-done | bytes 163872 | tf_op jit(solution)/shard_map/ppermute | solution.py:268
  15.8 3.5 %collective-permute-start.4 = (bf16[2,2,2,32,640]{4,3,2,1,0:T(8,128)(2,1)S(1)}, bf16[2,2,2,32,640]{4,3,2,1,0:T(8,128)(2,1)S(1)}, u32[]{:S(2)}, u32[]{:S(2)}) collective-permute-start(bf16[2,2,2,32,640]{4,3,2,1,0:T(8,128)(2,1)S(1)} %maximum_select_fusion.1), channel_id=1, source_target_pairs={{0,1},{1,0},{2,3},{3,2},{4,5},{5,4},{6,7},{7,6},{8,9},{9,8},{10,11... | collective-permute-start | bytes 983048 | tf_op jit(solution)/shard_map/ppermute | solution.py:268
  19.4 1.1 %collective-permute-done.4 = bf16[2,2,2,32,640]{4,3,2,1,0:T(8,128)(2,1)S(1)} collective-permute-done((bf16[2,2,2,32,640]{4,3,2,1,0:T(8,128)(2,1)S(1)}, bf16[2,2,2,32,640]{4,3,2,1,0:T(8,128)(2,1)S(1)}, u32[]{:S(2)}, u32[]{:S(2)}) %collective-permute-start.4) | collective-permute-done | bytes 327712 | tf_op jit(solution)/shard_map/ppermute | solution.py:268
  21.5 3.8 %shard_map.91 = bf16[512,512]{1,0:T(8,128)(2,1)} custom-call(s32[256]{0:T(256)} %select_n.180.blk_ref, bf16[65,32,128]{2,1,0:T(8,128)(2,1)} %concatenate.23.blocks_ref, bf16[512,512]{1,0:T(8,128)(2,1)} %bitcast.77, bf16[16,32,640]{2,1,0:T(8,128)(2,1)} %bitcast.64), custom_call_target="tpu_custom_call" | custom-call | tf_op jit(solution)/shard_map/pallas_call | solution.py:121
  25.3 5.4 %all-to-all-start = ((bf16[16,32,512]{2,1,0:T(8,128)(2,1)}), bf16[16,32,512]{2,1,0:T(8,128)(2,1)S(1)}, u32[]{:S(2)}, u32[]{:S(2)}) async-start(bf16[16,32,512]{2,1,0:T(8,128)(2,1)} %bitcast.71), calls=%async_computation | async-start | bytes 1048576 | tf_op jit(solution)/shard_map/all_to_all | solution.py:318
  30.9 0.7 %select_reduce_fusion.1 = bf16[9,16,144]{2,1,0:T(8,128)(2,1)} fusion(f32[3,9,144]{2,1,0:T(8,128)S(1)} %fusion.2, pred[3,16,144]{2,1,0:T(8,128)(4,1)S(1)} %broadcast_compare_fusion.1), kind=kLoop, calls=%fused_computation.8 | loop fusion | flops 103680 | bytes 63936 | tf_op jit(solution)/shard_map/reduce_sum | solution.py:191
  31.8 1.2 %select_reduce_fusion = bf16[9,16,8,144]{3,2,1,0:T(8,128)(2,1)} fusion(f32[3,9,8,144]{3,2,1,0:T(8,128)S(1)} %fusion.11, pred[3,16,8,144]{3,2,1,0:T(8,128)(4,1)S(1)} %broadcast_compare_fusion), kind=kLoop, calls=%fused_computation.1 | loop fusion | flops 829440 | bytes 511488 | tf_op jit(solution)/shard_map/reduce_sum | solution.py:191
  33.1 11.7 %all-to-all-done = bf16[16,32,512]{2,1,0:T(8,128)(2,1)S(1)} async-done(((bf16[16,32,512]{2,1,0:T(8,128)(2,1)}), bf16[16,32,512]{2,1,0:T(8,128)(2,1)S(1)}, u32[]{:S(2)}, u32[]{:S(2)}) %all-to-all-start) | async-done | bytes 524320 | tf_op jit(solution)/shard_map/all_to_all | solution.py:318
  45.4 2.4 %collective-permute-start.6 = (bf16[528,256]{1,0:T(8,128)(2,1)S(1)}, bf16[528,256]{1,0:T(8,128)(2,1)S(1)}, u32[]{:S(2)}, u32[]{:S(2)}) collective-permute-start(bf16[528,256]{1,0:T(8,128)(2,1)S(1)} %get-tuple-element.29), channel_id=1, source_target_pairs={{1,0},{2,1},{3,2},{4,3},{5,4},{6,5},{7,6},{8,7},{9,8},{10,9},{11,1... | collective-permute-start | bytes 811016 | tf_op jit(solution)/shard_map/ppermute | solution.py:345
  47.8 3.2 %collective-permute-start.5 = (bf16[528,256]{1,0:T(8,128)(2,1)S(1)}, bf16[528,256]{1,0:T(8,128)(2,1)S(1)}, u32[]{:S(2)}, u32[]{:S(2)}) collective-permute-start(bf16[528,256]{1,0:T(8,128)(2,1)S(1)} %get-tuple-element.30), channel_id=1, source_target_pairs={{0,1},{1,2},{2,3},{3,4},{4,5},{5,6},{6,7},{7,8},{8,9},{9,10},{10,1... | collective-permute-start | bytes 811016 | tf_op jit(solution)/shard_map/ppermute | solution.py:344
  51.0 0.7 %add_convert_fusion.ends_ref = s32[2]{0:T(128)} fusion(pred[1]{0:T(512)(128)(4,1)} %bitcast.1, pred[1]{0:T(512)(128)(4,1)} %bitcast), kind=kLoop, calls=%fused_computation.52 | loop fusion | flops 4 | bytes 10 | tf_op jit(solution)/shard_map/convert_element_type | solution.py:340
  51.7 1.5 %collective-permute-done.6.high_ref = bf16[528,256]{1,0:T(8,128)(2,1)S(1)} collective-permute-done((bf16[528,256]{1,0:T(8,128)(2,1)S(1)}, bf16[528,256]{1,0:T(8,128)(2,1)S(1)}, u32[]{:S(2)}, u32[]{:S(2)}) %collective-permute-start.6) | collective-permute-done | bytes 270368 | tf_op jit(solution)/shard_map/ppermute | solution.py:345
  53.2 2.8 %collective-permute-done.5.low_ref = bf16[528,256]{1,0:T(8,128)(2,1)S(1)} collective-permute-done((bf16[528,256]{1,0:T(8,128)(2,1)S(1)}, bf16[528,256]{1,0:T(8,128)(2,1)S(1)}, u32[]{:S(2)}, u32[]{:S(2)}) %collective-permute-start.5) | collective-permute-done | bytes 270368 | tf_op jit(solution)/shard_map/ppermute | solution.py:344
  56.0 0.7 %copy-done.5 = bf16[528,256]{1,0:T(8,128)(2,1)} copy-done((bf16[528,256]{1,0:T(8,128)(2,1)}, bf16[528,256]{1,0:T(8,128)(2,1)S(1)}, u32[]{:S(2)}) %copy-start.5) | copy-done | bytes 270360
  56.7 4.9 %shard_map.92 = f32[4,64,128]{2,1,0:T(8,128)} custom-call(s32[2]{0:T(128)} %add_convert_fusion.ends_ref, bf16[528,256]{1,0:T(8,128)(2,1)} %copy-done.5, bf16[528,512]{1,0:T(8,128)(2,1)} %bitcast.62, bf16[528,256]{1,0:T(8,128)(2,1)} %copy-done.4, bf16[3,3,128,144]{3,2,1,0:T(8,128)(2,1)} %bitcast.68, bf16[3,3,16,144]{3,2,1,0:T(8,128)(2,1)} %bitcast.79), custom_call_target="tpu_custom_call" | custom-call | tf_op jit(solution)/shard_map/pallas_call | solution.py:226
  (57 shorter events, 4.7 us)
Async XLA Ops:
  0.0 31.6 %copy-start = (bf16[3,3,3,8,8]{4,3,2,1,0:T(8,128)(2,1)S(1)}, bf16[3,3,3,8,8]{4,3,2,1,0:T(8,128)(2,1)}, u32[]{:S(2)}) copy-start(bf16[3,3,3,8,8]{4,3,2,1,0:T(8,128)(2,1)} %param.18) | copy-start | bytes 10372
  0.0 9.2 %copy-start.3 = (bf16[1,32,8192]{2,1,0:T(8,128)(2,1)S(1)}, bf16[1,32,8192]{2,1,0:T(8,128)(2,1)}, u32[]{:S(2)}) copy-start(bf16[1,32,8192]{2,1,0:T(8,128)(2,1)} %param.11) | copy-start | bytes 1572868
  1.5 9.0 %collective-permute-start.1 = (bf16[32,640]{1,0:T(8,128)(2,1)S(1)}, bf16[32,640]{1,0:T(8,128)(2,1)S(1)}, u32[]{:S(2)}, u32[]{:S(2)}) collective-permute-start(bf16[32,640]{1,0:T(8,128)(2,1)S(1)} %get-tuple-element.34), channel_id=1, source_target_pairs={{0,8},{1,9},{2,10},{3,11},{4,12},{5,13},{6,14},{7,15},{8,0},{9,1},... | collective-permute-start | bytes 122888 | tf_op jit(solution)/shard_map/ppermute | solution.py:260
  4.7 5.9 %collective-permute-start = (bf16[32,640]{1,0:T(8,128)(2,1)S(1)}, bf16[32,640]{1,0:T(8,128)(2,1)S(1)}, u32[]{:S(2)}, u32[]{:S(2)}) collective-permute-start(bf16[32,640]{1,0:T(8,128)(2,1)S(1)} %get-tuple-element.34), channel_id=1, source_target_pairs={{0,4},{1,5},{2,6},{3,7},{4,0},{5,1},{6,2},{7,3},{8,12},{9,13},{10,... | collective-permute-start | bytes 122888 | tf_op jit(solution)/shard_map/ppermute | solution.py:260
  5.9 4.8 %collective-permute-start.2 = (bf16[32,640]{1,0:T(8,128)(2,1)S(1)}, bf16[32,640]{1,0:T(8,128)(2,1)S(1)}, u32[]{:S(2)}, u32[]{:S(2)}) collective-permute-start(bf16[32,640]{1,0:T(8,128)(2,1)S(1)} %get-tuple-element.34), channel_id=1, source_target_pairs={{0,12},{1,13},{2,14},{3,15},{4,8},{5,9},{6,10},{7,11},{8,4},{9,5},... | collective-permute-start | bytes 122888 | tf_op jit(solution)/shard_map/ppermute | solution.py:260
  11.5 4.2 %collective-permute-start.3 = (bf16[2,2,32,640]{3,2,1,0:T(8,128)(2,1)S(1)}, bf16[2,2,32,640]{3,2,1,0:T(8,128)(2,1)S(1)}, u32[]{:S(2)}, u32[]{:S(2)}) collective-permute-start(bf16[2,2,32,640]{3,2,1,0:T(8,128)(2,1)S(1)} %broadcast_select_fusion), channel_id=1, source_target_pairs={{0,2},{1,3},{2,0},{3,1},{4,6},{5,7},{6,4},{7,5},{8,10},{9,11},{10,... | collective-permute-start | bytes 491528 | tf_op jit(solution)/shard_map/ppermute | solution.py:268
  15.8 4.7 %collective-permute-start.4 = (bf16[2,2,2,32,640]{4,3,2,1,0:T(8,128)(2,1)S(1)}, bf16[2,2,2,32,640]{4,3,2,1,0:T(8,128)(2,1)S(1)}, u32[]{:S(2)}, u32[]{:S(2)}) collective-permute-start(bf16[2,2,2,32,640]{4,3,2,1,0:T(8,128)(2,1)S(1)} %maximum_select_fusion.1), channel_id=1, source_target_pairs={{0,1},{1,0},{2,3},{3,2},{4,5},{5,4},{6,7},{7,6},{8,9},{9,8},{10,11... | collective-permute-start | bytes 983048 | tf_op jit(solution)/shard_map/ppermute | solution.py:268
  20.6 0.8 %copy-start.2 = (bf16[2,2,2,2,32,640]{5,4,3,2,1,0:T(8,128)(2,1)}, bf16[2,2,2,2,32,640]{5,4,3,2,1,0:T(8,128)(2,1)S(1)}, u32[]{:S(2)}) copy-start(bf16[2,2,2,2,32,640]{5,4,3,2,1,0:T(8,128)(2,1)S(1)} %maximum_select_fusion) | copy-start | bytes 1966084
  25.3 5.4 %copy-start.6 = (bf16[3,3,3,8]{3,2,1,0:T(4,128)(2,1)S(1)}, bf16[3,3,3,8]{3,2,1,0:T(4,128)(2,1)}, u32[]{:S(2)}) copy-start(bf16[3,3,3,8]{3,2,1,0:T(4,128)(2,1)} %param.19) | copy-start | bytes 1300
  25.3 19.5 %all-to-all-start = ((bf16[16,32,512]{2,1,0:T(8,128)(2,1)}), bf16[16,32,512]{2,1,0:T(8,128)(2,1)S(1)}, u32[]{:S(2)}, u32[]{:S(2)}) async-start(bf16[16,32,512]{2,1,0:T(8,128)(2,1)} %bitcast.71), calls=%async_computation | async-start | bytes 1048576 | tf_op jit(solution)/shard_map/all_to_all | solution.py:318
  45.4 10.6 %copy-start.1 = (bf16[66,8,512]{2,1,0:T(8,128)(2,1)}, bf16[66,8,512]{2,1,0:T(8,128)(2,1)S(1)}, u32[]{:S(2)}) copy-start(bf16[66,8,512]{2,1,0:T(8,128)(2,1)S(1)} %copy.52) | copy-start | bytes 1622020
  45.4 7.8 %collective-permute-start.6 = (bf16[528,256]{1,0:T(8,128)(2,1)S(1)}, bf16[528,256]{1,0:T(8,128)(2,1)S(1)}, u32[]{:S(2)}, u32[]{:S(2)}) collective-permute-start(bf16[528,256]{1,0:T(8,128)(2,1)S(1)} %get-tuple-element.29), channel_id=1, source_target_pairs={{1,0},{2,1},{3,2},{4,3},{5,4},{6,5},{7,6},{8,7},{9,8},{10,9},{11,1... | collective-permute-start | bytes 811016 | tf_op jit(solution)/shard_map/ppermute | solution.py:345
  47.8 8.1 %collective-permute-start.5 = (bf16[528,256]{1,0:T(8,128)(2,1)S(1)}, bf16[528,256]{1,0:T(8,128)(2,1)S(1)}, u32[]{:S(2)}, u32[]{:S(2)}) collective-permute-start(bf16[528,256]{1,0:T(8,128)(2,1)S(1)} %get-tuple-element.30), channel_id=1, source_target_pairs={{0,1},{1,2},{2,3},{3,4},{4,5},{5,6},{6,7},{7,8},{8,9},{9,10},{10,1... | collective-permute-start | bytes 811016 | tf_op jit(solution)/shard_map/ppermute | solution.py:344
  53.2 2.8 %copy-start.4 = (bf16[528,256]{1,0:T(8,128)(2,1)}, bf16[528,256]{1,0:T(8,128)(2,1)S(1)}, u32[]{:S(2)}) copy-start(bf16[528,256]{1,0:T(8,128)(2,1)S(1)} %collective-permute-done.6.high_ref) | copy-start | bytes 811012
  56.0 0.7 %copy-start.5 = (bf16[528,256]{1,0:T(8,128)(2,1)}, bf16[528,256]{1,0:T(8,128)(2,1)S(1)}, u32[]{:S(2)}) copy-start(bf16[528,256]{1,0:T(8,128)(2,1)S(1)} %collective-permute-done.5.low_ref) | copy-start | bytes 811012

commit v23 on v22

--- a/solution.py
+++ b/solution.py
@@ -313,7 +313,7 @@
         blk, blocks, weight_table.reshape(slots * block_width, tpix), ref_all, units
     )
     corr_all, kern_one, kern_two = lax.optimization_barrier((corr_all, kern_one, kern_two))
-    first = banded(kern_one, DEPTH // 4)
+    first = banded(kern_one, DEPTH // 8)
     second = banded(kern_two, DEPTH // 4)
     arriving = lax.all_to_all(
         corr_all.reshape(owners, cap * GROUPS, tpix),

time: 62 us -> 63.3 us (1.021)
  the two profiles are of different devices: /device:TPU:1 before, /device:TPU:13 now
where the time goes in v23:
time: 63.3 us; the launch traced here: 62.7 us
  waiting for transfers between devices  22.7 us (36%)
  starting transfers between devices  18.5 us (29%)
  Pallas kernels  8.51 us (13%)
  other arithmetic  6.49 us (10%)
  local copies, waits for them, and re-layouts  5.44 us (9%)
  matrix products  0.76 us (1%)
    all_to_all x1, waiting for transfers between devices, body(): lax.all_to_all(corr_all.reshape(owners, cap * GROUPS, tpix), 'view', spli...  11.7 us
    all_to_all x1, starting transfers between devices, body(): lax.all_to_all(corr_all.reshape(owners, cap * GROUPS, tpix), 'view', spli...  6.67 us
    ppermute x1, waiting for transfers between devices, body(): high = lax.ppermute(volume[:, :2 * columns], 'view', backward)  5.27 us
    ppermute x2, waiting for transfers between devices, gather_view(): lax.ppermute(gathered, 'view', [(i, i ^ stride) for i in range(count)])  4.89 us
    pallas_call x1, Pallas kernels, conv_pair(): pl.pallas_call(functools.partial(conv_pair_kernel, rows=rows, cols=cols,...  4.68 us
    pallas_call x1, Pallas kernels, correlate(): pl.pallas_call(correlate_kernel, out_shape=jax.ShapeDtypeStruct((units *...  3.83 us
    ppermute x1, starting transfers between devices, body(): lax.ppermute(volume[:, volume.shape[1] - 2 * columns:], 'view', forward)  3.64 us
    ppermute x3, starting transfers between devices, gather_view(): lax.ppermute(gathered, 'view', [(i, i ^ m * top) for i in range(count)])  3.49 us
  transfers between devices with their start and end apart: 8, of which 5 were waited for; matrix products, arithmetic and copies ran while one was open for 13% of the time, Pallas kernels for 0%

profile of v23, /device:TPU:13, one launch (start us, length us, event | category | flops | bytes accessed | tf_op | source)
XLA Modules:
  0.0 62.7 jit_solution(5072980257431947199)
XLA Ops:
  0.0 0.7 %fusion.18 = bf16[64]{0:T(256)(128)(2,1)S(1)} fusion(s32[1,64]{1,0:T(1,128)} %param.17, s32[1,64]{1,0:T(1,128)} %param.16), kind=kLoop, calls=%fused_computation.66 | loop fusion | flops 192 | bytes 640 | tf_op jit(solution)/shard_map/convert_element_type | solution.py:308
  0.7 0.8 %fusion.20 = (bf16[1,32,640]{2,1,0:T(8,128)(2,1)S(1)}, bf16[32,640]{1,0:T(8,128)(2,1)S(1)}) fusion(bf16[32,128]{1,0:T(8,128)(2,1)S(1)} %pad_bitcast_fusion, bf16[32,512]{1,0:T(8,128)(2,1)} %bitcast.85), kind=kLoop, calls=%fused_computation.72 | loop fusion | flops 81920 | bytes 122880 | tf_op jit(solution)/shard_map/broadcast_in_dim | solution.py:311
  1.5 1.3 %collective-permute-start.2 = (bf16[32,640]{1,0:T(8,128)(2,1)S(1)}, bf16[32,640]{1,0:T(8,128)(2,1)S(1)}, u32[]{:S(2)}, u32[]{:S(2)}) collective-permute-start(bf16[32,640]{1,0:T(8,128)(2,1)S(1)} %get-tuple-element.34), channel_id=1, source_target_pairs={{0,12},{1,13},{2,14},{3,15},{4,8},{5,9},{6,10},{7,11},{8,4},{9,5},... | collective-permute-start | bytes 122888 | tf_op jit(solution)/shard_map/ppermute | solution.py:260
  2.8 1.1 %collective-permute-start.1 = (bf16[32,640]{1,0:T(8,128)(2,1)S(1)}, bf16[32,640]{1,0:T(8,128)(2,1)S(1)}, u32[]{:S(2)}, u32[]{:S(2)}) collective-permute-start(bf16[32,640]{1,0:T(8,128)(2,1)S(1)} %get-tuple-element.34), channel_id=1, source_target_pairs={{0,8},{1,9},{2,10},{3,11},{4,12},{5,13},{6,14},{7,15},{8,0},{9,1},... | collective-permute-start | bytes 122888 | tf_op jit(solution)/shard_map/ppermute | solution.py:260
  3.8 1.1 %collective-permute-start = (bf16[32,640]{1,0:T(8,128)(2,1)S(1)}, bf16[32,640]{1,0:T(8,128)(2,1)S(1)}, u32[]{:S(2)}, u32[]{:S(2)}) collective-permute-start(bf16[32,640]{1,0:T(8,128)(2,1)S(1)} %get-tuple-element.34), channel_id=1, source_target_pairs={{0,4},{1,5},{2,6},{3,7},{4,0},{5,1},{6,2},{7,3},{8,12},{9,13},{10,... | collective-permute-start | bytes 122888 | tf_op jit(solution)/shard_map/ppermute | solution.py:260
  5.7 0.7 %fusion.7 = pred[64,4]{0,1:T(4,128)(4,1)S(1)} fusion(s32[64,4]{0,1:T(4,128)} %bitcast.86, pred[64,4]{0,1:T(4,128)(4,1)S(1)} %iota_compare_fusion.3), kind=kLoop, calls=%fused_computation.33 | loop fusion | flops 2816 | bytes 1536 | tf_op jit(solution)/shard_map/reduce_or | solution.py:306
  6.4 0.7 %select_reduce_fusion.2 = s32[64,4]{0,1:T(4,128)S(1)} fusion(s32[64,4]{0,1:T(4,128)} %bitcast.88, s32[64,4]{0,1:T(4,128)} %bitcast.87), kind=kLoop, calls=%fused_computation.27 | loop fusion | flops 2816 | bytes 3072 | tf_op jit(solution)/shard_map/reduce_sum | solution.py:305
  7.5 0.7 %select_n.194.blk_ref = s32[256]{0:T(256)} reshape(s32[64,4]{1,0:T(8,128)S(1)} %copy.34) | data formatting | bytes 2048 | tf_op jit(solution)/shard_map/jit(_where)/select_n | solution.py:307
  8.2 1.2 %copy.46 = bf16[4,8,64,128]{3,2,1,0:T(8,128)(2,1)S(1)} copy(bf16[4,8,64,128]{3,1,2,0:T(8,128)(2,1)} %bitcast.74) | data formatting | bytes 1048576
  9.7 0.8 %concatenate.23.blocks_ref = bf16[65,32,128]{2,1,0:T(8,128)(2,1)} pad(bf16[64,32,128]{2,1,0:T(8,128)(2,1)S(1)} %bitcast.68, bf16[]{:T(256)} %constant.168.clone.1), padding=0_1x0_0x0_0 | pad | bytes 1056770 | tf_op jit(solution)/shard_map/concatenate | solution.py:302
  11.7 3.8 %collective-permute-done.3 = bf16[2,2,32,640]{3,2,1,0:T(8,128)(2,1)S(1)} collective-permute-done((bf16[2,2,32,640]{3,2,1,0:T(8,128)(2,1)S(1)}, bf16[2,2,32,640]{3,2,1,0:T(8,128)(2,1)S(1)}, u32[]{:S(2)}, u32[]{:S(2)}) %collective-permute-start.3) | collective-permute-done | bytes 163872 | tf_op jit(solution)/shard_map/ppermute | solution.py:268
  15.5 2.5 %collective-permute-start.4 = (bf16[2,2,2,32,640]{4,3,2,1,0:T(8,128)(2,1)S(1)}, bf16[2,2,2,32,640]{4,3,2,1,0:T(8,128)(2,1)S(1)}, u32[]{:S(2)}, u32[]{:S(2)}) collective-permute-start(bf16[2,2,2,32,640]{4,3,2,1,0:T(8,128)(2,1)S(1)} %maximum_select_fusion.1), channel_id=1, source_target_pairs={{0,1},{1,0},{2,3},{3,2},{4,5},{5,4},{6,7},{7,6},{8,9},{9,8},{10,11... | collective-permute-start | bytes 983048 | tf_op jit(solution)/shard_map/ppermute | solution.py:268
  18.2 1.1 %collective-permute-done.4 = bf16[2,2,2,32,640]{4,3,2,1,0:T(8,128)(2,1)S(1)} collective-permute-done((bf16[2,2,2,32,640]{4,3,2,1,0:T(8,128)(2,1)S(1)}, bf16[2,2,2,32,640]{4,3,2,1,0:T(8,128)(2,1)S(1)}, u32[]{:S(2)}, u32[]{:S(2)}) %collective-permute-start.4) | collective-permute-done | bytes 327712 | tf_op jit(solution)/shard_map/ppermute | solution.py:268
  20.2 3.8 %shard_map.91 = bf16[512,512]{1,0:T(8,128)(2,1)} custom-call(s32[256]{0:T(256)} %select_n.194.blk_ref, bf16[65,32,128]{2,1,0:T(8,128)(2,1)} %concatenate.23.blocks_ref, bf16[512,512]{1,0:T(8,128)(2,1)} %bitcast.77, bf16[16,32,640]{2,1,0:T(8,128)(2,1)} %bitcast.64), custom_call_target="tpu_custom_call" | custom-call | tf_op jit(solution)/shard_map/pallas_call | solution.py:121
  24.1 6.7 %all-to-all-start = ((bf16[16,32,512]{2,1,0:T(8,128)(2,1)}), bf16[16,32,512]{2,1,0:T(8,128)(2,1)S(1)}, u32[]{:S(2)}, u32[]{:S(2)}) async-start(bf16[16,32,512]{2,1,0:T(8,128)(2,1)} %bitcast.70), calls=%async_computation | async-start | bytes 1048576 | tf_op jit(solution)/shard_map/all_to_all | solution.py:318
  31.0 0.7 %select_reduce_fusion.1 = bf16[9,16,144]{2,1,0:T(8,128)(2,1)} fusion(f32[3,9,144]{2,1,0:T(8,128)S(1)} %fusion.2, pred[3,16,144]{2,1,0:T(8,128)(4,1)S(1)} %broadcast_compare_fusion.1), kind=kLoop, calls=%fused_computation.8 | loop fusion | flops 103680 | bytes 63936 | tf_op jit(solution)/shard_map/reduce_sum | solution.py:191
  31.9 0.8 %select_reduce_fusion = bf16[9,8,8,80]{3,2,1,0:T(8,128)(2,1)} fusion(f32[3,9,8,80]{3,2,1,0:T(8,128)S(1)} %fusion.13, pred[3,8,8,80]{3,2,1,0:T(8,128)(4,1)S(1)} %broadcast_compare_fusion), kind=kLoop, calls=%fused_computation.3 | loop fusion | flops 230400 | bytes 176640 | tf_op jit(solution)/shard_map/reduce_sum | solution.py:191
  32.6 11.7 %all-to-all-done = bf16[16,32,512]{2,1,0:T(8,128)(2,1)S(1)} async-done(((bf16[16,32,512]{2,1,0:T(8,128)(2,1)}), bf16[16,32,512]{2,1,0:T(8,128)(2,1)S(1)}, u32[]{:S(2)}, u32[]{:S(2)}) %all-to-all-start) | async-done | bytes 524320 | tf_op jit(solution)/shard_map/all_to_all | solution.py:318
  45.0 3.6 %collective-permute-start.5 = (bf16[528,256]{1,0:T(8,128)(2,1)S(1)}, bf16[528,256]{1,0:T(8,128)(2,1)S(1)}, u32[]{:S(2)}, u32[]{:S(2)}) collective-permute-start(bf16[528,256]{1,0:T(8,128)(2,1)S(1)} %get-tuple-element.30), channel_id=1, source_target_pairs={{0,1},{1,2},{2,3},{3,4},{4,5},{5,6},{6,7},{7,8},{8,9},{9,10},{10,1... | collective-permute-start | bytes 811016 | tf_op jit(solution)/shard_map/ppermute | solution.py:344
  48.7 1.9 %collective-permute-start.6 = (bf16[528,256]{1,0:T(8,128)(2,1)S(1)}, bf16[528,256]{1,0:T(8,128)(2,1)S(1)}, u32[]{:S(2)}, u32[]{:S(2)}) collective-permute-start(bf16[528,256]{1,0:T(8,128)(2,1)S(1)} %get-tuple-element.29), channel_id=1, source_target_pairs={{1,0},{2,1},{3,2},{4,3},{5,4},{6,5},{7,6},{8,7},{9,8},{10,9},{11,1... | collective-permute-start | bytes 811016 | tf_op jit(solution)/shard_map/ppermute | solution.py:345
  51.2 0.8 %collective-permute-done.5.low_ref = bf16[528,256]{1,0:T(8,128)(2,1)S(1)} collective-permute-done((bf16[528,256]{1,0:T(8,128)(2,1)S(1)}, bf16[528,256]{1,0:T(8,128)(2,1)S(1)}, u32[]{:S(2)}, u32[]{:S(2)}) %collective-permute-start.5) | collective-permute-done | bytes 270368 | tf_op jit(solution)/shard_map/ppermute | solution.py:344
  52.1 5.3 %collective-permute-done.6.high_ref = bf16[528,256]{1,0:T(8,128)(2,1)S(1)} collective-permute-done((bf16[528,256]{1,0:T(8,128)(2,1)S(1)}, bf16[528,256]{1,0:T(8,128)(2,1)S(1)}, u32[]{:S(2)}, u32[]{:S(2)}) %collective-permute-start.6) | collective-permute-done | bytes 270368 | tf_op jit(solution)/shard_map/ppermute | solution.py:345
  57.3 0.7 %copy-done.4 = bf16[528,256]{1,0:T(8,128)(2,1)} copy-done((bf16[528,256]{1,0:T(8,128)(2,1)}, bf16[528,256]{1,0:T(8,128)(2,1)S(1)}, u32[]{:S(2)}) %copy-start.4) | copy-done | bytes 270360
  58.0 4.7 %shard_map.92 = f32[4,64,128]{2,1,0:T(8,128)} custom-call(s32[2]{0:T(128)} %add_convert_fusion.ends_ref, bf16[528,256]{1,0:T(8,128)(2,1)} %copy-done.3, bf16[528,512]{1,0:T(8,128)(2,1)} %bitcast.62, bf16[528,256]{1,0:T(8,128)(2,1)} %copy-done.4, bf16[3,3,64,80]{3,2,1,0:T(8,128)(2,1)} %bitcast.73, bf16[3,3,16,144]{3,2,1,0:T(8,128)(2,1)} %bitcast.79), custom_call_target="tpu_custom_call" | custom-call | tf_op jit(solution)/shard_map/pallas_call | solution.py:226
  (56 shorter events, 5.3 us)
Async XLA Ops:
  0.0 31.7 %copy-start = (bf16[3,3,3,8,8]{4,3,2,1,0:T(8,128)(2,1)S(1)}, bf16[3,3,3,8,8]{4,3,2,1,0:T(8,128)(2,1)}, u32[]{:S(2)}) copy-start(bf16[3,3,3,8,8]{4,3,2,1,0:T(8,128)(2,1)} %param.18) | copy-start | bytes 10372
  1.5 9.1 %collective-permute-start.2 = (bf16[32,640]{1,0:T(8,128)(2,1)S(1)}, bf16[32,640]{1,0:T(8,128)(2,1)S(1)}, u32[]{:S(2)}, u32[]{:S(2)}) collective-permute-start(bf16[32,640]{1,0:T(8,128)(2,1)S(1)} %get-tuple-element.34), channel_id=1, source_target_pairs={{0,12},{1,13},{2,14},{3,15},{4,8},{5,9},{6,10},{7,11},{8,4},{9,5},... | collective-permute-start | bytes 122888 | tf_op jit(solution)/shard_map/ppermute | solution.py:260
  2.8 7.8 %collective-permute-start.1 = (bf16[32,640]{1,0:T(8,128)(2,1)S(1)}, bf16[32,640]{1,0:T(8,128)(2,1)S(1)}, u32[]{:S(2)}, u32[]{:S(2)}) collective-permute-start(bf16[32,640]{1,0:T(8,128)(2,1)S(1)} %get-tuple-element.34), channel_id=1, source_target_pairs={{0,8},{1,9},{2,10},{3,11},{4,12},{5,13},{6,14},{7,15},{8,0},{9,1},... | collective-permute-start | bytes 122888 | tf_op jit(solution)/shard_map/ppermute | solution.py:260
  3.8 6.7 %collective-permute-start = (bf16[32,640]{1,0:T(8,128)(2,1)S(1)}, bf16[32,640]{1,0:T(8,128)(2,1)S(1)}, u32[]{:S(2)}, u32[]{:S(2)}) collective-permute-start(bf16[32,640]{1,0:T(8,128)(2,1)S(1)} %get-tuple-element.34), channel_id=1, source_target_pairs={{0,4},{1,5},{2,6},{3,7},{4,0},{5,1},{6,2},{7,3},{8,12},{9,13},{10,... | collective-permute-start | bytes 122888 | tf_op jit(solution)/shard_map/ppermute | solution.py:260
  11.2 4.2 %collective-permute-start.3 = (bf16[2,2,32,640]{3,2,1,0:T(8,128)(2,1)S(1)}, bf16[2,2,32,640]{3,2,1,0:T(8,128)(2,1)S(1)}, u32[]{:S(2)}, u32[]{:S(2)}) collective-permute-start(bf16[2,2,32,640]{3,2,1,0:T(8,128)(2,1)S(1)} %broadcast_select_fusion), channel_id=1, source_target_pairs={{0,2},{1,3},{2,0},{3,1},{4,6},{5,7},{6,4},{7,5},{8,10},{9,11},{10,... | collective-permute-start | bytes 491528 | tf_op jit(solution)/shard_map/ppermute | solution.py:268
  15.5 3.8 %collective-permute-start.4 = (bf16[2,2,2,32,640]{4,3,2,1,0:T(8,128)(2,1)S(1)}, bf16[2,2,2,32,640]{4,3,2,1,0:T(8,128)(2,1)S(1)}, u32[]{:S(2)}, u32[]{:S(2)}) collective-permute-start(bf16[2,2,2,32,640]{4,3,2,1,0:T(8,128)(2,1)S(1)} %maximum_select_fusion.1), channel_id=1, source_target_pairs={{0,1},{1,0},{2,3},{3,2},{4,5},{5,4},{6,7},{7,6},{8,9},{9,8},{10,11... | collective-permute-start | bytes 983048 | tf_op jit(solution)/shard_map/ppermute | solution.py:268
  19.4 0.8 %copy-start.2 = (bf16[2,2,2,2,32,640]{5,4,3,2,1,0:T(8,128)(2,1)}, bf16[2,2,2,2,32,640]{5,4,3,2,1,0:T(8,128)(2,1)S(1)}, u32[]{:S(2)}) copy-start(bf16[2,2,2,2,32,640]{5,4,3,2,1,0:T(8,128)(2,1)S(1)} %maximum_select_fusion) | copy-start | bytes 1966084
  24.1 6.8 %copy-start.5 = (bf16[3,3,3,8]{3,2,1,0:T(4,128)(2,1)S(1)}, bf16[3,3,3,8]{3,2,1,0:T(4,128)(2,1)}, u32[]{:S(2)}) copy-start(bf16[3,3,3,8]{3,2,1,0:T(4,128)(2,1)} %param.19) | copy-start | bytes 1300
  24.1 20.3 %all-to-all-start = ((bf16[16,32,512]{2,1,0:T(8,128)(2,1)}), bf16[16,32,512]{2,1,0:T(8,128)(2,1)S(1)}, u32[]{:S(2)}, u32[]{:S(2)}) async-start(bf16[16,32,512]{2,1,0:T(8,128)(2,1)} %bitcast.70), calls=%async_computation | async-start | bytes 1048576 | tf_op jit(solution)/shard_map/all_to_all | solution.py:318
  44.9 12.4 %copy-start.1 = (bf16[66,8,512]{2,1,0:T(8,128)(2,1)}, bf16[66,8,512]{2,1,0:T(8,128)(2,1)S(1)}, u32[]{:S(2)}) copy-start(bf16[66,8,512]{2,1,0:T(8,128)(2,1)S(1)} %copy.56) | copy-start | bytes 1622020
  45.0 7.1 %collective-permute-start.5 = (bf16[528,256]{1,0:T(8,128)(2,1)S(1)}, bf16[528,256]{1,0:T(8,128)(2,1)S(1)}, u32[]{:S(2)}, u32[]{:S(2)}) collective-permute-start(bf16[528,256]{1,0:T(8,128)(2,1)S(1)} %get-tuple-element.30), channel_id=1, source_target_pairs={{0,1},{1,2},{2,3},{3,4},{4,5},{5,6},{6,7},{7,8},{8,9},{9,10},{10,1... | collective-permute-start | bytes 811016 | tf_op jit(solution)/shard_map/ppermute | solution.py:344
  48.7 8.7 %collective-permute-start.6 = (bf16[528,256]{1,0:T(8,128)(2,1)S(1)}, bf16[528,256]{1,0:T(8,128)(2,1)S(1)}, u32[]{:S(2)}, u32[]{:S(2)}) collective-permute-start(bf16[528,256]{1,0:T(8,128)(2,1)S(1)} %get-tuple-element.29), channel_id=1, source_target_pairs={{1,0},{2,1},{3,2},{4,3},{5,4},{6,5},{7,6},{8,7},{9,8},{10,9},{11,1... | collective-permute-start | bytes 811016 | tf_op jit(solution)/shard_map/ppermute | solution.py:345
  52.1 5.3 %copy-start.3 = (bf16[528,256]{1,0:T(8,128)(2,1)}, bf16[528,256]{1,0:T(8,128)(2,1)S(1)}, u32[]{:S(2)}) copy-start(bf16[528,256]{1,0:T(8,128)(2,1)S(1)} %collective-permute-done.5.low_ref) | copy-start | bytes 811012
  57.3 0.7 %copy-start.4 = (bf16[528,256]{1,0:T(8,128)(2,1)}, bf16[528,256]{1,0:T(8,128)(2,1)S(1)}, u32[]{:S(2)}) copy-start(bf16[528,256]{1,0:T(8,128)(2,1)S(1)} %collective-permute-done.6.high_ref) | copy-start | bytes 811012

commit v24 on v23

--- a/solution.py
+++ b/solution.py
@@ -313,7 +313,7 @@
         blk, blocks, weight_table.reshape(slots * block_width, tpix), ref_all, units
     )
     corr_all, kern_one, kern_two = lax.optimization_barrier((corr_all, kern_one, kern_two))
-    first = banded(kern_one, DEPTH // 8)
+    first = banded(kern_one, DEPTH // 2)
     second = banded(kern_two, DEPTH // 4)
     arriving = lax.all_to_all(
         corr_all.reshape(owners, cap * GROUPS, tpix),

time: 63.3 us -> 65.8 us (1.039)
  the two profiles are of different devices: /device:TPU:13 before, /device:TPU:1 now
where the time goes in v24:
time: 65.8 us; the launch traced here: 65.2 us
  starting transfers between devices  20.2 us (31%)
  waiting for transfers between devices  18.8 us (29%)
  Pallas kernels  11.4 us (17%)
  other arithmetic  8.27 us (13%)
  local copies, waits for them, and re-layouts  5.44 us (8%)
  matrix products  0.81 us (1%)
    all_to_all x1, waiting for transfers between devices, body(): lax.all_to_all(corr_all.reshape(owners, cap * GROUPS, tpix), 'view', spli...  10.5 us
    pallas_call x1, Pallas kernels, conv_pair(): pl.pallas_call(functools.partial(conv_pair_kernel, rows=rows, cols=cols,...  7.63 us
    all_to_all x1, starting transfers between devices, body(): lax.all_to_all(corr_all.reshape(owners, cap * GROUPS, tpix), 'view', spli...  6.37 us
    ppermute x3, starting transfers between devices, gather_view(): lax.ppermute(gathered, 'view', [(i, i ^ m * top) for i in range(count)])  4.44 us
    ppermute x2, waiting for transfers between devices, gather_view(): lax.ppermute(gathered, 'view', [(i, i ^ stride) for i in range(count)])  3.98 us
    ppermute x2, starting transfers between devices, gather_view(): lax.ppermute(gathered, 'view', [(i, i ^ stride) for i in range(count)])  3.83 us
    pallas_call x1, Pallas kernels, correlate(): pl.pallas_call(correlate_kernel, out_shape=jax.ShapeDtypeStruct((units *...  3.81 us
    ppermute x1, starting transfers between devices, body(): lax.ppermute(volume[:, volume.shape[1] - 2 * columns:], 'view', forward)  3.16 us
  transfers between devices with their start and end apart: 8, of which 5 were waited for; matrix products, arithmetic and copies ran while one was open for 15% of the time, Pallas kernels for 0%

profile of v24, /device:TPU:1, one launch (start us, length us, event | category | flops | bytes accessed | tf_op | source)
XLA Modules:
  0.0 65.2 jit_solution(14455030570988440642)
XLA Ops:
  0.0 0.7 %fusion.25 = bf16[64]{0:T(256)(128)(2,1)S(1)} fusion(s32[1,64]{1,0:T(1,128)} %param.17, s32[1,64]{1,0:T(1,128)} %param.16), kind=kLoop, calls=%fused_computation.72 | loop fusion | flops 192 | bytes 640 | tf_op jit(solution)/shard_map/convert_element_type | solution.py:308
  0.7 0.8 %fusion.27 = (bf16[1,32,640]{2,1,0:T(8,128)(2,1)S(1)}, bf16[32,640]{1,0:T(8,128)(2,1)S(1)}) fusion(bf16[32,128]{1,0:T(8,128)(2,1)S(1)} %pad_bitcast_fusion, bf16[32,512]{1,0:T(8,128)(2,1)} %bitcast.85), kind=kLoop, calls=%fused_computation.78 | loop fusion | flops 81920 | bytes 122880 | tf_op jit(solution)/shard_map/broadcast_in_dim | solution.py:311
  1.5 3.1 %collective-permute-start.1 = (bf16[32,640]{1,0:T(8,128)(2,1)S(1)}, bf16[32,640]{1,0:T(8,128)(2,1)S(1)}, u32[]{:S(2)}, u32[]{:S(2)}) collective-permute-start(bf16[32,640]{1,0:T(8,128)(2,1)S(1)} %get-tuple-element.34), channel_id=1, source_target_pairs={{0,8},{1,9},{2,10},{3,11},{4,12},{5,13},{6,14},{7,15},{8,0},{9,1},... | collective-permute-start | bytes 122888 | tf_op jit(solution)/shard_map/ppermute | solution.py:260
  4.6 1.3 %collective-permute-start = (bf16[32,640]{1,0:T(8,128)(2,1)S(1)}, bf16[32,640]{1,0:T(8,128)(2,1)S(1)}, u32[]{:S(2)}, u32[]{:S(2)}) collective-permute-start(bf16[32,640]{1,0:T(8,128)(2,1)S(1)} %get-tuple-element.34), channel_id=1, source_target_pairs={{0,4},{1,5},{2,6},{3,7},{4,0},{5,1},{6,2},{7,3},{8,12},{9,13},{10,... | collective-permute-start | bytes 122888 | tf_op jit(solution)/shard_map/ppermute | solution.py:260
  6.7 0.7 %fusion.11 = pred[64,4]{0,1:T(4,128)(4,1)S(1)} fusion(s32[64,4]{0,1:T(4,128)} %bitcast.86, pred[64,4]{0,1:T(4,128)(4,1)S(1)} %iota_compare_fusion.3), kind=kLoop, calls=%fused_computation.41 | loop fusion | flops 2816 | bytes 1536 | tf_op jit(solution)/shard_map/reduce_or | solution.py:306
  7.4 0.7 %select_reduce_fusion.2 = s32[64,4]{0,1:T(4,128)S(1)} fusion(s32[64,4]{0,1:T(4,128)} %bitcast.88, s32[64,4]{0,1:T(4,128)} %bitcast.87), kind=kLoop, calls=%fused_computation.35 | loop fusion | flops 2816 | bytes 3072 | tf_op jit(solution)/shard_map/reduce_sum | solution.py:305
  8.6 0.7 %select_n.194.blk_ref = s32[256]{0:T(256)} reshape(s32[64,4]{1,0:T(8,128)S(1)} %copy.32) | data formatting | bytes 2048 | tf_op jit(solution)/shard_map/jit(_where)/select_n | solution.py:307
  9.3 1.2 %copy.42 = bf16[4,8,64,128]{3,2,1,0:T(8,128)(2,1)S(1)} copy(bf16[4,8,64,128]{3,1,2,0:T(8,128)(2,1)} %bitcast.74) | data formatting | bytes 1048576
  10.8 0.8 %concatenate.23.blocks_ref = bf16[65,32,128]{2,1,0:T(8,128)(2,1)} pad(bf16[64,32,128]{2,1,0:T(8,128)(2,1)S(1)} %bitcast.69, bf16[]{:T(256)} %constant.168.clone.1), padding=0_1x0_0x0_0 | pad | bytes 1056770 | tf_op jit(solution)/shard_map/concatenate | solution.py:302
  12.4 1.3 %collective-permute-start.3 = (bf16[2,2,32,640]{3,2,1,0:T(8,128)(2,1)S(1)}, bf16[2,2,32,640]{3,2,1,0:T(8,128)(2,1)S(1)}, u32[]{:S(2)}, u32[]{:S(2)}) collective-permute-start(bf16[2,2,32,640]{3,2,1,0:T(8,128)(2,1)S(1)} %broadcast_select_fusion), channel_id=1, source_target_pairs={{0,2},{1,3},{2,0},{3,1},{4,6},{5,7},{6,4},{7,5},{8,10},{9,11},{10,... | collective-permute-start | bytes 491528 | tf_op jit(solution)/shard_map/ppermute | solution.py:268
  13.8 2.8 %collective-permute-done.3 = bf16[2,2,32,640]{3,2,1,0:T(8,128)(2,1)S(1)} collective-permute-done((bf16[2,2,32,640]{3,2,1,0:T(8,128)(2,1)S(1)}, bf16[2,2,32,640]{3,2,1,0:T(8,128)(2,1)S(1)}, u32[]{:S(2)}, u32[]{:S(2)}) %collective-permute-start.3) | collective-permute-done | bytes 163872 | tf_op jit(solution)/shard_map/ppermute | solution.py:268
  16.7 2.5 %collective-permute-start.4 = (bf16[2,2,2,32,640]{4,3,2,1,0:T(8,128)(2,1)S(1)}, bf16[2,2,2,32,640]{4,3,2,1,0:T(8,128)(2,1)S(1)}, u32[]{:S(2)}, u32[]{:S(2)}) collective-permute-start(bf16[2,2,2,32,640]{4,3,2,1,0:T(8,128)(2,1)S(1)} %maximum_select_fusion.1), channel_id=1, source_target_pairs={{0,1},{1,0},{2,3},{3,2},{4,5},{5,4},{6,7},{7,6},{8,9},{9,8},{10,11... | collective-permute-start | bytes 983048 | tf_op jit(solution)/shard_map/ppermute | solution.py:268
  19.4 1.1 %collective-permute-done.4 = bf16[2,2,2,32,640]{4,3,2,1,0:T(8,128)(2,1)S(1)} collective-permute-done((bf16[2,2,2,32,640]{4,3,2,1,0:T(8,128)(2,1)S(1)}, bf16[2,2,2,32,640]{4,3,2,1,0:T(8,128)(2,1)S(1)}, u32[]{:S(2)}, u32[]{:S(2)}) %collective-permute-start.4) | collective-permute-done | bytes 327712 | tf_op jit(solution)/shard_map/ppermute | solution.py:268
  21.4 3.8 %shard_map.91 = bf16[512,512]{1,0:T(8,128)(2,1)} custom-call(s32[256]{0:T(256)} %select_n.194.blk_ref, bf16[65,32,128]{2,1,0:T(8,128)(2,1)} %concatenate.23.blocks_ref, bf16[512,512]{1,0:T(8,128)(2,1)} %bitcast.77, bf16[16,32,640]{2,1,0:T(8,128)(2,1)} %bitcast.65), custom_call_target="tpu_custom_call" | custom-call | tf_op jit(solution)/shard_map/pallas_call | solution.py:121
  25.2 6.4 %all-to-all-start = ((bf16[16,32,512]{2,1,0:T(8,128)(2,1)}), bf16[16,32,512]{2,1,0:T(8,128)(2,1)S(1)}, u32[]{:S(2)}, u32[]{:S(2)}) async-start(bf16[16,32,512]{2,1,0:T(8,128)(2,1)} %bitcast.71), calls=%async_computation | async-start | bytes 1048576 | tf_op jit(solution)/shard_map/all_to_all | solution.py:318
  31.8 0.7 %select_reduce_fusion.1 = bf16[9,16,144]{2,1,0:T(8,128)(2,1)} fusion(f32[3,9,144]{2,1,0:T(8,128)S(1)} %fusion.3, pred[3,16,144]{2,1,0:T(8,128)(4,1)S(1)} %broadcast_compare_fusion.1), kind=kLoop, calls=%fused_computation.9 | loop fusion | flops 103680 | bytes 63936 | tf_op jit(solution)/shard_map/reduce_sum | solution.py:191
  32.8 2.4 %select_reduce_fusion = bf16[9,32,8,272]{3,2,1,0:T(8,128)(2,1)} fusion(f32[3,9,8,272]{3,2,1,0:T(8,128)S(1)} %fusion.6, pred[3,32,8,272]{3,2,1,0:T(8,128)(4,1)S(1)} %broadcast_compare_fusion), kind=kLoop, calls=%fused_computation.1 | loop fusion | flops 3133440 | bytes 1697280 | tf_op jit(solution)/shard_map/reduce_sum | solution.py:191
  35.2 10.5 %all-to-all-done = bf16[16,32,512]{2,1,0:T(8,128)(2,1)S(1)} async-done(((bf16[16,32,512]{2,1,0:T(8,128)(2,1)}), bf16[16,32,512]{2,1,0:T(8,128)(2,1)S(1)}, u32[]{:S(2)}, u32[]{:S(2)}) %all-to-all-start) | async-done | bytes 524320 | tf_op jit(solution)/shard_map/all_to_all | solution.py:318
  46.4 2.4 %collective-permute-start.6 = (bf16[528,256]{1,0:T(8,128)(2,1)S(1)}, bf16[528,256]{1,0:T(8,128)(2,1)S(1)}, u32[]{:S(2)}, u32[]{:S(2)}) collective-permute-start(bf16[528,256]{1,0:T(8,128)(2,1)S(1)} %get-tuple-element.29), channel_id=1, source_target_pairs={{1,0},{2,1},{3,2},{4,3},{5,4},{6,5},{7,6},{8,7},{9,8},{10,9},{11,1... | collective-permute-start | bytes 811016 | tf_op jit(solution)/shard_map/ppermute | solution.py:345
  48.8 3.2 %collective-permute-start.5 = (bf16[528,256]{1,0:T(8,128)(2,1)S(1)}, bf16[528,256]{1,0:T(8,128)(2,1)S(1)}, u32[]{:S(2)}, u32[]{:S(2)}) collective-permute-start(bf16[528,256]{1,0:T(8,128)(2,1)S(1)} %get-tuple-element.30), channel_id=1, source_target_pairs={{0,1},{1,2},{2,3},{3,4},{4,5},{5,6},{6,7},{7,8},{8,9},{9,10},{10,1... | collective-permute-start | bytes 811016 | tf_op jit(solution)/shard_map/ppermute | solution.py:344
  52.6 1.6 %collective-permute-done.6.high_ref = bf16[528,256]{1,0:T(8,128)(2,1)S(1)} collective-permute-done((bf16[528,256]{1,0:T(8,128)(2,1)S(1)}, bf16[528,256]{1,0:T(8,128)(2,1)S(1)}, u32[]{:S(2)}, u32[]{:S(2)}) %collective-permute-start.6) | collective-permute-done | bytes 270368 | tf_op jit(solution)/shard_map/ppermute | solution.py:345
  54.1 2.8 %collective-permute-done.5.low_ref = bf16[528,256]{1,0:T(8,128)(2,1)S(1)} collective-permute-done((bf16[528,256]{1,0:T(8,128)(2,1)S(1)}, bf16[528,256]{1,0:T(8,128)(2,1)S(1)}, u32[]{:S(2)}, u32[]{:S(2)}) %collective-permute-start.5) | collective-permute-done | bytes 270368 | tf_op jit(solution)/shard_map/ppermute | solution.py:344
  56.9 0.7 %copy-done.4 = bf16[528,256]{1,0:T(8,128)(2,1)} copy-done((bf16[528,256]{1,0:T(8,128)(2,1)}, bf16[528,256]{1,0:T(8,128)(2,1)S(1)}, u32[]{:S(2)}) %copy-start.4) | copy-done | bytes 270360
  57.6 7.6 %shard_map.92 = f32[4,64,128]{2,1,0:T(8,128)} custom-call(s32[2]{0:T(128)} %add_convert_fusion.ends_ref, bf16[528,256]{1,0:T(8,128)(2,1)} %copy-done.4, bf16[528,512]{1,0:T(8,128)(2,1)} %bitcast.63, bf16[528,256]{1,0:T(8,128)(2,1)} %copy-done.3, bf16[3,3,256,272]{3,2,1,0:T(8,128)(2,1)} %bitcast.61, bf16[3,3,16,144]{3,2,1,0:T(8,128)(2,1)} %bitcast.79), custom_call_target="tpu_custom_call" | custom-call | tf_op jit(solution)/shard_map/pallas_call | solution.py:226
  (57 shorter events, 5.2 us)
Async XLA Ops:
  0.0 32.5 %copy-start = (bf16[3,3,3,8,8]{4,3,2,1,0:T(8,128)(2,1)S(1)}, bf16[3,3,3,8,8]{4,3,2,1,0:T(8,128)(2,1)}, u32[]{:S(2)}) copy-start(bf16[3,3,3,8,8]{4,3,2,1,0:T(8,128)(2,1)} %param.18) | copy-start | bytes 10372
  1.5 10.1 %collective-permute-start.1 = (bf16[32,640]{1,0:T(8,128)(2,1)S(1)}, bf16[32,640]{1,0:T(8,128)(2,1)S(1)}, u32[]{:S(2)}, u32[]{:S(2)}) collective-permute-start(bf16[32,640]{1,0:T(8,128)(2,1)S(1)} %get-tuple-element.34), channel_id=1, source_target_pairs={{0,8},{1,9},{2,10},{3,11},{4,12},{5,13},{6,14},{7,15},{8,0},{9,1},... | collective-permute-start | bytes 122888 | tf_op jit(solution)/shard_map/ppermute | solution.py:260
  4.6 7.0 %collective-permute-start = (bf16[32,640]{1,0:T(8,128)(2,1)S(1)}, bf16[32,640]{1,0:T(8,128)(2,1)S(1)}, u32[]{:S(2)}, u32[]{:S(2)}) collective-permute-start(bf16[32,640]{1,0:T(8,128)(2,1)S(1)} %get-tuple-element.34), channel_id=1, source_target_pairs={{0,4},{1,5},{2,6},{3,7},{4,0},{5,1},{6,2},{7,3},{8,12},{9,13},{10,... | collective-permute-start | bytes 122888 | tf_op jit(solution)/shard_map/ppermute | solution.py:260
  5.9 5.7 %collective-permute-start.2 = (bf16[32,640]{1,0:T(8,128)(2,1)S(1)}, bf16[32,640]{1,0:T(8,128)(2,1)S(1)}, u32[]{:S(2)}, u32[]{:S(2)}) collective-permute-start(bf16[32,640]{1,0:T(8,128)(2,1)S(1)} %get-tuple-element.34), channel_id=1, source_target_pairs={{0,12},{1,13},{2,14},{3,15},{4,8},{5,9},{6,10},{7,11},{8,4},{9,5},... | collective-permute-start | bytes 122888 | tf_op jit(solution)/shard_map/ppermute | solution.py:260
  12.4 4.2 %collective-permute-start.3 = (bf16[2,2,32,640]{3,2,1,0:T(8,128)(2,1)S(1)}, bf16[2,2,32,640]{3,2,1,0:T(8,128)(2,1)S(1)}, u32[]{:S(2)}, u32[]{:S(2)}) collective-permute-start(bf16[2,2,32,640]{3,2,1,0:T(8,128)(2,1)S(1)} %broadcast_select_fusion), channel_id=1, source_target_pairs={{0,2},{1,3},{2,0},{3,1},{4,6},{5,7},{6,4},{7,5},{8,10},{9,11},{10,... | collective-permute-start | bytes 491528 | tf_op jit(solution)/shard_map/ppermute | solution.py:268
  16.7 3.8 %collective-permute-start.4 = (bf16[2,2,2,32,640]{4,3,2,1,0:T(8,128)(2,1)S(1)}, bf16[2,2,2,32,640]{4,3,2,1,0:T(8,128)(2,1)S(1)}, u32[]{:S(2)}, u32[]{:S(2)}) collective-permute-start(bf16[2,2,2,32,640]{4,3,2,1,0:T(8,128)(2,1)S(1)} %maximum_select_fusion.1), channel_id=1, source_target_pairs={{0,1},{1,0},{2,3},{3,2},{4,5},{5,4},{6,7},{7,6},{8,9},{9,8},{10,11... | collective-permute-start | bytes 983048 | tf_op jit(solution)/shard_map/ppermute | solution.py:268
  20.6 0.8 %copy-start.2 = (bf16[2,2,2,2,32,640]{5,4,3,2,1,0:T(8,128)(2,1)}, bf16[2,2,2,2,32,640]{5,4,3,2,1,0:T(8,128)(2,1)S(1)}, u32[]{:S(2)}) copy-start(bf16[2,2,2,2,32,640]{5,4,3,2,1,0:T(8,128)(2,1)S(1)} %maximum_select_fusion) | copy-start | bytes 1966084
  20.6 11.0 %copy-start.5 = (bf16[3,3,3,8]{3,2,1,0:T(4,128)(2,1)S(1)}, bf16[3,3,3,8]{3,2,1,0:T(4,128)(2,1)}, u32[]{:S(2)}) copy-start(bf16[3,3,3,8]{3,2,1,0:T(4,128)(2,1)} %param.19) | copy-start | bytes 1300
  25.2 20.4 %all-to-all-start = ((bf16[16,32,512]{2,1,0:T(8,128)(2,1)}), bf16[16,32,512]{2,1,0:T(8,128)(2,1)S(1)}, u32[]{:S(2)}, u32[]{:S(2)}) async-start(bf16[16,32,512]{2,1,0:T(8,128)(2,1)} %bitcast.71), calls=%async_computation | async-start | bytes 1048576 | tf_op jit(solution)/shard_map/all_to_all | solution.py:318
  46.3 10.6 %copy-start.1 = (bf16[66,8,512]{2,1,0:T(8,128)(2,1)}, bf16[66,8,512]{2,1,0:T(8,128)(2,1)S(1)}, u32[]{:S(2)}) copy-start(bf16[66,8,512]{2,1,0:T(8,128)(2,1)S(1)} %copy.52) | copy-start | bytes 1622020
  46.4 7.8 %collective-permute-start.6 = (bf16[528,256]{1,0:T(8,128)(2,1)S(1)}, bf16[528,256]{1,0:T(8,128)(2,1)S(1)}, u32[]{:S(2)}, u32[]{:S(2)}) collective-permute-start(bf16[528,256]{1,0:T(8,128)(2,1)S(1)} %get-tuple-element.29), channel_id=1, source_target_pairs={{1,0},{2,1},{3,2},{4,3},{5,4},{6,5},{7,6},{8,7},{9,8},{10,9},{11,1... | collective-permute-start | bytes 811016 | tf_op jit(solution)/shard_map/ppermute | solution.py:345
  48.8 8.1 %collective-permute-start.5 = (bf16[528,256]{1,0:T(8,128)(2,1)S(1)}, bf16[528,256]{1,0:T(8,128)(2,1)S(1)}, u32[]{:S(2)}, u32[]{:S(2)}) collective-permute-start(bf16[528,256]{1,0:T(8,128)(2,1)S(1)} %get-tuple-element.30), channel_id=1, source_target_pairs={{0,1},{1,2},{2,3},{3,4},{4,5},{5,6},{6,7},{7,8},{8,9},{9,10},{10,1... | collective-permute-start | bytes 811016 | tf_op jit(solution)/shard_map/ppermute | solution.py:344
  54.1 2.8 %copy-start.3 = (bf16[528,256]{1,0:T(8,128)(2,1)}, bf16[528,256]{1,0:T(8,128)(2,1)S(1)}, u32[]{:S(2)}) copy-start(bf16[528,256]{1,0:T(8,128)(2,1)S(1)} %collective-permute-done.6.high_ref) | copy-start | bytes 811012
  56.9 0.7 %copy-start.4 = (bf16[528,256]{1,0:T(8,128)(2,1)}, bf16[528,256]{1,0:T(8,128)(2,1)S(1)}, u32[]{:S(2)}) copy-start(bf16[528,256]{1,0:T(8,128)(2,1)S(1)} %collective-permute-done.5.low_ref) | copy-start | bytes 811012

commit v25 on v22

--- a/solution.py
+++ b/solution.py
@@ -74,7 +74,7 @@
 
 
 def correlate_kernel(blk_ref, blocks_ref, table_ref, ref_ref, out_ref, arranged, products):
-    chunk = 32
+    chunk = 64
     slots = table_ref.shape[0] // blocks_ref.shape[2]
     width = blocks_ref.shape[2]
     channels = blocks_ref.shape[1]
@@ -117,7 +117,7 @@
 def correlate(blk, blocks, table, refs, units):
     channels, width = blocks.shape[1], blocks.shape[2]
     tpix = table.shape[1]
-    chunk = 32
+    chunk = 64
     return pl.pallas_call(
         correlate_kernel,
         out_shape=jax.ShapeDtypeStruct((units * GROUPS, tpix), jnp.bfloat16),

time: 62 us -> 62.1 us (level)
  no operation moved by 1% of the time
where the time goes in v25:
time: 62.1 us; the launch traced here: 61.7 us
  starting transfers between devices  20.2 us (33%)
  waiting for transfers between devices  20.1 us (32%)
  Pallas kernels  8.78 us (14%)
  other arithmetic  7.07 us (11%)
  local copies, waits for them, and re-layouts  4.47 us (7%)
  matrix products  0.77 us (1%)
    all_to_all x1, waiting for transfers between devices, body(): lax.all_to_all(corr_all.reshape(owners, cap * GROUPS, tpix), 'view', spli...  11.7 us
    all_to_all x1, starting transfers between devices, body(): lax.all_to_all(corr_all.reshape(owners, cap * GROUPS, tpix), 'view', spli...  5.38 us
    pallas_call x1, Pallas kernels, conv_pair(): pl.pallas_call(functools.partial(conv_pair_kernel, rows=rows, cols=cols,...  4.88 us
    ppermute x2, starting transfers between devices, gather_view(): lax.ppermute(gathered, 'view', [(i, i ^ stride) for i in range(count)])  4.8 us
    ppermute x3, starting transfers between devices, gather_view(): lax.ppermute(gathered, 'view', [(i, i ^ m * top) for i in range(count)])  4.44 us
    ppermute x2, waiting for transfers between devices, gather_view(): lax.ppermute(gathered, 'view', [(i, i ^ stride) for i in range(count)])  3.98 us
    pallas_call x1, Pallas kernels, correlate(): pl.pallas_call(correlate_kernel, out_shape=jax.ShapeDtypeStruct((units *...  3.9 us
    ppermute x1, starting transfers between devices, body(): lax.ppermute(volume[:, volume.shape[1] - 2 * columns:], 'view', forward)  3.16 us
  transfers between devices with their start and end apart: 8, of which 6 were waited for; matrix products, arithmetic and copies ran while one was open for 12% of the time, Pallas kernels for 0%

profile of v25, /device:TPU:1, one launch (start us, length us, event | category | flops | bytes accessed | tf_op | source)
XLA Modules:
  0.0 61.7 jit_solution(8736711514115761029)
XLA Ops:
  0.0 0.7 %fusion.18 = bf16[64]{0:T(256)(128)(2,1)S(1)} fusion(s32[1,64]{1,0:T(1,128)} %param.17, s32[1,64]{1,0:T(1,128)} %param.16), kind=kLoop, calls=%fused_computation.60 | loop fusion | flops 192 | bytes 640 | tf_op jit(solution)/shard_map/convert_element_type | solution.py:308
  0.7 0.8 %fusion.20 = (bf16[1,32,640]{2,1,0:T(8,128)(2,1)S(1)}, bf16[32,640]{1,0:T(8,128)(2,1)S(1)}) fusion(bf16[32,128]{1,0:T(8,128)(2,1)S(1)} %pad_bitcast_fusion, bf16[32,512]{1,0:T(8,128)(2,1)} %bitcast.85), kind=kLoop, calls=%fused_computation.66 | loop fusion | flops 81920 | bytes 122880 | tf_op jit(solution)/shard_map/broadcast_in_dim | solution.py:311
  1.5 3.1 %collective-permute-start.1 = (bf16[32,640]{1,0:T(8,128)(2,1)S(1)}, bf16[32,640]{1,0:T(8,128)(2,1)S(1)}, u32[]{:S(2)}, u32[]{:S(2)}) collective-permute-start(bf16[32,640]{1,0:T(8,128)(2,1)S(1)} %get-tuple-element.34), channel_id=1, source_target_pairs={{0,8},{1,9},{2,10},{3,11},{4,12},{5,13},{6,14},{7,15},{8,0},{9,1},... | collective-permute-start | bytes 122888 | tf_op jit(solution)/shard_map/ppermute | solution.py:260
  4.7 1.3 %collective-permute-start = (bf16[32,640]{1,0:T(8,128)(2,1)S(1)}, bf16[32,640]{1,0:T(8,128)(2,1)S(1)}, u32[]{:S(2)}, u32[]{:S(2)}) collective-permute-start(bf16[32,640]{1,0:T(8,128)(2,1)S(1)} %get-tuple-element.34), channel_id=1, source_target_pairs={{0,4},{1,5},{2,6},{3,7},{4,0},{5,1},{6,2},{7,3},{8,12},{9,13},{10,... | collective-permute-start | bytes 122888 | tf_op jit(solution)/shard_map/ppermute | solution.py:260
  6.7 0.7 %fusion.10 = pred[64,4]{0,1:T(4,128)(4,1)S(1)} fusion(s32[64,4]{0,1:T(4,128)} %bitcast.86, pred[64,4]{0,1:T(4,128)(4,1)S(1)} %iota_compare_fusion.2), kind=kLoop, calls=%fused_computation.40 | loop fusion | flops 2816 | bytes 1536 | tf_op jit(solution)/shard_map/reduce_or | solution.py:306
  7.4 0.7 %select_reduce_fusion.2 = s32[64,4]{0,1:T(4,128)S(1)} fusion(s32[64,4]{0,1:T(4,128)} %bitcast.88, s32[64,4]{0,1:T(4,128)} %bitcast.87), kind=kLoop, calls=%fused_computation.33 | loop fusion | flops 2816 | bytes 3072 | tf_op jit(solution)/shard_map/reduce_sum | solution.py:305
  8.5 0.7 %select_n.180.blk_ref = s32[256]{0:T(256)} reshape(s32[64,4]{1,0:T(8,128)S(1)} %copy.32) | data formatting | bytes 2048 | tf_op jit(solution)/shard_map/jit(_where)/select_n | solution.py:307
  9.7 0.9 %concatenate.23.blocks_ref = bf16[65,32,128]{2,1,0:T(8,128)(2,1)} pad(bf16[64,32,128]{2,1,0:T(8,128)(2,1)S(1)} %bitcast.69, bf16[]{:T(256)} %constant.153.clone.1), padding=0_1x0_0x0_0 | pad | bytes 1056770 | tf_op jit(solution)/shard_map/concatenate | solution.py:302
  11.5 1.3 %collective-permute-start.3 = (bf16[2,2,32,640]{3,2,1,0:T(8,128)(2,1)S(1)}, bf16[2,2,32,640]{3,2,1,0:T(8,128)(2,1)S(1)}, u32[]{:S(2)}, u32[]{:S(2)}) collective-permute-start(bf16[2,2,32,640]{3,2,1,0:T(8,128)(2,1)S(1)} %broadcast_select_fusion), channel_id=1, source_target_pairs={{0,2},{1,3},{2,0},{3,1},{4,6},{5,7},{6,4},{7,5},{8,10},{9,11},{10,... | collective-permute-start | bytes 491528 | tf_op jit(solution)/shard_map/ppermute | solution.py:268
  12.9 2.8 %collective-permute-done.3 = bf16[2,2,32,640]{3,2,1,0:T(8,128)(2,1)S(1)} collective-permute-done((bf16[2,2,32,640]{3,2,1,0:T(8,128)(2,1)S(1)}, bf16[2,2,32,640]{3,2,1,0:T(8,128)(2,1)S(1)}, u32[]{:S(2)}, u32[]{:S(2)}) %collective-permute-start.3) | collective-permute-done | bytes 163872 | tf_op jit(solution)/shard_map/ppermute | solution.py:268
  15.8 3.5 %collective-permute-start.4 = (bf16[2,2,2,32,640]{4,3,2,1,0:T(8,128)(2,1)S(1)}, bf16[2,2,2,32,640]{4,3,2,1,0:T(8,128)(2,1)S(1)}, u32[]{:S(2)}, u32[]{:S(2)}) collective-permute-start(bf16[2,2,2,32,640]{4,3,2,1,0:T(8,128)(2,1)S(1)} %maximum_select_fusion.1), channel_id=1, source_target_pairs={{0,1},{1,0},{2,3},{3,2},{4,5},{5,4},{6,7},{7,6},{8,9},{9,8},{10,11... | collective-permute-start | bytes 983048 | tf_op jit(solution)/shard_map/ppermute | solution.py:268
  19.4 1.1 %collective-permute-done.4 = bf16[2,2,2,32,640]{4,3,2,1,0:T(8,128)(2,1)S(1)} collective-permute-done((bf16[2,2,2,32,640]{4,3,2,1,0:T(8,128)(2,1)S(1)}, bf16[2,2,2,32,640]{4,3,2,1,0:T(8,128)(2,1)S(1)}, u32[]{:S(2)}, u32[]{:S(2)}) %collective-permute-start.4) | collective-permute-done | bytes 327712 | tf_op jit(solution)/shard_map/ppermute | solution.py:268
  21.5 3.9 %shard_map.91 = bf16[512,512]{1,0:T(8,128)(2,1)} custom-call(s32[256]{0:T(256)} %select_n.180.blk_ref, bf16[65,32,128]{2,1,0:T(8,128)(2,1)} %concatenate.23.blocks_ref, bf16[512,512]{1,0:T(8,128)(2,1)} %bitcast.77, bf16[16,32,640]{2,1,0:T(8,128)(2,1)} %bitcast.64), custom_call_target="tpu_custom_call" | custom-call | tf_op jit(solution)/shard_map/pallas_call | solution.py:121
  25.4 5.4 %all-to-all-start = ((bf16[16,32,512]{2,1,0:T(8,128)(2,1)}), bf16[16,32,512]{2,1,0:T(8,128)(2,1)S(1)}, u32[]{:S(2)}, u32[]{:S(2)}) async-start(bf16[16,32,512]{2,1,0:T(8,128)(2,1)} %bitcast.71), calls=%async_computation | async-start | bytes 1048576 | tf_op jit(solution)/shard_map/all_to_all | solution.py:318
  31.0 0.7 %select_reduce_fusion.1 = bf16[9,16,144]{2,1,0:T(8,128)(2,1)} fusion(f32[3,9,144]{2,1,0:T(8,128)S(1)} %fusion.2, pred[3,16,144]{2,1,0:T(8,128)(4,1)S(1)} %broadcast_compare_fusion.1), kind=kLoop, calls=%fused_computation.8 | loop fusion | flops 103680 | bytes 63936 | tf_op jit(solution)/shard_map/reduce_sum | solution.py:191
  31.9 1.2 %select_reduce_fusion = bf16[9,16,8,144]{3,2,1,0:T(8,128)(2,1)} fusion(f32[3,9,8,144]{3,2,1,0:T(8,128)S(1)} %fusion.11, pred[3,16,8,144]{3,2,1,0:T(8,128)(4,1)S(1)} %broadcast_compare_fusion), kind=kLoop, calls=%fused_computation.1 | loop fusion | flops 829440 | bytes 511488 | tf_op jit(solution)/shard_map/reduce_sum | solution.py:191
  33.1 11.7 %all-to-all-done = bf16[16,32,512]{2,1,0:T(8,128)(2,1)S(1)} async-done(((bf16[16,32,512]{2,1,0:T(8,128)(2,1)}), bf16[16,32,512]{2,1,0:T(8,128)(2,1)S(1)}, u32[]{:S(2)}, u32[]{:S(2)}) %all-to-all-start) | async-done | bytes 524320 | tf_op jit(solution)/shard_map/all_to_all | solution.py:318
  45.5 2.4 %collective-permute-start.6 = (bf16[528,256]{1,0:T(8,128)(2,1)S(1)}, bf16[528,256]{1,0:T(8,128)(2,1)S(1)}, u32[]{:S(2)}, u32[]{:S(2)}) collective-permute-start(bf16[528,256]{1,0:T(8,128)(2,1)S(1)} %get-tuple-element.29), channel_id=1, source_target_pairs={{1,0},{2,1},{3,2},{4,3},{5,4},{6,5},{7,6},{8,7},{9,8},{10,9},{11,1... | collective-permute-start | bytes 811016 | tf_op jit(solution)/shard_map/ppermute | solution.py:345
  47.9 3.2 %collective-permute-start.5 = (bf16[528,256]{1,0:T(8,128)(2,1)S(1)}, bf16[528,256]{1,0:T(8,128)(2,1)S(1)}, u32[]{:S(2)}, u32[]{:S(2)}) collective-permute-start(bf16[528,256]{1,0:T(8,128)(2,1)S(1)} %get-tuple-element.30), channel_id=1, source_target_pairs={{0,1},{1,2},{2,3},{3,4},{4,5},{5,6},{6,7},{7,8},{8,9},{9,10},{10,1... | collective-permute-start | bytes 811016 | tf_op jit(solution)/shard_map/ppermute | solution.py:344
  51.1 0.7 %add_convert_fusion.ends_ref = s32[2]{0:T(128)} fusion(pred[1]{0:T(512)(128)(4,1)} %bitcast.1, pred[1]{0:T(512)(128)(4,1)} %bitcast), kind=kLoop, calls=%fused_computation.52 | loop fusion | flops 4 | bytes 10 | tf_op jit(solution)/shard_map/convert_element_type | solution.py:340
  51.8 1.5 %collective-permute-done.6.high_ref = bf16[528,256]{1,0:T(8,128)(2,1)S(1)} collective-permute-done((bf16[528,256]{1,0:T(8,128)(2,1)S(1)}, bf16[528,256]{1,0:T(8,128)(2,1)S(1)}, u32[]{:S(2)}, u32[]{:S(2)}) %collective-permute-start.6) | collective-permute-done | bytes 270368 | tf_op jit(solution)/shard_map/ppermute | solution.py:345
  53.3 2.8 %collective-permute-done.5.low_ref = bf16[528,256]{1,0:T(8,128)(2,1)S(1)} collective-permute-done((bf16[528,256]{1,0:T(8,128)(2,1)S(1)}, bf16[528,256]{1,0:T(8,128)(2,1)S(1)}, u32[]{:S(2)}, u32[]{:S(2)}) %collective-permute-start.5) | collective-permute-done | bytes 270368 | tf_op jit(solution)/shard_map/ppermute | solution.py:344
  56.1 0.7 %copy-done.5 = bf16[528,256]{1,0:T(8,128)(2,1)} copy-done((bf16[528,256]{1,0:T(8,128)(2,1)}, bf16[528,256]{1,0:T(8,128)(2,1)S(1)}, u32[]{:S(2)}) %copy-start.5) | copy-done | bytes 270360
  56.8 4.9 %shard_map.92 = f32[4,64,128]{2,1,0:T(8,128)} custom-call(s32[2]{0:T(128)} %add_convert_fusion.ends_ref, bf16[528,256]{1,0:T(8,128)(2,1)} %copy-done.5, bf16[528,512]{1,0:T(8,128)(2,1)} %bitcast.62, bf16[528,256]{1,0:T(8,128)(2,1)} %copy-done.4, bf16[3,3,128,144]{3,2,1,0:T(8,128)(2,1)} %bitcast.68, bf16[3,3,16,144]{3,2,1,0:T(8,128)(2,1)} %bitcast.79), custom_call_target="tpu_custom_call" | custom-call | tf_op jit(solution)/shard_map/pallas_call | solution.py:226
  (57 shorter events, 4.7 us)
Async XLA Ops:
  0.0 31.7 %copy-start = (bf16[3,3,3,8,8]{4,3,2,1,0:T(8,128)(2,1)S(1)}, bf16[3,3,3,8,8]{4,3,2,1,0:T(8,128)(2,1)}, u32[]{:S(2)}) copy-start(bf16[3,3,3,8,8]{4,3,2,1,0:T(8,128)(2,1)} %param.18) | copy-start | bytes 10372
  0.0 9.2 %copy-start.3 = (bf16[1,32,8192]{2,1,0:T(8,128)(2,1)S(1)}, bf16[1,32,8192]{2,1,0:T(8,128)(2,1)}, u32[]{:S(2)}) copy-start(bf16[1,32,8192]{2,1,0:T(8,128)(2,1)} %param.11) | copy-start | bytes 1572868
  1.5 9.0 %collective-permute-start.1 = (bf16[32,640]{1,0:T(8,128)(2,1)S(1)}, bf16[32,640]{1,0:T(8,128)(2,1)S(1)}, u32[]{:S(2)}, u32[]{:S(2)}) collective-permute-start(bf16[32,640]{1,0:T(8,128)(2,1)S(1)} %get-tuple-element.34), channel_id=1, source_target_pairs={{0,8},{1,9},{2,10},{3,11},{4,12},{5,13},{6,14},{7,15},{8,0},{9,1},... | collective-permute-start | bytes 122888 | tf_op jit(solution)/shard_map/ppermute | solution.py:260
  4.7 5.9 %collective-permute-start = (bf16[32,640]{1,0:T(8,128)(2,1)S(1)}, bf16[32,640]{1,0:T(8,128)(2,1)S(1)}, u32[]{:S(2)}, u32[]{:S(2)}) collective-permute-start(bf16[32,640]{1,0:T(8,128)(2,1)S(1)} %get-tuple-element.34), channel_id=1, source_target_pairs={{0,4},{1,5},{2,6},{3,7},{4,0},{5,1},{6,2},{7,3},{8,12},{9,13},{10,... | collective-permute-start | bytes 122888 | tf_op jit(solution)/shard_map/ppermute | solution.py:260
  5.9 4.8 %collective-permute-start.2 = (bf16[32,640]{1,0:T(8,128)(2,1)S(1)}, bf16[32,640]{1,0:T(8,128)(2,1)S(1)}, u32[]{:S(2)}, u32[]{:S(2)}) collective-permute-start(bf16[32,640]{1,0:T(8,128)(2,1)S(1)} %get-tuple-element.34), channel_id=1, source_target_pairs={{0,12},{1,13},{2,14},{3,15},{4,8},{5,9},{6,10},{7,11},{8,4},{9,5},... | collective-permute-start | bytes 122888 | tf_op jit(solution)/shard_map/ppermute | solution.py:260
  11.5 4.2 %collective-permute-start.3 = (bf16[2,2,32,640]{3,2,1,0:T(8,128)(2,1)S(1)}, bf16[2,2,32,640]{3,2,1,0:T(8,128)(2,1)S(1)}, u32[]{:S(2)}, u32[]{:S(2)}) collective-permute-start(bf16[2,2,32,640]{3,2,1,0:T(8,128)(2,1)S(1)} %broadcast_select_fusion), channel_id=1, source_target_pairs={{0,2},{1,3},{2,0},{3,1},{4,6},{5,7},{6,4},{7,5},{8,10},{9,11},{10,... | collective-permute-start | bytes 491528 | tf_op jit(solution)/shard_map/ppermute | solution.py:268
  15.8 4.7 %collective-permute-start.4 = (bf16[2,2,2,32,640]{4,3,2,1,0:T(8,128)(2,1)S(1)}, bf16[2,2,2,32,640]{4,3,2,1,0:T(8,128)(2,1)S(1)}, u32[]{:S(2)}, u32[]{:S(2)}) collective-permute-start(bf16[2,2,2,32,640]{4,3,2,1,0:T(8,128)(2,1)S(1)} %maximum_select_fusion.1), channel_id=1, source_target_pairs={{0,1},{1,0},{2,3},{3,2},{4,5},{5,4},{6,7},{7,6},{8,9},{9,8},{10,11... | collective-permute-start | bytes 983048 | tf_op jit(solution)/shard_map/ppermute | solution.py:268
  20.6 0.8 %copy-start.2 = (bf16[2,2,2,2,32,640]{5,4,3,2,1,0:T(8,128)(2,1)}, bf16[2,2,2,2,32,640]{5,4,3,2,1,0:T(8,128)(2,1)S(1)}, u32[]{:S(2)}) copy-start(bf16[2,2,2,2,32,640]{5,4,3,2,1,0:T(8,128)(2,1)S(1)} %maximum_select_fusion) | copy-start | bytes 1966084
  25.4 5.4 %copy-start.6 = (bf16[3,3,3,8]{3,2,1,0:T(4,128)(2,1)S(1)}, bf16[3,3,3,8]{3,2,1,0:T(4,128)(2,1)}, u32[]{:S(2)}) copy-start(bf16[3,3,3,8]{3,2,1,0:T(4,128)(2,1)} %param.19) | copy-start | bytes 1300
  25.4 19.5 %all-to-all-start = ((bf16[16,32,512]{2,1,0:T(8,128)(2,1)}), bf16[16,32,512]{2,1,0:T(8,128)(2,1)S(1)}, u32[]{:S(2)}, u32[]{:S(2)}) async-start(bf16[16,32,512]{2,1,0:T(8,128)(2,1)} %bitcast.71), calls=%async_computation | async-start | bytes 1048576 | tf_op jit(solution)/shard_map/all_to_all | solution.py:318
  45.5 10.6 %copy-start.1 = (bf16[66,8,512]{2,1,0:T(8,128)(2,1)}, bf16[66,8,512]{2,1,0:T(8,128)(2,1)S(1)}, u32[]{:S(2)}) copy-start(bf16[66,8,512]{2,1,0:T(8,128)(2,1)S(1)} %copy.52) | copy-start | bytes 1622020
  45.5 7.8 %collective-permute-start.6 = (bf16[528,256]{1,0:T(8,128)(2,1)S(1)}, bf16[528,256]{1,0:T(8,128)(2,1)S(1)}, u32[]{:S(2)}, u32[]{:S(2)}) collective-permute-start(bf16[528,256]{1,0:T(8,128)(2,1)S(1)} %get-tuple-element.29), channel_id=1, source_target_pairs={{1,0},{2,1},{3,2},{4,3},{5,4},{6,5},{7,6},{8,7},{9,8},{10,9},{11,1... | collective-permute-start | bytes 811016 | tf_op jit(solution)/shard_map/ppermute | solution.py:345
  47.9 8.1 %collective-permute-start.5 = (bf16[528,256]{1,0:T(8,128)(2,1)S(1)}, bf16[528,256]{1,0:T(8,128)(2,1)S(1)}, u32[]{:S(2)}, u32[]{:S(2)}) collective-permute-start(bf16[528,256]{1,0:T(8,128)(2,1)S(1)} %get-tuple-element.30), channel_id=1, source_target_pairs={{0,1},{1,2},{2,3},{3,4},{4,5},{5,6},{6,7},{7,8},{8,9},{9,10},{10,1... | collective-permute-start | bytes 811016 | tf_op jit(solution)/shard_map/ppermute | solution.py:344
  53.3 2.8 %copy-start.4 = (bf16[528,256]{1,0:T(8,128)(2,1)}, bf16[528,256]{1,0:T(8,128)(2,1)S(1)}, u32[]{:S(2)}) copy-start(bf16[528,256]{1,0:T(8,128)(2,1)S(1)} %collective-permute-done.6.high_ref) | copy-start | bytes 811012
  56.1 0.7 %copy-start.5 = (bf16[528,256]{1,0:T(8,128)(2,1)}, bf16[528,256]{1,0:T(8,128)(2,1)S(1)}, u32[]{:S(2)}) copy-start(bf16[528,256]{1,0:T(8,128)(2,1)S(1)} %collective-permute-done.5.low_ref) | copy-start | bytes 811012

commit v26 on v22

--- a/solution.py
+++ b/solution.py
@@ -307,7 +307,11 @@
     blk = jnp.where(alive, picked, nblocks).reshape(-1).astype(jnp.int32)
     depth_code = jnp.where(counts > 0, depth_plane[0], -1).astype(jnp.bfloat16)
 
-    tag_block = jnp.pad(depth_code, (0, channels * 128 - units)).reshape(channels, 128)
+    if units <= 128:
+        code_row = jnp.where(block_count > 0, depth_plane, -1).astype(jnp.bfloat16)
+        tag_block = jnp.pad(code_row, ((0, channels - 1), (0, 128 - units)))
+    else:
+        tag_block = jnp.pad(depth_code, (0, channels * 128 - units)).reshape(channels, 128)
     ref_all = gather_view(jnp.concatenate([ref_feat[0], tag_block], axis=1)[None])
     corr_all = correlate(
         blk, blocks, weight_table.reshape(slots * block_width, tpix), ref_all, units

time: 62 us -> 62 us (level)
  no operation moved by 1% of the time
where the time goes in v26:
time: 62 us; the launch traced here: 61.6 us
  starting transfers between devices  20.2 us (33%)
  waiting for transfers between devices  20.1 us (32%)
  Pallas kernels  8.67 us (14%)
  other arithmetic  7.07 us (11%)
  local copies, waits for them, and re-layouts  4.47 us (7%)
  matrix products  0.77 us (1%)
    all_to_all x1, waiting for transfers between devices, body(): lax.all_to_all(corr_all.reshape(owners, cap * GROUPS, tpix), 'view', spli...  11.7 us
    all_to_all x1, starting transfers between devices, body(): lax.all_to_all(corr_all.reshape(owners, cap * GROUPS, tpix), 'view', spli...  5.39 us
    pallas_call x1, Pallas kernels, conv_pair(): pl.pallas_call(functools.partial(conv_pair_kernel, rows=rows, cols=cols,...  4.88 us
    ppermute x2, starting transfers between devices, gather_view(): lax.ppermute(gathered, 'view', [(i, i ^ stride) for i in range(count)])  4.8 us
    ppermute x3, starting transfers between devices, gather_view(): lax.ppermute(gathered, 'view', [(i, i ^ m * top) for i in range(count)])  4.44 us
    ppermute x2, waiting for transfers between devices, gather_view(): lax.ppermute(gathered, 'view', [(i, i ^ stride) for i in range(count)])  3.98 us
    pallas_call x1, Pallas kernels, correlate(): pl.pallas_call(correlate_kernel, out_shape=jax.ShapeDtypeStruct((units *...  3.79 us
    ppermute x1, starting transfers between devices, body(): lax.ppermute(volume[:, volume.shape[1] - 2 * columns:], 'view', forward)  3.16 us
  transfers between devices with their start and end apart: 8, of which 6 were waited for; matrix products, arithmetic and copies ran while one was open for 12% of the time, Pallas kernels for 0%

profile of v26, /device:TPU:1, one launch (start us, length us, event | category | flops | bytes accessed | tf_op | source)
XLA Modules:
  0.0 61.6 jit_solution(4554804113247559881)
XLA Ops:
  0.0 0.7 %fusion.20 = bf16[1,64]{1,0:T(2,128)(2,1)S(1)} fusion(s32[1,64]{1,0:T(1,128)} %param.17, s32[1,64]{1,0:T(1,128)} %param.16), kind=kLoop, calls=%fused_computation.61 | loop fusion | flops 192 | bytes 640 | tf_op jit(solution)/shard_map/convert_element_type | solution.py:311
  0.7 0.8 %fusion.22 = (bf16[1,32,640]{2,1,0:T(8,128)(2,1)S(1)}, bf16[32,640]{1,0:T(8,128)(2,1)S(1)}) fusion(bf16[1,64]{1,0:T(2,128)(2,1)S(1)} %fusion.20, bf16[32,512]{1,0:T(8,128)(2,1)} %bitcast.80), kind=kLoop, calls=%fused_computation.67 | loop fusion | flops 122880 | bytes 114816 | tf_op jit(solution)/shard_map/broadcast_in_dim | solution.py:315
  1.5 3.1 %collective-permute-start.1 = (bf16[32,640]{1,0:T(8,128)(2,1)S(1)}, bf16[32,640]{1,0:T(8,128)(2,1)S(1)}, u32[]{:S(2)}, u32[]{:S(2)}) collective-permute-start(bf16[32,640]{1,0:T(8,128)(2,1)S(1)} %get-tuple-element.34), channel_id=1, source_target_pairs={{0,8},{1,9},{2,10},{3,11},{4,12},{5,13},{6,14},{7,15},{8,0},{9,1},... | collective-permute-start | bytes 122888 | tf_op jit(solution)/shard_map/ppermute | solution.py:260
  4.6 1.3 %collective-permute-start = (bf16[32,640]{1,0:T(8,128)(2,1)S(1)}, bf16[32,640]{1,0:T(8,128)(2,1)S(1)}, u32[]{:S(2)}, u32[]{:S(2)}) collective-permute-start(bf16[32,640]{1,0:T(8,128)(2,1)S(1)} %get-tuple-element.34), channel_id=1, source_target_pairs={{0,4},{1,5},{2,6},{3,7},{4,0},{5,1},{6,2},{7,3},{8,12},{9,13},{10,... | collective-permute-start | bytes 122888 | tf_op jit(solution)/shard_map/ppermute | solution.py:260
  6.7 0.7 %fusion.12 = pred[64,4]{0,1:T(4,128)(4,1)S(1)} fusion(s32[64,4]{0,1:T(4,128)} %bitcast.81, pred[64,4]{0,1:T(4,128)(4,1)S(1)} %iota_compare_fusion.3), kind=kLoop, calls=%fused_computation.41 | loop fusion | flops 2816 | bytes 1536 | tf_op jit(solution)/shard_map/reduce_or | solution.py:306
  7.4 0.7 %select_reduce_fusion.2 = s32[64,4]{0,1:T(4,128)S(1)} fusion(s32[64,4]{0,1:T(4,128)} %bitcast.83, s32[64,4]{0,1:T(4,128)} %bitcast.82), kind=kLoop, calls=%fused_computation.35 | loop fusion | flops 2816 | bytes 3072 | tf_op jit(solution)/shard_map/reduce_sum | solution.py:305
  8.5 0.7 %select_n.180.blk_ref = s32[256]{0:T(256)} reshape(s32[64,4]{1,0:T(8,128)S(1)} %copy.32) | data formatting | bytes 2048 | tf_op jit(solution)/shard_map/jit(_where)/select_n | solution.py:307
  9.6 0.9 %concatenate.23.blocks_ref = bf16[65,32,128]{2,1,0:T(8,128)(2,1)} pad(bf16[64,32,128]{2,1,0:T(8,128)(2,1)S(1)} %bitcast.64, bf16[]{:T(256)} %constant.153.clone.1), padding=0_1x0_0x0_0 | pad | bytes 1056770 | tf_op jit(solution)/shard_map/concatenate | solution.py:302
  11.5 1.3 %collective-permute-start.3 = (bf16[2,2,32,640]{3,2,1,0:T(8,128)(2,1)S(1)}, bf16[2,2,32,640]{3,2,1,0:T(8,128)(2,1)S(1)}, u32[]{:S(2)}, u32[]{:S(2)}) collective-permute-start(bf16[2,2,32,640]{3,2,1,0:T(8,128)(2,1)S(1)} %broadcast_select_fusion), channel_id=1, source_target_pairs={{0,2},{1,3},{2,0},{3,1},{4,6},{5,7},{6,4},{7,5},{8,10},{9,11},{10,... | collective-permute-start | bytes 491528 | tf_op jit(solution)/shard_map/ppermute | solution.py:268
  12.9 2.8 %collective-permute-done.3 = bf16[2,2,32,640]{3,2,1,0:T(8,128)(2,1)S(1)} collective-permute-done((bf16[2,2,32,640]{3,2,1,0:T(8,128)(2,1)S(1)}, bf16[2,2,32,640]{3,2,1,0:T(8,128)(2,1)S(1)}, u32[]{:S(2)}, u32[]{:S(2)}) %collective-permute-start.3) | collective-permute-done | bytes 163872 | tf_op jit(solution)/shard_map/ppermute | solution.py:268
  15.8 3.5 %collective-permute-start.4 = (bf16[2,2,2,32,640]{4,3,2,1,0:T(8,128)(2,1)S(1)}, bf16[2,2,2,32,640]{4,3,2,1,0:T(8,128)(2,1)S(1)}, u32[]{:S(2)}, u32[]{:S(2)}) collective-permute-start(bf16[2,2,2,32,640]{4,3,2,1,0:T(8,128)(2,1)S(1)} %maximum_select_fusion.1), channel_id=1, source_target_pairs={{0,1},{1,0},{2,3},{3,2},{4,5},{5,4},{6,7},{7,6},{8,9},{9,8},{10,11... | collective-permute-start | bytes 983048 | tf_op jit(solution)/shard_map/ppermute | solution.py:268
  19.4 1.1 %collective-permute-done.4 = bf16[2,2,2,32,640]{4,3,2,1,0:T(8,128)(2,1)S(1)} collective-permute-done((bf16[2,2,2,32,640]{4,3,2,1,0:T(8,128)(2,1)S(1)}, bf16[2,2,2,32,640]{4,3,2,1,0:T(8,128)(2,1)S(1)}, u32[]{:S(2)}, u32[]{:S(2)}) %collective-permute-start.4) | collective-permute-done | bytes 327712 | tf_op jit(solution)/shard_map/ppermute | solution.py:268
  21.5 3.8 %shard_map.91 = bf16[512,512]{1,0:T(8,128)(2,1)} custom-call(s32[256]{0:T(256)} %select_n.180.blk_ref, bf16[65,32,128]{2,1,0:T(8,128)(2,1)} %concatenate.23.blocks_ref, bf16[512,512]{1,0:T(8,128)(2,1)} %bitcast.72, bf16[16,32,640]{2,1,0:T(8,128)(2,1)} %bitcast.59), custom_call_target="tpu_custom_call" | custom-call | tf_op jit(solution)/shard_map/pallas_call | solution.py:121
  25.3 5.4 %all-to-all-start = ((bf16[16,32,512]{2,1,0:T(8,128)(2,1)}), bf16[16,32,512]{2,1,0:T(8,128)(2,1)S(1)}, u32[]{:S(2)}, u32[]{:S(2)}) async-start(bf16[16,32,512]{2,1,0:T(8,128)(2,1)} %bitcast.66), calls=%async_computation | async-start | bytes 1048576 | tf_op jit(solution)/shard_map/all_to_all | solution.py:322
  30.9 0.7 %select_reduce_fusion.1 = bf16[9,16,144]{2,1,0:T(8,128)(2,1)} fusion(f32[3,9,144]{2,1,0:T(8,128)S(1)} %fusion.4, pred[3,16,144]{2,1,0:T(8,128)(4,1)S(1)} %broadcast_compare_fusion.1), kind=kLoop, calls=%fused_computation.8 | loop fusion | flops 103680 | bytes 63936 | tf_op jit(solution)/shard_map/reduce_sum | solution.py:191
  31.8 1.2 %select_reduce_fusion = bf16[9,16,8,144]{3,2,1,0:T(8,128)(2,1)} fusion(f32[3,9,8,144]{3,2,1,0:T(8,128)S(1)} %fusion.13, pred[3,16,8,144]{3,2,1,0:T(8,128)(4,1)S(1)} %broadcast_compare_fusion), kind=kLoop, calls=%fused_computation.1 | loop fusion | flops 829440 | bytes 511488 | tf_op jit(solution)/shard_map/reduce_sum | solution.py:191
  33.0 11.7 %all-to-all-done = bf16[16,32,512]{2,1,0:T(8,128)(2,1)S(1)} async-done(((bf16[16,32,512]{2,1,0:T(8,128)(2,1)}), bf16[16,32,512]{2,1,0:T(8,128)(2,1)S(1)}, u32[]{:S(2)}, u32[]{:S(2)}) %all-to-all-start) | async-done | bytes 524320 | tf_op jit(solution)/shard_map/all_to_all | solution.py:322
  45.4 2.4 %collective-permute-start.6 = (bf16[528,256]{1,0:T(8,128)(2,1)S(1)}, bf16[528,256]{1,0:T(8,128)(2,1)S(1)}, u32[]{:S(2)}, u32[]{:S(2)}) collective-permute-start(bf16[528,256]{1,0:T(8,128)(2,1)S(1)} %get-tuple-element.29), channel_id=1, source_target_pairs={{1,0},{2,1},{3,2},{4,3},{5,4},{6,5},{7,6},{8,7},{9,8},{10,9},{11,1... | collective-permute-start | bytes 811016 | tf_op jit(solution)/shard_map/ppermute | solution.py:349
  47.8 3.2 %collective-permute-start.5 = (bf16[528,256]{1,0:T(8,128)(2,1)S(1)}, bf16[528,256]{1,0:T(8,128)(2,1)S(1)}, u32[]{:S(2)}, u32[]{:S(2)}) collective-permute-start(bf16[528,256]{1,0:T(8,128)(2,1)S(1)} %get-tuple-element.30), channel_id=1, source_target_pairs={{0,1},{1,2},{2,3},{3,4},{4,5},{5,6},{6,7},{7,8},{8,9},{9,10},{10,1... | collective-permute-start | bytes 811016 | tf_op jit(solution)/shard_map/ppermute | solution.py:348
  51.0 0.7 %add_convert_fusion.ends_ref = s32[2]{0:T(128)} fusion(pred[1]{0:T(512)(128)(4,1)} %bitcast.1, pred[1]{0:T(512)(128)(4,1)} %bitcast), kind=kLoop, calls=%fused_computation.53 | loop fusion | flops 4 | bytes 10 | tf_op jit(solution)/shard_map/convert_element_type | solution.py:344
  51.7 1.5 %collective-permute-done.6.high_ref = bf16[528,256]{1,0:T(8,128)(2,1)S(1)} collective-permute-done((bf16[528,256]{1,0:T(8,128)(2,1)S(1)}, bf16[528,256]{1,0:T(8,128)(2,1)S(1)}, u32[]{:S(2)}, u32[]{:S(2)}) %collective-permute-start.6) | collective-permute-done | bytes 270368 | tf_op jit(solution)/shard_map/ppermute | solution.py:349
  53.2 2.8 %collective-permute-done.5.low_ref = bf16[528,256]{1,0:T(8,128)(2,1)S(1)} collective-permute-done((bf16[528,256]{1,0:T(8,128)(2,1)S(1)}, bf16[528,256]{1,0:T(8,128)(2,1)S(1)}, u32[]{:S(2)}, u32[]{:S(2)}) %collective-permute-start.5) | collective-permute-done | bytes 270368 | tf_op jit(solution)/shard_map/ppermute | solution.py:348
  56.0 0.7 %copy-done.5 = bf16[528,256]{1,0:T(8,128)(2,1)} copy-done((bf16[528,256]{1,0:T(8,128)(2,1)}, bf16[528,256]{1,0:T(8,128)(2,1)S(1)}, u32[]{:S(2)}) %copy-start.5) | copy-done | bytes 270360
  56.7 4.9 %shard_map.92 = f32[4,64,128]{2,1,0:T(8,128)} custom-call(s32[2]{0:T(128)} %add_convert_fusion.ends_ref, bf16[528,256]{1,0:T(8,128)(2,1)} %copy-done.5, bf16[528,512]{1,0:T(8,128)(2,1)} %bitcast.57, bf16[528,256]{1,0:T(8,128)(2,1)} %copy-done.4, bf16[3,3,128,144]{3,2,1,0:T(8,128)(2,1)} %bitcast.63, bf16[3,3,16,144]{3,2,1,0:T(8,128)(2,1)} %bitcast.74), custom_call_target="tpu_custom_call" | custom-call | tf_op jit(solution)/shard_map/pallas_call | solution.py:226
  (56 shorter events, 4.7 us)
Async XLA Ops:
  0.0 31.6 %copy-start = (bf16[3,3,3,8,8]{4,3,2,1,0:T(8,128)(2,1)S(1)}, bf16[3,3,3,8,8]{4,3,2,1,0:T(8,128)(2,1)}, u32[]{:S(2)}) copy-start(bf16[3,3,3,8,8]{4,3,2,1,0:T(8,128)(2,1)} %param.18) | copy-start | bytes 10372
  0.0 9.2 %copy-start.3 = (bf16[1,32,8192]{2,1,0:T(8,128)(2,1)S(1)}, bf16[1,32,8192]{2,1,0:T(8,128)(2,1)}, u32[]{:S(2)}) copy-start(bf16[1,32,8192]{2,1,0:T(8,128)(2,1)} %param.11) | copy-start | bytes 1572868
  1.5 9.0 %collective-permute-start.1 = (bf16[32,640]{1,0:T(8,128)(2,1)S(1)}, bf16[32,640]{1,0:T(8,128)(2,1)S(1)}, u32[]{:S(2)}, u32[]{:S(2)}) collective-permute-start(bf16[32,640]{1,0:T(8,128)(2,1)S(1)} %get-tuple-element.34), channel_id=1, source_target_pairs={{0,8},{1,9},{2,10},{3,11},{4,12},{5,13},{6,14},{7,15},{8,0},{9,1},... | collective-permute-start | bytes 122888 | tf_op jit(solution)/shard_map/ppermute | solution.py:260
  4.6 5.9 %collective-permute-start = (bf16[32,640]{1,0:T(8,128)(2,1)S(1)}, bf16[32,640]{1,0:T(8,128)(2,1)S(1)}, u32[]{:S(2)}, u32[]{:S(2)}) collective-permute-start(bf16[32,640]{1,0:T(8,128)(2,1)S(1)} %get-tuple-element.34), channel_id=1, source_target_pairs={{0,4},{1,5},{2,6},{3,7},{4,0},{5,1},{6,2},{7,3},{8,12},{9,13},{10,... | collective-permute-start | bytes 122888 | tf_op jit(solution)/shard_map/ppermute | solution.py:260
  5.9 4.8 %collective-permute-start.2 = (bf16[32,640]{1,0:T(8,128)(2,1)S(1)}, bf16[32,640]{1,0:T(8,128)(2,1)S(1)}, u32[]{:S(2)}, u32[]{:S(2)}) collective-permute-start(bf16[32,640]{1,0:T(8,128)(2,1)S(1)} %get-tuple-element.34), channel_id=1, source_target_pairs={{0,12},{1,13},{2,14},{3,15},{4,8},{5,9},{6,10},{7,11},{8,4},{9,5},... | collective-permute-start | bytes 122888 | tf_op jit(solution)/shard_map/ppermute | solution.py:260
  11.5 4.2 %collective-permute-start.3 = (bf16[2,2,32,640]{3,2,1,0:T(8,128)(2,1)S(1)}, bf16[2,2,32,640]{3,2,1,0:T(8,128)(2,1)S(1)}, u32[]{:S(2)}, u32[]{:S(2)}) collective-permute-start(bf16[2,2,32,640]{3,2,1,0:T(8,128)(2,1)S(1)} %broadcast_select_fusion), channel_id=1, source_target_pairs={{0,2},{1,3},{2,0},{3,1},{4,6},{5,7},{6,4},{7,5},{8,10},{9,11},{10,... | collective-permute-start | bytes 491528 | tf_op jit(solution)/shard_map/ppermute | solution.py:268
  15.8 4.7 %collective-permute-start.4 = (bf16[2,2,2,32,640]{4,3,2,1,0:T(8,128)(2,1)S(1)}, bf16[2,2,2,32,640]{4,3,2,1,0:T(8,128)(2,1)S(1)}, u32[]{:S(2)}, u32[]{:S(2)}) collective-permute-start(bf16[2,2,2,32,640]{4,3,2,1,0:T(8,128)(2,1)S(1)} %maximum_select_fusion.1), channel_id=1, source_target_pairs={{0,1},{1,0},{2,3},{3,2},{4,5},{5,4},{6,7},{7,6},{8,9},{9,8},{10,11... | collective-permute-start | bytes 983048 | tf_op jit(solution)/shard_map/ppermute | solution.py:268
  20.6 0.8 %copy-start.2 = (bf16[2,2,2,2,32,640]{5,4,3,2,1,0:T(8,128)(2,1)}, bf16[2,2,2,2,32,640]{5,4,3,2,1,0:T(8,128)(2,1)S(1)}, u32[]{:S(2)}) copy-start(bf16[2,2,2,2,32,640]{5,4,3,2,1,0:T(8,128)(2,1)S(1)} %maximum_select_fusion) | copy-start | bytes 1966084
  25.3 5.4 %copy-start.6 = (bf16[3,3,3,8]{3,2,1,0:T(4,128)(2,1)S(1)}, bf16[3,3,3,8]{3,2,1,0:T(4,128)(2,1)}, u32[]{:S(2)}) copy-start(bf16[3,3,3,8]{3,2,1,0:T(4,128)(2,1)} %param.19) | copy-start | bytes 1300
  25.3 19.5 %all-to-all-start = ((bf16[16,32,512]{2,1,0:T(8,128)(2,1)}), bf16[16,32,512]{2,1,0:T(8,128)(2,1)S(1)}, u32[]{:S(2)}, u32[]{:S(2)}) async-start(bf16[16,32,512]{2,1,0:T(8,128)(2,1)} %bitcast.66), calls=%async_computation | async-start | bytes 1048576 | tf_op jit(solution)/shard_map/all_to_all | solution.py:322
  45.4 10.6 %copy-start.1 = (bf16[66,8,512]{2,1,0:T(8,128)(2,1)}, bf16[66,8,512]{2,1,0:T(8,128)(2,1)S(1)}, u32[]{:S(2)}) copy-start(bf16[66,8,512]{2,1,0:T(8,128)(2,1)S(1)} %copy.52) | copy-start | bytes 1622020
  45.4 7.8 %collective-permute-start.6 = (bf16[528,256]{1,0:T(8,128)(2,1)S(1)}, bf16[528,256]{1,0:T(8,128)(2,1)S(1)}, u32[]{:S(2)}, u32[]{:S(2)}) collective-permute-start(bf16[528,256]{1,0:T(8,128)(2,1)S(1)} %get-tuple-element.29), channel_id=1, source_target_pairs={{1,0},{2,1},{3,2},{4,3},{5,4},{6,5},{7,6},{8,7},{9,8},{10,9},{11,1... | collective-permute-start | bytes 811016 | tf_op jit(solution)/shard_map/ppermute | solution.py:349
  47.8 8.1 %collective-permute-start.5 = (bf16[528,256]{1,0:T(8,128)(2,1)S(1)}, bf16[528,256]{1,0:T(8,128)(2,1)S(1)}, u32[]{:S(2)}, u32[]{:S(2)}) collective-permute-start(bf16[528,256]{1,0:T(8,128)(2,1)S(1)} %get-tuple-element.30), channel_id=1, source_target_pairs={{0,1},{1,2},{2,3},{3,4},{4,5},{5,6},{6,7},{7,8},{8,9},{9,10},{10,1... | collective-permute-start | bytes 811016 | tf_op jit(solution)/shard_map/ppermute | solution.py:348
  53.2 2.8 %copy-start.4 = (bf16[528,256]{1,0:T(8,128)(2,1)}, bf16[528,256]{1,0:T(8,128)(2,1)S(1)}, u32[]{:S(2)}) copy-start(bf16[528,256]{1,0:T(8,128)(2,1)S(1)} %collective-permute-done.6.high_ref) | copy-start | bytes 811012
  56.0 0.7 %copy-start.5 = (bf16[528,256]{1,0:T(8,128)(2,1)}, bf16[528,256]{1,0:T(8,128)(2,1)S(1)}, u32[]{:S(2)}) copy-start(bf16[528,256]{1,0:T(8,128)(2,1)S(1)} %collective-permute-done.5.low_ref) | copy-start | bytes 811012

commit v27 on v22

--- a/solution.py
+++ b/solution.py
@@ -314,7 +314,7 @@
     )
     corr_all, kern_one, kern_two = lax.optimization_barrier((corr_all, kern_one, kern_two))
     first = banded(kern_one, DEPTH // 4)
-    second = banded(kern_two, DEPTH // 4)
+    second = banded(kern_two, DEPTH // 8)
     arriving = lax.all_to_all(
         corr_all.reshape(owners, cap * GROUPS, tpix),
         "view",

time: 62 us -> 62.1 us (level)
  no operation moved by 1% of the time
where the time goes in v27:
time: 62.1 us; the launch traced here: 61.6 us
  waiting for transfers between devices  20.3 us (33%)
  starting transfers between devices  20.1 us (32%)
  Pallas kernels  8.77 us (14%)
  other arithmetic  6.96 us (11%)
  local copies, waits for them, and re-layouts  4.42 us (7%)
  matrix products  0.77 us (1%)
    all_to_all x1, waiting for transfers between devices, body(): lax.all_to_all(corr_all.reshape(owners, cap * GROUPS, tpix), 'view', spli...  11.8 us
    all_to_all x1, starting transfers between devices, body(): lax.all_to_all(corr_all.reshape(owners, cap * GROUPS, tpix), 'view', spli...  5.34 us
    pallas_call x1, Pallas kernels, conv_pair(): pl.pallas_call(functools.partial(conv_pair_kernel, rows=rows, cols=cols,...  4.93 us
    ppermute x2, starting transfers between devices, gather_view(): lax.ppermute(gathered, 'view', [(i, i ^ stride) for i in range(count)])  4.8 us
    ppermute x3, starting transfers between devices, gather_view(): lax.ppermute(gathered, 'view', [(i, i ^ m * top) for i in range(count)])  4.44 us
    ppermute x2, waiting for transfers between devices, gather_view(): lax.ppermute(gathered, 'view', [(i, i ^ stride) for i in range(count)])  3.98 us
    pallas_call x1, Pallas kernels, correlate(): pl.pallas_call(correlate_kernel, out_shape=jax.ShapeDtypeStruct((units *...  3.84 us
    ppermute x1, starting transfers between devices, body(): lax.ppermute(volume[:, volume.shape[1] - 2 * columns:], 'view', forward)  3.16 us
  transfers between devices with their start and end apart: 8, of which 6 were waited for; matrix products, arithmetic and copies ran while one was open for 12% of the time, Pallas kernels for 0%

profile of v27, /device:TPU:1, one launch (start us, length us, event | category | flops | bytes accessed | tf_op | source)
XLA Modules:
  0.0 61.6 jit_solution(3107474535176137948)
XLA Ops:
  0.0 0.7 %fusion.18 = bf16[64]{0:T(256)(128)(2,1)S(1)} fusion(s32[1,64]{1,0:T(1,128)} %param.17, s32[1,64]{1,0:T(1,128)} %param.16), kind=kLoop, calls=%fused_computation.66 | loop fusion | flops 192 | bytes 640 | tf_op jit(solution)/shard_map/convert_element_type | solution.py:308
  0.7 0.8 %fusion.20 = (bf16[1,32,640]{2,1,0:T(8,128)(2,1)S(1)}, bf16[32,640]{1,0:T(8,128)(2,1)S(1)}) fusion(bf16[32,128]{1,0:T(8,128)(2,1)S(1)} %pad_bitcast_fusion, bf16[32,512]{1,0:T(8,128)(2,1)} %bitcast.85), kind=kLoop, calls=%fused_computation.72 | loop fusion | flops 81920 | bytes 122880 | tf_op jit(solution)/shard_map/broadcast_in_dim | solution.py:311
  1.5 3.1 %collective-permute-start.1 = (bf16[32,640]{1,0:T(8,128)(2,1)S(1)}, bf16[32,640]{1,0:T(8,128)(2,1)S(1)}, u32[]{:S(2)}, u32[]{:S(2)}) collective-permute-start(bf16[32,640]{1,0:T(8,128)(2,1)S(1)} %get-tuple-element.34), channel_id=1, source_target_pairs={{0,8},{1,9},{2,10},{3,11},{4,12},{5,13},{6,14},{7,15},{8,0},{9,1},... | collective-permute-start | bytes 122888 | tf_op jit(solution)/shard_map/ppermute | solution.py:260
  4.7 1.3 %collective-permute-start = (bf16[32,640]{1,0:T(8,128)(2,1)S(1)}, bf16[32,640]{1,0:T(8,128)(2,1)S(1)}, u32[]{:S(2)}, u32[]{:S(2)}) collective-permute-start(bf16[32,640]{1,0:T(8,128)(2,1)S(1)} %get-tuple-element.34), channel_id=1, source_target_pairs={{0,4},{1,5},{2,6},{3,7},{4,0},{5,1},{6,2},{7,3},{8,12},{9,13},{10,... | collective-permute-start | bytes 122888 | tf_op jit(solution)/shard_map/ppermute | solution.py:260
  6.0 0.7 %iota_compare_fusion.3 = pred[64,4]{0,1:T(4,128)(4,1)S(1)} fusion(s32[64]{0:T(128)} %bitcast.89), kind=kLoop, calls=%fused_computation.52 | loop fusion | flops 256 | bytes 512 | tf_op jit(solution)/shard_map/lt | solution.py:304
  6.7 0.7 %fusion.8 = pred[64,4]{0,1:T(4,128)(4,1)S(1)} fusion(s32[64,4]{0,1:T(4,128)} %bitcast.86, pred[64,4]{0,1:T(4,128)(4,1)S(1)} %iota_compare_fusion.3), kind=kLoop, calls=%fused_computation.37 | loop fusion | flops 2816 | bytes 1536 | tf_op jit(solution)/shard_map/reduce_or | solution.py:306
  7.4 0.7 %select_reduce_fusion.2 = s32[64,4]{0,1:T(4,128)S(1)} fusion(s32[64,4]{0,1:T(4,128)} %bitcast.88, s32[64,4]{0,1:T(4,128)} %bitcast.87), kind=kLoop, calls=%fused_computation.30 | loop fusion | flops 2816 | bytes 3072 | tf_op jit(solution)/shard_map/reduce_sum | solution.py:305
  8.5 0.7 %select_n.194.blk_ref = s32[256]{0:T(256)} reshape(s32[64,4]{1,0:T(8,128)S(1)} %copy.32) | data formatting | bytes 2048 | tf_op jit(solution)/shard_map/jit(_where)/select_n | solution.py:307
  9.7 0.8 %concatenate.23.blocks_ref = bf16[65,32,128]{2,1,0:T(8,128)(2,1)} pad(bf16[64,32,128]{2,1,0:T(8,128)(2,1)S(1)} %bitcast.69, bf16[]{:T(256)} %constant.168.clone.1), padding=0_1x0_0x0_0 | pad | bytes 1056770 | tf_op jit(solution)/shard_map/concatenate | solution.py:302
  11.5 1.3 %collective-permute-start.3 = (bf16[2,2,32,640]{3,2,1,0:T(8,128)(2,1)S(1)}, bf16[2,2,32,640]{3,2,1,0:T(8,128)(2,1)S(1)}, u32[]{:S(2)}, u32[]{:S(2)}) collective-permute-start(bf16[2,2,32,640]{3,2,1,0:T(8,128)(2,1)S(1)} %broadcast_select_fusion), channel_id=1, source_target_pairs={{0,2},{1,3},{2,0},{3,1},{4,6},{5,7},{6,4},{7,5},{8,10},{9,11},{10,... | collective-permute-start | bytes 491528 | tf_op jit(solution)/shard_map/ppermute | solution.py:268
  12.9 2.8 %collective-permute-done.3 = bf16[2,2,32,640]{3,2,1,0:T(8,128)(2,1)S(1)} collective-permute-done((bf16[2,2,32,640]{3,2,1,0:T(8,128)(2,1)S(1)}, bf16[2,2,32,640]{3,2,1,0:T(8,128)(2,1)S(1)}, u32[]{:S(2)}, u32[]{:S(2)}) %collective-permute-start.3) | collective-permute-done | bytes 163872 | tf_op jit(solution)/shard_map/ppermute | solution.py:268
  15.8 3.5 %collective-permute-start.4 = (bf16[2,2,2,32,640]{4,3,2,1,0:T(8,128)(2,1)S(1)}, bf16[2,2,2,32,640]{4,3,2,1,0:T(8,128)(2,1)S(1)}, u32[]{:S(2)}, u32[]{:S(2)}) collective-permute-start(bf16[2,2,2,32,640]{4,3,2,1,0:T(8,128)(2,1)S(1)} %maximum_select_fusion.1), channel_id=1, source_target_pairs={{0,1},{1,0},{2,3},{3,2},{4,5},{5,4},{6,7},{7,6},{8,9},{9,8},{10,11... | collective-permute-start | bytes 983048 | tf_op jit(solution)/shard_map/ppermute | solution.py:268
  19.4 1.1 %collective-permute-done.4 = bf16[2,2,2,32,640]{4,3,2,1,0:T(8,128)(2,1)S(1)} collective-permute-done((bf16[2,2,2,32,640]{4,3,2,1,0:T(8,128)(2,1)S(1)}, bf16[2,2,2,32,640]{4,3,2,1,0:T(8,128)(2,1)S(1)}, u32[]{:S(2)}, u32[]{:S(2)}) %collective-permute-start.4) | collective-permute-done | bytes 327712 | tf_op jit(solution)/shard_map/ppermute | solution.py:268
  21.5 3.8 %shard_map.91 = bf16[512,512]{1,0:T(8,128)(2,1)} custom-call(s32[256]{0:T(256)} %select_n.194.blk_ref, bf16[65,32,128]{2,1,0:T(8,128)(2,1)} %concatenate.23.blocks_ref, bf16[512,512]{1,0:T(8,128)(2,1)} %bitcast.77, bf16[16,32,640]{2,1,0:T(8,128)(2,1)} %bitcast.64), custom_call_target="tpu_custom_call" | custom-call | tf_op jit(solution)/shard_map/pallas_call | solution.py:121
  25.3 5.3 %all-to-all-start = ((bf16[16,32,512]{2,1,0:T(8,128)(2,1)}), bf16[16,32,512]{2,1,0:T(8,128)(2,1)S(1)}, u32[]{:S(2)}, u32[]{:S(2)}) async-start(bf16[16,32,512]{2,1,0:T(8,128)(2,1)} %bitcast.71), calls=%async_computation | async-start | bytes 1048576 | tf_op jit(solution)/shard_map/all_to_all | solution.py:318
  30.9 0.6 %select_reduce_fusion.1 = bf16[9,8,80]{2,1,0:T(8,128)(2,1)} fusion(f32[3,9,80]{2,1,0:T(8,128)S(1)} %fusion.2, pred[3,8,80]{2,1,0:T(8,128)(4,1)S(1)} %broadcast_compare_fusion.1), kind=kLoop, calls=%fused_computation.17 | loop fusion | flops 28800 | bytes 22080 | tf_op jit(solution)/shard_map/reduce_sum | solution.py:191
  31.8 1.2 %select_reduce_fusion = bf16[9,16,8,144]{3,2,1,0:T(8,128)(2,1)} fusion(f32[3,9,8,144]{3,2,1,0:T(8,128)S(1)} %fusion.10, pred[3,16,8,144]{3,2,1,0:T(8,128)(4,1)S(1)} %broadcast_compare_fusion), kind=kLoop, calls=%fused_computation.1 | loop fusion | flops 829440 | bytes 511488 | tf_op jit(solution)/shard_map/reduce_sum | solution.py:191
  33.0 11.8 %all-to-all-done = bf16[16,32,512]{2,1,0:T(8,128)(2,1)S(1)} async-done(((bf16[16,32,512]{2,1,0:T(8,128)(2,1)}), bf16[16,32,512]{2,1,0:T(8,128)(2,1)S(1)}, u32[]{:S(2)}, u32[]{:S(2)}) %all-to-all-start) | async-done | bytes 524320 | tf_op jit(solution)/shard_map/all_to_all | solution.py:318
  45.4 2.4 %collective-permute-start.6 = (bf16[528,256]{1,0:T(8,128)(2,1)S(1)}, bf16[528,256]{1,0:T(8,128)(2,1)S(1)}, u32[]{:S(2)}, u32[]{:S(2)}) collective-permute-start(bf16[528,256]{1,0:T(8,128)(2,1)S(1)} %get-tuple-element.29), channel_id=1, source_target_pairs={{1,0},{2,1},{3,2},{4,3},{5,4},{6,5},{7,6},{8,7},{9,8},{10,9},{11,1... | collective-permute-start | bytes 811016 | tf_op jit(solution)/shard_map/ppermute | solution.py:345
  47.8 3.2 %collective-permute-start.5 = (bf16[528,256]{1,0:T(8,128)(2,1)S(1)}, bf16[528,256]{1,0:T(8,128)(2,1)S(1)}, u32[]{:S(2)}, u32[]{:S(2)}) collective-permute-start(bf16[528,256]{1,0:T(8,128)(2,1)S(1)} %get-tuple-element.30), channel_id=1, source_target_pairs={{0,1},{1,2},{2,3},{3,4},{4,5},{5,6},{6,7},{7,8},{8,9},{9,10},{10,1... | collective-permute-start | bytes 811016 | tf_op jit(solution)/shard_map/ppermute | solution.py:344
  51.6 1.6 %collective-permute-done.6.high_ref = bf16[528,256]{1,0:T(8,128)(2,1)S(1)} collective-permute-done((bf16[528,256]{1,0:T(8,128)(2,1)S(1)}, bf16[528,256]{1,0:T(8,128)(2,1)S(1)}, u32[]{:S(2)}, u32[]{:S(2)}) %collective-permute-start.6) | collective-permute-done | bytes 270368 | tf_op jit(solution)/shard_map/ppermute | solution.py:345
  53.2 2.8 %collective-permute-done.5.low_ref = bf16[528,256]{1,0:T(8,128)(2,1)S(1)} collective-permute-done((bf16[528,256]{1,0:T(8,128)(2,1)S(1)}, bf16[528,256]{1,0:T(8,128)(2,1)S(1)}, u32[]{:S(2)}, u32[]{:S(2)}) %collective-permute-start.5) | collective-permute-done | bytes 270368 | tf_op jit(solution)/shard_map/ppermute | solution.py:344
  56.0 0.7 %copy-done.5 = bf16[528,256]{1,0:T(8,128)(2,1)} copy-done((bf16[528,256]{1,0:T(8,128)(2,1)}, bf16[528,256]{1,0:T(8,128)(2,1)S(1)}, u32[]{:S(2)}) %copy-start.5) | copy-done | bytes 270360
  56.7 4.9 %shard_map.92 = f32[4,64,128]{2,1,0:T(8,128)} custom-call(s32[2]{0:T(128)} %add_convert_fusion.ends_ref, bf16[528,256]{1,0:T(8,128)(2,1)} %copy-done.5, bf16[528,512]{1,0:T(8,128)(2,1)} %bitcast.62, bf16[528,256]{1,0:T(8,128)(2,1)} %copy-done.4, bf16[3,3,128,144]{3,2,1,0:T(8,128)(2,1)} %bitcast.68, bf16[3,3,8,80]{3,2,1,0:T(8,128)(2,1)} %bitcast.80), custom_call_target="tpu_custom_call" | custom-call | tf_op jit(solution)/shard_map/pallas_call | solution.py:226
  (58 shorter events, 4.7 us)
Async XLA Ops:
  0.0 31.5 %copy-start = (bf16[3,3,3,8,8]{4,3,2,1,0:T(8,128)(2,1)S(1)}, bf16[3,3,3,8,8]{4,3,2,1,0:T(8,128)(2,1)}, u32[]{:S(2)}) copy-start(bf16[3,3,3,8,8]{4,3,2,1,0:T(8,128)(2,1)} %param.18) | copy-start | bytes 10372
  0.0 9.2 %copy-start.3 = (bf16[1,32,8192]{2,1,0:T(8,128)(2,1)S(1)}, bf16[1,32,8192]{2,1,0:T(8,128)(2,1)}, u32[]{:S(2)}) copy-start(bf16[1,32,8192]{2,1,0:T(8,128)(2,1)} %param.11) | copy-start | bytes 1572868
  1.5 9.0 %collective-permute-start.1 = (bf16[32,640]{1,0:T(8,128)(2,1)S(1)}, bf16[32,640]{1,0:T(8,128)(2,1)S(1)}, u32[]{:S(2)}, u32[]{:S(2)}) collective-permute-start(bf16[32,640]{1,0:T(8,128)(2,1)S(1)} %get-tuple-element.34), channel_id=1, source_target_pairs={{0,8},{1,9},{2,10},{3,11},{4,12},{5,13},{6,14},{7,15},{8,0},{9,1},... | collective-permute-start | bytes 122888 | tf_op jit(solution)/shard_map/ppermute | solution.py:260
  4.7 5.9 %collective-permute-start = (bf16[32,640]{1,0:T(8,128)(2,1)S(1)}, bf16[32,640]{1,0:T(8,128)(2,1)S(1)}, u32[]{:S(2)}, u32[]{:S(2)}) collective-permute-start(bf16[32,640]{1,0:T(8,128)(2,1)S(1)} %get-tuple-element.34), channel_id=1, source_target_pairs={{0,4},{1,5},{2,6},{3,7},{4,0},{5,1},{6,2},{7,3},{8,12},{9,13},{10,... | collective-permute-start | bytes 122888 | tf_op jit(solution)/shard_map/ppermute | solution.py:260
  5.9 4.8 %collective-permute-start.2 = (bf16[32,640]{1,0:T(8,128)(2,1)S(1)}, bf16[32,640]{1,0:T(8,128)(2,1)S(1)}, u32[]{:S(2)}, u32[]{:S(2)}) collective-permute-start(bf16[32,640]{1,0:T(8,128)(2,1)S(1)} %get-tuple-element.34), channel_id=1, source_target_pairs={{0,12},{1,13},{2,14},{3,15},{4,8},{5,9},{6,10},{7,11},{8,4},{9,5},... | collective-permute-start | bytes 122888 | tf_op jit(solution)/shard_map/ppermute | solution.py:260
  11.5 4.2 %collective-permute-start.3 = (bf16[2,2,32,640]{3,2,1,0:T(8,128)(2,1)S(1)}, bf16[2,2,32,640]{3,2,1,0:T(8,128)(2,1)S(1)}, u32[]{:S(2)}, u32[]{:S(2)}) collective-permute-start(bf16[2,2,32,640]{3,2,1,0:T(8,128)(2,1)S(1)} %broadcast_select_fusion), channel_id=1, source_target_pairs={{0,2},{1,3},{2,0},{3,1},{4,6},{5,7},{6,4},{7,5},{8,10},{9,11},{10,... | collective-permute-start | bytes 491528 | tf_op jit(solution)/shard_map/ppermute | solution.py:268
  15.8 4.7 %collective-permute-start.4 = (bf16[2,2,2,32,640]{4,3,2,1,0:T(8,128)(2,1)S(1)}, bf16[2,2,2,32,640]{4,3,2,1,0:T(8,128)(2,1)S(1)}, u32[]{:S(2)}, u32[]{:S(2)}) collective-permute-start(bf16[2,2,2,32,640]{4,3,2,1,0:T(8,128)(2,1)S(1)} %maximum_select_fusion.1), channel_id=1, source_target_pairs={{0,1},{1,0},{2,3},{3,2},{4,5},{5,4},{6,7},{7,6},{8,9},{9,8},{10,11... | collective-permute-start | bytes 983048 | tf_op jit(solution)/shard_map/ppermute | solution.py:268
  20.6 0.8 %copy-start.2 = (bf16[2,2,2,2,32,640]{5,4,3,2,1,0:T(8,128)(2,1)}, bf16[2,2,2,2,32,640]{5,4,3,2,1,0:T(8,128)(2,1)S(1)}, u32[]{:S(2)}) copy-start(bf16[2,2,2,2,32,640]{5,4,3,2,1,0:T(8,128)(2,1)S(1)} %maximum_select_fusion) | copy-start | bytes 1966084
  25.3 5.3 %copy-start.6 = (bf16[3,3,3,8]{3,2,1,0:T(4,128)(2,1)S(1)}, bf16[3,3,3,8]{3,2,1,0:T(4,128)(2,1)}, u32[]{:S(2)}) copy-start(bf16[3,3,3,8]{3,2,1,0:T(4,128)(2,1)} %param.19) | copy-start | bytes 1300
  25.3 19.4 %all-to-all-start = ((bf16[16,32,512]{2,1,0:T(8,128)(2,1)}), bf16[16,32,512]{2,1,0:T(8,128)(2,1)S(1)}, u32[]{:S(2)}, u32[]{:S(2)}) async-start(bf16[16,32,512]{2,1,0:T(8,128)(2,1)} %bitcast.71), calls=%async_computation | async-start | bytes 1048576 | tf_op jit(solution)/shard_map/all_to_all | solution.py:318
  45.4 10.6 %copy-start.1 = (bf16[66,8,512]{2,1,0:T(8,128)(2,1)}, bf16[66,8,512]{2,1,0:T(8,128)(2,1)S(1)}, u32[]{:S(2)}) copy-start(bf16[66,8,512]{2,1,0:T(8,128)(2,1)S(1)} %copy.52) | copy-start | bytes 1622020
  45.4 7.8 %collective-permute-start.6 = (bf16[528,256]{1,0:T(8,128)(2,1)S(1)}, bf16[528,256]{1,0:T(8,128)(2,1)S(1)}, u32[]{:S(2)}, u32[]{:S(2)}) collective-permute-start(bf16[528,256]{1,0:T(8,128)(2,1)S(1)} %get-tuple-element.29), channel_id=1, source_target_pairs={{1,0},{2,1},{3,2},{4,3},{5,4},{6,5},{7,6},{8,7},{9,8},{10,9},{11,1... | collective-permute-start | bytes 811016 | tf_op jit(solution)/shard_map/ppermute | solution.py:345
  47.8 8.1 %collective-permute-start.5 = (bf16[528,256]{1,0:T(8,128)(2,1)S(1)}, bf16[528,256]{1,0:T(8,128)(2,1)S(1)}, u32[]{:S(2)}, u32[]{:S(2)}) collective-permute-start(bf16[528,256]{1,0:T(8,128)(2,1)S(1)} %get-tuple-element.30), channel_id=1, source_target_pairs={{0,1},{1,2},{2,3},{3,4},{4,5},{5,6},{6,7},{7,8},{8,9},{9,10},{10,1... | collective-permute-start | bytes 811016 | tf_op jit(solution)/shard_map/ppermute | solution.py:344
  53.2 2.8 %copy-start.4 = (bf16[528,256]{1,0:T(8,128)(2,1)}, bf16[528,256]{1,0:T(8,128)(2,1)S(1)}, u32[]{:S(2)}) copy-start(bf16[528,256]{1,0:T(8,128)(2,1)S(1)} %collective-permute-done.6.high_ref) | copy-start | bytes 811012
  56.0 0.7 %copy-start.5 = (bf16[528,256]{1,0:T(8,128)(2,1)}, bf16[528,256]{1,0:T(8,128)(2,1)S(1)}, u32[]{:S(2)}) copy-start(bf16[528,256]{1,0:T(8,128)(2,1)S(1)} %collective-permute-done.5.low_ref) | copy-start | bytes 811012

commit v28 on v21

--- a/solution.py
+++ b/solution.py
@@ -74,7 +74,7 @@
 
 
 def correlate_kernel(blk_ref, bit_ref, blocks_ref, table_ref, ref_ref, partner_ref, out_ref, arranged, products, *, pairs):
-    chunk = 16
+    chunk = 32
     slots = table_ref.shape[0] // blocks_ref.shape[2]
     width = blocks_ref.shape[2]
     channels = blocks_ref.shape[1]
@@ -117,13 +117,13 @@
             ).astype(out_ref.dtype)
         return carry
 
-    lax.fori_loop(0, units // chunk, step, 0, unroll=2)
+    lax.fori_loop(0, units // chunk, step, 0, unroll=True)
 
 
 def correlate(blk, blocks, table, mine, partner, bit, units):
     channels = blocks.shape[1]
     tpix = table.shape[1]
-    chunk = 16
+    chunk = 32
     pairs = bit is not None
     bits = jnp.reshape(bit if pairs else 0, (1,)).astype(jnp.int32)
     return pl.pallas_call(
@@ -321,7 +321,11 @@
     blk = jnp.where(alive, picked, nblocks).reshape(-1).astype(jnp.int32)
     depth_code = jnp.where(counts > 0, depth_plane[0], -1).astype(jnp.bfloat16)
 
-    tag_block = jnp.pad(depth_code, (0, channels * 128 - units)).reshape(channels, 128)
+    if units <= 128:
+        code_row = jnp.where(block_count > 0, depth_plane, -1).astype(jnp.bfloat16)
+        tag_block = jnp.pad(code_row, ((0, channels - 1), (0, 128 - units)))
+    else:
+        tag_block = jnp.pad(depth_code, (0, channels * 128 - units)).reshape(channels, 128)
     mine, partner, bit = gather_view(
         jnp.concatenate([ref_feat[0], tag_block], axis=1)[None], split=True
     )

time: 62 us -> 61.7 us (level)
  no operation moved by 1% of the time
where the time goes in v28:
time: 61.7 us; the launch traced here: 61.2 us
  waiting for transfers between devices  20.3 us (33%)
  starting transfers between devices  20.1 us (33%)
  Pallas kernels  8.72 us (14%)
  other arithmetic  6.79 us (11%)
  local copies, waits for them, and re-layouts  4.28 us (7%)
  matrix products  0.78 us (1%)
    all_to_all x1, waiting for transfers between devices, body(): lax.all_to_all(corr_all.reshape(owners, cap * GROUPS, tpix), 'view', spli...  11.7 us
    all_to_all x1, starting transfers between devices, body(): lax.all_to_all(corr_all.reshape(owners, cap * GROUPS, tpix), 'view', spli...  5.32 us
    pallas_call x1, Pallas kernels, conv_pair(): pl.pallas_call(functools.partial(conv_pair_kernel, rows=rows, cols=cols,...  4.88 us
    ppermute x2, starting transfers between devices, gather_view(): lax.ppermute(gathered, 'view', [(i, i ^ stride) for i in range(count)])  4.8 us
    ppermute x3, starting transfers between devices, gather_view(): lax.ppermute(gathered, 'view', [(i, i ^ m * top) for i in range(count)])  4.44 us
    ppermute x2, waiting for transfers between devices, gather_view(): lax.ppermute(gathered, 'view', [(i, i ^ stride) for i in range(count)])  4.07 us
    pallas_call x1, Pallas kernels, correlate(): pl.pallas_call(functools.partial(correlate_kernel, pairs=pairs), out_shap...  3.84 us
    ppermute x1, starting transfers between devices, body(): lax.ppermute(volume[:, volume.shape[1] - 2 * columns:], 'view', forward)  3.16 us
  transfers between devices with their start and end apart: 8, of which 6 were waited for; matrix products, arithmetic and copies ran while one was open for 12% of the time, Pallas kernels for 0%

profile of v28, /device:TPU:1, one launch (start us, length us, event | category | flops | bytes accessed | tf_op | source)
XLA Modules:
  0.0 61.2 jit_solution(8128309501221221573)
XLA Ops:
  0.0 0.7 %fusion.20 = bf16[1,64]{1,0:T(2,128)(2,1)S(1)} fusion(s32[1,64]{1,0:T(1,128)} %param.17, s32[1,64]{1,0:T(1,128)} %param.16), kind=kLoop, calls=%fused_computation.60 | loop fusion | flops 192 | bytes 640 | tf_op jit(solution)/shard_map/convert_element_type | solution.py:325
  0.7 0.8 %fusion.22 = (bf16[1,32,640]{2,1,0:T(8,128)(2,1)S(1)}, bf16[32,640]{1,0:T(8,128)(2,1)S(1)}) fusion(bf16[1,64]{1,0:T(2,128)(2,1)S(1)} %fusion.20, bf16[32,512]{1,0:T(8,128)(2,1)} %bitcast.82), kind=kLoop, calls=%fused_computation.66 | loop fusion | flops 122880 | bytes 114816 | tf_op jit(solution)/shard_map/broadcast_in_dim | solution.py:330
  1.5 3.1 %collective-permute-start.1 = (bf16[32,640]{1,0:T(8,128)(2,1)S(1)}, bf16[32,640]{1,0:T(8,128)(2,1)S(1)}, u32[]{:S(2)}, u32[]{:S(2)}) collective-permute-start(bf16[32,640]{1,0:T(8,128)(2,1)S(1)} %get-tuple-element.32), channel_id=1, source_target_pairs={{0,8},{1,9},{2,10},{3,11},{4,12},{5,13},{6,14},{7,15},{8,0},{9,1},... | collective-permute-start | bytes 122888 | tf_op jit(solution)/shard_map/ppermute | solution.py:271
  4.6 1.3 %collective-permute-start = (bf16[32,640]{1,0:T(8,128)(2,1)S(1)}, bf16[32,640]{1,0:T(8,128)(2,1)S(1)}, u32[]{:S(2)}, u32[]{:S(2)}) collective-permute-start(bf16[32,640]{1,0:T(8,128)(2,1)S(1)} %get-tuple-element.32), channel_id=1, source_target_pairs={{0,4},{1,5},{2,6},{3,7},{4,0},{5,1},{6,2},{7,3},{8,12},{9,13},{10,... | collective-permute-start | bytes 122888 | tf_op jit(solution)/shard_map/ppermute | solution.py:271
  6.0 0.7 %iota_compare_fusion.3 = pred[64,4]{0,1:T(4,128)(4,1)S(1)} fusion(s32[64]{0:T(128)} %bitcast.86), kind=kLoop, calls=%fused_computation.51 | loop fusion | flops 256 | bytes 512 | tf_op jit(solution)/shard_map/lt | solution.py:318
  6.7 0.7 %fusion.12 = pred[64,4]{0,1:T(4,128)(4,1)S(1)} fusion(s32[64,4]{0,1:T(4,128)} %bitcast.83, pred[64,4]{0,1:T(4,128)(4,1)S(1)} %iota_compare_fusion.3), kind=kLoop, calls=%fused_computation.40 | loop fusion | flops 2816 | bytes 1536 | tf_op jit(solution)/shard_map/reduce_or | solution.py:320
  7.4 0.7 %select_reduce_fusion.2 = s32[64,4]{0,1:T(4,128)S(1)} fusion(s32[64,4]{0,1:T(4,128)} %bitcast.85, s32[64,4]{0,1:T(4,128)} %bitcast.84), kind=kLoop, calls=%fused_computation.34 | loop fusion | flops 2816 | bytes 3072 | tf_op jit(solution)/shard_map/reduce_sum | solution.py:319
  8.5 0.7 %select_n.162.blk_ref = s32[256]{0:T(256)} reshape(s32[64,4]{1,0:T(8,128)S(1)} %copy.28) | data formatting | bytes 2048 | tf_op jit(solution)/shard_map/jit(_where)/select_n | solution.py:321
  9.6 0.8 %concatenate.9.blocks_ref = bf16[65,32,128]{2,1,0:T(8,128)(2,1)} pad(bf16[64,32,128]{2,1,0:T(8,128)(2,1)S(1)} %bitcast.63, bf16[]{:T(256)} %constant.144.clone.1), padding=0_1x0_0x0_0 | pad | bytes 1056770 | tf_op jit(solution)/shard_map/concatenate | solution.py:316
  11.4 1.3 %collective-permute-start.3 = (bf16[2,2,32,640]{3,2,1,0:T(8,128)(2,1)S(1)}, bf16[2,2,32,640]{3,2,1,0:T(8,128)(2,1)S(1)}, u32[]{:S(2)}, u32[]{:S(2)}) collective-permute-start(bf16[2,2,32,640]{3,2,1,0:T(8,128)(2,1)S(1)} %broadcast_select_fusion), channel_id=1, source_target_pairs={{0,2},{1,3},{2,0},{3,1},{4,6},{5,7},{6,4},{7,5},{8,10},{9,11},{10,... | collective-permute-start | bytes 491528 | tf_op jit(solution)/shard_map/ppermute | solution.py:279
  12.8 2.8 %collective-permute-done.3 = bf16[2,2,32,640]{3,2,1,0:T(8,128)(2,1)S(1)} collective-permute-done((bf16[2,2,32,640]{3,2,1,0:T(8,128)(2,1)S(1)}, bf16[2,2,32,640]{3,2,1,0:T(8,128)(2,1)S(1)}, u32[]{:S(2)}, u32[]{:S(2)}) %collective-permute-start.3) | collective-permute-done | bytes 163872 | tf_op jit(solution)/shard_map/ppermute | solution.py:279
  15.7 3.5 %collective-permute-start.4 = (bf16[2,2,2,32,640]{4,3,2,1,0:T(8,128)(2,1)S(1)}, bf16[2,2,2,32,640]{4,3,2,1,0:T(8,128)(2,1)S(1)}, u32[]{:S(2)}, u32[]{:S(2)}) collective-permute-start(bf16[2,2,2,32,640]{4,3,2,1,0:T(8,128)(2,1)S(1)} %maximum_select_fusion), channel_id=1, source_target_pairs={{0,1},{1,0},{2,3},{3,2},{4,5},{5,4},{6,7},{7,6},{8,9},{9,8},{10,11... | collective-permute-start | bytes 983048 | tf_op jit(solution)/shard_map/ppermute | solution.py:279
  19.2 1.2 %collective-permute-done.4 = bf16[2,2,2,32,640]{4,3,2,1,0:T(8,128)(2,1)S(1)} collective-permute-done((bf16[2,2,2,32,640]{4,3,2,1,0:T(8,128)(2,1)S(1)}, bf16[2,2,2,32,640]{4,3,2,1,0:T(8,128)(2,1)S(1)}, u32[]{:S(2)}, u32[]{:S(2)}) %collective-permute-start.4) | collective-permute-done | bytes 327712 | tf_op jit(solution)/shard_map/ppermute | solution.py:279
  21.2 3.8 %shard_map.91 = bf16[512,512]{1,0:T(8,128)(2,1)} custom-call(s32[256]{0:T(256)} %select_n.162.blk_ref, s32[1]{0:T(128)} %bitcast.20.bit_ref, bf16[65,32,128]{2,1,0:T(8,128)(2,1)} %concatenate.9.blocks_ref, bf16[512,512]{1,0:T(8,128)(2,1)} %bitcast.69, bf16[8,32,640]{2,1,0:T(8,128)(2,1)} %bitcast.66, bf16[8,32,640]{2,1,0:T(8,128)(2,1)} %bitcast.74), custom_call_target="tpu_custom_call" | custom-call | tf_op jit(solution)/shard_map/pallas_call | solution.py:129
  25.0 5.3 %all-to-all-start = ((bf16[16,32,512]{2,1,0:T(8,128)(2,1)}), bf16[16,32,512]{2,1,0:T(8,128)(2,1)S(1)}, u32[]{:S(2)}, u32[]{:S(2)}) async-start(bf16[16,32,512]{2,1,0:T(8,128)(2,1)} %bitcast.62), calls=%async_computation | async-start | bytes 1048576 | tf_op jit(solution)/shard_map/all_to_all | solution.py:338
  30.6 0.7 %select_reduce_fusion.1 = bf16[9,16,144]{2,1,0:T(8,128)(2,1)} fusion(f32[3,9,144]{2,1,0:T(8,128)S(1)} %fusion.4, pred[3,16,144]{2,1,0:T(8,128)(4,1)S(1)} %broadcast_compare_fusion.1), kind=kLoop, calls=%fused_computation.7 | loop fusion | flops 103680 | bytes 63936 | tf_op jit(solution)/shard_map/reduce_sum | solution.py:201
  31.5 1.2 %select_reduce_fusion = bf16[9,16,8,144]{3,2,1,0:T(8,128)(2,1)} fusion(f32[3,9,8,144]{3,2,1,0:T(8,128)S(1)} %fusion.13, pred[3,16,8,144]{3,2,1,0:T(8,128)(4,1)S(1)} %broadcast_compare_fusion), kind=kLoop, calls=%fused_computation.1 | loop fusion | flops 829440 | bytes 511488 | tf_op jit(solution)/shard_map/reduce_sum | solution.py:201
  32.7 11.7 %all-to-all-done = bf16[16,32,512]{2,1,0:T(8,128)(2,1)S(1)} async-done(((bf16[16,32,512]{2,1,0:T(8,128)(2,1)}), bf16[16,32,512]{2,1,0:T(8,128)(2,1)S(1)}, u32[]{:S(2)}, u32[]{:S(2)}) %all-to-all-start) | async-done | bytes 524320 | tf_op jit(solution)/shard_map/all_to_all | solution.py:338
  45.1 2.4 %collective-permute-start.6 = (bf16[528,256]{1,0:T(8,128)(2,1)S(1)}, bf16[528,256]{1,0:T(8,128)(2,1)S(1)}, u32[]{:S(2)}, u32[]{:S(2)}) collective-permute-start(bf16[528,256]{1,0:T(8,128)(2,1)S(1)} %get-tuple-element.29), channel_id=1, source_target_pairs={{1,0},{2,1},{3,2},{4,3},{5,4},{6,5},{7,6},{8,7},{9,8},{10,9},{11,1... | collective-permute-start | bytes 811016 | tf_op jit(solution)/shard_map/ppermute | solution.py:372
  47.5 3.2 %collective-permute-start.5 = (bf16[528,256]{1,0:T(8,128)(2,1)S(1)}, bf16[528,256]{1,0:T(8,128)(2,1)S(1)}, u32[]{:S(2)}, u32[]{:S(2)}) collective-permute-start(bf16[528,256]{1,0:T(8,128)(2,1)S(1)} %get-tuple-element.30), channel_id=1, source_target_pairs={{0,1},{1,2},{2,3},{3,4},{4,5},{5,6},{6,7},{7,8},{8,9},{9,10},{10,1... | collective-permute-start | bytes 811016 | tf_op jit(solution)/shard_map/ppermute | solution.py:371
  51.3 1.5 %collective-permute-done.6.high_ref = bf16[528,256]{1,0:T(8,128)(2,1)S(1)} collective-permute-done((bf16[528,256]{1,0:T(8,128)(2,1)S(1)}, bf16[528,256]{1,0:T(8,128)(2,1)S(1)}, u32[]{:S(2)}, u32[]{:S(2)}) %collective-permute-start.6) | collective-permute-done | bytes 270368 | tf_op jit(solution)/shard_map/ppermute | solution.py:372
  52.9 2.8 %collective-permute-done.5.low_ref = bf16[528,256]{1,0:T(8,128)(2,1)S(1)} collective-permute-done((bf16[528,256]{1,0:T(8,128)(2,1)S(1)}, bf16[528,256]{1,0:T(8,128)(2,1)S(1)}, u32[]{:S(2)}, u32[]{:S(2)}) %collective-permute-start.5) | collective-permute-done | bytes 270368 | tf_op jit(solution)/shard_map/ppermute | solution.py:371
  55.6 0.7 %copy-done.6 = bf16[528,256]{1,0:T(8,128)(2,1)} copy-done((bf16[528,256]{1,0:T(8,128)(2,1)}, bf16[528,256]{1,0:T(8,128)(2,1)S(1)}, u32[]{:S(2)}) %copy-start.6) | copy-done | bytes 270360
  56.3 4.9 %shard_map.92 = f32[4,64,128]{2,1,0:T(8,128)} custom-call(s32[2]{0:T(128)} %add_convert_fusion.ends_ref, bf16[528,256]{1,0:T(8,128)(2,1)} %copy-done.6, bf16[528,512]{1,0:T(8,128)(2,1)} %bitcast.60, bf16[528,256]{1,0:T(8,128)(2,1)} %copy-done.5, bf16[3,3,128,144]{3,2,1,0:T(8,128)(2,1)} %bitcast.61, bf16[3,3,16,144]{3,2,1,0:T(8,128)(2,1)} %bitcast.75), custom_call_target="tpu_custom_call" | custom-call | tf_op jit(solution)/shard_map/pallas_call | solution.py:236
  (57 shorter events, 4.4 us)
Async XLA Ops:
  0.0 31.3 %copy-start = (bf16[3,3,3,8,8]{4,3,2,1,0:T(8,128)(2,1)S(1)}, bf16[3,3,3,8,8]{4,3,2,1,0:T(8,128)(2,1)}, u32[]{:S(2)}) copy-start(bf16[3,3,3,8,8]{4,3,2,1,0:T(8,128)(2,1)} %param.18) | copy-start | bytes 10372
  0.0 9.2 %copy-start.3 = (bf16[1,32,8192]{2,1,0:T(8,128)(2,1)S(1)}, bf16[1,32,8192]{2,1,0:T(8,128)(2,1)}, u32[]{:S(2)}) copy-start(bf16[1,32,8192]{2,1,0:T(8,128)(2,1)} %param.11) | copy-start | bytes 1572868
  1.5 9.0 %collective-permute-start.1 = (bf16[32,640]{1,0:T(8,128)(2,1)S(1)}, bf16[32,640]{1,0:T(8,128)(2,1)S(1)}, u32[]{:S(2)}, u32[]{:S(2)}) collective-permute-start(bf16[32,640]{1,0:T(8,128)(2,1)S(1)} %get-tuple-element.32), channel_id=1, source_target_pairs={{0,8},{1,9},{2,10},{3,11},{4,12},{5,13},{6,14},{7,15},{8,0},{9,1},... | collective-permute-start | bytes 122888 | tf_op jit(solution)/shard_map/ppermute | solution.py:271
  4.6 5.8 %collective-permute-start = (bf16[32,640]{1,0:T(8,128)(2,1)S(1)}, bf16[32,640]{1,0:T(8,128)(2,1)S(1)}, u32[]{:S(2)}, u32[]{:S(2)}) collective-permute-start(bf16[32,640]{1,0:T(8,128)(2,1)S(1)} %get-tuple-element.32), channel_id=1, source_target_pairs={{0,4},{1,5},{2,6},{3,7},{4,0},{5,1},{6,2},{7,3},{8,12},{9,13},{10,... | collective-permute-start | bytes 122888 | tf_op jit(solution)/shard_map/ppermute | solution.py:271
  5.9 4.8 %collective-permute-start.2 = (bf16[32,640]{1,0:T(8,128)(2,1)S(1)}, bf16[32,640]{1,0:T(8,128)(2,1)S(1)}, u32[]{:S(2)}, u32[]{:S(2)}) collective-permute-start(bf16[32,640]{1,0:T(8,128)(2,1)S(1)} %get-tuple-element.32), channel_id=1, source_target_pairs={{0,12},{1,13},{2,14},{3,15},{4,8},{5,9},{6,10},{7,11},{8,4},{9,5},... | collective-permute-start | bytes 122888 | tf_op jit(solution)/shard_map/ppermute | solution.py:271
  11.4 4.2 %collective-permute-start.3 = (bf16[2,2,32,640]{3,2,1,0:T(8,128)(2,1)S(1)}, bf16[2,2,32,640]{3,2,1,0:T(8,128)(2,1)S(1)}, u32[]{:S(2)}, u32[]{:S(2)}) collective-permute-start(bf16[2,2,32,640]{3,2,1,0:T(8,128)(2,1)S(1)} %broadcast_select_fusion), channel_id=1, source_target_pairs={{0,2},{1,3},{2,0},{3,1},{4,6},{5,7},{6,4},{7,5},{8,10},{9,11},{10,... | collective-permute-start | bytes 491528 | tf_op jit(solution)/shard_map/ppermute | solution.py:279
  15.7 5.1 %copy-start.2 = (bf16[2,2,2,32,640]{4,3,2,1,0:T(8,128)(2,1)}, bf16[2,2,2,32,640]{4,3,2,1,0:T(8,128)(2,1)S(1)}, u32[]{:S(2)}) copy-start(bf16[2,2,2,32,640]{4,3,2,1,0:T(8,128)(2,1)S(1)} %maximum_select_fusion) | copy-start | bytes 983044
  15.7 4.7 %collective-permute-start.4 = (bf16[2,2,2,32,640]{4,3,2,1,0:T(8,128)(2,1)S(1)}, bf16[2,2,2,32,640]{4,3,2,1,0:T(8,128)(2,1)S(1)}, u32[]{:S(2)}, u32[]{:S(2)}) collective-permute-start(bf16[2,2,2,32,640]{4,3,2,1,0:T(8,128)(2,1)S(1)} %maximum_select_fusion), channel_id=1, source_target_pairs={{0,1},{1,0},{2,3},{3,2},{4,5},{5,4},{6,7},{7,6},{8,9},{9,8},{10,11... | collective-permute-start | bytes 983048 | tf_op jit(solution)/shard_map/ppermute | solution.py:279
  20.5 0.7 %copy-start.4 = (bf16[2,2,2,32,640]{4,3,2,1,0:T(8,128)(2,1)}, bf16[2,2,2,32,640]{4,3,2,1,0:T(8,128)(2,1)S(1)}, u32[]{:S(2)}) copy-start(bf16[2,2,2,32,640]{4,3,2,1,0:T(8,128)(2,1)S(1)} %collective-permute-done.4) | copy-start | bytes 983044
  25.0 5.3 %copy-start.7 = (bf16[3,3,3,8]{3,2,1,0:T(4,128)(2,1)S(1)}, bf16[3,3,3,8]{3,2,1,0:T(4,128)(2,1)}, u32[]{:S(2)}) copy-start(bf16[3,3,3,8]{3,2,1,0:T(4,128)(2,1)} %param.19) | copy-start | bytes 1300
  25.0 19.4 %all-to-all-start = ((bf16[16,32,512]{2,1,0:T(8,128)(2,1)}), bf16[16,32,512]{2,1,0:T(8,128)(2,1)S(1)}, u32[]{:S(2)}, u32[]{:S(2)}) async-start(bf16[16,32,512]{2,1,0:T(8,128)(2,1)} %bitcast.62), calls=%async_computation | async-start | bytes 1048576 | tf_op jit(solution)/shard_map/all_to_all | solution.py:338
  45.0 10.6 %copy-start.1 = (bf16[66,8,512]{2,1,0:T(8,128)(2,1)}, bf16[66,8,512]{2,1,0:T(8,128)(2,1)S(1)}, u32[]{:S(2)}) copy-start(bf16[66,8,512]{2,1,0:T(8,128)(2,1)S(1)} %copy.46) | copy-start | bytes 1622020
  45.1 7.8 %collective-permute-start.6 = (bf16[528,256]{1,0:T(8,128)(2,1)S(1)}, bf16[528,256]{1,0:T(8,128)(2,1)S(1)}, u32[]{:S(2)}, u32[]{:S(2)}) collective-permute-start(bf16[528,256]{1,0:T(8,128)(2,1)S(1)} %get-tuple-element.29), channel_id=1, source_target_pairs={{1,0},{2,1},{3,2},{4,3},{5,4},{6,5},{7,6},{8,7},{9,8},{10,9},{11,1... | collective-permute-start | bytes 811016 | tf_op jit(solution)/shard_map/ppermute | solution.py:372
  47.5 8.1 %collective-permute-start.5 = (bf16[528,256]{1,0:T(8,128)(2,1)S(1)}, bf16[528,256]{1,0:T(8,128)(2,1)S(1)}, u32[]{:S(2)}, u32[]{:S(2)}) collective-permute-start(bf16[528,256]{1,0:T(8,128)(2,1)S(1)} %get-tuple-element.30), channel_id=1, source_target_pairs={{0,1},{1,2},{2,3},{3,4},{4,5},{5,6},{6,7},{7,8},{8,9},{9,10},{10,1... | collective-permute-start | bytes 811016 | tf_op jit(solution)/shard_map/ppermute | solution.py:371
  52.9 2.8 %copy-start.5 = (bf16[528,256]{1,0:T(8,128)(2,1)}, bf16[528,256]{1,0:T(8,128)(2,1)S(1)}, u32[]{:S(2)}) copy-start(bf16[528,256]{1,0:T(8,128)(2,1)S(1)} %collective-permute-done.6.high_ref) | copy-start | bytes 811012
  55.6 0.7 %copy-start.6 = (bf16[528,256]{1,0:T(8,128)(2,1)}, bf16[528,256]{1,0:T(8,128)(2,1)S(1)}, u32[]{:S(2)}) copy-start(bf16[528,256]{1,0:T(8,128)(2,1)S(1)} %collective-permute-done.5.low_ref) | copy-start | bytes 811012
